TPU v7x, 32 devices: a whole 2x2x4 slice. The times are simulated.
32 devices in a mesh: sky: 8 (over z, y), los: 4 (over x, core).
Axes of the slice: x: 2, y: 2, z: 4, core: 2. Of those that a mesh axis runs over, the one named last changes fastest.
Arguments:
- features: bfloat16 [32, 16, 32, 128], P(None, 'sky', 'los'), may hold values from -6 to 6
- pre_first: bfloat16 [32, 16, 32, 128], P(None, 'sky', 'los'), may hold values from -8 to 8
- pre_second: bfloat16 [32, 16, 32, 128], P(None, 'sky', 'los'), may hold values from -8 to 8
- w_first: bfloat16 [3, 3, 3, 32, 32], replicated, may hold values from -0.21875 to 0.21875
- w_second: bfloat16 [3, 3, 3, 32, 32], replicated, may hold values from -0.21875 to 0.21875
- w_out: bfloat16 [3, 32], replicated, may hold values from -1 to 1
- b_out: float32 [3], replicated, may hold values from -1 to 1
- y_target: float32 [16, 128], P('sky'), may hold values from -6 to 6
- k_target: float32 [16, 128], P('sky'), may hold values from -6 to 6
Outputs:
- grad_features: bfloat16 [32, 16, 32, 128], P(None, 'sky', 'los')
- grad_first: float32 [3, 3, 3, 32, 32], replicated
- grad_second: float32 [3, 3, 3, 32, 32], replicated
- grad_out: float32 [3, 32], replicated
- grad_bias: float32 [3], replicated
All inputs are finite; a program needn't handle non-finite values.
Results may differ from a plain program's by a relative error of at most 0.0067.
Values may be sent and summed in bfloat16 or wider, within the bound.
No kernel may reach another device: no remote copies, remote signals or barrier semaphores. Data moves between devices by JAX's collectives and lax.ppermute only.
A program may use at most 64 MiB of HBM per device.

v0:
```python
import math

import jax
import jax.numpy as jnp
from jax import lax
from jax.sharding import PartitionSpec as P


def extended(block, sides, width):
    for axis, dim in sides:
        count = lax.axis_size(axis)
        forward = [(i, i + 1) for i in range(count - 1)]
        forward.append((count - 1, 0))
        backward = [(target, source) for source, target in forward]
        low = lax.ppermute(
            lax.slice_in_dim(block, block.shape[dim] - width, None, axis=dim), axis, forward
        )
        high = lax.ppermute(lax.slice_in_dim(block, 0, width, axis=dim), axis, backward)
        block = jnp.concatenate([low, block, high], axis=dim)
    return block


def butterfly_sum(value, axes):
    for axis in axes:
        count = lax.axis_size(axis)
        if count & (count - 1):
            value = lax.psum(value, axis)
            continue
        step = 1
        while step < count:
            pairs = [(i, i ^ step) for i in range(count)]
            value = value + lax.ppermute(value, axis, pairs)
            step *= 2
    return value


def pack_rows(parts):
    flat = jnp.concatenate([part.reshape(-1) for part in parts])
    rows = -(-flat.shape[0] // 128)
    flat = jnp.pad(flat, (0, rows * 128 - flat.shape[0]))
    return flat.reshape(rows, 128)


def unpack_rows(packed, shapes):
    flat = packed.reshape(-1)
    parts = []
    start = 0
    for shape in shapes:
        size = math.prod(shape)
        parts.append(flat[start : start + size].reshape(shape))
        start += size
    return parts


def silu_slope(value):
    sigma = jax.nn.sigmoid(value)
    return sigma * (1.0 + value * (1.0 - sigma))


def wrap_columns(field):
    return jnp.concatenate((field[..., -1:], field, field[..., :1]), axis=-1)


def spread_local(weight, padded, shape):
    kernel = jnp.transpose(weight[::-1, ::-1, ::-1], (4, 3, 0, 1, 2))
    return lax.conv_general_dilated(
        padded[None],
        kernel,
        (1, 1, 1),
        "VALID",
        dimension_numbers=("NCDHW", "OIDHW", "NCDHW"),
        preferred_element_type=jnp.float32,
    )[0]


def taps_from_inputs(grad_field, padded_inputs):
    shape = grad_field.shape
    taps_list = []
    for tap_x in range(3):
        for tap_z in range(3):
            for tap_y in range(3):
                window = padded_inputs[
                    :, tap_x : tap_x + shape[1], tap_z : tap_z + shape[2], tap_y : tap_y + shape[3]
                ]
                taps_list.append(
                    jnp.einsum(
                        "oxzy,ixzy->oi", grad_field, window, preferred_element_type=jnp.float32
                    )
                )
    return jnp.stack(taps_list).reshape(3, 3, 3, shape[0], padded_inputs.shape[0])


def per_device(
    features, pre_first, pre_second, w_first, w_second, w_out, b_out, y_target, k_target
):
    count_sky = lax.axis_size("sky")
    count_los = lax.axis_size("los")
    depth_all = pre_first.shape[2] * count_los
    norm_factor = 1.0 / math.sqrt(features.shape[1] * count_sky * features.shape[3] * depth_all)
    shape = features.shape
    first_wide = pre_first.astype(jnp.float32)
    second_wide = pre_second.astype(jnp.float32)
    hidden_second = jax.nn.silu(second_wide).astype(jnp.bfloat16)
    heads_raw = jnp.einsum(
        "oi,ixzy->oxzy", w_out, hidden_second, preferred_element_type=jnp.float32
    )
    heads_raw = heads_raw + b_out[:, None, None, None]
    pressure = jax.nn.softplus(heads_raw[0])
    density = jax.nn.softplus(heads_raw[1])
    velocity = heads_raw[2]
    y_part = jnp.sum(pressure, axis=1) / depth_all
    k_part = -jnp.sum(density * velocity, axis=1) / depth_all
    y_map, k_map = butterfly_sum(jnp.stack((y_part, k_part)), ("los",))
    y_resid = y_map - y_target
    k_resid = k_map - k_target
    y_resid = y_resid[:, None, :]
    k_resid = k_resid[:, None, :]
    head_grad = jnp.stack(
        (
            y_resid * jax.nn.sigmoid(heads_raw[0]),
            -k_resid * velocity * jax.nn.sigmoid(heads_raw[1]),
            -k_resid * density,
        )
    ).astype(jnp.bfloat16)
    grad_out = (
        jnp.einsum("oxzy,ixzy->oi", head_grad, hidden_second, preferred_element_type=jnp.float32)
        * norm_factor
    )
    grad_bias = jnp.sum(head_grad.astype(jnp.float32), axis=(1, 2, 3)) * norm_factor
    back_second = jnp.einsum("oi,oxzy->ixzy", w_out, head_grad, preferred_element_type=jnp.float32)
    grad_second_pre = (back_second * silu_slope(second_wide)).astype(jnp.bfloat16)
    second_padded = wrap_columns(extended(grad_second_pre, (("sky", 1), ("los", 2)), 1))
    back_first = spread_local(w_second, second_padded, shape)
    grad_first_pre = (back_first * silu_slope(first_wide)).astype(jnp.bfloat16)
    first_padded = wrap_columns(extended(grad_first_pre, (("sky", 1), ("los", 2)), 1))
    grad_features = spread_local(w_first, first_padded, shape).astype(jnp.bfloat16)
    saved_padded = wrap_columns(
        extended(jnp.stack((features, pre_first)), (("sky", 2), ("los", 3)), 1)
    )
    hidden_padded = jax.nn.silu(saved_padded[1].astype(jnp.float32)).astype(jnp.bfloat16)
    grad_second = taps_from_inputs(grad_second_pre, hidden_padded)
    grad_first = taps_from_inputs(grad_first_pre, saved_padded[0])
    early = (grad_second * norm_factor, grad_out, grad_bias)
    early_shapes = [part.shape for part in early]
    grad_second, grad_out, grad_bias = unpack_rows(
        butterfly_sum(pack_rows(early), ("los", "sky")), early_shapes
    )
    (grad_first,) = unpack_rows(
        butterfly_sum(pack_rows((grad_first * norm_factor,)), ("los", "sky")), [grad_first.shape]
    )
    return (grad_features, grad_first, grad_second, grad_out, grad_bias)


def solution(mesh):
    in_specs = (
        P(None, "sky", "los", None),
        P(None, "sky", "los", None),
        P(None, "sky", "los", None),
        P(),
        P(),
        P(),
        P(),
        P("sky", None),
        P("sky", None),
    )
    out_specs = (P(None, "sky", "los", None), P(), P(), P(), P())
    return jax.shard_map(
        per_device, mesh=mesh, in_specs=in_specs, out_specs=out_specs, check_vma=False
    )
```

profile of v0, /device:TPU:0, one launch (start us, length us, event | category | flops | bytes accessed | tf_op | source)
XLA Modules:
  0.0 89.1 jit_solution(9824571850576005771)
XLA Ops:
  0.7 1.1 %fusion.98 = bf16[32,2,8,128]{3,0,2,1:T(8,128)(2,1)S(1)} fusion(bf16[32,2,8,128]{3,2,1,0:T(8,128)(2,1)} %param.11), kind=kLoop, calls=%fused_computation.163 | loop fusion | flops 393216 | bytes 262144 | tf_op jit(solution)/shard_map/convert_element_type | solution.py:103
  5.8 2.6 %collective-permute-start.1 = (f32[2,2,128]{2,1,0:T(2,128)S(1)}, f32[2,2,128]{2,1,0:T(2,128)S(1)}, u32[]{:S(2)}, u32[]{:S(2)}) collective-permute-start(f32[2,2,128]{2,1,0:T(2,128)S(1)} %fusion.184), channel_id=1, source_target_pairs={{0,2},{1,3},{2,0},{3,1},{4,6},{5,7},{6,4},{7,5},{8,10},{9,11},{10,... | collective-permute-start | bytes 6152 | tf_op jit(solution)/shard_map/ppermute | solution.py:32
  8.4 4.6 %collective-permute-start.11 = (bf16[2,32,1,8,128]{4,1,3,2,0:T(8,128)(2,1)S(1)}, bf16[2,32,1,8,128]{4,1,3,2,0:T(8,128)(2,1)S(1)}, u32[]{:S(2)}, u32[]{:S(2)}) collective-permute-start(bf16[2,32,1,8,128]{4,1,3,2,0:T(8,128)(2,1)S(1)} %get-tuple-element.28), channel_id=1, source_target_pairs={{4,0},{8,4},{12,8},{16,12},{20,16},{24,20},{28,24},{0,28},{5,1},{9... | collective-permute-start | bytes 393224 | tf_op jit(solution)/shard_map/ppermute | solution.py:18
  13.5 4.8 %collective-permute-start.3 = (bf16[32,1,8,128]{3,0,2,1:T(8,128)(2,1)S(1)}, bf16[32,1,8,128]{3,0,2,1:T(8,128)(2,1)S(1)}, u32[]{:S(2)}, u32[]{:S(2)}) collective-permute-start(bf16[32,1,8,128]{3,0,2,1:T(8,128)(2,1)S(1)} %get-tuple-element.36), channel_id=1, source_target_pairs={{4,0},{8,4},{12,8},{16,12},{20,16},{24,20},{28,24},{0,28},{5,1},{9... | collective-permute-start | bytes 196616 | tf_op jit(solution)/shard_map/ppermute | solution.py:18
  18.4 1.8 %collective-permute-done.3 = bf16[32,1,8,128]{3,0,2,1:T(8,128)(2,1)S(1)} collective-permute-done((bf16[32,1,8,128]{3,0,2,1:T(8,128)(2,1)S(1)}, bf16[32,1,8,128]{3,0,2,1:T(8,128)(2,1)S(1)}, u32[]{:S(2)}, u32[]{:S(2)}) %collective-permute-start.3) | collective-permute-done | bytes 65568 | tf_op jit(solution)/shard_map/ppermute | solution.py:18
  20.1 5.1 %collective-permute-done.2 = bf16[32,1,8,128]{3,0,2,1:T(8,128)(2,1)S(1)} collective-permute-done((bf16[32,1,8,128]{3,0,2,1:T(8,128)(2,1)S(1)}, bf16[32,1,8,128]{3,0,2,1:T(8,128)(2,1)S(1)}, u32[]{:S(2)}, u32[]{:S(2)}) %collective-permute-start.2) | collective-permute-done | bytes 65568 | tf_op jit(solution)/shard_map/ppermute | solution.py:15
  25.9 1.2 %collective-permute-done.5 = bf16[32,4,1,128]{3,0,2,1:T(8,128)(2,1)S(1)} collective-permute-done((bf16[32,4,1,128]{3,0,2,1:T(8,128)(2,1)S(1)}, bf16[32,4,1,128]{3,0,2,1:T(8,128)(2,1)S(1)}, u32[]{:S(2)}, u32[]{:S(2)}) %collective-permute-start.5) | collective-permute-done | bytes 32800 | tf_op jit(solution)/shard_map/ppermute | solution.py:18
  27.0 1.6 %collective-permute-done.4 = bf16[32,4,1,128]{3,0,2,1:T(8,128)(2,1)S(1)} collective-permute-done((bf16[32,4,1,128]{3,0,2,1:T(8,128)(2,1)S(1)}, bf16[32,4,1,128]{3,0,2,1:T(8,128)(2,1)S(1)}, u32[]{:S(2)}, u32[]{:S(2)}) %collective-permute-start.4) | collective-permute-done | bytes 32800 | tf_op jit(solution)/shard_map/ppermute | solution.py:15
  29.3 2.1 %copy.111 = bf16[32,4,10,1,130]{0,1,4,2,3:T(4,128)(2,1)S(1)} copy(bf16[32,4,10,1,130]{4,0,2,1,3:T(8,128)(2,1)S(1)} %maximum_bitcast_fusion) | data formatting | bytes 665600
  32.8 1.8 %fusion.19 = f32[2,8,8,17,32]{4,2,3,1,0:T(8,128)S(1)} fusion(bf16[3,3,3,32,32]{4,3,2,1,0:T(8,128)(2,1)S(1)} %copy-done, bf16[32,4,10,1,7,2]{0,4,5,2,1,3:T(8,128)(2,1)S(1)} %slice.338, bf16[32,4,10,1,8,17]{0,4,5,2,1,3:T(8,128)(2,1)S(1)} %copy.42, pred[8,17]{0,1:T(8,128)(4,1)S(1)} %copy-done.7), kind=kOutput, calls=%fused_computation.18 | convolution fusion | flops 121561088 | bytes 717960 | tf_op jit(solution)/shard_map/conv_general_dilated | solution.py:66
  35.9 2.0 %collective-permute-start.6 = (bf16[32,1,8,128]{3,0,2,1:T(8,128)(2,1)S(1)}, bf16[32,1,8,128]{3,0,2,1:T(8,128)(2,1)S(1)}, u32[]{:S(2)}, u32[]{:S(2)}) collective-permute-start(bf16[32,1,8,128]{3,0,2,1:T(8,128)(2,1)S(1)} %get-tuple-element.33), channel_id=1, source_target_pairs={{0,4},{4,8},{8,12},{12,16},{16,20},{20,24},{24,28},{28,0},{1,5},{5... | collective-permute-start | bytes 196616 | tf_op jit(solution)/shard_map/ppermute | solution.py:15
  38.5 1.7 %collective-permute-done.7 = bf16[32,1,8,128]{3,0,2,1:T(8,128)(2,1)S(1)} collective-permute-done((bf16[32,1,8,128]{3,0,2,1:T(8,128)(2,1)S(1)}, bf16[32,1,8,128]{3,0,2,1:T(8,128)(2,1)S(1)}, u32[]{:S(2)}, u32[]{:S(2)}) %collective-permute-start.7) | collective-permute-done | bytes 65568 | tf_op jit(solution)/shard_map/ppermute | solution.py:18
  40.2 2.8 %collective-permute-done.6 = bf16[32,1,8,128]{3,0,2,1:T(8,128)(2,1)S(1)} collective-permute-done((bf16[32,1,8,128]{3,0,2,1:T(8,128)(2,1)S(1)}, bf16[32,1,8,128]{3,0,2,1:T(8,128)(2,1)S(1)}, u32[]{:S(2)}, u32[]{:S(2)}) %collective-permute-start.6) | collective-permute-done | bytes 65568 | tf_op jit(solution)/shard_map/ppermute | solution.py:15
  58.5 1.2 %collective-permute-start.15 = (f32[216,128]{1,0:T(8,128)S(1)}, f32[216,128]{1,0:T(8,128)S(1)}, u32[]{:S(2)}, u32[]{:S(2)}) collective-permute-start(f32[216,128]{1,0:T(8,128)S(1)} %add.99), channel_id=1, source_target_pairs={{0,2},{1,3},{2,0},{3,1},{4,6},{5,7},{6,4},{7,5},{8,10},{9,11},{10,... | collective-permute-start | bytes 331784 | tf_op jit(solution)/shard_map/ppermute | solution.py:32
  59.7 1.2 %collective-permute-start.20 = (f32[217,128]{1,0:T(8,128)S(1)}, f32[217,128]{1,0:T(8,128)S(1)}, u32[]{:S(2)}, u32[]{:S(2)}) collective-permute-start(f32[217,128]{1,0:T(8,128)S(1)} %fusion.185), channel_id=1, source_target_pairs={{0,2},{1,3},{2,0},{3,1},{4,6},{5,7},{6,4},{7,5},{8,10},{9,11},{10,... | collective-permute-start | bytes 333320 | tf_op jit(solution)/shard_map/ppermute | solution.py:32
  61.1 3.3 %collective-permute-done.15 = f32[216,128]{1,0:T(8,128)S(1)} collective-permute-done((f32[216,128]{1,0:T(8,128)S(1)}, f32[216,128]{1,0:T(8,128)S(1)}, u32[]{:S(2)}, u32[]{:S(2)}) %collective-permute-start.15) | collective-permute-done | bytes 110624 | tf_op jit(solution)/shard_map/ppermute | solution.py:32
  64.5 1.9 %collective-permute-done.20 = f32[217,128]{1,0:T(8,128)S(1)} collective-permute-done((f32[217,128]{1,0:T(8,128)S(1)}, f32[217,128]{1,0:T(8,128)S(1)}, u32[]{:S(2)}, u32[]{:S(2)}) %collective-permute-start.20) | collective-permute-done | bytes 111136 | tf_op jit(solution)/shard_map/ppermute | solution.py:32
  67.0 2.1 %copy.112 = bf16[32,4,10,1,130]{0,1,4,2,3:T(4,128)(2,1)S(1)} copy(bf16[32,4,10,1,130]{4,0,2,1,3:T(8,128)(2,1)S(1)} %maximum_bitcast_fusion.1) | data formatting | bytes 665600
  70.2 1.5 %collective-permute-done.21 = f32[217,128]{1,0:T(8,128)S(1)} collective-permute-done((f32[217,128]{1,0:T(8,128)S(1)}, f32[217,128]{1,0:T(8,128)S(1)}, u32[]{:S(2)}, u32[]{:S(2)}) %collective-permute-start.21) | collective-permute-done | bytes 111136 | tf_op jit(solution)/shard_map/ppermute | solution.py:32
  72.3 1.7 %fusion.22 = bf16[2,8,8,17,32]{4,2,3,1,0:T(8,128)(2,1)S(1)} fusion(bf16[3,3,3,32,32]{4,3,2,1,0:T(8,128)(2,1)S(1)} %copy-done.6, bf16[32,4,10,1,7,2]{0,4,5,2,1,3:T(8,128)(2,1)S(1)} %slice.344, bf16[32,4,10,1,8,17]{0,4,5,2,1,3:T(8,128)(2,1)S(1)} %copy.48, pred[8,17]{0,1:T(8,128)(4,1)S(1)} %copy-done.7), kind=kOutput, calls=%fused_computation.19 | convolution fusion | flops 121630720 | bytes 578696 | tf_op jit(solution)/shard_map/conv_general_dilated | solution.py:66
  74.1 1.9 %collective-permute-done.17 = f32[216,128]{1,0:T(8,128)S(1)} collective-permute-done((f32[216,128]{1,0:T(8,128)S(1)}, f32[216,128]{1,0:T(8,128)S(1)}, u32[]{:S(2)}, u32[]{:S(2)}) %collective-permute-start.17) | collective-permute-done | bytes 110624 | tf_op jit(solution)/shard_map/ppermute | solution.py:32
  76.1 1.8 %collective-permute-done.22 = f32[217,128]{1,0:T(8,128)S(1)} collective-permute-done((f32[217,128]{1,0:T(8,128)S(1)}, f32[217,128]{1,0:T(8,128)S(1)}, u32[]{:S(2)}, u32[]{:S(2)}) %collective-permute-start.22) | collective-permute-done | bytes 111136 | tf_op jit(solution)/shard_map/ppermute | solution.py:32
  78.0 1.1 %collective-permute-start.23 = (f32[217,128]{1,0:T(8,128)S(1)}, f32[217,128]{1,0:T(8,128)S(1)}, u32[]{:S(2)}, u32[]{:S(2)}) collective-permute-start(f32[217,128]{1,0:T(8,128)S(1)} %add.108), channel_id=1, source_target_pairs={{0,16},{4,20},{8,24},{12,28},{16,0},{20,4},{24,8},{28,12},{1,17},{... | collective-permute-start | bytes 333320 | tf_op jit(solution)/shard_map/ppermute | solution.py:32
  80.2 5.4 %collective-permute-done.18 = f32[216,128]{1,0:T(8,128)S(1)} collective-permute-done((f32[216,128]{1,0:T(8,128)S(1)}, f32[216,128]{1,0:T(8,128)S(1)}, u32[]{:S(2)}, u32[]{:S(2)}) %collective-permute-start.18) | collective-permute-done | bytes 110624 | tf_op jit(solution)/shard_map/ppermute | solution.py:32
  (167 shorter events, 31.7 us)
Async XLA Ops:
  3.4 2.4 %collective-permute-start = (f32[2,2,128]{2,1,0:T(2,128)S(1)}, f32[2,2,128]{2,1,0:T(2,128)S(1)}, u32[]{:S(2)}, u32[]{:S(2)}) collective-permute-start(f32[2,2,128]{2,1,0:T(2,128)S(1)} %pad_maximum_fusion.16), channel_id=1, source_target_pairs={{0,1},{1,0},{2,3},{3,2},{4,5},{5,4},{6,7},{7,6},{8,9},{9,8},{10,11... | collective-permute-start | bytes 6152 | tf_op jit(solution)/shard_map/ppermute | solution.py:32
  5.8 7.2 %collective-permute-start.1 = (f32[2,2,128]{2,1,0:T(2,128)S(1)}, f32[2,2,128]{2,1,0:T(2,128)S(1)}, u32[]{:S(2)}, u32[]{:S(2)}) collective-permute-start(f32[2,2,128]{2,1,0:T(2,128)S(1)} %fusion.184), channel_id=1, source_target_pairs={{0,2},{1,3},{2,0},{3,1},{4,6},{5,7},{6,4},{7,5},{8,10},{9,11},{10,... | collective-permute-start | bytes 6152 | tf_op jit(solution)/shard_map/ppermute | solution.py:32
  8.4 29.5 %collective-permute-start.11 = (bf16[2,32,1,8,128]{4,1,3,2,0:T(8,128)(2,1)S(1)}, bf16[2,32,1,8,128]{4,1,3,2,0:T(8,128)(2,1)S(1)}, u32[]{:S(2)}, u32[]{:S(2)}) collective-permute-start(bf16[2,32,1,8,128]{4,1,3,2,0:T(8,128)(2,1)S(1)} %get-tuple-element.28), channel_id=1, source_target_pairs={{4,0},{8,4},{12,8},{16,12},{20,16},{24,20},{28,24},{0,28},{5,1},{9... | collective-permute-start | bytes 393224 | tf_op jit(solution)/shard_map/ppermute | solution.py:18
  13.0 24.9 %collective-permute-start.10 = (bf16[2,32,1,8,128]{4,1,3,2,0:T(8,128)(2,1)S(1)}, bf16[2,32,1,8,128]{4,1,3,2,0:T(8,128)(2,1)S(1)}, u32[]{:S(2)}, u32[]{:S(2)}) collective-permute-start(bf16[2,32,1,8,128]{4,1,3,2,0:T(8,128)(2,1)S(1)} %get-tuple-element.27), channel_id=1, source_target_pairs={{0,4},{4,8},{8,12},{12,16},{16,20},{20,24},{24,28},{28,0},{1,5},{5... | collective-permute-start | bytes 393224 | tf_op jit(solution)/shard_map/ppermute | solution.py:15
  13.5 6.7 %collective-permute-start.3 = (bf16[32,1,8,128]{3,0,2,1:T(8,128)(2,1)S(1)}, bf16[32,1,8,128]{3,0,2,1:T(8,128)(2,1)S(1)}, u32[]{:S(2)}, u32[]{:S(2)}) collective-permute-start(bf16[32,1,8,128]{3,0,2,1:T(8,128)(2,1)S(1)} %get-tuple-element.36), channel_id=1, source_target_pairs={{4,0},{8,4},{12,8},{16,12},{20,16},{24,20},{28,24},{0,28},{5,1},{9... | collective-permute-start | bytes 196616 | tf_op jit(solution)/shard_map/ppermute | solution.py:18
  18.2 7.0 %collective-permute-start.2 = (bf16[32,1,8,128]{3,0,2,1:T(8,128)(2,1)S(1)}, bf16[32,1,8,128]{3,0,2,1:T(8,128)(2,1)S(1)}, u32[]{:S(2)}, u32[]{:S(2)}) collective-permute-start(bf16[32,1,8,128]{3,0,2,1:T(8,128)(2,1)S(1)} %get-tuple-element.35), channel_id=1, source_target_pairs={{0,4},{4,8},{8,12},{12,16},{16,20},{20,24},{24,28},{28,0},{1,5},{5... | collective-permute-start | bytes 196616 | tf_op jit(solution)/shard_map/ppermute | solution.py:15
  25.2 1.8 %collective-permute-start.5 = (bf16[32,4,1,128]{3,0,2,1:T(8,128)(2,1)S(1)}, bf16[32,4,1,128]{3,0,2,1:T(8,128)(2,1)S(1)}, u32[]{:S(2)}, u32[]{:S(2)}) collective-permute-start(bf16[32,4,1,128]{3,0,2,1:T(8,128)(2,1)S(1)} %get-tuple-element.32), channel_id=1, source_target_pairs={{1,0},{2,1},{3,2},{0,3},{5,4},{6,5},{7,6},{4,7},{9,8},{10,9},{11,1... | collective-permute-start | bytes 98312 | tf_op jit(solution)/shard_map/ppermute | solution.py:18
  25.3 3.4 %collective-permute-start.4 = (bf16[32,4,1,128]{3,0,2,1:T(8,128)(2,1)S(1)}, bf16[32,4,1,128]{3,0,2,1:T(8,128)(2,1)S(1)}, u32[]{:S(2)}, u32[]{:S(2)}) collective-permute-start(bf16[32,4,1,128]{3,0,2,1:T(8,128)(2,1)S(1)} %get-tuple-element.31), channel_id=1, source_target_pairs={{0,1},{1,2},{2,3},{3,0},{4,5},{5,6},{6,7},{7,4},{8,9},{9,10},{10,1... | collective-permute-start | bytes 98312 | tf_op jit(solution)/shard_map/ppermute | solution.py:15
  35.8 4.3 %collective-permute-start.7 = (bf16[32,1,8,128]{3,0,2,1:T(8,128)(2,1)S(1)}, bf16[32,1,8,128]{3,0,2,1:T(8,128)(2,1)S(1)}, u32[]{:S(2)}, u32[]{:S(2)}) collective-permute-start(bf16[32,1,8,128]{3,0,2,1:T(8,128)(2,1)S(1)} %get-tuple-element.34), channel_id=1, source_target_pairs={{4,0},{8,4},{12,8},{16,12},{20,16},{24,20},{28,24},{0,28},{5,1},{9... | collective-permute-start | bytes 196616 | tf_op jit(solution)/shard_map/ppermute | solution.py:18
  35.9 7.0 %collective-permute-start.6 = (bf16[32,1,8,128]{3,0,2,1:T(8,128)(2,1)S(1)}, bf16[32,1,8,128]{3,0,2,1:T(8,128)(2,1)S(1)}, u32[]{:S(2)}, u32[]{:S(2)}) collective-permute-start(bf16[32,1,8,128]{3,0,2,1:T(8,128)(2,1)S(1)} %get-tuple-element.33), channel_id=1, source_target_pairs={{0,4},{4,8},{8,12},{12,16},{16,20},{20,24},{24,28},{28,0},{1,5},{5... | collective-permute-start | bytes 196616 | tf_op jit(solution)/shard_map/ppermute | solution.py:15
  38.0 5.6 %collective-permute-start.13 = (bf16[2,32,4,1,128]{4,1,3,2,0:T(8,128)(2,1)S(1)}, bf16[2,32,4,1,128]{4,1,3,2,0:T(8,128)(2,1)S(1)}, u32[]{:S(2)}, u32[]{:S(2)}) collective-permute-start(bf16[2,32,4,1,128]{4,1,3,2,0:T(8,128)(2,1)S(1)} %get-tuple-element.22), channel_id=1, source_target_pairs={{1,0},{2,1},{3,2},{0,3},{5,4},{6,5},{7,6},{4,7},{9,8},{10,9},{11,1... | collective-permute-start | bytes 196616 | tf_op jit(solution)/shard_map/ppermute | solution.py:18
  38.0 5.5 %collective-permute-start.12 = (bf16[2,32,4,1,128]{4,1,3,2,0:T(8,128)(2,1)S(1)}, bf16[2,32,4,1,128]{4,1,3,2,0:T(8,128)(2,1)S(1)}, u32[]{:S(2)}, u32[]{:S(2)}) collective-permute-start(bf16[2,32,4,1,128]{4,1,3,2,0:T(8,128)(2,1)S(1)} %get-tuple-element.21), channel_id=1, source_target_pairs={{0,1},{1,2},{2,3},{3,0},{4,5},{5,6},{6,7},{7,4},{8,9},{9,10},{10,1... | collective-permute-start | bytes 196616 | tf_op jit(solution)/shard_map/ppermute | solution.py:15
  42.9 15.4 %collective-permute-start.9 = (bf16[32,4,1,128]{3,0,2,1:T(8,128)(2,1)S(1)}, bf16[32,4,1,128]{3,0,2,1:T(8,128)(2,1)S(1)}, u32[]{:S(2)}, u32[]{:S(2)}) collective-permute-start(bf16[32,4,1,128]{3,0,2,1:T(8,128)(2,1)S(1)} %get-tuple-element.30), channel_id=1, source_target_pairs={{1,0},{2,1},{3,2},{0,3},{5,4},{6,5},{7,6},{4,7},{9,8},{10,9},{11,1... | collective-permute-start | bytes 98312 | tf_op jit(solution)/shard_map/ppermute | solution.py:18
  43.0 15.4 %collective-permute-start.8 = (bf16[32,4,1,128]{3,0,2,1:T(8,128)(2,1)S(1)}, bf16[32,4,1,128]{3,0,2,1:T(8,128)(2,1)S(1)}, u32[]{:S(2)}, u32[]{:S(2)}) collective-permute-start(bf16[32,4,1,128]{3,0,2,1:T(8,128)(2,1)S(1)} %get-tuple-element.29), channel_id=1, source_target_pairs={{0,1},{1,2},{2,3},{3,0},{4,5},{5,6},{6,7},{7,4},{8,9},{9,10},{10,1... | collective-permute-start | bytes 98312 | tf_op jit(solution)/shard_map/ppermute | solution.py:15
  51.3 7.2 %collective-permute-start.14 = (f32[216,128]{1,0:T(8,128)S(1)}, f32[216,128]{1,0:T(8,128)S(1)}, u32[]{:S(2)}, u32[]{:S(2)}) collective-permute-start(f32[216,128]{1,0:T(8,128)S(1)} %mul.96), channel_id=1, source_target_pairs={{0,1},{1,0},{2,3},{3,2},{4,5},{5,4},{6,7},{7,6},{8,9},{9,8},{10,11... | collective-permute-start | bytes 331784 | tf_op jit(solution)/shard_map/ppermute | solution.py:32
  58.3 1.4 %collective-permute-start.19 = (f32[217,128]{1,0:T(8,128)S(1)}, f32[217,128]{1,0:T(8,128)S(1)}, u32[]{:S(2)}, u32[]{:S(2)}) collective-permute-start(f32[217,128]{1,0:T(8,128)S(1)} %pad_bitcast_fusion), channel_id=1, source_target_pairs={{0,1},{1,0},{2,3},{3,2},{4,5},{5,4},{6,7},{7,6},{8,9},{9,8},{10,11... | collective-permute-start | bytes 333320 | tf_op jit(solution)/shard_map/ppermute | solution.py:32
  58.5 5.9 %collective-permute-start.15 = (f32[216,128]{1,0:T(8,128)S(1)}, f32[216,128]{1,0:T(8,128)S(1)}, u32[]{:S(2)}, u32[]{:S(2)}) collective-permute-start(f32[216,128]{1,0:T(8,128)S(1)} %add.99), channel_id=1, source_target_pairs={{0,2},{1,3},{2,0},{3,1},{4,6},{5,7},{6,4},{7,5},{8,10},{9,11},{10,... | collective-permute-start | bytes 331784 | tf_op jit(solution)/shard_map/ppermute | solution.py:32
  59.7 6.7 %collective-permute-start.20 = (f32[217,128]{1,0:T(8,128)S(1)}, f32[217,128]{1,0:T(8,128)S(1)}, u32[]{:S(2)}, u32[]{:S(2)}) collective-permute-start(f32[217,128]{1,0:T(8,128)S(1)} %fusion.185), channel_id=1, source_target_pairs={{0,2},{1,3},{2,0},{3,1},{4,6},{5,7},{6,4},{7,5},{8,10},{9,11},{10,... | collective-permute-start | bytes 333320 | tf_op jit(solution)/shard_map/ppermute | solution.py:32
  64.4 5.7 %collective-permute-start.16 = (f32[216,128]{1,0:T(8,128)S(1)}, f32[216,128]{1,0:T(8,128)S(1)}, u32[]{:S(2)}, u32[]{:S(2)}) collective-permute-start(f32[216,128]{1,0:T(8,128)S(1)} %add.100), channel_id=1, source_target_pairs={{0,4},{4,0},{8,12},{12,8},{16,20},{20,16},{24,28},{28,24},{1,5},{5... | collective-permute-start | bytes 331784 | tf_op jit(solution)/shard_map/ppermute | solution.py:32
  66.5 5.2 %collective-permute-start.21 = (f32[217,128]{1,0:T(8,128)S(1)}, f32[217,128]{1,0:T(8,128)S(1)}, u32[]{:S(2)}, u32[]{:S(2)}) collective-permute-start(f32[217,128]{1,0:T(8,128)S(1)} %fusion.249), channel_id=1, source_target_pairs={{0,4},{4,0},{8,12},{12,8},{16,20},{20,16},{24,28},{28,24},{1,5},{5... | collective-permute-start | bytes 333320 | tf_op jit(solution)/shard_map/ppermute | solution.py:32
  70.1 5.9 %collective-permute-start.17 = (f32[216,128]{1,0:T(8,128)S(1)}, f32[216,128]{1,0:T(8,128)S(1)}, u32[]{:S(2)}, u32[]{:S(2)}) collective-permute-start(f32[216,128]{1,0:T(8,128)S(1)} %add.101), channel_id=1, source_target_pairs={{0,8},{4,12},{8,0},{12,4},{16,24},{20,28},{24,16},{28,20},{1,9},{5... | collective-permute-start | bytes 331784 | tf_op jit(solution)/shard_map/ppermute | solution.py:32
  71.7 6.2 %collective-permute-start.22 = (f32[217,128]{1,0:T(8,128)S(1)}, f32[217,128]{1,0:T(8,128)S(1)}, u32[]{:S(2)}, u32[]{:S(2)}) collective-permute-start(f32[217,128]{1,0:T(8,128)S(1)} %add.107), channel_id=1, source_target_pairs={{0,8},{4,12},{8,0},{12,4},{16,24},{20,28},{24,16},{28,20},{1,9},{5... | collective-permute-start | bytes 333320 | tf_op jit(solution)/shard_map/ppermute | solution.py:32
  76.0 9.6 %collective-permute-start.18 = (f32[216,128]{1,0:T(8,128)S(1)}, f32[216,128]{1,0:T(8,128)S(1)}, u32[]{:S(2)}, u32[]{:S(2)}) collective-permute-start(f32[216,128]{1,0:T(8,128)S(1)} %add.102), channel_id=1, source_target_pairs={{0,16},{4,20},{8,24},{12,28},{16,0},{20,4},{24,8},{28,12},{1,17},{... | collective-permute-start | bytes 331784 | tf_op jit(solution)/shard_map/ppermute | solution.py:32
  78.0 8.9 %collective-permute-start.23 = (f32[217,128]{1,0:T(8,128)S(1)}, f32[217,128]{1,0:T(8,128)S(1)}, u32[]{:S(2)}, u32[]{:S(2)}) collective-permute-start(f32[217,128]{1,0:T(8,128)S(1)} %add.108), channel_id=1, source_target_pairs={{0,16},{4,20},{8,24},{12,28},{16,0},{20,4},{24,8},{28,12},{1,17},{... | collective-permute-start | bytes 333320 | tf_op jit(solution)/shard_map/ppermute | solution.py:32
  (8 other events, 85.7 us)
where the time goes:
time: 89.4 us; the launch traced here: 89.1 us
  waiting for transfers between devices  30.3 us (34%)
  starting transfers between devices  21.5 us (24%)
  matrix products  16.5 us (18%)
  local copies, waits for them, and re-layouts  14.9 us (17%)
  other arithmetic  4.67 us (5%)
  between operations  1.21 us (1%)
    ppermute x12, waiting for transfers between devices, butterfly_sum(): value = value + lax.ppermute(value, axis, pairs)  16.3 us
    dot_general x54, matrix products, taps_from_inputs(): jnp.einsum('oxzy,ixzy->oi', grad_field, window, preferred_element_type=jn...  11.8 us
    ppermute x6, starting transfers between devices, extended(): lax.ppermute(lax.slice_in_dim(block, 0, width, axis=dim), axis, backward)  9.62 us
    ppermute x6, waiting for transfers between devices, extended(): lax.ppermute(lax.slice_in_dim(block, block.shape[dim] - width, None, axis...  9.45 us
    ppermute x12, starting transfers between devices, butterfly_sum(): value = value + lax.ppermute(value, axis, pairs)  8.42 us
    unnamed x22, local copies, waits for them, and re-layouts  8.37 us
    ppermute x6, waiting for transfers between devices, extended(): lax.ppermute(lax.slice_in_dim(block, 0, width, axis=dim), axis, backward)  4.6 us
    ppermute x6, starting transfers between devices, extended(): lax.ppermute(lax.slice_in_dim(block, block.shape[dim] - width, None, axis...  3.51 us
  transfers between devices with their start and end apart: 24, of which 13 were waited for; matrix products, arithmetic and copies ran while one was open for 34% of the time, Pallas kernels for 0%

commit v1 on v0

--- a/solution.py
+++ b/solution.py
@@ -20,13 +20,13 @@
     return block
 
 
-def butterfly_sum(value, axes):
+def butterfly_sum(value, axes, skip=0):
     for axis in axes:
         count = lax.axis_size(axis)
         if count & (count - 1):
             value = lax.psum(value, axis)
             continue
-        step = 1
+        step = 2 if skip and axis == axes[0] else 1
         while step < count:
             pairs = [(i, i ^ step) for i in range(count)]
             value = value + lax.ppermute(value, axis, pairs)
@@ -34,9 +34,26 @@
     return value
 
 
+def split_sum(value, axes):
+    first = axes[0]
+    if lax.axis_size(first) % 2:
+        return butterfly_sum(value, axes)
+    half = value.shape[0] // 2
+    pairs = [(i, i ^ 1) for i in range(lax.axis_size(first))]
+    upper = lax.axis_index(first) % 2 == 1
+    keep = jnp.where(upper, value[half:], value[:half])
+    send = jnp.where(upper, value[:half], value[half:])
+    keep = keep + lax.ppermute(send, first, pairs)
+    keep = butterfly_sum(keep, axes, skip=1)
+    other = lax.ppermute(keep, first, pairs)
+    return jnp.where(
+        upper, jnp.concatenate((other, keep)), jnp.concatenate((keep, other))
+    )
+
+
 def pack_rows(parts):
     flat = jnp.concatenate([part.reshape(-1) for part in parts])
-    rows = -(-flat.shape[0] // 128)
+    rows = -(-flat.shape[0] // 2048) * 16
     flat = jnp.pad(flat, (0, rows * 128 - flat.shape[0]))
     return flat.reshape(rows, 128)
 
@@ -143,10 +160,10 @@
     early = (grad_second * norm_factor, grad_out, grad_bias)
     early_shapes = [part.shape for part in early]
     grad_second, grad_out, grad_bias = unpack_rows(
-        butterfly_sum(pack_rows(early), ("los", "sky")), early_shapes
+        split_sum(pack_rows(early), ("los", "sky")), early_shapes
     )
     (grad_first,) = unpack_rows(
-        butterfly_sum(pack_rows((grad_first * norm_factor,)), ("los", "sky")), [grad_first.shape]
+        split_sum(pack_rows((grad_first * norm_factor,)), ("los", "sky")), [grad_first.shape]
     )
     return (grad_features, grad_first, grad_second, grad_out, grad_bias)
 

time: 89.4 us -> 86.5 us (0.968)
  waiting for transfers between devices: 30.3 us -> 22.7 us
  starting transfers between devices: 21.5 us -> 26 us
    ppermute x12 -> x10, waiting for transfers between devices: 16.3 us -> 6.45 us  [butterfly_sum(): value = value + lax.ppermute(value, axis, pairs)]
    ppermute x12 -> x10, starting transfers between devices: 8.42 us -> 11.8 us  [butterfly_sum(): value = value + lax.ppermute(value, axis, pairs)]
    ppermute x0 -> x4, waiting for transfers between devices: none -> 2.16 us  [the longest x2 1.14 us: split_sum(): keep = keep + lax.ppermute(send, first, pairs)]
    ppermute x0 -> x4, starting transfers between devices: none -> 1.01 us  [the longest x2 0.87 us: split_sum(): keep = keep + lax.ppermute(send, first, pairs)]
    another operation x1 -> x0, local copies, waits for them, and re-layouts: 0.92 us -> none  [unpack_rows(): parts.append(flat[start:start + size].reshape(shape))]
    reshape x1 -> x2, local copies, waits for them, and re-layouts: 0.92 us -> 1.84 us  [unpack_rows(): parts.append(flat[start:start + size].reshape(shape))]
    unnamed x22 -> x24, local copies, waits for them, and re-layouts: 8.37 us -> 8.37 us
  transfers between devices with their start and end apart: 24 -> 26, of which waited for: 13 -> 14; matrix products, arithmetic and copies ran while one was open for 34% -> 34% of each run, Pallas kernels for 0% -> 0%
where the time goes in v1:
time: 86.5 us; the launch traced here: 86.2 us
  starting transfers between devices  26 us (30%)
  waiting for transfers between devices  22.7 us (26%)
  matrix products  16.4 us (19%)
  local copies, waits for them, and re-layouts  15.2 us (18%)
  other arithmetic  4.64 us (5%)
  between operations  1.28 us (1%)
    ppermute x10, starting transfers between devices, butterfly_sum(): value = value + lax.ppermute(value, axis, pairs)  11.8 us
    dot_general x54, matrix products, taps_from_inputs(): jnp.einsum('oxzy,ixzy->oi', grad_field, window, preferred_element_type=jn...  11.8 us
    ppermute x6, starting transfers between devices, extended(): lax.ppermute(lax.slice_in_dim(block, 0, width, axis=dim), axis, backward)  9.62 us
    ppermute x6, waiting for transfers between devices, extended(): lax.ppermute(lax.slice_in_dim(block, block.shape[dim] - width, None, axis...  9.45 us
    unnamed x24, local copies, waits for them, and re-layouts  8.37 us
    ppermute x10, waiting for transfers between devices, butterfly_sum(): value = value + lax.ppermute(value, axis, pairs)  6.45 us
    ppermute x6, waiting for transfers between devices, extended(): lax.ppermute(lax.slice_in_dim(block, 0, width, axis=dim), axis, backward)  4.6 us
    ppermute x6, starting transfers between devices, extended(): lax.ppermute(lax.slice_in_dim(block, block.shape[dim] - width, None, axis...  3.51 us
  transfers between devices with their start and end apart: 26, of which 14 were waited for; matrix products, arithmetic and copies ran while one was open for 34% of the time, Pallas kernels for 0%

profile of v1, /device:TPU:0, one launch (start us, length us, event | category | flops | bytes accessed | tf_op | source)
XLA Modules:
  0.0 86.2 jit_solution(1808472600457886399)
XLA Ops:
  0.7 1.1 %fusion.98 = bf16[32,2,8,128]{3,0,2,1:T(8,128)(2,1)S(1)} fusion(bf16[32,2,8,128]{3,2,1,0:T(8,128)(2,1)} %param.11), kind=kLoop, calls=%fused_computation.163 | loop fusion | flops 393216 | bytes 262144 | tf_op jit(solution)/shard_map/convert_element_type | solution.py:120
  5.8 2.6 %collective-permute-start.1 = (f32[2,2,128]{2,1,0:T(2,128)S(1)}, f32[2,2,128]{2,1,0:T(2,128)S(1)}, u32[]{:S(2)}, u32[]{:S(2)}) collective-permute-start(f32[2,2,128]{2,1,0:T(2,128)S(1)} %fusion.189), channel_id=1, source_target_pairs={{0,2},{1,3},{2,0},{3,1},{4,6},{5,7},{6,4},{7,5},{8,10},{9,11},{10,... | collective-permute-start | bytes 6152 | tf_op jit(solution)/shard_map/ppermute | solution.py:32
  8.4 4.6 %collective-permute-start.11 = (bf16[2,32,1,8,128]{4,1,3,2,0:T(8,128)(2,1)S(1)}, bf16[2,32,1,8,128]{4,1,3,2,0:T(8,128)(2,1)S(1)}, u32[]{:S(2)}, u32[]{:S(2)}) collective-permute-start(bf16[2,32,1,8,128]{4,1,3,2,0:T(8,128)(2,1)S(1)} %get-tuple-element.28), channel_id=1, source_target_pairs={{4,0},{8,4},{12,8},{16,12},{20,16},{24,20},{28,24},{0,28},{5,1},{9... | collective-permute-start | bytes 393224 | tf_op jit(solution)/shard_map/ppermute | solution.py:18
  13.5 4.8 %collective-permute-start.3 = (bf16[32,1,8,128]{3,0,2,1:T(8,128)(2,1)S(1)}, bf16[32,1,8,128]{3,0,2,1:T(8,128)(2,1)S(1)}, u32[]{:S(2)}, u32[]{:S(2)}) collective-permute-start(bf16[32,1,8,128]{3,0,2,1:T(8,128)(2,1)S(1)} %get-tuple-element.36), channel_id=1, source_target_pairs={{4,0},{8,4},{12,8},{16,12},{20,16},{24,20},{28,24},{0,28},{5,1},{9... | collective-permute-start | bytes 196616 | tf_op jit(solution)/shard_map/ppermute | solution.py:18
  18.4 1.8 %collective-permute-done.3 = bf16[32,1,8,128]{3,0,2,1:T(8,128)(2,1)S(1)} collective-permute-done((bf16[32,1,8,128]{3,0,2,1:T(8,128)(2,1)S(1)}, bf16[32,1,8,128]{3,0,2,1:T(8,128)(2,1)S(1)}, u32[]{:S(2)}, u32[]{:S(2)}) %collective-permute-start.3) | collective-permute-done | bytes 65568 | tf_op jit(solution)/shard_map/ppermute | solution.py:18
  20.1 5.1 %collective-permute-done.2 = bf16[32,1,8,128]{3,0,2,1:T(8,128)(2,1)S(1)} collective-permute-done((bf16[32,1,8,128]{3,0,2,1:T(8,128)(2,1)S(1)}, bf16[32,1,8,128]{3,0,2,1:T(8,128)(2,1)S(1)}, u32[]{:S(2)}, u32[]{:S(2)}) %collective-permute-start.2) | collective-permute-done | bytes 65568 | tf_op jit(solution)/shard_map/ppermute | solution.py:15
  25.9 1.2 %collective-permute-done.5 = bf16[32,4,1,128]{3,0,2,1:T(8,128)(2,1)S(1)} collective-permute-done((bf16[32,4,1,128]{3,0,2,1:T(8,128)(2,1)S(1)}, bf16[32,4,1,128]{3,0,2,1:T(8,128)(2,1)S(1)}, u32[]{:S(2)}, u32[]{:S(2)}) %collective-permute-start.5) | collective-permute-done | bytes 32800 | tf_op jit(solution)/shard_map/ppermute | solution.py:18
  27.0 1.6 %collective-permute-done.4 = bf16[32,4,1,128]{3,0,2,1:T(8,128)(2,1)S(1)} collective-permute-done((bf16[32,4,1,128]{3,0,2,1:T(8,128)(2,1)S(1)}, bf16[32,4,1,128]{3,0,2,1:T(8,128)(2,1)S(1)}, u32[]{:S(2)}, u32[]{:S(2)}) %collective-permute-start.4) | collective-permute-done | bytes 32800 | tf_op jit(solution)/shard_map/ppermute | solution.py:15
  29.3 2.1 %copy.111 = bf16[32,4,10,1,130]{0,1,4,2,3:T(4,128)(2,1)S(1)} copy(bf16[32,4,10,1,130]{4,0,2,1,3:T(8,128)(2,1)S(1)} %maximum_bitcast_fusion) | data formatting | bytes 665600
  32.8 1.7 %fusion.19 = f32[2,8,8,17,32]{4,2,3,1,0:T(8,128)S(1)} fusion(bf16[3,3,3,32,32]{4,3,2,1,0:T(8,128)(2,1)S(1)} %copy-done, bf16[32,4,10,1,7,2]{0,4,5,2,1,3:T(8,128)(2,1)S(1)} %slice.399, bf16[32,4,10,1,8,17]{0,4,5,2,1,3:T(8,128)(2,1)S(1)} %copy.42, pred[8,17]{0,1:T(8,128)(4,1)S(1)} %copy-done.8), kind=kOutput, calls=%fused_computation.18 | convolution fusion | flops 121561088 | bytes 717960 | tf_op jit(solution)/shard_map/conv_general_dilated | solution.py:83
  35.9 2.0 %collective-permute-start.6 = (bf16[32,1,8,128]{3,0,2,1:T(8,128)(2,1)S(1)}, bf16[32,1,8,128]{3,0,2,1:T(8,128)(2,1)S(1)}, u32[]{:S(2)}, u32[]{:S(2)}) collective-permute-start(bf16[32,1,8,128]{3,0,2,1:T(8,128)(2,1)S(1)} %get-tuple-element.33), channel_id=1, source_target_pairs={{0,4},{4,8},{8,12},{12,16},{16,20},{20,24},{24,28},{28,0},{1,5},{5... | collective-permute-start | bytes 196616 | tf_op jit(solution)/shard_map/ppermute | solution.py:15
  38.5 1.7 %collective-permute-done.7 = bf16[32,1,8,128]{3,0,2,1:T(8,128)(2,1)S(1)} collective-permute-done((bf16[32,1,8,128]{3,0,2,1:T(8,128)(2,1)S(1)}, bf16[32,1,8,128]{3,0,2,1:T(8,128)(2,1)S(1)}, u32[]{:S(2)}, u32[]{:S(2)}) %collective-permute-start.7) | collective-permute-done | bytes 65568 | tf_op jit(solution)/shard_map/ppermute | solution.py:18
  40.1 2.8 %collective-permute-done.6 = bf16[32,1,8,128]{3,0,2,1:T(8,128)(2,1)S(1)} collective-permute-done((bf16[32,1,8,128]{3,0,2,1:T(8,128)(2,1)S(1)}, bf16[32,1,8,128]{3,0,2,1:T(8,128)(2,1)S(1)}, u32[]{:S(2)}, u32[]{:S(2)}) %collective-permute-start.6) | collective-permute-done | bytes 65568 | tf_op jit(solution)/shard_map/ppermute | solution.py:15
  58.7 1.1 %collective-permute-done.20 = f32[112,128]{1,0:T(8,128)S(1)} collective-permute-done((f32[112,128]{1,0:T(8,128)S(1)}, f32[112,128]{1,0:T(8,128)S(1)}, u32[]{:S(2)}, u32[]{:S(2)}) %collective-permute-start.20) | collective-permute-done | bytes 57376 | tf_op jit(solution)/shard_map/ppermute | solution.py:46
  59.9 1.2 %collective-permute-start.21 = (f32[112,128]{1,0:T(8,128)S(1)}, f32[112,128]{1,0:T(8,128)S(1)}, u32[]{:S(2)}, u32[]{:S(2)}) collective-permute-start(f32[112,128]{1,0:T(8,128)S(1)} %select_add_fusion), channel_id=1, source_target_pairs={{0,2},{1,3},{2,0},{3,1},{4,6},{5,7},{6,4},{7,5},{8,10},{9,11},{10,... | collective-permute-start | bytes 172040 | tf_op jit(solution)/shard_map/ppermute | solution.py:32
  62.1 2.5 %collective-permute-done.21 = f32[112,128]{1,0:T(8,128)S(1)} collective-permute-done((f32[112,128]{1,0:T(8,128)S(1)}, f32[112,128]{1,0:T(8,128)S(1)}, u32[]{:S(2)}, u32[]{:S(2)}) %collective-permute-start.21) | collective-permute-done | bytes 57376 | tf_op jit(solution)/shard_map/ppermute | solution.py:32
  65.4 1.6 %collective-permute-start.16 = (f32[112,128]{1,0:T(8,128)S(1)}, f32[112,128]{1,0:T(8,128)S(1)}, u32[]{:S(2)}, u32[]{:S(2)}) collective-permute-start(f32[112,128]{1,0:T(8,128)S(1)} %add.108), channel_id=1, source_target_pairs={{0,4},{4,0},{8,12},{12,8},{16,20},{20,16},{24,28},{28,24},{1,5},{5... | collective-permute-start | bytes 172040 | tf_op jit(solution)/shard_map/ppermute | solution.py:32
  67.0 1.9 %collective-permute-done.22 = f32[112,128]{1,0:T(8,128)S(1)} collective-permute-done((f32[112,128]{1,0:T(8,128)S(1)}, f32[112,128]{1,0:T(8,128)S(1)}, u32[]{:S(2)}, u32[]{:S(2)}) %collective-permute-start.22) | collective-permute-done | bytes 57376 | tf_op jit(solution)/shard_map/ppermute | solution.py:32
  69.4 2.1 %copy.112 = bf16[32,4,10,1,130]{0,1,4,2,3:T(4,128)(2,1)S(1)} copy(bf16[32,4,10,1,130]{4,0,2,1,3:T(8,128)(2,1)S(1)} %maximum_bitcast_fusion.1) | data formatting | bytes 665600
  72.4 2.1 %collective-permute-start.17 = (f32[112,128]{1,0:T(8,128)S(1)}, f32[112,128]{1,0:T(8,128)S(1)}, u32[]{:S(2)}, u32[]{:S(2)}) collective-permute-start(f32[112,128]{1,0:T(8,128)S(1)} %add.109), channel_id=1, source_target_pairs={{0,8},{4,12},{8,0},{12,4},{16,24},{20,28},{24,16},{28,20},{1,9},{5... | collective-permute-start | bytes 172040 | tf_op jit(solution)/shard_map/ppermute | solution.py:32
  74.6 1.7 %fusion.22 = bf16[2,8,8,17,32]{4,2,3,1,0:T(8,128)(2,1)S(1)} fusion(bf16[3,3,3,32,32]{4,3,2,1,0:T(8,128)(2,1)S(1)} %copy-done.7, bf16[32,4,10,1,7,2]{0,4,5,2,1,3:T(8,128)(2,1)S(1)} %slice.405, bf16[32,4,10,1,8,17]{0,4,5,2,1,3:T(8,128)(2,1)S(1)} %copy.48, pred[8,17]{0,1:T(8,128)(4,1)S(1)} %copy-done.8), kind=kOutput, calls=%fused_computation.19 | convolution fusion | flops 121630720 | bytes 578696 | tf_op jit(solution)/shard_map/conv_general_dilated | solution.py:83
  76.7 2.7 %collective-permute-start.18 = (f32[112,128]{1,0:T(8,128)S(1)}, f32[112,128]{1,0:T(8,128)S(1)}, u32[]{:S(2)}, u32[]{:S(2)}) collective-permute-start(f32[112,128]{1,0:T(8,128)S(1)} %add.110), channel_id=1, source_target_pairs={{0,16},{4,20},{8,24},{12,28},{16,0},{20,4},{24,8},{28,12},{1,17},{... | collective-permute-start | bytes 172040 | tf_op jit(solution)/shard_map/ppermute | solution.py:32
  80.0 1.0 %copy.53 = bf16[32,2,8,128]{3,2,1,0:T(8,128)(2,1)} copy(bf16[32,2,8,128]{0,2,3,1:T(8,128)(2,1)S(1)} %slice_bitcast_fusion.2) | data formatting | bytes 262144
  82.1 1.0 %collective-permute-done.19 = f32[112,128]{1,0:T(8,128)S(1)} collective-permute-done((f32[112,128]{1,0:T(8,128)S(1)}, f32[112,128]{1,0:T(8,128)S(1)}, u32[]{:S(2)}, u32[]{:S(2)}) %collective-permute-start.19) | collective-permute-done | bytes 57376 | tf_op jit(solution)/shard_map/ppermute | solution.py:48
  (181 shorter events, 33.0 us)
Async XLA Ops:
  3.4 2.4 %collective-permute-start = (f32[2,2,128]{2,1,0:T(2,128)S(1)}, f32[2,2,128]{2,1,0:T(2,128)S(1)}, u32[]{:S(2)}, u32[]{:S(2)}) collective-permute-start(f32[2,2,128]{2,1,0:T(2,128)S(1)} %pad_maximum_fusion.18), channel_id=1, source_target_pairs={{0,1},{1,0},{2,3},{3,2},{4,5},{5,4},{6,7},{7,6},{8,9},{9,8},{10,11... | collective-permute-start | bytes 6152 | tf_op jit(solution)/shard_map/ppermute | solution.py:32
  5.8 7.2 %collective-permute-start.1 = (f32[2,2,128]{2,1,0:T(2,128)S(1)}, f32[2,2,128]{2,1,0:T(2,128)S(1)}, u32[]{:S(2)}, u32[]{:S(2)}) collective-permute-start(f32[2,2,128]{2,1,0:T(2,128)S(1)} %fusion.189), channel_id=1, source_target_pairs={{0,2},{1,3},{2,0},{3,1},{4,6},{5,7},{6,4},{7,5},{8,10},{9,11},{10,... | collective-permute-start | bytes 6152 | tf_op jit(solution)/shard_map/ppermute | solution.py:32
  8.4 29.5 %collective-permute-start.11 = (bf16[2,32,1,8,128]{4,1,3,2,0:T(8,128)(2,1)S(1)}, bf16[2,32,1,8,128]{4,1,3,2,0:T(8,128)(2,1)S(1)}, u32[]{:S(2)}, u32[]{:S(2)}) collective-permute-start(bf16[2,32,1,8,128]{4,1,3,2,0:T(8,128)(2,1)S(1)} %get-tuple-element.28), channel_id=1, source_target_pairs={{4,0},{8,4},{12,8},{16,12},{20,16},{24,20},{28,24},{0,28},{5,1},{9... | collective-permute-start | bytes 393224 | tf_op jit(solution)/shard_map/ppermute | solution.py:18
  13.0 24.9 %collective-permute-start.10 = (bf16[2,32,1,8,128]{4,1,3,2,0:T(8,128)(2,1)S(1)}, bf16[2,32,1,8,128]{4,1,3,2,0:T(8,128)(2,1)S(1)}, u32[]{:S(2)}, u32[]{:S(2)}) collective-permute-start(bf16[2,32,1,8,128]{4,1,3,2,0:T(8,128)(2,1)S(1)} %get-tuple-element.27), channel_id=1, source_target_pairs={{0,4},{4,8},{8,12},{12,16},{16,20},{20,24},{24,28},{28,0},{1,5},{5... | collective-permute-start | bytes 393224 | tf_op jit(solution)/shard_map/ppermute | solution.py:15
  13.5 6.7 %collective-permute-start.3 = (bf16[32,1,8,128]{3,0,2,1:T(8,128)(2,1)S(1)}, bf16[32,1,8,128]{3,0,2,1:T(8,128)(2,1)S(1)}, u32[]{:S(2)}, u32[]{:S(2)}) collective-permute-start(bf16[32,1,8,128]{3,0,2,1:T(8,128)(2,1)S(1)} %get-tuple-element.36), channel_id=1, source_target_pairs={{4,0},{8,4},{12,8},{16,12},{20,16},{24,20},{28,24},{0,28},{5,1},{9... | collective-permute-start | bytes 196616 | tf_op jit(solution)/shard_map/ppermute | solution.py:18
  18.2 7.0 %collective-permute-start.2 = (bf16[32,1,8,128]{3,0,2,1:T(8,128)(2,1)S(1)}, bf16[32,1,8,128]{3,0,2,1:T(8,128)(2,1)S(1)}, u32[]{:S(2)}, u32[]{:S(2)}) collective-permute-start(bf16[32,1,8,128]{3,0,2,1:T(8,128)(2,1)S(1)} %get-tuple-element.35), channel_id=1, source_target_pairs={{0,4},{4,8},{8,12},{12,16},{16,20},{20,24},{24,28},{28,0},{1,5},{5... | collective-permute-start | bytes 196616 | tf_op jit(solution)/shard_map/ppermute | solution.py:15
  25.2 1.8 %collective-permute-start.5 = (bf16[32,4,1,128]{3,0,2,1:T(8,128)(2,1)S(1)}, bf16[32,4,1,128]{3,0,2,1:T(8,128)(2,1)S(1)}, u32[]{:S(2)}, u32[]{:S(2)}) collective-permute-start(bf16[32,4,1,128]{3,0,2,1:T(8,128)(2,1)S(1)} %get-tuple-element.32), channel_id=1, source_target_pairs={{1,0},{2,1},{3,2},{0,3},{5,4},{6,5},{7,6},{4,7},{9,8},{10,9},{11,1... | collective-permute-start | bytes 98312 | tf_op jit(solution)/shard_map/ppermute | solution.py:18
  25.3 3.4 %collective-permute-start.4 = (bf16[32,4,1,128]{3,0,2,1:T(8,128)(2,1)S(1)}, bf16[32,4,1,128]{3,0,2,1:T(8,128)(2,1)S(1)}, u32[]{:S(2)}, u32[]{:S(2)}) collective-permute-start(bf16[32,4,1,128]{3,0,2,1:T(8,128)(2,1)S(1)} %get-tuple-element.31), channel_id=1, source_target_pairs={{0,1},{1,2},{2,3},{3,0},{4,5},{5,6},{6,7},{7,4},{8,9},{9,10},{10,1... | collective-permute-start | bytes 98312 | tf_op jit(solution)/shard_map/ppermute | solution.py:15
  35.8 4.3 %collective-permute-start.7 = (bf16[32,1,8,128]{3,0,2,1:T(8,128)(2,1)S(1)}, bf16[32,1,8,128]{3,0,2,1:T(8,128)(2,1)S(1)}, u32[]{:S(2)}, u32[]{:S(2)}) collective-permute-start(bf16[32,1,8,128]{3,0,2,1:T(8,128)(2,1)S(1)} %get-tuple-element.34), channel_id=1, source_target_pairs={{4,0},{8,4},{12,8},{16,12},{20,16},{24,20},{28,24},{0,28},{5,1},{9... | collective-permute-start | bytes 196616 | tf_op jit(solution)/shard_map/ppermute | solution.py:18
  35.9 7.0 %collective-permute-start.6 = (bf16[32,1,8,128]{3,0,2,1:T(8,128)(2,1)S(1)}, bf16[32,1,8,128]{3,0,2,1:T(8,128)(2,1)S(1)}, u32[]{:S(2)}, u32[]{:S(2)}) collective-permute-start(bf16[32,1,8,128]{3,0,2,1:T(8,128)(2,1)S(1)} %get-tuple-element.33), channel_id=1, source_target_pairs={{0,4},{4,8},{8,12},{12,16},{16,20},{20,24},{24,28},{28,0},{1,5},{5... | collective-permute-start | bytes 196616 | tf_op jit(solution)/shard_map/ppermute | solution.py:15
  37.9 5.6 %collective-permute-start.13 = (bf16[2,32,4,1,128]{4,1,3,2,0:T(8,128)(2,1)S(1)}, bf16[2,32,4,1,128]{4,1,3,2,0:T(8,128)(2,1)S(1)}, u32[]{:S(2)}, u32[]{:S(2)}) collective-permute-start(bf16[2,32,4,1,128]{4,1,3,2,0:T(8,128)(2,1)S(1)} %get-tuple-element.22), channel_id=1, source_target_pairs={{1,0},{2,1},{3,2},{0,3},{5,4},{6,5},{7,6},{4,7},{9,8},{10,9},{11,1... | collective-permute-start | bytes 196616 | tf_op jit(solution)/shard_map/ppermute | solution.py:18
  38.0 5.5 %collective-permute-start.12 = (bf16[2,32,4,1,128]{4,1,3,2,0:T(8,128)(2,1)S(1)}, bf16[2,32,4,1,128]{4,1,3,2,0:T(8,128)(2,1)S(1)}, u32[]{:S(2)}, u32[]{:S(2)}) collective-permute-start(bf16[2,32,4,1,128]{4,1,3,2,0:T(8,128)(2,1)S(1)} %get-tuple-element.21), channel_id=1, source_target_pairs={{0,1},{1,2},{2,3},{3,0},{4,5},{5,6},{6,7},{7,4},{8,9},{9,10},{10,1... | collective-permute-start | bytes 196616 | tf_op jit(solution)/shard_map/ppermute | solution.py:15
  42.9 15.8 %collective-permute-start.9 = (bf16[32,4,1,128]{3,0,2,1:T(8,128)(2,1)S(1)}, bf16[32,4,1,128]{3,0,2,1:T(8,128)(2,1)S(1)}, u32[]{:S(2)}, u32[]{:S(2)}) collective-permute-start(bf16[32,4,1,128]{3,0,2,1:T(8,128)(2,1)S(1)} %get-tuple-element.30), channel_id=1, source_target_pairs={{1,0},{2,1},{3,2},{0,3},{5,4},{6,5},{7,6},{4,7},{9,8},{10,9},{11,1... | collective-permute-start | bytes 98312 | tf_op jit(solution)/shard_map/ppermute | solution.py:18
  43.0 15.7 %collective-permute-start.8 = (bf16[32,4,1,128]{3,0,2,1:T(8,128)(2,1)S(1)}, bf16[32,4,1,128]{3,0,2,1:T(8,128)(2,1)S(1)}, u32[]{:S(2)}, u32[]{:S(2)}) collective-permute-start(bf16[32,4,1,128]{3,0,2,1:T(8,128)(2,1)S(1)} %get-tuple-element.29), channel_id=1, source_target_pairs={{0,1},{1,2},{2,3},{3,0},{4,5},{5,6},{6,7},{7,4},{8,9},{9,10},{10,1... | collective-permute-start | bytes 98312 | tf_op jit(solution)/shard_map/ppermute | solution.py:15
  57.6 3.5 %collective-permute-start.14 = (f32[112,128]{1,0:T(8,128)S(1)}, f32[112,128]{1,0:T(8,128)S(1)}, u32[]{:S(2)}, u32[]{:S(2)}) collective-permute-start(f32[112,128]{1,0:T(8,128)S(1)} %fusion.160), channel_id=1, source_target_pairs={{0,1},{1,0},{2,3},{3,2},{4,5},{5,4},{6,7},{7,6},{8,9},{9,8},{10,11... | collective-permute-start | bytes 172040 | tf_op jit(solution)/shard_map/ppermute | solution.py:46
  59.9 4.7 %collective-permute-start.21 = (f32[112,128]{1,0:T(8,128)S(1)}, f32[112,128]{1,0:T(8,128)S(1)}, u32[]{:S(2)}, u32[]{:S(2)}) collective-permute-start(f32[112,128]{1,0:T(8,128)S(1)} %select_add_fusion), channel_id=1, source_target_pairs={{0,2},{1,3},{2,0},{3,1},{4,6},{5,7},{6,4},{7,5},{8,10},{9,11},{10,... | collective-permute-start | bytes 172040 | tf_op jit(solution)/shard_map/ppermute | solution.py:32
  61.1 4.2 %collective-permute-start.15 = (f32[112,128]{1,0:T(8,128)S(1)}, f32[112,128]{1,0:T(8,128)S(1)}, u32[]{:S(2)}, u32[]{:S(2)}) collective-permute-start(f32[112,128]{1,0:T(8,128)S(1)} %select_add_fusion.1), channel_id=1, source_target_pairs={{0,2},{1,3},{2,0},{3,1},{4,6},{5,7},{6,4},{7,5},{8,10},{9,11},{10,... | collective-permute-start | bytes 172040 | tf_op jit(solution)/shard_map/ppermute | solution.py:32
  64.6 4.2 %collective-permute-start.22 = (f32[112,128]{1,0:T(8,128)S(1)}, f32[112,128]{1,0:T(8,128)S(1)}, u32[]{:S(2)}, u32[]{:S(2)}) collective-permute-start(f32[112,128]{1,0:T(8,128)S(1)} %add.114), channel_id=1, source_target_pairs={{0,4},{4,0},{8,12},{12,8},{16,20},{20,16},{24,28},{28,24},{1,5},{5... | collective-permute-start | bytes 172040 | tf_op jit(solution)/shard_map/ppermute | solution.py:32
  65.4 7.0 %collective-permute-start.16 = (f32[112,128]{1,0:T(8,128)S(1)}, f32[112,128]{1,0:T(8,128)S(1)}, u32[]{:S(2)}, u32[]{:S(2)}) collective-permute-start(f32[112,128]{1,0:T(8,128)S(1)} %add.108), channel_id=1, source_target_pairs={{0,4},{4,0},{8,12},{12,8},{16,20},{20,16},{24,28},{28,24},{1,5},{5... | collective-permute-start | bytes 172040 | tf_op jit(solution)/shard_map/ppermute | solution.py:32
  68.9 5.6 %collective-permute-start.23 = (f32[112,128]{1,0:T(8,128)S(1)}, f32[112,128]{1,0:T(8,128)S(1)}, u32[]{:S(2)}, u32[]{:S(2)}) collective-permute-start(f32[112,128]{1,0:T(8,128)S(1)} %add.115), channel_id=1, source_target_pairs={{0,8},{4,12},{8,0},{12,4},{16,24},{20,28},{24,16},{28,20},{1,9},{5... | collective-permute-start | bytes 172040 | tf_op jit(solution)/shard_map/ppermute | solution.py:32
  72.4 4.2 %collective-permute-start.17 = (f32[112,128]{1,0:T(8,128)S(1)}, f32[112,128]{1,0:T(8,128)S(1)}, u32[]{:S(2)}, u32[]{:S(2)}) collective-permute-start(f32[112,128]{1,0:T(8,128)S(1)} %add.109), channel_id=1, source_target_pairs={{0,8},{4,12},{8,0},{12,4},{16,24},{20,28},{24,16},{28,20},{1,9},{5... | collective-permute-start | bytes 172040 | tf_op jit(solution)/shard_map/ppermute | solution.py:32
  74.5 5.3 %collective-permute-start.24 = (f32[112,128]{1,0:T(8,128)S(1)}, f32[112,128]{1,0:T(8,128)S(1)}, u32[]{:S(2)}, u32[]{:S(2)}) collective-permute-start(f32[112,128]{1,0:T(8,128)S(1)} %add.116), channel_id=1, source_target_pairs={{0,16},{4,20},{8,24},{12,28},{16,0},{20,4},{24,8},{28,12},{1,17},{... | collective-permute-start | bytes 172040 | tf_op jit(solution)/shard_map/ppermute | solution.py:32
  76.7 5.1 %collective-permute-start.18 = (f32[112,128]{1,0:T(8,128)S(1)}, f32[112,128]{1,0:T(8,128)S(1)}, u32[]{:S(2)}, u32[]{:S(2)}) collective-permute-start(f32[112,128]{1,0:T(8,128)S(1)} %add.110), channel_id=1, source_target_pairs={{0,16},{4,20},{8,24},{12,28},{16,0},{20,4},{24,8},{28,12},{1,17},{... | collective-permute-start | bytes 172040 | tf_op jit(solution)/shard_map/ppermute | solution.py:32
  79.9 2.1 %collective-permute-start.25 = (f32[112,128]{1,0:T(8,128)S(1)}, f32[112,128]{1,0:T(8,128)S(1)}, u32[]{:S(2)}, u32[]{:S(2)}) collective-permute-start(f32[112,128]{1,0:T(8,128)S(1)} %add.117), channel_id=1, source_target_pairs={{0,1},{1,0},{2,3},{3,2},{4,5},{5,4},{6,7},{7,6},{8,9},{9,8},{10,11... | collective-permute-start | bytes 172040 | tf_op jit(solution)/shard_map/ppermute | solution.py:48
  (12 other events, 90.2 us)

commit v2 on v1

--- a/solution.py
+++ b/solution.py
@@ -92,19 +92,20 @@
 
 def taps_from_inputs(grad_field, padded_inputs):
     shape = grad_field.shape
-    taps_list = []
-    for tap_x in range(3):
-        for tap_z in range(3):
-            for tap_y in range(3):
-                window = padded_inputs[
-                    :, tap_x : tap_x + shape[1], tap_z : tap_z + shape[2], tap_y : tap_y + shape[3]
-                ]
-                taps_list.append(
-                    jnp.einsum(
-                        "oxzy,ixzy->oi", grad_field, window, preferred_element_type=jnp.float32
-                    )
-                )
-    return jnp.stack(taps_list).reshape(3, 3, 3, shape[0], padded_inputs.shape[0])
+    windows = jnp.stack(
+        [
+            padded_inputs[
+                :, tap_x : tap_x + shape[1], tap_z : tap_z + shape[2], tap_y : tap_y + shape[3]
+            ]
+            for tap_x in range(3)
+            for tap_z in range(3)
+            for tap_y in range(3)
+        ]
+    )
+    taps = jnp.einsum(
+        "oxzy,tixzy->toi", grad_field, windows, preferred_element_type=jnp.float32
+    )
+    return taps.reshape(3, 3, 3, shape[0], padded_inputs.shape[0])
 
 
 def per_device(

time: 86.5 us -> 82.1 us (0.949)
  waiting for transfers between devices: 22.7 us -> 13.8 us
  matrix products: 16.4 us -> 7.68 us
  starting transfers between devices: 26 us -> 33.2 us
  local copies, waits for them, and re-layouts: 15.2 us -> 20.5 us
    dot_general x54 -> x2, matrix products: 11.8 us -> 2.09 us  [taps_from_inputs(): jnp.einsum('oxzy,tixzy->toi', grad_field, windows, preferred_element_type...]
    ppermute x6, starting transfers between devices: 9.62 us -> 17.6 us  [extended(): lax.ppermute(lax.slice_in_dim(block, 0, width, axis=dim), axis, backward)]
    ppermute x6, waiting for transfers between devices: 9.45 us -> 4.52 us  [extended(): lax.ppermute(lax.slice_in_dim(block, block.shape[dim] - width, None, axis...]
    ppermute x6, waiting for transfers between devices: 4.6 us -> 0.02 us  [extended(): lax.ppermute(lax.slice_in_dim(block, 0, width, axis=dim), axis, backward)]
    unnamed x24 -> x68, local copies, waits for them, and re-layouts: 8.37 us -> 12.8 us
    ppermute x6, starting transfers between devices: 3.51 us -> 2.12 us  [extended(): lax.ppermute(lax.slice_in_dim(block, block.shape[dim] - width, None, axis...]
    ppermute x10, waiting for transfers between devices: 6.45 us -> 7.39 us  [butterfly_sum(): value = value + lax.ppermute(value, axis, pairs)]
    dot_general x1, matrix products: 0.23 us -> 1.15 us  [per_device(): jnp.einsum('oi,oxzy->ixzy', w_out, head_grad, preferred_element_type=jnp....]
  transfers between devices with their start and end apart: 26 -> 26, of which waited for: 14 -> 9; matrix products, arithmetic and copies ran while one was open for 34% -> 34% of each run, Pallas kernels for 0% -> 0%
where the time goes in v2:
time: 82.1 us; the launch traced here: 81.8 us
  starting transfers between devices  33.2 us (40%)
  local copies, waits for them, and re-layouts  20.5 us (25%)
  waiting for transfers between devices  13.8 us (17%)
  matrix products  7.68 us (9%)
  other arithmetic  5.2 us (6%)
  between operations  1.55 us (2%)
    ppermute x6, starting transfers between devices, extended(): lax.ppermute(lax.slice_in_dim(block, 0, width, axis=dim), axis, backward)  17.6 us
    unnamed x68, local copies, waits for them, and re-layouts  12.8 us
    ppermute x10, starting transfers between devices, butterfly_sum(): value = value + lax.ppermute(value, axis, pairs)  12.6 us
    ppermute x10, waiting for transfers between devices, butterfly_sum(): value = value + lax.ppermute(value, axis, pairs)  7.39 us
    ppermute x6, waiting for transfers between devices, extended(): lax.ppermute(lax.slice_in_dim(block, block.shape[dim] - width, None, axis...  4.52 us
    conv_general_dilated x2, matrix products, spread_local(): lax.conv_general_dilated(padded[None], kernel, (1, 1, 1), 'VALID', dimens...  3.49 us
    ppermute x6, starting transfers between devices, extended(): lax.ppermute(lax.slice_in_dim(block, block.shape[dim] - width, None, axis...  2.12 us
    dot_general x2, matrix products, taps_from_inputs(): jnp.einsum('oxzy,tixzy->toi', grad_field, windows, preferred_element_type...  2.09 us
  transfers between devices with their start and end apart: 26, of which 9 were waited for; matrix products, arithmetic and copies ran while one was open for 34% of the time, Pallas kernels for 0%

profile of v2, /device:TPU:0, one launch (start us, length us, event | category | flops | bytes accessed | tf_op | source)
XLA Modules:
  0.0 81.8 jit_solution(3893597219144076451)
XLA Ops:
  5.7 2.6 %collective-permute-start.1 = (f32[2,2,128]{2,1,0:T(2,128)S(1)}, f32[2,2,128]{2,1,0:T(2,128)S(1)}, u32[]{:S(2)}, u32[]{:S(2)}) collective-permute-start(f32[2,2,128]{2,1,0:T(2,128)S(1)} %fusion.141), channel_id=1, source_target_pairs={{0,2},{1,3},{2,0},{3,1},{4,6},{5,7},{6,4},{7,5},{8,10},{9,11},{10,... | collective-permute-start | bytes 6152 | tf_op jit(solution)/shard_map/ppermute | solution.py:32
  8.3 1.6 %collective-permute-start.10 = (bf16[2,32,1,8,128]{4,1,3,2,0:T(8,128)(2,1)S(1)}, bf16[2,32,1,8,128]{4,1,3,2,0:T(8,128)(2,1)S(1)}, u32[]{:S(2)}, u32[]{:S(2)}) collective-permute-start(bf16[2,32,1,8,128]{4,1,3,2,0:T(8,128)(2,1)S(1)} %get-tuple-element.27), channel_id=1, source_target_pairs={{0,4},{4,8},{8,12},{12,16},{16,20},{20,24},{24,28},{28,0},{1,5},{5... | collective-permute-start | bytes 393224 | tf_op jit(solution)/shard_map/ppermute | solution.py:15
  9.9 3.2 %collective-permute-start.11 = (bf16[2,32,1,8,128]{4,1,3,2,0:T(8,128)(2,1)S(1)}, bf16[2,32,1,8,128]{4,1,3,2,0:T(8,128)(2,1)S(1)}, u32[]{:S(2)}, u32[]{:S(2)}) collective-permute-start(bf16[2,32,1,8,128]{4,1,3,2,0:T(8,128)(2,1)S(1)} %get-tuple-element.28), channel_id=1, source_target_pairs={{4,0},{8,4},{12,8},{16,12},{20,16},{24,20},{28,24},{0,28},{5,1},{9... | collective-permute-start | bytes 393224 | tf_op jit(solution)/shard_map/ppermute | solution.py:18
  13.9 1.1 %fusion.34 = bf16[32,2,8,128]{3,0,2,1:T(8,128)(2,1)S(1)} fusion(bf16[32,2,8,128]{3,2,1,0:T(8,128)(2,1)} %param.11, bf16[3,2,8,128]{3,2,1,0:T(8,128)(2,1)S(1)} %get-tuple-element.18, bf16[3,32]{1,0:T(4,128)(2,1)} %param.14), kind=kOutput, calls=%fused_computation.33 | convolution fusion | flops 1048576 | bytes 274624 | tf_op jit(solution)/shard_map/oi,oxzy->ixzy/dot_general | solution.py:148
  15.2 4.7 %collective-permute-start.3 = (bf16[32,1,8,128]{3,0,2,1:T(8,128)(2,1)S(1)}, bf16[32,1,8,128]{3,0,2,1:T(8,128)(2,1)S(1)}, u32[]{:S(2)}, u32[]{:S(2)}) collective-permute-start(bf16[32,1,8,128]{3,0,2,1:T(8,128)(2,1)S(1)} %get-tuple-element.36), channel_id=1, source_target_pairs={{4,0},{8,4},{12,8},{16,12},{20,16},{24,20},{28,24},{0,28},{5,1},{9... | collective-permute-start | bytes 196616 | tf_op jit(solution)/shard_map/ppermute | solution.py:18
  20.0 2.1 %collective-permute-done.2 = bf16[32,1,8,128]{3,0,2,1:T(8,128)(2,1)S(1)} collective-permute-done((bf16[32,1,8,128]{3,0,2,1:T(8,128)(2,1)S(1)}, bf16[32,1,8,128]{3,0,2,1:T(8,128)(2,1)S(1)}, u32[]{:S(2)}, u32[]{:S(2)}) %collective-permute-start.2) | collective-permute-done | bytes 65568 | tf_op jit(solution)/shard_map/ppermute | solution.py:15
  22.2 1.7 %collective-permute-start.5 = (bf16[32,4,1,128]{3,0,2,1:T(8,128)(2,1)S(1)}, bf16[32,4,1,128]{3,0,2,1:T(8,128)(2,1)S(1)}, u32[]{:S(2)}, u32[]{:S(2)}) collective-permute-start(bf16[32,4,1,128]{3,0,2,1:T(8,128)(2,1)S(1)} %get-tuple-element.32), channel_id=1, source_target_pairs={{1,0},{2,1},{3,2},{0,3},{5,4},{6,5},{7,6},{4,7},{9,8},{10,9},{11,1... | collective-permute-start | bytes 98312 | tf_op jit(solution)/shard_map/ppermute | solution.py:18
  24.0 1.5 %collective-permute-done.4 = bf16[32,4,1,128]{3,0,2,1:T(8,128)(2,1)S(1)} collective-permute-done((bf16[32,4,1,128]{3,0,2,1:T(8,128)(2,1)S(1)}, bf16[32,4,1,128]{3,0,2,1:T(8,128)(2,1)S(1)}, u32[]{:S(2)}, u32[]{:S(2)}) %collective-permute-start.4) | collective-permute-done | bytes 32800 | tf_op jit(solution)/shard_map/ppermute | solution.py:15
  26.2 2.1 %copy.96 = bf16[32,4,10,1,130]{0,1,4,2,3:T(4,128)(2,1)S(1)} copy(bf16[32,4,10,1,130]{4,0,2,1,3:T(8,128)(2,1)S(1)} %maximum_bitcast_fusion) | data formatting | bytes 665600
  29.2 1.8 %fusion.19 = f32[2,8,8,17,32]{4,2,3,1,0:T(8,128)S(1)} fusion(bf16[3,3,3,32,32]{4,3,2,1,0:T(8,128)(2,1)S(1)} %copy-done, bf16[32,4,10,1,7,2]{0,4,5,2,1,3:T(8,128)(2,1)S(1)} %slice.399, bf16[32,4,10,1,8,17]{0,4,5,2,1,3:T(8,128)(2,1)S(1)} %copy.46, pred[8,17]{0,1:T(8,128)(4,1)S(1)} %copy-done.4), kind=kOutput, calls=%fused_computation.18 | convolution fusion | flops 121561088 | bytes 717960 | tf_op jit(solution)/shard_map/conv_general_dilated | solution.py:83
  32.1 4.8 %collective-permute-start.7 = (bf16[32,1,8,128]{3,0,2,1:T(8,128)(2,1)S(1)}, bf16[32,1,8,128]{3,0,2,1:T(8,128)(2,1)S(1)}, u32[]{:S(2)}, u32[]{:S(2)}) collective-permute-start(bf16[32,1,8,128]{3,0,2,1:T(8,128)(2,1)S(1)} %get-tuple-element.34), channel_id=1, source_target_pairs={{4,0},{8,4},{12,8},{16,12},{20,16},{24,20},{28,24},{0,28},{5,1},{9... | collective-permute-start | bytes 196616 | tf_op jit(solution)/shard_map/ppermute | solution.py:18
  37.3 1.5 %collective-permute-start.13 = (bf16[2,32,4,1,128]{4,1,3,2,0:T(8,128)(2,1)S(1)}, bf16[2,32,4,1,128]{4,1,3,2,0:T(8,128)(2,1)S(1)}, u32[]{:S(2)}, u32[]{:S(2)}) collective-permute-start(bf16[2,32,4,1,128]{4,1,3,2,0:T(8,128)(2,1)S(1)} %get-tuple-element.22), channel_id=1, source_target_pairs={{1,0},{2,1},{3,2},{0,3},{5,4},{6,5},{7,6},{4,7},{9,8},{10,9},{11,1... | collective-permute-start | bytes 196616 | tf_op jit(solution)/shard_map/ppermute | solution.py:18
  39.7 1.7 %collective-permute-start.9 = (bf16[32,4,1,128]{3,0,2,1:T(8,128)(2,1)S(1)}, bf16[32,4,1,128]{3,0,2,1:T(8,128)(2,1)S(1)}, u32[]{:S(2)}, u32[]{:S(2)}) collective-permute-start(bf16[32,4,1,128]{3,0,2,1:T(8,128)(2,1)S(1)} %get-tuple-element.30), channel_id=1, source_target_pairs={{1,0},{2,1},{3,2},{0,3},{5,4},{6,5},{7,6},{4,7},{9,8},{10,9},{11,1... | collective-permute-start | bytes 98312 | tf_op jit(solution)/shard_map/ppermute | solution.py:18
  49.9 1.0 %fusion.30 = f32[27,32,32]{1,2,0:T(8,128)S(1)} fusion(bf16[27,32,2,8,128]{4,1,3,2,0:T(8,128)(2,1)S(1)} %fusion.52, bf16[32,2,8,128]{3,0,2,1:T(8,128)(2,1)S(1)} %fusion.34), kind=kOutput, calls=%fused_computation.27 | convolution fusion | flops 113273856 | bytes 3780608 | tf_op jit(solution)/shard_map/oxzy,tixzy->toi/dot_general | solution.py:105
  53.6 1.8 %collective-permute-start.21 = (f32[112,128]{1,0:T(8,128)S(1)}, f32[112,128]{1,0:T(8,128)S(1)}, u32[]{:S(2)}, u32[]{:S(2)}) collective-permute-start(f32[112,128]{1,0:T(8,128)S(1)} %select_add_fusion), channel_id=1, source_target_pairs={{0,2},{1,3},{2,0},{3,1},{4,6},{5,7},{6,4},{7,5},{8,10},{9,11},{10,... | collective-permute-start | bytes 172040 | tf_op jit(solution)/shard_map/ppermute | solution.py:32
  55.8 2.1 %collective-permute-done.21 = f32[112,128]{1,0:T(8,128)S(1)} collective-permute-done((f32[112,128]{1,0:T(8,128)S(1)}, f32[112,128]{1,0:T(8,128)S(1)}, u32[]{:S(2)}, u32[]{:S(2)}) %collective-permute-start.21) | collective-permute-done | bytes 57376 | tf_op jit(solution)/shard_map/ppermute | solution.py:32
  58.1 1.6 %collective-permute-done.15 = f32[112,128]{1,0:T(8,128)S(1)} collective-permute-done((f32[112,128]{1,0:T(8,128)S(1)}, f32[112,128]{1,0:T(8,128)S(1)}, u32[]{:S(2)}, u32[]{:S(2)}) %collective-permute-start.15) | collective-permute-done | bytes 57376 | tf_op jit(solution)/shard_map/ppermute | solution.py:32
  60.2 2.1 %collective-permute-done.22 = f32[112,128]{1,0:T(8,128)S(1)} collective-permute-done((f32[112,128]{1,0:T(8,128)S(1)}, f32[112,128]{1,0:T(8,128)S(1)}, u32[]{:S(2)}, u32[]{:S(2)}) %collective-permute-start.22) | collective-permute-done | bytes 57376 | tf_op jit(solution)/shard_map/ppermute | solution.py:32
  62.8 2.3 %copy.97 = bf16[32,4,10,1,130]{0,1,4,2,3:T(4,128)(2,1)S(1)} copy(bf16[32,4,10,1,130]{4,0,2,1,3:T(8,128)(2,1)S(1)} %maximum_bitcast_fusion.1) | data formatting | bytes 665600
  66.1 2.1 %collective-permute-start.17 = (f32[112,128]{1,0:T(8,128)S(1)}, f32[112,128]{1,0:T(8,128)S(1)}, u32[]{:S(2)}, u32[]{:S(2)}) collective-permute-start(f32[112,128]{1,0:T(8,128)S(1)} %add.109), channel_id=1, source_target_pairs={{0,8},{4,12},{8,0},{12,4},{16,24},{20,28},{24,16},{28,20},{1,9},{5... | collective-permute-start | bytes 172040 | tf_op jit(solution)/shard_map/ppermute | solution.py:32
  68.2 2.3 %collective-permute-start.24 = (f32[112,128]{1,0:T(8,128)S(1)}, f32[112,128]{1,0:T(8,128)S(1)}, u32[]{:S(2)}, u32[]{:S(2)}) collective-permute-start(f32[112,128]{1,0:T(8,128)S(1)} %add.116), channel_id=1, source_target_pairs={{0,16},{4,20},{8,24},{12,28},{16,0},{20,4},{24,8},{28,12},{1,17},{... | collective-permute-start | bytes 172040 | tf_op jit(solution)/shard_map/ppermute | solution.py:32
  70.5 1.7 %fusion.22 = bf16[2,8,8,17,32]{4,2,3,1,0:T(8,128)(2,1)S(1)} fusion(bf16[3,3,3,32,32]{4,3,2,1,0:T(8,128)(2,1)S(1)} %copy-done.3, bf16[32,4,10,1,7,2]{0,4,5,2,1,3:T(8,128)(2,1)S(1)} %slice.405, bf16[32,4,10,1,8,17]{0,4,5,2,1,3:T(8,128)(2,1)S(1)} %copy.52, pred[8,17]{0,1:T(8,128)(4,1)S(1)} %copy-done.4), kind=kOutput, calls=%fused_computation.19 | convolution fusion | flops 121630720 | bytes 578696 | tf_op jit(solution)/shard_map/conv_general_dilated | solution.py:83
  72.3 2.4 %collective-permute-start.18 = (f32[112,128]{1,0:T(8,128)S(1)}, f32[112,128]{1,0:T(8,128)S(1)}, u32[]{:S(2)}, u32[]{:S(2)}) collective-permute-start(f32[112,128]{1,0:T(8,128)S(1)} %add.110), channel_id=1, source_target_pairs={{0,16},{4,20},{8,24},{12,28},{16,0},{20,4},{24,8},{28,12},{1,17},{... | collective-permute-start | bytes 172040 | tf_op jit(solution)/shard_map/ppermute | solution.py:32
  75.9 1.6 %collective-permute-done.18 = f32[112,128]{1,0:T(8,128)S(1)} collective-permute-done((f32[112,128]{1,0:T(8,128)S(1)}, f32[112,128]{1,0:T(8,128)S(1)}, u32[]{:S(2)}, u32[]{:S(2)}) %collective-permute-start.18) | collective-permute-done | bytes 57376 | tf_op jit(solution)/shard_map/ppermute | solution.py:32
  (177 shorter events, 28.9 us)
Async XLA Ops:
  3.3 2.4 %collective-permute-start = (f32[2,2,128]{2,1,0:T(2,128)S(1)}, f32[2,2,128]{2,1,0:T(2,128)S(1)}, u32[]{:S(2)}, u32[]{:S(2)}) collective-permute-start(f32[2,2,128]{2,1,0:T(2,128)S(1)} %pad_maximum_fusion.18), channel_id=1, source_target_pairs={{0,1},{1,0},{2,3},{3,2},{4,5},{5,4},{6,7},{7,6},{8,9},{9,8},{10,11... | collective-permute-start | bytes 6152 | tf_op jit(solution)/shard_map/ppermute | solution.py:32
  5.7 7.4 %collective-permute-start.1 = (f32[2,2,128]{2,1,0:T(2,128)S(1)}, f32[2,2,128]{2,1,0:T(2,128)S(1)}, u32[]{:S(2)}, u32[]{:S(2)}) collective-permute-start(f32[2,2,128]{2,1,0:T(2,128)S(1)} %fusion.141), channel_id=1, source_target_pairs={{0,2},{1,3},{2,0},{3,1},{4,6},{5,7},{6,4},{7,5},{8,10},{9,11},{10,... | collective-permute-start | bytes 6152 | tf_op jit(solution)/shard_map/ppermute | solution.py:32
  8.3 28.6 %collective-permute-start.10 = (bf16[2,32,1,8,128]{4,1,3,2,0:T(8,128)(2,1)S(1)}, bf16[2,32,1,8,128]{4,1,3,2,0:T(8,128)(2,1)S(1)}, u32[]{:S(2)}, u32[]{:S(2)}) collective-permute-start(bf16[2,32,1,8,128]{4,1,3,2,0:T(8,128)(2,1)S(1)} %get-tuple-element.27), channel_id=1, source_target_pairs={{0,4},{4,8},{8,12},{12,16},{16,20},{20,24},{24,28},{28,0},{1,5},{5... | collective-permute-start | bytes 393224 | tf_op jit(solution)/shard_map/ppermute | solution.py:15
  9.9 27.0 %collective-permute-start.11 = (bf16[2,32,1,8,128]{4,1,3,2,0:T(8,128)(2,1)S(1)}, bf16[2,32,1,8,128]{4,1,3,2,0:T(8,128)(2,1)S(1)}, u32[]{:S(2)}, u32[]{:S(2)}) collective-permute-start(bf16[2,32,1,8,128]{4,1,3,2,0:T(8,128)(2,1)S(1)} %get-tuple-element.28), channel_id=1, source_target_pairs={{4,0},{8,4},{12,8},{16,12},{20,16},{24,20},{28,24},{0,28},{5,1},{9... | collective-permute-start | bytes 393224 | tf_op jit(solution)/shard_map/ppermute | solution.py:18
  15.1 7.0 %collective-permute-start.2 = (bf16[32,1,8,128]{3,0,2,1:T(8,128)(2,1)S(1)}, bf16[32,1,8,128]{3,0,2,1:T(8,128)(2,1)S(1)}, u32[]{:S(2)}, u32[]{:S(2)}) collective-permute-start(bf16[32,1,8,128]{3,0,2,1:T(8,128)(2,1)S(1)} %get-tuple-element.35), channel_id=1, source_target_pairs={{0,4},{4,8},{8,12},{12,16},{16,20},{20,24},{24,28},{28,0},{1,5},{5... | collective-permute-start | bytes 196616 | tf_op jit(solution)/shard_map/ppermute | solution.py:15
  15.2 7.0 %collective-permute-start.3 = (bf16[32,1,8,128]{3,0,2,1:T(8,128)(2,1)S(1)}, bf16[32,1,8,128]{3,0,2,1:T(8,128)(2,1)S(1)}, u32[]{:S(2)}, u32[]{:S(2)}) collective-permute-start(bf16[32,1,8,128]{3,0,2,1:T(8,128)(2,1)S(1)} %get-tuple-element.36), channel_id=1, source_target_pairs={{4,0},{8,4},{12,8},{16,12},{20,16},{24,20},{28,24},{0,28},{5,1},{9... | collective-permute-start | bytes 196616 | tf_op jit(solution)/shard_map/ppermute | solution.py:18
  22.1 3.4 %collective-permute-start.4 = (bf16[32,4,1,128]{3,0,2,1:T(8,128)(2,1)S(1)}, bf16[32,4,1,128]{3,0,2,1:T(8,128)(2,1)S(1)}, u32[]{:S(2)}, u32[]{:S(2)}) collective-permute-start(bf16[32,4,1,128]{3,0,2,1:T(8,128)(2,1)S(1)} %get-tuple-element.31), channel_id=1, source_target_pairs={{0,1},{1,2},{2,3},{3,0},{4,5},{5,6},{6,7},{7,4},{8,9},{9,10},{10,1... | collective-permute-start | bytes 98312 | tf_op jit(solution)/shard_map/ppermute | solution.py:15
  22.2 3.3 %collective-permute-start.5 = (bf16[32,4,1,128]{3,0,2,1:T(8,128)(2,1)S(1)}, bf16[32,4,1,128]{3,0,2,1:T(8,128)(2,1)S(1)}, u32[]{:S(2)}, u32[]{:S(2)}) collective-permute-start(bf16[32,4,1,128]{3,0,2,1:T(8,128)(2,1)S(1)} %get-tuple-element.32), channel_id=1, source_target_pairs={{1,0},{2,1},{3,2},{0,3},{5,4},{6,5},{7,6},{4,7},{9,8},{10,9},{11,1... | collective-permute-start | bytes 98312 | tf_op jit(solution)/shard_map/ppermute | solution.py:18
  32.1 7.6 %collective-permute-start.6 = (bf16[32,1,8,128]{3,0,2,1:T(8,128)(2,1)S(1)}, bf16[32,1,8,128]{3,0,2,1:T(8,128)(2,1)S(1)}, u32[]{:S(2)}, u32[]{:S(2)}) collective-permute-start(bf16[32,1,8,128]{3,0,2,1:T(8,128)(2,1)S(1)} %get-tuple-element.33), channel_id=1, source_target_pairs={{0,4},{4,8},{8,12},{12,16},{16,20},{20,24},{24,28},{28,0},{1,5},{5... | collective-permute-start | bytes 196616 | tf_op jit(solution)/shard_map/ppermute | solution.py:15
  32.1 7.5 %collective-permute-start.7 = (bf16[32,1,8,128]{3,0,2,1:T(8,128)(2,1)S(1)}, bf16[32,1,8,128]{3,0,2,1:T(8,128)(2,1)S(1)}, u32[]{:S(2)}, u32[]{:S(2)}) collective-permute-start(bf16[32,1,8,128]{3,0,2,1:T(8,128)(2,1)S(1)} %get-tuple-element.34), channel_id=1, source_target_pairs={{4,0},{8,4},{12,8},{16,12},{20,16},{24,20},{28,24},{0,28},{5,1},{9... | collective-permute-start | bytes 196616 | tf_op jit(solution)/shard_map/ppermute | solution.py:18
  36.9 4.5 %collective-permute-start.12 = (bf16[2,32,4,1,128]{4,1,3,2,0:T(8,128)(2,1)S(1)}, bf16[2,32,4,1,128]{4,1,3,2,0:T(8,128)(2,1)S(1)}, u32[]{:S(2)}, u32[]{:S(2)}) collective-permute-start(bf16[2,32,4,1,128]{4,1,3,2,0:T(8,128)(2,1)S(1)} %get-tuple-element.21), channel_id=1, source_target_pairs={{0,1},{1,2},{2,3},{3,0},{4,5},{5,6},{6,7},{7,4},{8,9},{9,10},{10,1... | collective-permute-start | bytes 196616 | tf_op jit(solution)/shard_map/ppermute | solution.py:15
  37.3 4.2 %collective-permute-start.13 = (bf16[2,32,4,1,128]{4,1,3,2,0:T(8,128)(2,1)S(1)}, bf16[2,32,4,1,128]{4,1,3,2,0:T(8,128)(2,1)S(1)}, u32[]{:S(2)}, u32[]{:S(2)}) collective-permute-start(bf16[2,32,4,1,128]{4,1,3,2,0:T(8,128)(2,1)S(1)} %get-tuple-element.22), channel_id=1, source_target_pairs={{1,0},{2,1},{3,2},{0,3},{5,4},{6,5},{7,6},{4,7},{9,8},{10,9},{11,1... | collective-permute-start | bytes 196616 | tf_op jit(solution)/shard_map/ppermute | solution.py:18
  39.7 13.0 %collective-permute-start.8 = (bf16[32,4,1,128]{3,0,2,1:T(8,128)(2,1)S(1)}, bf16[32,4,1,128]{3,0,2,1:T(8,128)(2,1)S(1)}, u32[]{:S(2)}, u32[]{:S(2)}) collective-permute-start(bf16[32,4,1,128]{3,0,2,1:T(8,128)(2,1)S(1)} %get-tuple-element.29), channel_id=1, source_target_pairs={{0,1},{1,2},{2,3},{3,0},{4,5},{5,6},{6,7},{7,4},{8,9},{9,10},{10,1... | collective-permute-start | bytes 98312 | tf_op jit(solution)/shard_map/ppermute | solution.py:15
  39.7 13.0 %collective-permute-start.9 = (bf16[32,4,1,128]{3,0,2,1:T(8,128)(2,1)S(1)}, bf16[32,4,1,128]{3,0,2,1:T(8,128)(2,1)S(1)}, u32[]{:S(2)}, u32[]{:S(2)}) collective-permute-start(bf16[32,4,1,128]{3,0,2,1:T(8,128)(2,1)S(1)} %get-tuple-element.30), channel_id=1, source_target_pairs={{1,0},{2,1},{3,2},{0,3},{5,4},{6,5},{7,6},{4,7},{9,8},{10,9},{11,1... | collective-permute-start | bytes 98312 | tf_op jit(solution)/shard_map/ppermute | solution.py:18
  51.5 3.9 %collective-permute-start.14 = (f32[112,128]{1,0:T(8,128)S(1)}, f32[112,128]{1,0:T(8,128)S(1)}, u32[]{:S(2)}, u32[]{:S(2)}) collective-permute-start(f32[112,128]{1,0:T(8,128)S(1)} %fusion.112), channel_id=1, source_target_pairs={{0,1},{1,0},{2,3},{3,2},{4,5},{5,4},{6,7},{7,6},{8,9},{9,8},{10,11... | collective-permute-start | bytes 172040 | tf_op jit(solution)/shard_map/ppermute | solution.py:46
  53.6 4.2 %collective-permute-start.21 = (f32[112,128]{1,0:T(8,128)S(1)}, f32[112,128]{1,0:T(8,128)S(1)}, u32[]{:S(2)}, u32[]{:S(2)}) collective-permute-start(f32[112,128]{1,0:T(8,128)S(1)} %select_add_fusion), channel_id=1, source_target_pairs={{0,2},{1,3},{2,0},{3,1},{4,6},{5,7},{6,4},{7,5},{8,10},{9,11},{10,... | collective-permute-start | bytes 172040 | tf_op jit(solution)/shard_map/ppermute | solution.py:32
  55.4 4.2 %collective-permute-start.15 = (f32[112,128]{1,0:T(8,128)S(1)}, f32[112,128]{1,0:T(8,128)S(1)}, u32[]{:S(2)}, u32[]{:S(2)}) collective-permute-start(f32[112,128]{1,0:T(8,128)S(1)} %select_add_fusion.1), channel_id=1, source_target_pairs={{0,2},{1,3},{2,0},{3,1},{4,6},{5,7},{6,4},{7,5},{8,10},{9,11},{10,... | collective-permute-start | bytes 172040 | tf_op jit(solution)/shard_map/ppermute | solution.py:32
  57.8 4.5 %collective-permute-start.22 = (f32[112,128]{1,0:T(8,128)S(1)}, f32[112,128]{1,0:T(8,128)S(1)}, u32[]{:S(2)}, u32[]{:S(2)}) collective-permute-start(f32[112,128]{1,0:T(8,128)S(1)} %add.114), channel_id=1, source_target_pairs={{0,4},{4,0},{8,12},{12,8},{16,20},{20,16},{24,28},{28,24},{1,5},{5... | collective-permute-start | bytes 172040 | tf_op jit(solution)/shard_map/ppermute | solution.py:32
  59.7 6.4 %collective-permute-start.16 = (f32[112,128]{1,0:T(8,128)S(1)}, f32[112,128]{1,0:T(8,128)S(1)}, u32[]{:S(2)}, u32[]{:S(2)}) collective-permute-start(f32[112,128]{1,0:T(8,128)S(1)} %add.108), channel_id=1, source_target_pairs={{0,4},{4,0},{8,12},{12,8},{16,20},{20,16},{24,28},{28,24},{1,5},{5... | collective-permute-start | bytes 172040 | tf_op jit(solution)/shard_map/ppermute | solution.py:32
  62.3 5.9 %collective-permute-start.23 = (f32[112,128]{1,0:T(8,128)S(1)}, f32[112,128]{1,0:T(8,128)S(1)}, u32[]{:S(2)}, u32[]{:S(2)}) collective-permute-start(f32[112,128]{1,0:T(8,128)S(1)} %add.115), channel_id=1, source_target_pairs={{0,8},{4,12},{8,0},{12,4},{16,24},{20,28},{24,16},{28,20},{1,9},{5... | collective-permute-start | bytes 172040 | tf_op jit(solution)/shard_map/ppermute | solution.py:32
  66.1 6.2 %collective-permute-start.17 = (f32[112,128]{1,0:T(8,128)S(1)}, f32[112,128]{1,0:T(8,128)S(1)}, u32[]{:S(2)}, u32[]{:S(2)}) collective-permute-start(f32[112,128]{1,0:T(8,128)S(1)} %add.109), channel_id=1, source_target_pairs={{0,8},{4,12},{8,0},{12,4},{16,24},{20,28},{24,16},{28,20},{1,9},{5... | collective-permute-start | bytes 172040 | tf_op jit(solution)/shard_map/ppermute | solution.py:32
  68.2 6.5 %collective-permute-start.24 = (f32[112,128]{1,0:T(8,128)S(1)}, f32[112,128]{1,0:T(8,128)S(1)}, u32[]{:S(2)}, u32[]{:S(2)}) collective-permute-start(f32[112,128]{1,0:T(8,128)S(1)} %add.116), channel_id=1, source_target_pairs={{0,16},{4,20},{8,24},{12,28},{16,0},{20,4},{24,8},{28,12},{1,17},{... | collective-permute-start | bytes 172040 | tf_op jit(solution)/shard_map/ppermute | solution.py:32
  72.3 5.1 %collective-permute-start.18 = (f32[112,128]{1,0:T(8,128)S(1)}, f32[112,128]{1,0:T(8,128)S(1)}, u32[]{:S(2)}, u32[]{:S(2)}) collective-permute-start(f32[112,128]{1,0:T(8,128)S(1)} %add.110), channel_id=1, source_target_pairs={{0,16},{4,20},{8,24},{12,28},{16,0},{20,4},{24,8},{28,12},{1,17},{... | collective-permute-start | bytes 172040 | tf_op jit(solution)/shard_map/ppermute | solution.py:32
  74.7 2.8 %collective-permute-start.25 = (f32[112,128]{1,0:T(8,128)S(1)}, f32[112,128]{1,0:T(8,128)S(1)}, u32[]{:S(2)}, u32[]{:S(2)}) collective-permute-start(f32[112,128]{1,0:T(8,128)S(1)} %add.117), channel_id=1, source_target_pairs={{0,1},{1,0},{2,3},{3,2},{4,5},{5,4},{6,7},{7,6},{8,9},{9,8},{10,11... | collective-permute-start | bytes 172040 | tf_op jit(solution)/shard_map/ppermute | solution.py:48
  (8 other events, 45.0 us)

commit v3 on v2

--- a/solution.py
+++ b/solution.py
@@ -18,6 +18,56 @@
         high = lax.ppermute(lax.slice_in_dim(block, 0, width, axis=dim), axis, backward)
         block = jnp.concatenate([low, block, high], axis=dim)
     return block
+
+
+def haloed(block, dim_sky, dim_los):
+    count_sky = lax.axis_size("sky")
+    count_los = lax.axis_size("los")
+    extent_sky = block.shape[dim_sky]
+    extent_los = block.shape[dim_los]
+
+    def part(sky_range, los_range):
+        piece = lax.slice_in_dim(block, sky_range[0], sky_range[1], axis=dim_sky)
+        return lax.slice_in_dim(piece, los_range[0], los_range[1], axis=dim_los)
+
+    def shift(piece, step_sky, step_los):
+        pairs = [
+            (
+                sky * count_los + los,
+                (sky + step_sky) % count_sky * count_los + (los + step_los) % count_los,
+            )
+            for sky in range(count_sky)
+            for los in range(count_los)
+        ]
+        return lax.ppermute(piece, ("sky", "los"), pairs)
+
+    last_sky = (extent_sky - 1, extent_sky)
+    first_sky = (0, 1)
+    all_sky = (0, extent_sky)
+    last_los = (extent_los - 1, extent_los)
+    first_los = (0, 1)
+    all_los = (0, extent_los)
+    low_row = jnp.concatenate(
+        (
+            shift(part(last_sky, last_los), 1, 1),
+            shift(part(last_sky, all_los), 1, 0),
+            shift(part(last_sky, first_los), 1, -1),
+        ),
+        axis=dim_los,
+    )
+    middle = jnp.concatenate(
+        (shift(part(all_sky, last_los), 0, 1), block, shift(part(all_sky, first_los), 0, -1)),
+        axis=dim_los,
+    )
+    high_row = jnp.concatenate(
+        (
+            shift(part(first_sky, last_los), -1, 1),
+            shift(part(first_sky, all_los), -1, 0),
+            shift(part(first_sky, first_los), -1, -1),
+        ),
+        axis=dim_los,
+    )
+    return jnp.concatenate((low_row, middle, high_row), axis=dim_sky)
 
 
 def butterfly_sum(value, axes, skip=0):
@@ -147,13 +197,13 @@
     grad_bias = jnp.sum(head_grad.astype(jnp.float32), axis=(1, 2, 3)) * norm_factor
     back_second = jnp.einsum("oi,oxzy->ixzy", w_out, head_grad, preferred_element_type=jnp.float32)
     grad_second_pre = (back_second * silu_slope(second_wide)).astype(jnp.bfloat16)
-    second_padded = wrap_columns(extended(grad_second_pre, (("sky", 1), ("los", 2)), 1))
+    second_padded = wrap_columns(haloed(grad_second_pre, 1, 2))
     back_first = spread_local(w_second, second_padded, shape)
     grad_first_pre = (back_first * silu_slope(first_wide)).astype(jnp.bfloat16)
-    first_padded = wrap_columns(extended(grad_first_pre, (("sky", 1), ("los", 2)), 1))
+    first_padded = wrap_columns(haloed(grad_first_pre, 1, 2))
     grad_features = spread_local(w_first, first_padded, shape).astype(jnp.bfloat16)
     saved_padded = wrap_columns(
-        extended(jnp.stack((features, pre_first)), (("sky", 2), ("los", 3)), 1)
+        haloed(jnp.stack((features, pre_first)), 2, 3)
     )
     hidden_padded = jax.nn.silu(saved_padded[1].astype(jnp.float32)).astype(jnp.bfloat16)
     grad_second = taps_from_inputs(grad_second_pre, hidden_padded)

time: 82.1 us -> 104 us (1.27)
  starting transfers between devices: 33.2 us -> 57.2 us
  waiting for transfers between devices: 13.8 us -> 11 us
  other arithmetic: 5.2 us -> 6.35 us
    ppermute x12 -> x24, starting transfers between devices: 19.8 us -> 43.9 us  [shift(): return lax.ppermute(piece, ('sky', 'los'), pairs)]
    ppermute x12 -> x24, waiting for transfers between devices: 4.54 us -> 1.69 us  [shift(): return lax.ppermute(piece, ('sky', 'los'), pairs)]
    concatenate x1, other arithmetic: 0.78 us -> 1.99 us  [wrap_columns(): return jnp.concatenate((field[..., -1:], field, field[..., :1]), axis=-1)]
    unnamed x68 -> x66, local copies, waits for them, and re-layouts: 12.8 us -> 12.6 us
  transfers between devices with their start and end apart: 26 -> 38, of which waited for: 9 -> 8; matrix products, arithmetic and copies ran while one was open for 34% -> 25% of each run, Pallas kernels for 0% -> 0%
where the time goes in v3:
time: 104 us
  starting transfers between devices  57.2 us (55%)
  local copies, waits for them, and re-layouts  20.3 us (20%)
  waiting for transfers between devices  11 us (11%)
  matrix products  7.63 us (7%)
  other arithmetic  6.35 us (6%)
  between operations  1.59 us (2%)
    ppermute x24, starting transfers between devices, shift(): return lax.ppermute(piece, ('sky', 'los'), pairs)  43.9 us
    ppermute x10, starting transfers between devices, butterfly_sum(): value = value + lax.ppermute(value, axis, pairs)  12.6 us
    unnamed x66, local copies, waits for them, and re-layouts  12.6 us
    ppermute x10, waiting for transfers between devices, butterfly_sum(): value = value + lax.ppermute(value, axis, pairs)  8.32 us
    conv_general_dilated x2, matrix products, spread_local(): lax.conv_general_dilated(padded[None], kernel, (1, 1, 1), 'VALID', dimens...  3.44 us
    dot_general x2, matrix products, taps_from_inputs(): jnp.einsum('oxzy,tixzy->toi', grad_field, windows, preferred_element_type...  2.09 us
  transfers between devices with their start and end apart: 38, of which 8 were waited for; matrix products, arithmetic and copies ran while one was open for 25% of the time, Pallas kernels for 0%

profile of v3, /device:TPU:0, one launch (start us, length us, event | category | flops | bytes accessed | tf_op | source)
XLA Modules:
  0.0 104.1 jit_solution(7414431808216035607)
XLA Ops:
  5.8 2.6 %collective-permute-start.1 = (f32[2,2,128]{2,1,0:T(2,128)S(1)}, f32[2,2,128]{2,1,0:T(2,128)S(1)}, u32[]{:S(2)}, u32[]{:S(2)}) collective-permute-start(f32[2,2,128]{2,1,0:T(2,128)S(1)} %fusion.146), channel_id=1, source_target_pairs={{0,2},{1,3},{2,0},{3,1},{4,6},{5,7},{6,4},{7,5},{8,10},{9,11},{10,... | collective-permute-start | bytes 6152 | tf_op jit(solution)/shard_map/ppermute | solution.py:82
  8.3 1.6 %collective-permute-done.1 = f32[2,2,128]{2,1,0:T(2,128)S(1)} collective-permute-done((f32[2,2,128]{2,1,0:T(2,128)S(1)}, f32[2,2,128]{2,1,0:T(2,128)S(1)}, u32[]{:S(2)}, u32[]{:S(2)}) %collective-permute-start.1) | collective-permute-done | bytes 2080 | tf_op jit(solution)/shard_map/ppermute | solution.py:82
  13.1 4.3 %collective-permute-start.9 = (bf16[32,1,1,128]{3,0,2,1:T(8,128)(2,1)S(1)}, bf16[32,1,1,128]{3,0,2,1:T(8,128)(2,1)S(1)}, u32[]{:S(2)}, u32[]{:S(2)}) collective-permute-start(bf16[32,1,1,128]{3,0,2,1:T(8,128)(2,1)S(1)} %get-tuple-element.42), channel_id=1, source_target_pairs={{0,31},{1,28},{2,29},{3,30},{4,3},{5,0},{6,1},{7,2},{8,7},{9,4},{1... | collective-permute-start | bytes 24584 | tf_op jit(solution)/shard_map/ppermute | solution.py:42
  18.0 2.1 %collective-permute-start.4 = (bf16[32,1,1,128]{3,0,2,1:T(8,128)(2,1)S(1)}, bf16[32,1,1,128]{3,0,2,1:T(8,128)(2,1)S(1)}, u32[]{:S(2)}, u32[]{:S(2)}) collective-permute-start(bf16[32,1,1,128]{3,0,2,1:T(8,128)(2,1)S(1)} %get-tuple-element.44), channel_id=1, source_target_pairs={{0,7},{1,4},{2,5},{3,6},{4,11},{5,8},{6,9},{7,10},{8,15},{9,12},{1... | collective-permute-start | bytes 24584 | tf_op jit(solution)/shard_map/ppermute | solution.py:42
  22.1 4.9 %collective-permute-start.8 = (bf16[32,1,8,128]{3,0,2,1:T(8,128)(2,1)S(1)}, bf16[32,1,8,128]{3,0,2,1:T(8,128)(2,1)S(1)}, u32[]{:S(2)}, u32[]{:S(2)}) collective-permute-start(bf16[32,1,8,128]{3,0,2,1:T(8,128)(2,1)S(1)} %get-tuple-element.46), channel_id=1, source_target_pairs={{0,28},{1,29},{2,30},{3,31},{4,0},{5,1},{6,2},{7,3},{8,4},{9,5},{1... | collective-permute-start | bytes 196616 | tf_op jit(solution)/shard_map/ppermute | solution.py:42
  27.3 5.4 %collective-permute-start.23 = (bf16[2,32,1,1,128]{4,1,3,2,0:T(8,128)(2,1)S(1)}, bf16[2,32,1,1,128]{4,1,3,2,0:T(8,128)(2,1)S(1)}, u32[]{:S(2)}, u32[]{:S(2)}) collective-permute-start(bf16[2,32,1,1,128]{4,1,3,2,0:T(8,128)(2,1)S(1)} %get-tuple-element.27), channel_id=1, source_target_pairs={{0,29},{1,30},{2,31},{3,28},{4,1},{5,2},{6,3},{7,0},{8,5},{9,6},{1... | collective-permute-start | bytes 49160 | tf_op jit(solution)/shard_map/ppermute | solution.py:42
  32.7 2.5 %collective-permute-start.25 = (bf16[2,32,1,1,128]{4,1,3,2,0:T(8,128)(2,1)S(1)}, bf16[2,32,1,1,128]{4,1,3,2,0:T(8,128)(2,1)S(1)}, u32[]{:S(2)}, u32[]{:S(2)}) collective-permute-start(bf16[2,32,1,1,128]{4,1,3,2,0:T(8,128)(2,1)S(1)} %get-tuple-element.28), channel_id=1, source_target_pairs={{0,31},{1,28},{2,29},{3,30},{4,3},{5,0},{6,1},{7,2},{8,7},{9,4},{1... | collective-permute-start | bytes 49160 | tf_op jit(solution)/shard_map/ppermute | solution.py:42
  35.8 2.1 %copy.96 = bf16[32,4,10,1,130]{0,1,4,2,3:T(4,128)(2,1)S(1)} copy(bf16[32,4,10,1,130]{4,0,2,1,3:T(8,128)(2,1)S(1)} %maximum_bitcast_fusion) | data formatting | bytes 665600
  38.8 1.7 %fusion.19 = f32[2,8,8,17,32]{4,2,3,1,0:T(8,128)S(1)} fusion(bf16[3,3,3,32,32]{4,3,2,1,0:T(8,128)(2,1)S(1)} %copy-done, bf16[32,4,10,1,7,2]{0,4,5,2,1,3:T(8,128)(2,1)S(1)} %slice.477, bf16[32,4,10,1,8,17]{0,4,5,2,1,3:T(8,128)(2,1)S(1)} %copy.46, pred[8,17]{0,1:T(8,128)(4,1)S(1)} %copy-done.3), kind=kOutput, calls=%fused_computation.18 | convolution fusion | flops 121561088 | bytes 717960 | tf_op jit(solution)/shard_map/conv_general_dilated | solution.py:133
  41.6 1.8 %collective-permute-start.22 = (bf16[2,32,2,1,128]{4,1,3,2,0:T(8,128)(2,1)S(1)}, bf16[2,32,2,1,128]{4,1,3,2,0:T(8,128)(2,1)S(1)}, u32[]{:S(2)}, u32[]{:S(2)}) collective-permute-start(bf16[2,32,2,1,128]{4,1,3,2,0:T(8,128)(2,1)S(1)} %get-tuple-element.32), channel_id=1, source_target_pairs={{0,3},{1,0},{2,1},{3,2},{4,7},{5,4},{6,5},{7,6},{8,11},{9,8},{10,9... | collective-permute-start | bytes 98312 | tf_op jit(solution)/shard_map/ppermute | solution.py:42
  43.4 4.7 %collective-permute-start.24 = (bf16[2,32,1,8,128]{4,1,3,2,0:T(8,128)(2,1)S(1)}, bf16[2,32,1,8,128]{4,1,3,2,0:T(8,128)(2,1)S(1)}, u32[]{:S(2)}, u32[]{:S(2)}) collective-permute-start(bf16[2,32,1,8,128]{4,1,3,2,0:T(8,128)(2,1)S(1)} %get-tuple-element.30), channel_id=1, source_target_pairs={{0,28},{1,29},{2,30},{3,31},{4,0},{5,1},{6,2},{7,3},{8,4},{9,5},{1... | collective-permute-start | bytes 393224 | tf_op jit(solution)/shard_map/ppermute | solution.py:42
  48.2 5.3 %collective-permute-start.17 = (bf16[32,1,1,128]{3,0,2,1:T(8,128)(2,1)S(1)}, bf16[32,1,1,128]{3,0,2,1:T(8,128)(2,1)S(1)}, u32[]{:S(2)}, u32[]{:S(2)}) collective-permute-start(bf16[32,1,1,128]{3,0,2,1:T(8,128)(2,1)S(1)} %get-tuple-element.34), channel_id=1, source_target_pairs={{0,31},{1,28},{2,29},{3,30},{4,3},{5,0},{6,1},{7,2},{8,7},{9,4},{1... | collective-permute-start | bytes 24584 | tf_op jit(solution)/shard_map/ppermute | solution.py:42
  53.7 2.5 %collective-permute-start.12 = (bf16[32,1,1,128]{3,0,2,1:T(8,128)(2,1)S(1)}, bf16[32,1,1,128]{3,0,2,1:T(8,128)(2,1)S(1)}, u32[]{:S(2)}, u32[]{:S(2)}) collective-permute-start(bf16[32,1,1,128]{3,0,2,1:T(8,128)(2,1)S(1)} %get-tuple-element.36), channel_id=1, source_target_pairs={{0,7},{1,4},{2,5},{3,6},{4,11},{5,8},{6,9},{7,10},{8,15},{9,12},{1... | collective-permute-start | bytes 24584 | tf_op jit(solution)/shard_map/ppermute | solution.py:42
  56.5 2.0 %pad_maximum_fusion = bf16[2,32,4,10,130]{4,1,3,2,0:T(8,128)(2,1)S(1)} fusion(bf16[2,32,4,10,1]{4,1,3,2,0:T(8,128)(2,1)S(1)} %get-tuple-element.20, bf16[2,32,1,1,128]{4,1,3,2,0:T(8,128)(2,1)S(1)} %collective-permute-done.25, bf16[2,32,1,8,128]{4,1,3,2,0:T(8,128)(2,1)S(1)} %collective-permute-done.24, ...), kind=kLoop, calls=%fused_computation.24 | loop fusion | flops 7987200 | bytes 1331200 | tf_op jit(solution)/shard_map/concatenate | solution.py:128
  67.9 1.8 %collective-permute-start.14 = (bf16[32,2,1,128]{3,0,2,1:T(8,128)(2,1)S(1)}, bf16[32,2,1,128]{3,0,2,1:T(8,128)(2,1)S(1)}, u32[]{:S(2)}, u32[]{:S(2)}) collective-permute-start(bf16[32,2,1,128]{3,0,2,1:T(8,128)(2,1)S(1)} %get-tuple-element.40), channel_id=1, source_target_pairs={{0,3},{1,0},{2,1},{3,2},{4,7},{5,4},{6,5},{7,6},{8,11},{9,8},{10,9... | collective-permute-start | bytes 49160 | tf_op jit(solution)/shard_map/ppermute | solution.py:42
  69.7 4.7 %collective-permute-start.16 = (bf16[32,1,8,128]{3,0,2,1:T(8,128)(2,1)S(1)}, bf16[32,1,8,128]{3,0,2,1:T(8,128)(2,1)S(1)}, u32[]{:S(2)}, u32[]{:S(2)}) collective-permute-start(bf16[32,1,8,128]{3,0,2,1:T(8,128)(2,1)S(1)} %get-tuple-element.38), channel_id=1, source_target_pairs={{0,28},{1,29},{2,30},{3,31},{4,0},{5,1},{6,2},{7,3},{8,4},{9,5},{1... | collective-permute-start | bytes 196616 | tf_op jit(solution)/shard_map/ppermute | solution.py:42
  75.0 1.6 %collective-permute-done.11 = bf16[32,1,8,128]{3,0,2,1:T(8,128)(2,1)S(1)} collective-permute-done((bf16[32,1,8,128]{3,0,2,1:T(8,128)(2,1)S(1)}, bf16[32,1,8,128]{3,0,2,1:T(8,128)(2,1)S(1)}, u32[]{:S(2)}, u32[]{:S(2)}) %collective-permute-start.11) | collective-permute-done | bytes 65568 | tf_op jit(solution)/shard_map/ppermute | solution.py:42
  76.7 1.7 %collective-permute-start.33 = (f32[112,128]{1,0:T(8,128)S(1)}, f32[112,128]{1,0:T(8,128)S(1)}, u32[]{:S(2)}, u32[]{:S(2)}) collective-permute-start(f32[112,128]{1,0:T(8,128)S(1)} %select_add_fusion), channel_id=1, source_target_pairs={{0,2},{1,3},{2,0},{3,1},{4,6},{5,7},{6,4},{7,5},{8,10},{9,11},{10,... | collective-permute-start | bytes 172040 | tf_op jit(solution)/shard_map/ppermute | solution.py:82
  78.9 2.6 %collective-permute-done.33 = f32[112,128]{1,0:T(8,128)S(1)} collective-permute-done((f32[112,128]{1,0:T(8,128)S(1)}, f32[112,128]{1,0:T(8,128)S(1)}, u32[]{:S(2)}, u32[]{:S(2)}) %collective-permute-start.33) | collective-permute-done | bytes 57376 | tf_op jit(solution)/shard_map/ppermute | solution.py:82
  83.9 1.9 %collective-permute-done.34 = f32[112,128]{1,0:T(8,128)S(1)} collective-permute-done((f32[112,128]{1,0:T(8,128)S(1)}, f32[112,128]{1,0:T(8,128)S(1)}, u32[]{:S(2)}, u32[]{:S(2)}) %collective-permute-start.34) | collective-permute-done | bytes 57376 | tf_op jit(solution)/shard_map/ppermute | solution.py:82
  86.3 2.1 %copy.97 = bf16[32,4,10,1,130]{0,1,4,2,3:T(4,128)(2,1)S(1)} copy(bf16[32,4,10,1,130]{4,0,2,1,3:T(8,128)(2,1)S(1)} %maximum_bitcast_fusion.1) | data formatting | bytes 665600
  89.4 2.1 %collective-permute-start.29 = (f32[112,128]{1,0:T(8,128)S(1)}, f32[112,128]{1,0:T(8,128)S(1)}, u32[]{:S(2)}, u32[]{:S(2)}) collective-permute-start(f32[112,128]{1,0:T(8,128)S(1)} %add.109), channel_id=1, source_target_pairs={{0,8},{4,12},{8,0},{12,4},{16,24},{20,28},{24,16},{28,20},{1,9},{5... | collective-permute-start | bytes 172040 | tf_op jit(solution)/shard_map/ppermute | solution.py:82
  92.8 1.7 %fusion.22 = bf16[2,8,8,17,32]{4,2,3,1,0:T(8,128)(2,1)S(1)} fusion(bf16[3,3,3,32,32]{4,3,2,1,0:T(8,128)(2,1)S(1)} %copy-done.2, bf16[32,4,10,1,7,2]{0,4,5,2,1,3:T(8,128)(2,1)S(1)} %slice.489, bf16[32,4,10,1,8,17]{0,4,5,2,1,3:T(8,128)(2,1)S(1)} %copy.52, pred[8,17]{0,1:T(8,128)(4,1)S(1)} %copy-done.3), kind=kOutput, calls=%fused_computation.19 | convolution fusion | flops 121630720 | bytes 578696 | tf_op jit(solution)/shard_map/conv_general_dilated | solution.py:133
  94.6 2.6 %collective-permute-start.30 = (f32[112,128]{1,0:T(8,128)S(1)}, f32[112,128]{1,0:T(8,128)S(1)}, u32[]{:S(2)}, u32[]{:S(2)}) collective-permute-start(f32[112,128]{1,0:T(8,128)S(1)} %add.110), channel_id=1, source_target_pairs={{0,16},{4,20},{8,24},{12,28},{16,0},{20,4},{24,8},{28,12},{1,17},{... | collective-permute-start | bytes 172040 | tf_op jit(solution)/shard_map/ppermute | solution.py:82
  (201 shorter events, 36.4 us)
Async XLA Ops:
  12.1 8.8 %collective-permute-start.2 = (bf16[32,1,1,128]{3,0,2,1:T(8,128)(2,1)S(1)}, bf16[32,1,1,128]{3,0,2,1:T(8,128)(2,1)S(1)}, u32[]{:S(2)}, u32[]{:S(2)}) collective-permute-start(bf16[32,1,1,128]{3,0,2,1:T(8,128)(2,1)S(1)} %get-tuple-element.41), channel_id=1, source_target_pairs={{0,5},{1,6},{2,7},{3,4},{4,9},{5,10},{6,11},{7,8},{8,13},{9,14},{1... | collective-permute-start | bytes 24584 | tf_op jit(solution)/shard_map/ppermute | solution.py:42
  13.1 8.7 %collective-permute-start.9 = (bf16[32,1,1,128]{3,0,2,1:T(8,128)(2,1)S(1)}, bf16[32,1,1,128]{3,0,2,1:T(8,128)(2,1)S(1)}, u32[]{:S(2)}, u32[]{:S(2)}) collective-permute-start(bf16[32,1,1,128]{3,0,2,1:T(8,128)(2,1)S(1)} %get-tuple-element.42), channel_id=1, source_target_pairs={{0,31},{1,28},{2,29},{3,30},{4,3},{5,0},{6,1},{7,2},{8,7},{9,4},{1... | collective-permute-start | bytes 24584 | tf_op jit(solution)/shard_map/ppermute | solution.py:42
  18.0 9.1 %collective-permute-start.4 = (bf16[32,1,1,128]{3,0,2,1:T(8,128)(2,1)S(1)}, bf16[32,1,1,128]{3,0,2,1:T(8,128)(2,1)S(1)}, u32[]{:S(2)}, u32[]{:S(2)}) collective-permute-start(bf16[32,1,1,128]{3,0,2,1:T(8,128)(2,1)S(1)} %get-tuple-element.44), channel_id=1, source_target_pairs={{0,7},{1,4},{2,5},{3,6},{4,11},{5,8},{6,9},{7,10},{8,15},{9,12},{1... | collective-permute-start | bytes 24584 | tf_op jit(solution)/shard_map/ppermute | solution.py:42
  20.1 7.0 %collective-permute-start.5 = (bf16[32,2,1,128]{3,0,2,1:T(8,128)(2,1)S(1)}, bf16[32,2,1,128]{3,0,2,1:T(8,128)(2,1)S(1)}, u32[]{:S(2)}, u32[]{:S(2)}) collective-permute-start(bf16[32,2,1,128]{3,0,2,1:T(8,128)(2,1)S(1)} %get-tuple-element.47), channel_id=1, source_target_pairs={{0,1},{1,2},{2,3},{3,0},{4,5},{5,6},{6,7},{7,4},{8,9},{9,10},{10,1... | collective-permute-start | bytes 49160 | tf_op jit(solution)/shard_map/ppermute | solution.py:42
  20.9 6.4 %collective-permute-start.6 = (bf16[32,2,1,128]{3,0,2,1:T(8,128)(2,1)S(1)}, bf16[32,2,1,128]{3,0,2,1:T(8,128)(2,1)S(1)}, u32[]{:S(2)}, u32[]{:S(2)}) collective-permute-start(bf16[32,2,1,128]{3,0,2,1:T(8,128)(2,1)S(1)} %get-tuple-element.48), channel_id=1, source_target_pairs={{0,3},{1,0},{2,1},{3,2},{4,7},{5,4},{6,5},{7,6},{8,11},{9,8},{10,9... | collective-permute-start | bytes 49160 | tf_op jit(solution)/shard_map/ppermute | solution.py:42
  21.9 10.8 %collective-permute-start.3 = (bf16[32,1,8,128]{3,0,2,1:T(8,128)(2,1)S(1)}, bf16[32,1,8,128]{3,0,2,1:T(8,128)(2,1)S(1)}, u32[]{:S(2)}, u32[]{:S(2)}) collective-permute-start(bf16[32,1,8,128]{3,0,2,1:T(8,128)(2,1)S(1)} %get-tuple-element.45), channel_id=1, source_target_pairs={{0,4},{1,5},{2,6},{3,7},{4,8},{5,9},{6,10},{7,11},{8,12},{9,13},{1... | collective-permute-start | bytes 196616 | tf_op jit(solution)/shard_map/ppermute | solution.py:42
  22.1 13.0 %collective-permute-start.8 = (bf16[32,1,8,128]{3,0,2,1:T(8,128)(2,1)S(1)}, bf16[32,1,8,128]{3,0,2,1:T(8,128)(2,1)S(1)}, u32[]{:S(2)}, u32[]{:S(2)}) collective-permute-start(bf16[32,1,8,128]{3,0,2,1:T(8,128)(2,1)S(1)} %get-tuple-element.46), channel_id=1, source_target_pairs={{0,28},{1,29},{2,30},{3,31},{4,0},{5,1},{6,2},{7,3},{8,4},{9,5},{1... | collective-permute-start | bytes 196616 | tf_op jit(solution)/shard_map/ppermute | solution.py:42
  27.1 14.5 %collective-permute-start.18 = (bf16[2,32,1,1,128]{4,1,3,2,0:T(8,128)(2,1)S(1)}, bf16[2,32,1,1,128]{4,1,3,2,0:T(8,128)(2,1)S(1)}, u32[]{:S(2)}, u32[]{:S(2)}) collective-permute-start(bf16[2,32,1,1,128]{4,1,3,2,0:T(8,128)(2,1)S(1)} %get-tuple-element.25), channel_id=1, source_target_pairs={{0,5},{1,6},{2,7},{3,4},{4,9},{5,10},{6,11},{7,8},{8,13},{9,14},{1... | collective-permute-start | bytes 49160 | tf_op jit(solution)/shard_map/ppermute | solution.py:42
  27.1 16.3 %collective-permute-start.20 = (bf16[2,32,1,1,128]{4,1,3,2,0:T(8,128)(2,1)S(1)}, bf16[2,32,1,1,128]{4,1,3,2,0:T(8,128)(2,1)S(1)}, u32[]{:S(2)}, u32[]{:S(2)}) collective-permute-start(bf16[2,32,1,1,128]{4,1,3,2,0:T(8,128)(2,1)S(1)} %get-tuple-element.26), channel_id=1, source_target_pairs={{0,7},{1,4},{2,5},{3,6},{4,11},{5,8},{6,9},{7,10},{8,15},{9,12},{1... | collective-permute-start | bytes 49160 | tf_op jit(solution)/shard_map/ppermute | solution.py:42
  27.3 16.1 %collective-permute-start.23 = (bf16[2,32,1,1,128]{4,1,3,2,0:T(8,128)(2,1)S(1)}, bf16[2,32,1,1,128]{4,1,3,2,0:T(8,128)(2,1)S(1)}, u32[]{:S(2)}, u32[]{:S(2)}) collective-permute-start(bf16[2,32,1,1,128]{4,1,3,2,0:T(8,128)(2,1)S(1)} %get-tuple-element.27), channel_id=1, source_target_pairs={{0,29},{1,30},{2,31},{3,28},{4,1},{5,2},{6,3},{7,0},{8,5},{9,6},{1... | collective-permute-start | bytes 49160 | tf_op jit(solution)/shard_map/ppermute | solution.py:42
  32.7 15.5 %collective-permute-start.25 = (bf16[2,32,1,1,128]{4,1,3,2,0:T(8,128)(2,1)S(1)}, bf16[2,32,1,1,128]{4,1,3,2,0:T(8,128)(2,1)S(1)}, u32[]{:S(2)}, u32[]{:S(2)}) collective-permute-start(bf16[2,32,1,1,128]{4,1,3,2,0:T(8,128)(2,1)S(1)} %get-tuple-element.28), channel_id=1, source_target_pairs={{0,31},{1,28},{2,29},{3,30},{4,3},{5,0},{6,1},{7,2},{8,7},{9,4},{1... | collective-permute-start | bytes 49160 | tf_op jit(solution)/shard_map/ppermute | solution.py:42
  35.1 13.1 %collective-permute-start.21 = (bf16[2,32,2,1,128]{4,1,3,2,0:T(8,128)(2,1)S(1)}, bf16[2,32,2,1,128]{4,1,3,2,0:T(8,128)(2,1)S(1)}, u32[]{:S(2)}, u32[]{:S(2)}) collective-permute-start(bf16[2,32,2,1,128]{4,1,3,2,0:T(8,128)(2,1)S(1)} %get-tuple-element.31), channel_id=1, source_target_pairs={{0,1},{1,2},{2,3},{3,0},{4,5},{5,6},{6,7},{7,4},{8,9},{9,10},{10,1... | collective-permute-start | bytes 98312 | tf_op jit(solution)/shard_map/ppermute | solution.py:42
  41.6 11.9 %collective-permute-start.22 = (bf16[2,32,2,1,128]{4,1,3,2,0:T(8,128)(2,1)S(1)}, bf16[2,32,2,1,128]{4,1,3,2,0:T(8,128)(2,1)S(1)}, u32[]{:S(2)}, u32[]{:S(2)}) collective-permute-start(bf16[2,32,2,1,128]{4,1,3,2,0:T(8,128)(2,1)S(1)} %get-tuple-element.32), channel_id=1, source_target_pairs={{0,3},{1,0},{2,1},{3,2},{4,7},{5,4},{6,5},{7,6},{8,11},{9,8},{10,9... | collective-permute-start | bytes 98312 | tf_op jit(solution)/shard_map/ppermute | solution.py:42
  43.4 10.3 %collective-permute-start.19 = (bf16[2,32,1,8,128]{4,1,3,2,0:T(8,128)(2,1)S(1)}, bf16[2,32,1,8,128]{4,1,3,2,0:T(8,128)(2,1)S(1)}, u32[]{:S(2)}, u32[]{:S(2)}) collective-permute-start(bf16[2,32,1,8,128]{4,1,3,2,0:T(8,128)(2,1)S(1)} %get-tuple-element.29), channel_id=1, source_target_pairs={{0,4},{1,5},{2,6},{3,7},{4,8},{5,9},{6,10},{7,11},{8,12},{9,13},{1... | collective-permute-start | bytes 393224 | tf_op jit(solution)/shard_map/ppermute | solution.py:42
  43.4 12.7 %collective-permute-start.24 = (bf16[2,32,1,8,128]{4,1,3,2,0:T(8,128)(2,1)S(1)}, bf16[2,32,1,8,128]{4,1,3,2,0:T(8,128)(2,1)S(1)}, u32[]{:S(2)}, u32[]{:S(2)}) collective-permute-start(bf16[2,32,1,8,128]{4,1,3,2,0:T(8,128)(2,1)S(1)} %get-tuple-element.30), channel_id=1, source_target_pairs={{0,28},{1,29},{2,30},{3,31},{4,0},{5,1},{6,2},{7,3},{8,4},{9,5},{1... | collective-permute-start | bytes 393224 | tf_op jit(solution)/shard_map/ppermute | solution.py:42
  48.2 19.7 %collective-permute-start.10 = (bf16[32,1,1,128]{3,0,2,1:T(8,128)(2,1)S(1)}, bf16[32,1,1,128]{3,0,2,1:T(8,128)(2,1)S(1)}, u32[]{:S(2)}, u32[]{:S(2)}) collective-permute-start(bf16[32,1,1,128]{3,0,2,1:T(8,128)(2,1)S(1)} %get-tuple-element.33), channel_id=1, source_target_pairs={{0,5},{1,6},{2,7},{3,4},{4,9},{5,10},{6,11},{7,8},{8,13},{9,14},{1... | collective-permute-start | bytes 24584 | tf_op jit(solution)/shard_map/ppermute | solution.py:42
  48.2 21.5 %collective-permute-start.17 = (bf16[32,1,1,128]{3,0,2,1:T(8,128)(2,1)S(1)}, bf16[32,1,1,128]{3,0,2,1:T(8,128)(2,1)S(1)}, u32[]{:S(2)}, u32[]{:S(2)}) collective-permute-start(bf16[32,1,1,128]{3,0,2,1:T(8,128)(2,1)S(1)} %get-tuple-element.34), channel_id=1, source_target_pairs={{0,31},{1,28},{2,29},{3,30},{4,3},{5,0},{6,1},{7,2},{8,7},{9,4},{1... | collective-permute-start | bytes 24584 | tf_op jit(solution)/shard_map/ppermute | solution.py:42
  53.5 16.1 %collective-permute-start.15 = (bf16[32,1,1,128]{3,0,2,1:T(8,128)(2,1)S(1)}, bf16[32,1,1,128]{3,0,2,1:T(8,128)(2,1)S(1)}, u32[]{:S(2)}, u32[]{:S(2)}) collective-permute-start(bf16[32,1,1,128]{3,0,2,1:T(8,128)(2,1)S(1)} %get-tuple-element.35), channel_id=1, source_target_pairs={{0,29},{1,30},{2,31},{3,28},{4,1},{5,2},{6,3},{7,0},{8,5},{9,6},{1... | collective-permute-start | bytes 24584 | tf_op jit(solution)/shard_map/ppermute | solution.py:42
  53.7 20.7 %collective-permute-start.12 = (bf16[32,1,1,128]{3,0,2,1:T(8,128)(2,1)S(1)}, bf16[32,1,1,128]{3,0,2,1:T(8,128)(2,1)S(1)}, u32[]{:S(2)}, u32[]{:S(2)}) collective-permute-start(bf16[32,1,1,128]{3,0,2,1:T(8,128)(2,1)S(1)} %get-tuple-element.36), channel_id=1, source_target_pairs={{0,7},{1,4},{2,5},{3,6},{4,11},{5,8},{6,9},{7,10},{8,15},{9,12},{1... | collective-permute-start | bytes 24584 | tf_op jit(solution)/shard_map/ppermute | solution.py:42
  56.2 18.3 %collective-permute-start.13 = (bf16[32,2,1,128]{3,0,2,1:T(8,128)(2,1)S(1)}, bf16[32,2,1,128]{3,0,2,1:T(8,128)(2,1)S(1)}, u32[]{:S(2)}, u32[]{:S(2)}) collective-permute-start(bf16[32,2,1,128]{3,0,2,1:T(8,128)(2,1)S(1)} %get-tuple-element.39), channel_id=1, source_target_pairs={{0,1},{1,2},{2,3},{3,0},{4,5},{5,6},{6,7},{7,4},{8,9},{9,10},{10,1... | collective-permute-start | bytes 49160 | tf_op jit(solution)/shard_map/ppermute | solution.py:42
  67.9 7.1 %collective-permute-start.14 = (bf16[32,2,1,128]{3,0,2,1:T(8,128)(2,1)S(1)}, bf16[32,2,1,128]{3,0,2,1:T(8,128)(2,1)S(1)}, u32[]{:S(2)}, u32[]{:S(2)}) collective-permute-start(bf16[32,2,1,128]{3,0,2,1:T(8,128)(2,1)S(1)} %get-tuple-element.40), channel_id=1, source_target_pairs={{0,3},{1,0},{2,1},{3,2},{4,7},{5,4},{6,5},{7,6},{8,11},{9,8},{10,9... | collective-permute-start | bytes 49160 | tf_op jit(solution)/shard_map/ppermute | solution.py:42
  69.7 7.0 %collective-permute-start.11 = (bf16[32,1,8,128]{3,0,2,1:T(8,128)(2,1)S(1)}, bf16[32,1,8,128]{3,0,2,1:T(8,128)(2,1)S(1)}, u32[]{:S(2)}, u32[]{:S(2)}) collective-permute-start(bf16[32,1,8,128]{3,0,2,1:T(8,128)(2,1)S(1)} %get-tuple-element.37), channel_id=1, source_target_pairs={{0,4},{1,5},{2,6},{3,7},{4,8},{5,9},{6,10},{7,11},{8,12},{9,13},{1... | collective-permute-start | bytes 196616 | tf_op jit(solution)/shard_map/ppermute | solution.py:42
  69.7 7.0 %collective-permute-start.16 = (bf16[32,1,8,128]{3,0,2,1:T(8,128)(2,1)S(1)}, bf16[32,1,8,128]{3,0,2,1:T(8,128)(2,1)S(1)}, u32[]{:S(2)}, u32[]{:S(2)}) collective-permute-start(bf16[32,1,8,128]{3,0,2,1:T(8,128)(2,1)S(1)} %get-tuple-element.38), channel_id=1, source_target_pairs={{0,28},{1,29},{2,30},{3,31},{4,0},{5,1},{6,2},{7,3},{8,4},{9,5},{1... | collective-permute-start | bytes 196616 | tf_op jit(solution)/shard_map/ppermute | solution.py:42
  82.6 6.7 %collective-permute-start.28 = (f32[112,128]{1,0:T(8,128)S(1)}, f32[112,128]{1,0:T(8,128)S(1)}, u32[]{:S(2)}, u32[]{:S(2)}) collective-permute-start(f32[112,128]{1,0:T(8,128)S(1)} %add.108), channel_id=1, source_target_pairs={{0,4},{4,0},{8,12},{12,8},{16,20},{20,16},{24,28},{28,24},{1,5},{5... | collective-permute-start | bytes 172040 | tf_op jit(solution)/shard_map/ppermute | solution.py:82
  (18 other events, 103.0 us)

commit v4 on v2

--- a/solution.py
+++ b/solution.py
@@ -158,13 +158,10 @@
     hidden_padded = jax.nn.silu(saved_padded[1].astype(jnp.float32)).astype(jnp.bfloat16)
     grad_second = taps_from_inputs(grad_second_pre, hidden_padded)
     grad_first = taps_from_inputs(grad_first_pre, saved_padded[0])
-    early = (grad_second * norm_factor, grad_out, grad_bias)
-    early_shapes = [part.shape for part in early]
-    grad_second, grad_out, grad_bias = unpack_rows(
-        split_sum(pack_rows(early), ("los", "sky")), early_shapes
-    )
-    (grad_first,) = unpack_rows(
-        split_sum(pack_rows((grad_first * norm_factor,)), ("los", "sky")), [grad_first.shape]
+    reduced = (grad_first * norm_factor, grad_second * norm_factor, grad_out, grad_bias)
+    reduced_shapes = [part.shape for part in reduced]
+    grad_first, grad_second, grad_out, grad_bias = unpack_rows(
+        split_sum(pack_rows(reduced), ("los", "sky")), reduced_shapes
     )
     return (grad_features, grad_first, grad_second, grad_out, grad_bias)
 

time: 82.1 us -> 78.8 us (0.960)
  starting transfers between devices: 33.2 us -> 24.8 us
  waiting for transfers between devices: 13.8 us -> 18.4 us
    ppermute x10 -> x6, starting transfers between devices: 12.6 us -> 4.7 us  [butterfly_sum(): value = value + lax.ppermute(value, axis, pairs)]
    ppermute x10 -> x6, waiting for transfers between devices: 7.39 us -> 13.6 us  [butterfly_sum(): value = value + lax.ppermute(value, axis, pairs)]
    concatenate x1, local copies, waits for them, and re-layouts: 0.08 us -> 0.98 us  [pack_rows(): flat = jnp.concatenate([part.reshape(-1) for part in parts])]
    ppermute x2 -> x1, waiting for transfers between devices: 0.82 us -> 0.01 us  [split_sum(): keep = keep + lax.ppermute(send, first, pairs)]
    unnamed x68 -> x66, local copies, waits for them, and re-layouts: 12.8 us -> 12.6 us
  transfers between devices with their start and end apart: 26 -> 20, of which waited for: 9 -> 9; matrix products, arithmetic and copies ran while one was open for 34% -> 35% of each run, Pallas kernels for 0% -> 0%
where the time goes in v4:
time: 78.8 us; the launch traced here: 78.6 us
  starting transfers between devices  24.8 us (31%)
  local copies, waits for them, and re-layouts  21 us (27%)
  waiting for transfers between devices  18.4 us (23%)
  matrix products  7.68 us (10%)
  other arithmetic  5.16 us (7%)
  between operations  1.46 us (2%)
    ppermute x6, starting transfers between devices, extended(): lax.ppermute(lax.slice_in_dim(block, 0, width, axis=dim), axis, backward)  17.1 us
    ppermute x6, waiting for transfers between devices, butterfly_sum(): value = value + lax.ppermute(value, axis, pairs)  13.6 us
    unnamed x66, local copies, waits for them, and re-layouts  12.6 us
    ppermute x6, starting transfers between devices, butterfly_sum(): value = value + lax.ppermute(value, axis, pairs)  4.7 us
    ppermute x6, waiting for transfers between devices, extended(): lax.ppermute(lax.slice_in_dim(block, block.shape[dim] - width, None, axis...  4.47 us
    conv_general_dilated x2, matrix products, spread_local(): lax.conv_general_dilated(padded[None], kernel, (1, 1, 1), 'VALID', dimens...  3.49 us
    ppermute x6, starting transfers between devices, extended(): lax.ppermute(lax.slice_in_dim(block, block.shape[dim] - width, None, axis...  2.87 us
    dot_general x2, matrix products, taps_from_inputs(): jnp.einsum('oxzy,tixzy->toi', grad_field, windows, preferred_element_type...  2.09 us
  transfers between devices with their start and end apart: 20, of which 9 were waited for; matrix products, arithmetic and copies ran while one was open for 35% of the time, Pallas kernels for 0%

profile of v4, /device:TPU:0, one launch (start us, length us, event | category | flops | bytes accessed | tf_op | source)
XLA Modules:
  0.0 78.6 jit_solution(8502529638310159584)
XLA Ops:
  0.6 1.0 %fusion.48 = bf16[32,2,8,128]{3,0,2,1:T(8,128)(2,1)S(1)} fusion(bf16[32,2,8,128]{3,2,1,0:T(8,128)(2,1)} %param.11), kind=kLoop, calls=%fused_computation.61 | loop fusion | flops 393216 | bytes 262144 | tf_op jit(solution)/shard_map/convert_element_type | solution.py:121
  5.7 2.6 %collective-permute-start.1 = (f32[2,2,128]{2,1,0:T(2,128)S(1)}, f32[2,2,128]{2,1,0:T(2,128)S(1)}, u32[]{:S(2)}, u32[]{:S(2)}) collective-permute-start(f32[2,2,128]{2,1,0:T(2,128)S(1)} %fusion.138), channel_id=1, source_target_pairs={{0,2},{1,3},{2,0},{3,1},{4,6},{5,7},{6,4},{7,5},{8,10},{9,11},{10,... | collective-permute-start | bytes 6152 | tf_op jit(solution)/shard_map/ppermute | solution.py:32
  8.3 1.6 %collective-permute-start.10 = (bf16[2,32,1,8,128]{4,1,3,2,0:T(8,128)(2,1)S(1)}, bf16[2,32,1,8,128]{4,1,3,2,0:T(8,128)(2,1)S(1)}, u32[]{:S(2)}, u32[]{:S(2)}) collective-permute-start(bf16[2,32,1,8,128]{4,1,3,2,0:T(8,128)(2,1)S(1)} %get-tuple-element.27), channel_id=1, source_target_pairs={{0,4},{4,8},{8,12},{12,16},{16,20},{20,24},{24,28},{28,0},{1,5},{5... | collective-permute-start | bytes 393224 | tf_op jit(solution)/shard_map/ppermute | solution.py:15
  9.9 3.2 %collective-permute-start.11 = (bf16[2,32,1,8,128]{4,1,3,2,0:T(8,128)(2,1)S(1)}, bf16[2,32,1,8,128]{4,1,3,2,0:T(8,128)(2,1)S(1)}, u32[]{:S(2)}, u32[]{:S(2)}) collective-permute-start(bf16[2,32,1,8,128]{4,1,3,2,0:T(8,128)(2,1)S(1)} %get-tuple-element.28), channel_id=1, source_target_pairs={{4,0},{8,4},{12,8},{16,12},{20,16},{24,20},{28,24},{0,28},{5,1},{9... | collective-permute-start | bytes 393224 | tf_op jit(solution)/shard_map/ppermute | solution.py:18
  13.9 1.1 %fusion.34 = bf16[32,2,8,128]{3,0,2,1:T(8,128)(2,1)S(1)} fusion(bf16[32,2,8,128]{3,2,1,0:T(8,128)(2,1)} %param.11, bf16[3,2,8,128]{3,2,1,0:T(8,128)(2,1)S(1)} %get-tuple-element.18, bf16[3,32]{1,0:T(4,128)(2,1)} %param.14), kind=kOutput, calls=%fused_computation.33 | convolution fusion | flops 1048576 | bytes 274624 | tf_op jit(solution)/shard_map/oi,oxzy->ixzy/dot_general | solution.py:148
  15.2 4.7 %collective-permute-start.3 = (bf16[32,1,8,128]{3,0,2,1:T(8,128)(2,1)S(1)}, bf16[32,1,8,128]{3,0,2,1:T(8,128)(2,1)S(1)}, u32[]{:S(2)}, u32[]{:S(2)}) collective-permute-start(bf16[32,1,8,128]{3,0,2,1:T(8,128)(2,1)S(1)} %get-tuple-element.38), channel_id=1, source_target_pairs={{4,0},{8,4},{12,8},{16,12},{20,16},{24,20},{28,24},{0,28},{5,1},{9... | collective-permute-start | bytes 196616 | tf_op jit(solution)/shard_map/ppermute | solution.py:18
  20.0 2.1 %collective-permute-done.2 = bf16[32,1,8,128]{3,0,2,1:T(8,128)(2,1)S(1)} collective-permute-done((bf16[32,1,8,128]{3,0,2,1:T(8,128)(2,1)S(1)}, bf16[32,1,8,128]{3,0,2,1:T(8,128)(2,1)S(1)}, u32[]{:S(2)}, u32[]{:S(2)}) %collective-permute-start.2) | collective-permute-done | bytes 65568 | tf_op jit(solution)/shard_map/ppermute | solution.py:15
  22.2 1.7 %collective-permute-start.5 = (bf16[32,4,1,128]{3,0,2,1:T(8,128)(2,1)S(1)}, bf16[32,4,1,128]{3,0,2,1:T(8,128)(2,1)S(1)}, u32[]{:S(2)}, u32[]{:S(2)}) collective-permute-start(bf16[32,4,1,128]{3,0,2,1:T(8,128)(2,1)S(1)} %get-tuple-element.32), channel_id=1, source_target_pairs={{1,0},{2,1},{3,2},{0,3},{5,4},{6,5},{7,6},{4,7},{9,8},{10,9},{11,1... | collective-permute-start | bytes 98312 | tf_op jit(solution)/shard_map/ppermute | solution.py:18
  24.0 1.5 %collective-permute-done.4 = bf16[32,4,1,128]{3,0,2,1:T(8,128)(2,1)S(1)} collective-permute-done((bf16[32,4,1,128]{3,0,2,1:T(8,128)(2,1)S(1)}, bf16[32,4,1,128]{3,0,2,1:T(8,128)(2,1)S(1)}, u32[]{:S(2)}, u32[]{:S(2)}) %collective-permute-start.4) | collective-permute-done | bytes 32800 | tf_op jit(solution)/shard_map/ppermute | solution.py:15
  26.2 2.1 %copy.96 = bf16[32,4,10,1,130]{0,1,4,2,3:T(4,128)(2,1)S(1)} copy(bf16[32,4,10,1,130]{4,0,2,1,3:T(8,128)(2,1)S(1)} %maximum_bitcast_fusion) | data formatting | bytes 665600
  29.2 1.8 %fusion.19 = f32[2,8,8,17,32]{4,2,3,1,0:T(8,128)S(1)} fusion(bf16[3,3,3,32,32]{4,3,2,1,0:T(8,128)(2,1)S(1)} %copy-done, bf16[32,4,10,1,7,2]{0,4,5,2,1,3:T(8,128)(2,1)S(1)} %slice.366, bf16[32,4,10,1,8,17]{0,4,5,2,1,3:T(8,128)(2,1)S(1)} %copy.46, pred[8,17]{0,1:T(8,128)(4,1)S(1)} %copy-done.3), kind=kOutput, calls=%fused_computation.18 | convolution fusion | flops 121561088 | bytes 717960 | tf_op jit(solution)/shard_map/conv_general_dilated | solution.py:83
  32.7 1.3 %collective-permute-start.13 = (bf16[2,32,4,1,128]{4,1,3,2,0:T(8,128)(2,1)S(1)}, bf16[2,32,4,1,128]{4,1,3,2,0:T(8,128)(2,1)S(1)}, u32[]{:S(2)}, u32[]{:S(2)}) collective-permute-start(bf16[2,32,4,1,128]{4,1,3,2,0:T(8,128)(2,1)S(1)} %get-tuple-element.22), channel_id=1, source_target_pairs={{1,0},{2,1},{3,2},{0,3},{5,4},{6,5},{7,6},{4,7},{9,8},{10,9},{11,1... | collective-permute-start | bytes 196616 | tf_op jit(solution)/shard_map/ppermute | solution.py:18
  34.0 5.0 %collective-permute-start.7 = (bf16[32,1,8,128]{3,0,2,1:T(8,128)(2,1)S(1)}, bf16[32,1,8,128]{3,0,2,1:T(8,128)(2,1)S(1)}, u32[]{:S(2)}, u32[]{:S(2)}) collective-permute-start(bf16[32,1,8,128]{3,0,2,1:T(8,128)(2,1)S(1)} %get-tuple-element.36), channel_id=1, source_target_pairs={{4,0},{8,4},{12,8},{16,12},{20,16},{24,20},{28,24},{0,28},{5,1},{9... | collective-permute-start | bytes 196616 | tf_op jit(solution)/shard_map/ppermute | solution.py:18
  43.4 1.0 %fusion.32 = f32[27,32,32]{1,2,0:T(8,128)S(1)} fusion(bf16[27,32,2,8,128]{4,1,3,0,2:T(8,128)(2,1)S(1)} %fusion.79, bf16[32,2,8,128]{3,0,2,1:T(8,128)(2,1)S(1)} %fusion.44), kind=kOutput, calls=%fused_computation.30 | convolution fusion | flops 113273856 | bytes 3780608 | tf_op jit(solution)/shard_map/oxzy,tixzy->toi/dot_general | solution.py:105
  47.7 1.0 %fusion.30 = f32[27,32,32]{1,2,0:T(8,128)S(1)} fusion(bf16[27,32,2,8,128]{4,1,3,2,0:T(8,128)(2,1)S(1)} %fusion.52, bf16[32,2,8,128]{3,0,2,1:T(8,128)(2,1)S(1)} %fusion.34), kind=kOutput, calls=%fused_computation.27 | convolution fusion | flops 113273856 | bytes 3780608 | tf_op jit(solution)/shard_map/oxzy,tixzy->toi/dot_general | solution.py:105
  49.2 1.0 %concatenate.49 = f32[55395]{0:T(1024)S(1)} concatenate(f32[27648]{0:T(1024)S(1)} %mul.113, f32[27648]{0:T(1024)S(1)} %mul.117, f32[96]{0:T(128)S(1)} %reshape.93, f32[3]{0:T(128)S(1)} %broadcast_multiply_fusion), dimensions={0} | concatenate | bytes 443160 | tf_op jit(solution)/shard_map/concatenate | solution.py:55
  50.9 1.3 %collective-permute-start.9 = (bf16[32,4,1,128]{3,0,2,1:T(8,128)(2,1)S(1)}, bf16[32,4,1,128]{3,0,2,1:T(8,128)(2,1)S(1)}, u32[]{:S(2)}, u32[]{:S(2)}) collective-permute-start(bf16[32,4,1,128]{3,0,2,1:T(8,128)(2,1)S(1)} %get-tuple-element.30), channel_id=1, source_target_pairs={{1,0},{2,1},{3,2},{0,3},{5,4},{6,5},{7,6},{4,7},{9,8},{10,9},{11,1... | collective-permute-start | bytes 98312 | tf_op jit(solution)/shard_map/ppermute | solution.py:18
  53.9 3.2 %collective-permute-done.15 = f32[224,128]{1,0:T(8,128)S(1)} collective-permute-done((f32[224,128]{1,0:T(8,128)S(1)}, f32[224,128]{1,0:T(8,128)S(1)}, u32[]{:S(2)}, u32[]{:S(2)}) %collective-permute-start.15) | collective-permute-done | bytes 114720 | tf_op jit(solution)/shard_map/ppermute | solution.py:32
  57.4 4.6 %collective-permute-done.16 = f32[224,128]{1,0:T(8,128)S(1)} collective-permute-done((f32[224,128]{1,0:T(8,128)S(1)}, f32[224,128]{1,0:T(8,128)S(1)}, u32[]{:S(2)}, u32[]{:S(2)}) %collective-permute-start.16) | collective-permute-done | bytes 114720 | tf_op jit(solution)/shard_map/ppermute | solution.py:32
  62.5 2.1 %copy.97 = bf16[32,4,10,1,130]{0,1,4,2,3:T(4,128)(2,1)S(1)} copy(bf16[32,4,10,1,130]{4,0,2,1,3:T(8,128)(2,1)S(1)} %maximum_bitcast_fusion.1) | data formatting | bytes 665600
  65.6 1.3 %collective-permute-done.17 = f32[224,128]{1,0:T(8,128)S(1)} collective-permute-done((f32[224,128]{1,0:T(8,128)S(1)}, f32[224,128]{1,0:T(8,128)S(1)}, u32[]{:S(2)}, u32[]{:S(2)}) %collective-permute-start.17) | collective-permute-done | bytes 114720 | tf_op jit(solution)/shard_map/ppermute | solution.py:32
  67.7 1.7 %fusion.22 = bf16[2,8,8,17,32]{4,2,3,1,0:T(8,128)(2,1)S(1)} fusion(bf16[3,3,3,32,32]{4,3,2,1,0:T(8,128)(2,1)S(1)} %copy-done.2, bf16[32,4,10,1,7,2]{0,4,5,2,1,3:T(8,128)(2,1)S(1)} %slice.372, bf16[32,4,10,1,8,17]{0,4,5,2,1,3:T(8,128)(2,1)S(1)} %copy.52, pred[8,17]{0,1:T(8,128)(4,1)S(1)} %copy-done.3), kind=kOutput, calls=%fused_computation.19 | convolution fusion | flops 121630720 | bytes 578696 | tf_op jit(solution)/shard_map/conv_general_dilated | solution.py:83
  69.5 4.4 %collective-permute-done.18 = f32[224,128]{1,0:T(8,128)S(1)} collective-permute-done((f32[224,128]{1,0:T(8,128)S(1)}, f32[224,128]{1,0:T(8,128)S(1)}, u32[]{:S(2)}, u32[]{:S(2)}) %collective-permute-start.18) | collective-permute-done | bytes 114720 | tf_op jit(solution)/shard_map/ppermute | solution.py:32
  74.0 1.0 %copy.88 = bf16[32,2,8,128]{3,2,1,0:T(8,128)(2,1)} copy(bf16[32,2,8,128]{0,2,3,1:T(8,128)(2,1)S(1)} %slice_bitcast_fusion.2) | data formatting | bytes 262144
  (151 shorter events, 24.8 us)
Async XLA Ops:
  0.6 28.6 %copy-start = (bf16[3,3,3,32,32]{4,3,2,1,0:T(8,128)(2,1)S(1)}, bf16[3,3,3,32,32]{4,3,2,1,0:T(8,128)(2,1)}, u32[]{:S(2)}) copy-start(bf16[3,3,3,32,32]{4,3,2,1,0:T(8,128)(2,1)} %param.13) | copy-start | bytes 165892
  3.3 2.4 %collective-permute-start = (f32[2,2,128]{2,1,0:T(2,128)S(1)}, f32[2,2,128]{2,1,0:T(2,128)S(1)}, u32[]{:S(2)}, u32[]{:S(2)}) collective-permute-start(f32[2,2,128]{2,1,0:T(2,128)S(1)} %pad_maximum_fusion.17), channel_id=1, source_target_pairs={{0,1},{1,0},{2,3},{3,2},{4,5},{5,4},{6,7},{7,6},{8,9},{9,8},{10,11... | collective-permute-start | bytes 6152 | tf_op jit(solution)/shard_map/ppermute | solution.py:32
  5.7 7.4 %collective-permute-start.1 = (f32[2,2,128]{2,1,0:T(2,128)S(1)}, f32[2,2,128]{2,1,0:T(2,128)S(1)}, u32[]{:S(2)}, u32[]{:S(2)}) collective-permute-start(f32[2,2,128]{2,1,0:T(2,128)S(1)} %fusion.138), channel_id=1, source_target_pairs={{0,2},{1,3},{2,0},{3,1},{4,6},{5,7},{6,4},{7,5},{8,10},{9,11},{10,... | collective-permute-start | bytes 6152 | tf_op jit(solution)/shard_map/ppermute | solution.py:32
  8.3 23.8 %collective-permute-start.10 = (bf16[2,32,1,8,128]{4,1,3,2,0:T(8,128)(2,1)S(1)}, bf16[2,32,1,8,128]{4,1,3,2,0:T(8,128)(2,1)S(1)}, u32[]{:S(2)}, u32[]{:S(2)}) collective-permute-start(bf16[2,32,1,8,128]{4,1,3,2,0:T(8,128)(2,1)S(1)} %get-tuple-element.27), channel_id=1, source_target_pairs={{0,4},{4,8},{8,12},{12,16},{16,20},{20,24},{24,28},{28,0},{1,5},{5... | collective-permute-start | bytes 393224 | tf_op jit(solution)/shard_map/ppermute | solution.py:15
  9.9 22.2 %collective-permute-start.11 = (bf16[2,32,1,8,128]{4,1,3,2,0:T(8,128)(2,1)S(1)}, bf16[2,32,1,8,128]{4,1,3,2,0:T(8,128)(2,1)S(1)}, u32[]{:S(2)}, u32[]{:S(2)}) collective-permute-start(bf16[2,32,1,8,128]{4,1,3,2,0:T(8,128)(2,1)S(1)} %get-tuple-element.28), channel_id=1, source_target_pairs={{4,0},{8,4},{12,8},{16,12},{20,16},{24,20},{28,24},{0,28},{5,1},{9... | collective-permute-start | bytes 393224 | tf_op jit(solution)/shard_map/ppermute | solution.py:18
  15.1 7.0 %collective-permute-start.2 = (bf16[32,1,8,128]{3,0,2,1:T(8,128)(2,1)S(1)}, bf16[32,1,8,128]{3,0,2,1:T(8,128)(2,1)S(1)}, u32[]{:S(2)}, u32[]{:S(2)}) collective-permute-start(bf16[32,1,8,128]{3,0,2,1:T(8,128)(2,1)S(1)} %get-tuple-element.37), channel_id=1, source_target_pairs={{0,4},{4,8},{8,12},{12,16},{16,20},{20,24},{24,28},{28,0},{1,5},{5... | collective-permute-start | bytes 196616 | tf_op jit(solution)/shard_map/ppermute | solution.py:15
  15.2 7.0 %collective-permute-start.3 = (bf16[32,1,8,128]{3,0,2,1:T(8,128)(2,1)S(1)}, bf16[32,1,8,128]{3,0,2,1:T(8,128)(2,1)S(1)}, u32[]{:S(2)}, u32[]{:S(2)}) collective-permute-start(bf16[32,1,8,128]{3,0,2,1:T(8,128)(2,1)S(1)} %get-tuple-element.38), channel_id=1, source_target_pairs={{4,0},{8,4},{12,8},{16,12},{20,16},{24,20},{28,24},{0,28},{5,1},{9... | collective-permute-start | bytes 196616 | tf_op jit(solution)/shard_map/ppermute | solution.py:18
  22.1 3.4 %collective-permute-start.4 = (bf16[32,4,1,128]{3,0,2,1:T(8,128)(2,1)S(1)}, bf16[32,4,1,128]{3,0,2,1:T(8,128)(2,1)S(1)}, u32[]{:S(2)}, u32[]{:S(2)}) collective-permute-start(bf16[32,4,1,128]{3,0,2,1:T(8,128)(2,1)S(1)} %get-tuple-element.31), channel_id=1, source_target_pairs={{0,1},{1,2},{2,3},{3,0},{4,5},{5,6},{6,7},{7,4},{8,9},{9,10},{10,1... | collective-permute-start | bytes 98312 | tf_op jit(solution)/shard_map/ppermute | solution.py:15
  22.2 3.3 %collective-permute-start.5 = (bf16[32,4,1,128]{3,0,2,1:T(8,128)(2,1)S(1)}, bf16[32,4,1,128]{3,0,2,1:T(8,128)(2,1)S(1)}, u32[]{:S(2)}, u32[]{:S(2)}) collective-permute-start(bf16[32,4,1,128]{3,0,2,1:T(8,128)(2,1)S(1)} %get-tuple-element.32), channel_id=1, source_target_pairs={{1,0},{2,1},{3,2},{0,3},{5,4},{6,5},{7,6},{4,7},{9,8},{10,9},{11,1... | collective-permute-start | bytes 98312 | tf_op jit(solution)/shard_map/ppermute | solution.py:18
  26.2 3.1 %copy-start.3 = (pred[8,17]{0,1:T(8,128)(4,1)S(1)}, pred[8,17]{0,1:T(8,128)(4,1)}, u32[]{:S(2)}) copy-start(pred[8,17]{0,1:T(8,128)(4,1)} %constant.55) | copy-start | bytes 412
  31.0 0.9 %copy-start.1 = (bf16[32,2,8,128]{3,2,1,0:T(8,128)(2,1)S(1)}, bf16[32,2,8,128]{3,2,1,0:T(8,128)(2,1)}, u32[]{:S(2)}) copy-start(bf16[32,2,8,128]{3,2,1,0:T(8,128)(2,1)} %param.10) | copy-start | bytes 393220
  32.1 6.9 %collective-permute-start.12 = (bf16[2,32,4,1,128]{4,1,3,2,0:T(8,128)(2,1)S(1)}, bf16[2,32,4,1,128]{4,1,3,2,0:T(8,128)(2,1)S(1)}, u32[]{:S(2)}, u32[]{:S(2)}) collective-permute-start(bf16[2,32,4,1,128]{4,1,3,2,0:T(8,128)(2,1)S(1)} %get-tuple-element.21), channel_id=1, source_target_pairs={{0,1},{1,2},{2,3},{3,0},{4,5},{5,6},{6,7},{7,4},{8,9},{9,10},{10,1... | collective-permute-start | bytes 196616 | tf_op jit(solution)/shard_map/ppermute | solution.py:15
  32.7 6.3 %collective-permute-start.13 = (bf16[2,32,4,1,128]{4,1,3,2,0:T(8,128)(2,1)S(1)}, bf16[2,32,4,1,128]{4,1,3,2,0:T(8,128)(2,1)S(1)}, u32[]{:S(2)}, u32[]{:S(2)}) collective-permute-start(bf16[2,32,4,1,128]{4,1,3,2,0:T(8,128)(2,1)S(1)} %get-tuple-element.22), channel_id=1, source_target_pairs={{1,0},{2,1},{3,2},{0,3},{5,4},{6,5},{7,6},{4,7},{9,8},{10,9},{11,1... | collective-permute-start | bytes 196616 | tf_op jit(solution)/shard_map/ppermute | solution.py:18
  34.0 16.3 %collective-permute-start.6 = (bf16[32,1,8,128]{3,0,2,1:T(8,128)(2,1)S(1)}, bf16[32,1,8,128]{3,0,2,1:T(8,128)(2,1)S(1)}, u32[]{:S(2)}, u32[]{:S(2)}) collective-permute-start(bf16[32,1,8,128]{3,0,2,1:T(8,128)(2,1)S(1)} %get-tuple-element.35), channel_id=1, source_target_pairs={{0,4},{4,8},{8,12},{12,16},{16,20},{20,24},{24,28},{28,0},{1,5},{5... | collective-permute-start | bytes 196616 | tf_op jit(solution)/shard_map/ppermute | solution.py:15
  34.0 16.3 %collective-permute-start.7 = (bf16[32,1,8,128]{3,0,2,1:T(8,128)(2,1)S(1)}, bf16[32,1,8,128]{3,0,2,1:T(8,128)(2,1)S(1)}, u32[]{:S(2)}, u32[]{:S(2)}) collective-permute-start(bf16[32,1,8,128]{3,0,2,1:T(8,128)(2,1)S(1)} %get-tuple-element.36), channel_id=1, source_target_pairs={{4,0},{8,4},{12,8},{16,12},{20,16},{24,20},{28,24},{0,28},{5,1},{9... | collective-permute-start | bytes 196616 | tf_op jit(solution)/shard_map/ppermute | solution.py:18
  50.2 1.9 %collective-permute-start.14 = (f32[224,128]{1,0:T(8,128)S(1)}, f32[224,128]{1,0:T(8,128)S(1)}, u32[]{:S(2)}, u32[]{:S(2)}) collective-permute-start(f32[224,128]{1,0:T(8,128)S(1)} %fusion.109), channel_id=1, source_target_pairs={{0,1},{1,0},{2,3},{3,2},{4,5},{5,4},{6,7},{7,6},{8,9},{9,8},{10,11... | collective-permute-start | bytes 344072 | tf_op jit(solution)/shard_map/ppermute | solution.py:46
  50.3 3.4 %collective-permute-start.8 = (bf16[32,4,1,128]{3,0,2,1:T(8,128)(2,1)S(1)}, bf16[32,4,1,128]{3,0,2,1:T(8,128)(2,1)S(1)}, u32[]{:S(2)}, u32[]{:S(2)}) collective-permute-start(bf16[32,4,1,128]{3,0,2,1:T(8,128)(2,1)S(1)} %get-tuple-element.29), channel_id=1, source_target_pairs={{0,1},{1,2},{2,3},{3,0},{4,5},{5,6},{6,7},{7,4},{8,9},{9,10},{10,1... | collective-permute-start | bytes 98312 | tf_op jit(solution)/shard_map/ppermute | solution.py:15
  50.9 3.0 %collective-permute-start.9 = (bf16[32,4,1,128]{3,0,2,1:T(8,128)(2,1)S(1)}, bf16[32,4,1,128]{3,0,2,1:T(8,128)(2,1)S(1)}, u32[]{:S(2)}, u32[]{:S(2)}) collective-permute-start(bf16[32,4,1,128]{3,0,2,1:T(8,128)(2,1)S(1)} %get-tuple-element.30), channel_id=1, source_target_pairs={{1,0},{2,1},{3,2},{0,3},{5,4},{6,5},{7,6},{4,7},{9,8},{10,9},{11,1... | collective-permute-start | bytes 98312 | tf_op jit(solution)/shard_map/ppermute | solution.py:18
  52.2 5.0 %collective-permute-start.15 = (f32[224,128]{1,0:T(8,128)S(1)}, f32[224,128]{1,0:T(8,128)S(1)}, u32[]{:S(2)}, u32[]{:S(2)}) collective-permute-start(f32[224,128]{1,0:T(8,128)S(1)} %select_add_fusion), channel_id=1, source_target_pairs={{0,2},{1,3},{2,0},{3,1},{4,6},{5,7},{6,4},{7,5},{8,10},{9,11},{10,... | collective-permute-start | bytes 344072 | tf_op jit(solution)/shard_map/ppermute | solution.py:32
  57.1 4.9 %collective-permute-start.16 = (f32[224,128]{1,0:T(8,128)S(1)}, f32[224,128]{1,0:T(8,128)S(1)}, u32[]{:S(2)}, u32[]{:S(2)}) collective-permute-start(f32[224,128]{1,0:T(8,128)S(1)} %add.91), channel_id=1, source_target_pairs={{0,4},{4,0},{8,12},{12,8},{16,20},{20,16},{24,28},{28,24},{1,5},{5... | collective-permute-start | bytes 344072 | tf_op jit(solution)/shard_map/ppermute | solution.py:32
  62.0 4.9 %collective-permute-start.17 = (f32[224,128]{1,0:T(8,128)S(1)}, f32[224,128]{1,0:T(8,128)S(1)}, u32[]{:S(2)}, u32[]{:S(2)}) collective-permute-start(f32[224,128]{1,0:T(8,128)S(1)} %add.92), channel_id=1, source_target_pairs={{0,8},{4,12},{8,0},{12,4},{16,24},{20,28},{24,16},{28,20},{1,9},{5... | collective-permute-start | bytes 344072 | tf_op jit(solution)/shard_map/ppermute | solution.py:32
  64.6 3.1 %copy-start.2 = (bf16[3,3,3,32,32]{4,3,2,1,0:T(8,128)(2,1)S(1)}, bf16[3,3,3,32,32]{4,3,2,1,0:T(8,128)(2,1)}, u32[]{:S(2)}) copy-start(bf16[3,3,3,32,32]{4,3,2,1,0:T(8,128)(2,1)} %param.12) | copy-start | bytes 165892
  66.9 7.0 %collective-permute-start.18 = (f32[224,128]{1,0:T(8,128)S(1)}, f32[224,128]{1,0:T(8,128)S(1)}, u32[]{:S(2)}, u32[]{:S(2)}) collective-permute-start(f32[224,128]{1,0:T(8,128)S(1)} %add.93), channel_id=1, source_target_pairs={{0,16},{4,20},{8,24},{12,28},{16,0},{20,4},{24,8},{28,12},{1,17},{... | collective-permute-start | bytes 344072 | tf_op jit(solution)/shard_map/ppermute | solution.py:32
  73.9 1.4 %collective-permute-start.19 = (f32[224,128]{1,0:T(8,128)S(1)}, f32[224,128]{1,0:T(8,128)S(1)}, u32[]{:S(2)}, u32[]{:S(2)}) collective-permute-start(f32[224,128]{1,0:T(8,128)S(1)} %add.94), channel_id=1, source_target_pairs={{0,1},{1,0},{2,3},{3,2},{4,5},{5,4},{6,7},{7,6},{8,9},{9,8},{10,11... | collective-permute-start | bytes 344072 | tf_op jit(solution)/shard_map/ppermute | solution.py:48

commit v5 on v4

--- a/solution.py
+++ b/solution.py
@@ -147,14 +147,15 @@
     grad_bias = jnp.sum(head_grad.astype(jnp.float32), axis=(1, 2, 3)) * norm_factor
     back_second = jnp.einsum("oi,oxzy->ixzy", w_out, head_grad, preferred_element_type=jnp.float32)
     grad_second_pre = (back_second * silu_slope(second_wide)).astype(jnp.bfloat16)
-    second_padded = wrap_columns(extended(grad_second_pre, (("sky", 1), ("los", 2)), 1))
+    all_padded = wrap_columns(
+        extended(jnp.stack((grad_second_pre, features, pre_first)), (("sky", 2), ("los", 3)), 1)
+    )
+    second_padded = all_padded[0]
     back_first = spread_local(w_second, second_padded, shape)
     grad_first_pre = (back_first * silu_slope(first_wide)).astype(jnp.bfloat16)
     first_padded = wrap_columns(extended(grad_first_pre, (("sky", 1), ("los", 2)), 1))
     grad_features = spread_local(w_first, first_padded, shape).astype(jnp.bfloat16)
-    saved_padded = wrap_columns(
-        extended(jnp.stack((features, pre_first)), (("sky", 2), ("los", 3)), 1)
-    )
+    saved_padded = all_padded[1:]
     hidden_padded = jax.nn.silu(saved_padded[1].astype(jnp.float32)).astype(jnp.bfloat16)
     grad_second = taps_from_inputs(grad_second_pre, hidden_padded)
     grad_first = taps_from_inputs(grad_first_pre, saved_padded[0])

time: 78.8 us -> 81.8 us (1.038)
  waiting for transfers between devices: 18.4 us -> 21.9 us
  other arithmetic: 5.16 us -> 6.61 us
  starting transfers between devices: 24.8 us -> 23.8 us
    ppermute x6 -> x4, starting transfers between devices: 17.1 us -> 10.7 us  [extended(): lax.ppermute(lax.slice_in_dim(block, 0, width, axis=dim), axis, backward)]
    ppermute x6, starting transfers between devices: 4.7 us -> 9.15 us  [butterfly_sum(): value = value + lax.ppermute(value, axis, pairs)]
    ppermute x6 -> x4, waiting for transfers between devices: 4.47 us -> 6.96 us  [extended(): lax.ppermute(lax.slice_in_dim(block, block.shape[dim] - width, None, axis...]
    ppermute x6 -> x4, waiting for transfers between devices: 0.13 us -> 2.27 us  [extended(): lax.ppermute(lax.slice_in_dim(block, 0, width, axis=dim), axis, backward)]
    unnamed x66 -> x68, local copies, waits for them, and re-layouts: 12.6 us -> 10.7 us
    concatenate x1, other arithmetic: 0.78 us -> 2.62 us  [wrap_columns(): return jnp.concatenate((field[..., -1:], field, field[..., :1]), axis=-1)]
    ppermute x6, waiting for transfers between devices: 13.6 us -> 12.4 us  [butterfly_sum(): value = value + lax.ppermute(value, axis, pairs)]
    another operation x0 -> x1, local copies, waits for them, and re-layouts: none -> 1.04 us  [per_device(): jnp.stack((grad_second_pre, features, pre_first))]
  transfers between devices with their start and end apart: 20 -> 16, of which waited for: 9 -> 12; matrix products, arithmetic and copies ran while one was open for 35% -> 11% of each run, Pallas kernels for 0% -> 0%
where the time goes in v5:
time: 81.8 us; the launch traced here: 81.6 us
  starting transfers between devices  23.8 us (29%)
  waiting for transfers between devices  21.9 us (27%)
  local copies, waits for them, and re-layouts  20.2 us (25%)
  matrix products  7.62 us (9%)
  other arithmetic  6.61 us (8%)
  between operations  1.39 us (2%)
    ppermute x6, waiting for transfers between devices, butterfly_sum(): value = value + lax.ppermute(value, axis, pairs)  12.4 us
    unnamed x68, local copies, waits for them, and re-layouts  10.7 us
    ppermute x4, starting transfers between devices, extended(): lax.ppermute(lax.slice_in_dim(block, 0, width, axis=dim), axis, backward)  10.7 us
    ppermute x6, starting transfers between devices, butterfly_sum(): value = value + lax.ppermute(value, axis, pairs)  9.15 us
    ppermute x4, waiting for transfers between devices, extended(): lax.ppermute(lax.slice_in_dim(block, block.shape[dim] - width, None, axis...  6.96 us
    conv_general_dilated x2, matrix products, spread_local(): lax.conv_general_dilated(padded[None], kernel, (1, 1, 1), 'VALID', dimens...  3.43 us
    ppermute x4, starting transfers between devices, extended(): lax.ppermute(lax.slice_in_dim(block, block.shape[dim] - width, None, axis...  2.88 us
    concatenate x1, other arithmetic, wrap_columns(): return jnp.concatenate((field[..., -1:], field, field[..., :1]), axis=-1)  2.62 us
  transfers between devices with their start and end apart: 16, of which 12 were waited for; matrix products, arithmetic and copies ran while one was open for 11% of the time, Pallas kernels for 0%

profile of v5, /device:TPU:0, one launch (start us, length us, event | category | flops | bytes accessed | tf_op | source)
XLA Modules:
  0.0 81.6 jit_solution(1811263948636223971)
XLA Ops:
  4.6 2.8 %collective-permute-start.1 = (f32[2,2,128]{2,1,0:T(2,128)S(1)}, f32[2,2,128]{2,1,0:T(2,128)S(1)}, u32[]{:S(2)}, u32[]{:S(2)}) collective-permute-start(f32[2,2,128]{2,1,0:T(2,128)S(1)} %fusion.137), channel_id=1, source_target_pairs={{0,2},{1,3},{2,0},{3,1},{4,6},{5,7},{6,4},{7,5},{8,10},{9,11},{10,... | collective-permute-start | bytes 6152 | tf_op jit(solution)/shard_map/ppermute | solution.py:32
  7.4 1.0 %copy_bitcast_fusion = (bf16[1,32,2,8,128]{4,1,3,2,0:T(8,128)(2,1)S(1)}, bf16[1,32,2,8,128]{4,1,3,2,0:T(8,128)(2,1)S(1)}) fusion(bf16[32,2,8,128]{3,2,1,0:T(8,128)(2,1)} %param.9, bf16[32,2,8,128]{3,2,1,0:T(8,128)(2,1)} %param.10), kind=kLoop, calls=%fused_computation.176 | loop fusion | bytes 524288 | tf_op jit(solution)/shard_map/stack | solution.py:151
  9.9 1.1 %fusion.34 = bf16[32,2,8,128]{3,0,2,1:T(8,128)(2,1)S(1)} fusion(bf16[32,2,8,128]{3,2,1,0:T(8,128)(2,1)} %param.11, bf16[3,2,8,128]{3,2,1,0:T(8,128)(2,1)S(1)} %get-tuple-element.18, bf16[3,32]{1,0:T(4,128)(2,1)} %param.14), kind=kOutput, calls=%fused_computation.33 | convolution fusion | flops 1048576 | bytes 274624 | tf_op jit(solution)/shard_map/oi,oxzy->ixzy/dot_general | solution.py:148
  11.1 2.1 %collective-permute-start.2 = (bf16[3,32,1,8,128]{4,1,3,2,0:T(8,128)(2,1)S(1)}, bf16[3,32,1,8,128]{4,1,3,2,0:T(8,128)(2,1)S(1)}, u32[]{:S(2)}, u32[]{:S(2)}) collective-permute-start(bf16[3,32,1,8,128]{4,1,3,2,0:T(8,128)(2,1)S(1)} %get-tuple-element.25), channel_id=1, source_target_pairs={{0,4},{4,8},{8,12},{12,16},{16,20},{20,24},{24,28},{28,0},{1,5},{5... | collective-permute-start | bytes 589832 | tf_op jit(solution)/shard_map/ppermute | solution.py:15
  13.2 3.1 %collective-permute-start.3 = (bf16[3,32,1,8,128]{4,1,3,2,0:T(8,128)(2,1)S(1)}, bf16[3,32,1,8,128]{4,1,3,2,0:T(8,128)(2,1)S(1)}, u32[]{:S(2)}, u32[]{:S(2)}) collective-permute-start(bf16[3,32,1,8,128]{4,1,3,2,0:T(8,128)(2,1)S(1)} %get-tuple-element.26), channel_id=1, source_target_pairs={{4,0},{8,4},{12,8},{16,12},{20,16},{24,20},{28,24},{0,28},{5,1},{9... | collective-permute-start | bytes 589832 | tf_op jit(solution)/shard_map/ppermute | solution.py:18
  16.5 4.3 %collective-permute-done.2 = bf16[3,32,1,8,128]{4,1,3,2,0:T(8,128)(2,1)S(1)} collective-permute-done((bf16[3,32,1,8,128]{4,1,3,2,0:T(8,128)(2,1)S(1)}, bf16[3,32,1,8,128]{4,1,3,2,0:T(8,128)(2,1)S(1)}, u32[]{:S(2)}, u32[]{:S(2)}) %collective-permute-start.2) | collective-permute-done | bytes 196640 | tf_op jit(solution)/shard_map/ppermute | solution.py:15
  20.8 2.2 %collective-permute-done.3 = bf16[3,32,1,8,128]{4,1,3,2,0:T(8,128)(2,1)S(1)} collective-permute-done((bf16[3,32,1,8,128]{4,1,3,2,0:T(8,128)(2,1)S(1)}, bf16[3,32,1,8,128]{4,1,3,2,0:T(8,128)(2,1)S(1)}, u32[]{:S(2)}, u32[]{:S(2)}) %collective-permute-start.3) | collective-permute-done | bytes 196640 | tf_op jit(solution)/shard_map/ppermute | solution.py:18
  23.1 1.7 %collective-permute-start.5 = (bf16[3,32,4,1,128]{4,1,3,2,0:T(8,128)(2,1)S(1)}, bf16[3,32,4,1,128]{4,1,3,2,0:T(8,128)(2,1)S(1)}, u32[]{:S(2)}, u32[]{:S(2)}) collective-permute-start(bf16[3,32,4,1,128]{4,1,3,2,0:T(8,128)(2,1)S(1)} %get-tuple-element.24), channel_id=1, source_target_pairs={{1,0},{2,1},{3,2},{0,3},{5,4},{6,5},{7,6},{4,7},{9,8},{10,9},{11,1... | collective-permute-start | bytes 294920 | tf_op jit(solution)/shard_map/ppermute | solution.py:18
  24.9 2.2 %collective-permute-done.4 = bf16[3,32,4,1,128]{4,1,3,2,0:T(8,128)(2,1)S(1)} collective-permute-done((bf16[3,32,4,1,128]{4,1,3,2,0:T(8,128)(2,1)S(1)}, bf16[3,32,4,1,128]{4,1,3,2,0:T(8,128)(2,1)S(1)}, u32[]{:S(2)}, u32[]{:S(2)}) %collective-permute-start.4) | collective-permute-done | bytes 98336 | tf_op jit(solution)/shard_map/ppermute | solution.py:15
  27.8 2.6 %pad_maximum_fusion = bf16[3,32,4,10,130]{4,1,3,2,0:T(8,128)(2,1)S(1)} fusion(bf16[3,32,4,10,1]{4,1,3,2,0:T(8,128)(2,1)S(1)} %get-tuple-element.22, bf16[3,32,4,1,128]{4,1,3,2,0:T(8,128)(2,1)S(1)} %collective-permute-done.5, bf16[3,32,1,8,128]{4,1,3,2,0:T(8,128)(2,1)S(1)} %collective-permute-done.3, bf16[1,32,2,8,128]{4,1,3,2,0:T(8,128)(2,1)S(1)} %get-tuple-element.43, ...), kind=kLoop, calls=%fused_computation.3 | loop fusion | flops 8985600 | bytes 1996800 | tf_op jit(solution)/shard_map/concatenate | solution.py:78
  30.9 2.1 %copy.71 = bf16[32,4,10,1,130]{0,1,4,2,3:T(4,128)(2,1)S(1)} copy(bf16[32,4,10,1,130]{4,0,2,1,3:T(8,128)(2,1)S(1)} %get-tuple-element.20) | data formatting | bytes 665600
  34.0 1.7 %fusion.19 = f32[2,8,8,17,32]{4,2,3,1,0:T(8,128)S(1)} fusion(bf16[3,3,3,32,32]{4,3,2,1,0:T(8,128)(2,1)S(1)} %copy-done, bf16[32,4,10,1,7,2]{0,4,5,2,1,3:T(8,128)(2,1)S(1)} %slice.350, bf16[32,4,10,1,8,17]{0,4,5,2,1,3:T(8,128)(2,1)S(1)} %copy.48, pred[8,17]{0,1:T(8,128)(4,1)S(1)} %copy-done.5), kind=kOutput, calls=%fused_computation.19 | convolution fusion | flops 121561088 | bytes 717960 | tf_op jit(solution)/shard_map/conv_general_dilated | solution.py:83
  39.5 1.0 %fusion.32 = f32[27,32,32]{1,2,0:T(8,128)S(1)} fusion(bf16[27,32,2,8,128]{4,1,3,2,0:T(8,128)(2,1)S(1)} %fusion.78, bf16[32,2,8,128]{3,0,2,1:T(8,128)(2,1)S(1)} %fusion.44), kind=kOutput, calls=%fused_computation.30 | convolution fusion | flops 113273856 | bytes 3780608 | tf_op jit(solution)/shard_map/oxzy,tixzy->toi/dot_general | solution.py:105
  43.8 1.0 %fusion.30 = f32[27,32,32]{1,2,0:T(8,128)S(1)} fusion(bf16[27,32,2,8,128]{4,1,3,2,0:T(8,128)(2,1)S(1)} %fusion.51, bf16[32,2,8,128]{3,0,2,1:T(8,128)(2,1)S(1)} %copy-done.2), kind=kOutput, calls=%fused_computation.27 | convolution fusion | flops 113273856 | bytes 3780608 | tf_op jit(solution)/shard_map/oxzy,tixzy->toi/dot_general | solution.py:105
  45.7 4.4 %collective-permute-start.7 = (bf16[32,1,8,128]{3,0,2,1:T(8,128)(2,1)S(1)}, bf16[32,1,8,128]{3,0,2,1:T(8,128)(2,1)S(1)}, u32[]{:S(2)}, u32[]{:S(2)}) collective-permute-start(bf16[32,1,8,128]{3,0,2,1:T(8,128)(2,1)S(1)} %get-tuple-element.34), channel_id=1, source_target_pairs={{4,0},{8,4},{12,8},{16,12},{20,16},{24,20},{28,24},{0,28},{5,1},{9... | collective-permute-start | bytes 196616 | tf_op jit(solution)/shard_map/ppermute | solution.py:18
  51.1 1.1 %collective-permute-start.10 = (f32[224,128]{1,0:T(8,128)S(1)}, f32[224,128]{1,0:T(8,128)S(1)}, u32[]{:S(2)}, u32[]{:S(2)}) collective-permute-start(f32[224,128]{1,0:T(8,128)S(1)} %fusion.108), channel_id=1, source_target_pairs={{0,1},{1,0},{2,3},{3,2},{4,5},{5,4},{6,7},{7,6},{8,9},{9,8},{10,11... | collective-permute-start | bytes 344072 | tf_op jit(solution)/shard_map/ppermute | solution.py:46
  53.0 1.4 %collective-permute-start.9 = (bf16[32,4,1,128]{3,0,2,1:T(8,128)(2,1)S(1)}, bf16[32,4,1,128]{3,0,2,1:T(8,128)(2,1)S(1)}, u32[]{:S(2)}, u32[]{:S(2)}) collective-permute-start(bf16[32,4,1,128]{3,0,2,1:T(8,128)(2,1)S(1)} %get-tuple-element.30), channel_id=1, source_target_pairs={{1,0},{2,1},{3,2},{0,3},{5,4},{6,5},{7,6},{4,7},{9,8},{10,9},{11,1... | collective-permute-start | bytes 98312 | tf_op jit(solution)/shard_map/ppermute | solution.py:18
  54.4 1.9 %collective-permute-start.11 = (f32[224,128]{1,0:T(8,128)S(1)}, f32[224,128]{1,0:T(8,128)S(1)}, u32[]{:S(2)}, u32[]{:S(2)}) collective-permute-start(f32[224,128]{1,0:T(8,128)S(1)} %select_add_fusion), channel_id=1, source_target_pairs={{0,2},{1,3},{2,0},{3,1},{4,6},{5,7},{6,4},{7,5},{8,10},{9,11},{10,... | collective-permute-start | bytes 344072 | tf_op jit(solution)/shard_map/ppermute | solution.py:32
  56.4 3.7 %collective-permute-done.11 = f32[224,128]{1,0:T(8,128)S(1)} collective-permute-done((f32[224,128]{1,0:T(8,128)S(1)}, f32[224,128]{1,0:T(8,128)S(1)}, u32[]{:S(2)}, u32[]{:S(2)}) %collective-permute-start.11) | collective-permute-done | bytes 114720 | tf_op jit(solution)/shard_map/ppermute | solution.py:32
  61.0 4.0 %collective-permute-done.12 = f32[224,128]{1,0:T(8,128)S(1)} collective-permute-done((f32[224,128]{1,0:T(8,128)S(1)}, f32[224,128]{1,0:T(8,128)S(1)}, u32[]{:S(2)}, u32[]{:S(2)}) %collective-permute-start.12) | collective-permute-done | bytes 114720 | tf_op jit(solution)/shard_map/ppermute | solution.py:32
  66.3 2.1 %copy.72 = bf16[32,4,10,1,130]{0,1,4,2,3:T(4,128)(2,1)S(1)} copy(bf16[32,4,10,1,130]{4,0,2,1,3:T(8,128)(2,1)S(1)} %maximum_bitcast_fusion) | data formatting | bytes 665600
  69.9 2.3 %collective-permute-start.14 = (f32[224,128]{1,0:T(8,128)S(1)}, f32[224,128]{1,0:T(8,128)S(1)}, u32[]{:S(2)}, u32[]{:S(2)}) collective-permute-start(f32[224,128]{1,0:T(8,128)S(1)} %add.93), channel_id=1, source_target_pairs={{0,16},{4,20},{8,24},{12,28},{16,0},{20,4},{24,8},{28,12},{1,17},{... | collective-permute-start | bytes 344072 | tf_op jit(solution)/shard_map/ppermute | solution.py:32
  72.2 1.7 %fusion.22 = bf16[2,8,8,17,32]{4,2,3,1,0:T(8,128)(2,1)S(1)} fusion(bf16[3,3,3,32,32]{4,3,2,1,0:T(8,128)(2,1)S(1)} %copy-done.4, bf16[32,4,10,1,7,2]{0,4,5,2,1,3:T(8,128)(2,1)S(1)} %slice.356, bf16[32,4,10,1,8,17]{0,4,5,2,1,3:T(8,128)(2,1)S(1)} %copy.54, pred[8,17]{0,1:T(8,128)(4,1)S(1)} %copy-done.5), kind=kOutput, calls=%fused_computation.20 | convolution fusion | flops 121630720 | bytes 578696 | tf_op jit(solution)/shard_map/conv_general_dilated | solution.py:83
  74.0 2.9 %collective-permute-done.14 = f32[224,128]{1,0:T(8,128)S(1)} collective-permute-done((f32[224,128]{1,0:T(8,128)S(1)}, f32[224,128]{1,0:T(8,128)S(1)}, u32[]{:S(2)}, u32[]{:S(2)}) %collective-permute-start.14) | collective-permute-done | bytes 114720 | tf_op jit(solution)/shard_map/ppermute | solution.py:32
  (142 shorter events, 25.5 us)
Async XLA Ops:
  0.6 33.4 %copy-start = (bf16[3,3,3,32,32]{4,3,2,1,0:T(8,128)(2,1)S(1)}, bf16[3,3,3,32,32]{4,3,2,1,0:T(8,128)(2,1)}, u32[]{:S(2)}) copy-start(bf16[3,3,3,32,32]{4,3,2,1,0:T(8,128)(2,1)} %param.13) | copy-start | bytes 165892
  3.3 1.3 %collective-permute-start = (f32[2,2,128]{2,1,0:T(2,128)S(1)}, f32[2,2,128]{2,1,0:T(2,128)S(1)}, u32[]{:S(2)}, u32[]{:S(2)}) collective-permute-start(f32[2,2,128]{2,1,0:T(2,128)S(1)} %pad_maximum_fusion.14), channel_id=1, source_target_pairs={{0,1},{1,0},{2,3},{3,2},{4,5},{5,4},{6,7},{7,6},{8,9},{9,8},{10,11... | collective-permute-start | bytes 6152 | tf_op jit(solution)/shard_map/ppermute | solution.py:32
  4.6 4.4 %collective-permute-start.1 = (f32[2,2,128]{2,1,0:T(2,128)S(1)}, f32[2,2,128]{2,1,0:T(2,128)S(1)}, u32[]{:S(2)}, u32[]{:S(2)}) collective-permute-start(f32[2,2,128]{2,1,0:T(2,128)S(1)} %fusion.137), channel_id=1, source_target_pairs={{0,2},{1,3},{2,0},{3,1},{4,6},{5,7},{6,4},{7,5},{8,10},{9,11},{10,... | collective-permute-start | bytes 6152 | tf_op jit(solution)/shard_map/ppermute | solution.py:32
  11.0 16.8 %copy-start.1 = (bf16[32,2,8,128]{3,0,2,1:T(8,128)(2,1)}, bf16[32,2,8,128]{3,0,2,1:T(8,128)(2,1)S(1)}, u32[]{:S(2)}) copy-start(bf16[32,2,8,128]{3,0,2,1:T(8,128)(2,1)S(1)} %fusion.34) | copy-start | bytes 393220
  11.1 9.7 %collective-permute-start.2 = (bf16[3,32,1,8,128]{4,1,3,2,0:T(8,128)(2,1)S(1)}, bf16[3,32,1,8,128]{4,1,3,2,0:T(8,128)(2,1)S(1)}, u32[]{:S(2)}, u32[]{:S(2)}) collective-permute-start(bf16[3,32,1,8,128]{4,1,3,2,0:T(8,128)(2,1)S(1)} %get-tuple-element.25), channel_id=1, source_target_pairs={{0,4},{4,8},{8,12},{12,16},{16,20},{20,24},{24,28},{28,0},{1,5},{5... | collective-permute-start | bytes 589832 | tf_op jit(solution)/shard_map/ppermute | solution.py:15
  13.2 9.8 %collective-permute-start.3 = (bf16[3,32,1,8,128]{4,1,3,2,0:T(8,128)(2,1)S(1)}, bf16[3,32,1,8,128]{4,1,3,2,0:T(8,128)(2,1)S(1)}, u32[]{:S(2)}, u32[]{:S(2)}) collective-permute-start(bf16[3,32,1,8,128]{4,1,3,2,0:T(8,128)(2,1)S(1)} %get-tuple-element.26), channel_id=1, source_target_pairs={{4,0},{8,4},{12,8},{16,12},{20,16},{24,20},{28,24},{0,28},{5,1},{9... | collective-permute-start | bytes 589832 | tf_op jit(solution)/shard_map/ppermute | solution.py:18
  23.0 4.1 %collective-permute-start.4 = (bf16[3,32,4,1,128]{4,1,3,2,0:T(8,128)(2,1)S(1)}, bf16[3,32,4,1,128]{4,1,3,2,0:T(8,128)(2,1)S(1)}, u32[]{:S(2)}, u32[]{:S(2)}) collective-permute-start(bf16[3,32,4,1,128]{4,1,3,2,0:T(8,128)(2,1)S(1)} %get-tuple-element.23), channel_id=1, source_target_pairs={{0,1},{1,2},{2,3},{3,0},{4,5},{5,6},{6,7},{7,4},{8,9},{9,10},{10,1... | collective-permute-start | bytes 294920 | tf_op jit(solution)/shard_map/ppermute | solution.py:15
  23.1 4.1 %collective-permute-start.5 = (bf16[3,32,4,1,128]{4,1,3,2,0:T(8,128)(2,1)S(1)}, bf16[3,32,4,1,128]{4,1,3,2,0:T(8,128)(2,1)S(1)}, u32[]{:S(2)}, u32[]{:S(2)}) collective-permute-start(bf16[3,32,4,1,128]{4,1,3,2,0:T(8,128)(2,1)S(1)} %get-tuple-element.24), channel_id=1, source_target_pairs={{1,0},{2,1},{3,2},{0,3},{5,4},{6,5},{7,6},{4,7},{9,8},{10,9},{11,1... | collective-permute-start | bytes 294920 | tf_op jit(solution)/shard_map/ppermute | solution.py:18
  30.9 3.1 %copy-start.5 = (pred[8,17]{0,1:T(8,128)(4,1)S(1)}, pred[8,17]{0,1:T(8,128)(4,1)}, u32[]{:S(2)}) copy-start(pred[8,17]{0,1:T(8,128)(4,1)} %constant.55) | copy-start | bytes 412
  35.7 0.9 %copy-start.3 = (bf16[32,2,8,128]{3,2,1,0:T(8,128)(2,1)S(1)}, bf16[32,2,8,128]{3,2,1,0:T(8,128)(2,1)}, u32[]{:S(2)}) copy-start(bf16[32,2,8,128]{3,2,1,0:T(8,128)(2,1)} %param.10) | copy-start | bytes 393220
  41.1 2.8 %copy-start.2 = (bf16[32,2,8,128]{3,0,2,1:T(8,128)(2,1)S(1)}, bf16[32,2,8,128]{3,0,2,1:T(8,128)(2,1)}, u32[]{:S(2)}) copy-start(bf16[32,2,8,128]{3,0,2,1:T(8,128)(2,1)} %copy-done.1) | copy-start | bytes 393220
  45.4 7.2 %collective-permute-start.6 = (bf16[32,1,8,128]{3,0,2,1:T(8,128)(2,1)S(1)}, bf16[32,1,8,128]{3,0,2,1:T(8,128)(2,1)S(1)}, u32[]{:S(2)}, u32[]{:S(2)}) collective-permute-start(bf16[32,1,8,128]{3,0,2,1:T(8,128)(2,1)S(1)} %get-tuple-element.33), channel_id=1, source_target_pairs={{0,4},{4,8},{8,12},{12,16},{16,20},{20,24},{24,28},{28,0},{1,5},{5... | collective-permute-start | bytes 196616 | tf_op jit(solution)/shard_map/ppermute | solution.py:15
  45.7 6.9 %collective-permute-start.7 = (bf16[32,1,8,128]{3,0,2,1:T(8,128)(2,1)S(1)}, bf16[32,1,8,128]{3,0,2,1:T(8,128)(2,1)S(1)}, u32[]{:S(2)}, u32[]{:S(2)}) collective-permute-start(bf16[32,1,8,128]{3,0,2,1:T(8,128)(2,1)S(1)} %get-tuple-element.34), channel_id=1, source_target_pairs={{4,0},{8,4},{12,8},{16,12},{20,16},{24,20},{28,24},{0,28},{5,1},{9... | collective-permute-start | bytes 196616 | tf_op jit(solution)/shard_map/ppermute | solution.py:18
  51.1 3.3 %collective-permute-start.10 = (f32[224,128]{1,0:T(8,128)S(1)}, f32[224,128]{1,0:T(8,128)S(1)}, u32[]{:S(2)}, u32[]{:S(2)}) collective-permute-start(f32[224,128]{1,0:T(8,128)S(1)} %fusion.108), channel_id=1, source_target_pairs={{0,1},{1,0},{2,3},{3,2},{4,5},{5,4},{6,7},{7,6},{8,9},{9,8},{10,11... | collective-permute-start | bytes 344072 | tf_op jit(solution)/shard_map/ppermute | solution.py:46
  52.6 3.7 %collective-permute-start.8 = (bf16[32,4,1,128]{3,0,2,1:T(8,128)(2,1)S(1)}, bf16[32,4,1,128]{3,0,2,1:T(8,128)(2,1)S(1)}, u32[]{:S(2)}, u32[]{:S(2)}) collective-permute-start(bf16[32,4,1,128]{3,0,2,1:T(8,128)(2,1)S(1)} %get-tuple-element.29), channel_id=1, source_target_pairs={{0,1},{1,2},{2,3},{3,0},{4,5},{5,6},{6,7},{7,4},{8,9},{9,10},{10,1... | collective-permute-start | bytes 98312 | tf_op jit(solution)/shard_map/ppermute | solution.py:15
  53.0 3.4 %collective-permute-start.9 = (bf16[32,4,1,128]{3,0,2,1:T(8,128)(2,1)S(1)}, bf16[32,4,1,128]{3,0,2,1:T(8,128)(2,1)S(1)}, u32[]{:S(2)}, u32[]{:S(2)}) collective-permute-start(bf16[32,4,1,128]{3,0,2,1:T(8,128)(2,1)S(1)} %get-tuple-element.30), channel_id=1, source_target_pairs={{1,0},{2,1},{3,2},{0,3},{5,4},{6,5},{7,6},{4,7},{9,8},{10,9},{11,1... | collective-permute-start | bytes 98312 | tf_op jit(solution)/shard_map/ppermute | solution.py:18
  54.4 5.7 %collective-permute-start.11 = (f32[224,128]{1,0:T(8,128)S(1)}, f32[224,128]{1,0:T(8,128)S(1)}, u32[]{:S(2)}, u32[]{:S(2)}) collective-permute-start(f32[224,128]{1,0:T(8,128)S(1)} %select_add_fusion), channel_id=1, source_target_pairs={{0,2},{1,3},{2,0},{3,1},{4,6},{5,7},{6,4},{7,5},{8,10},{9,11},{10,... | collective-permute-start | bytes 344072 | tf_op jit(solution)/shard_map/ppermute | solution.py:32
  60.1 4.9 %collective-permute-start.12 = (f32[224,128]{1,0:T(8,128)S(1)}, f32[224,128]{1,0:T(8,128)S(1)}, u32[]{:S(2)}, u32[]{:S(2)}) collective-permute-start(f32[224,128]{1,0:T(8,128)S(1)} %add.91), channel_id=1, source_target_pairs={{0,4},{4,0},{8,12},{12,8},{16,20},{20,16},{24,28},{28,24},{1,5},{5... | collective-permute-start | bytes 344072 | tf_op jit(solution)/shard_map/ppermute | solution.py:32
  65.0 4.9 %collective-permute-start.13 = (f32[224,128]{1,0:T(8,128)S(1)}, f32[224,128]{1,0:T(8,128)S(1)}, u32[]{:S(2)}, u32[]{:S(2)}) collective-permute-start(f32[224,128]{1,0:T(8,128)S(1)} %add.92), channel_id=1, source_target_pairs={{0,8},{4,12},{8,0},{12,4},{16,24},{20,28},{24,16},{28,20},{1,9},{5... | collective-permute-start | bytes 344072 | tf_op jit(solution)/shard_map/ppermute | solution.py:32
  68.4 3.8 %copy-start.4 = (bf16[3,3,3,32,32]{4,3,2,1,0:T(8,128)(2,1)S(1)}, bf16[3,3,3,32,32]{4,3,2,1,0:T(8,128)(2,1)}, u32[]{:S(2)}) copy-start(bf16[3,3,3,32,32]{4,3,2,1,0:T(8,128)(2,1)} %param.12) | copy-start | bytes 165892
  69.9 7.0 %collective-permute-start.14 = (f32[224,128]{1,0:T(8,128)S(1)}, f32[224,128]{1,0:T(8,128)S(1)}, u32[]{:S(2)}, u32[]{:S(2)}) collective-permute-start(f32[224,128]{1,0:T(8,128)S(1)} %add.93), channel_id=1, source_target_pairs={{0,16},{4,20},{8,24},{12,28},{16,0},{20,4},{24,8},{28,12},{1,17},{... | collective-permute-start | bytes 344072 | tf_op jit(solution)/shard_map/ppermute | solution.py:32
  76.9 1.4 %collective-permute-start.15 = (f32[224,128]{1,0:T(8,128)S(1)}, f32[224,128]{1,0:T(8,128)S(1)}, u32[]{:S(2)}, u32[]{:S(2)}) collective-permute-start(f32[224,128]{1,0:T(8,128)S(1)} %add.94), channel_id=1, source_target_pairs={{0,1},{1,0},{2,3},{3,2},{4,5},{5,4},{6,7},{7,6},{8,9},{9,8},{10,11... | collective-permute-start | bytes 344072 | tf_op jit(solution)/shard_map/ppermute | solution.py:48

commit v6 on v4

--- a/solution.py
+++ b/solution.py
@@ -90,22 +90,20 @@
     )[0]
 
 
-def taps_from_inputs(grad_field, padded_inputs):
+def taps_from_inputs(grad_field, extended_inputs):
     shape = grad_field.shape
+    rolled = jnp.stack([jnp.roll(grad_field, tap_y - 1, axis=3) for tap_y in range(3)])
     windows = jnp.stack(
         [
-            padded_inputs[
-                :, tap_x : tap_x + shape[1], tap_z : tap_z + shape[2], tap_y : tap_y + shape[3]
-            ]
+            extended_inputs[:, tap_x : tap_x + shape[1], tap_z : tap_z + shape[2]]
             for tap_x in range(3)
             for tap_z in range(3)
-            for tap_y in range(3)
         ]
     )
     taps = jnp.einsum(
-        "oxzy,tixzy->toi", grad_field, windows, preferred_element_type=jnp.float32
+        "soxzy,tixzy->tsoi", rolled, windows, preferred_element_type=jnp.float32
     )
-    return taps.reshape(3, 3, 3, shape[0], padded_inputs.shape[0])
+    return taps.reshape(3, 3, 3, shape[0], extended_inputs.shape[0])
 
 
 def per_device(
@@ -152,9 +150,7 @@
     grad_first_pre = (back_first * silu_slope(first_wide)).astype(jnp.bfloat16)
     first_padded = wrap_columns(extended(grad_first_pre, (("sky", 1), ("los", 2)), 1))
     grad_features = spread_local(w_first, first_padded, shape).astype(jnp.bfloat16)
-    saved_padded = wrap_columns(
-        extended(jnp.stack((features, pre_first)), (("sky", 2), ("los", 3)), 1)
-    )
+    saved_padded = extended(jnp.stack((features, pre_first)), (("sky", 2), ("los", 3)), 1)
     hidden_padded = jax.nn.silu(saved_padded[1].astype(jnp.float32)).astype(jnp.bfloat16)
     grad_second = taps_from_inputs(grad_second_pre, hidden_padded)
     grad_first = taps_from_inputs(grad_first_pre, saved_padded[0])

time: 78.8 us -> 77.1 us (0.978)
  waiting for transfers between devices: 18.4 us -> 28.2 us
  starting transfers between devices: 24.8 us -> 19.4 us
  local copies, waits for them, and re-layouts: 21 us -> 17.8 us
  matrix products: 7.68 us -> 6.2 us
  other arithmetic: 5.16 us -> 3.98 us
    ppermute x6, starting transfers between devices: 17.1 us -> 10.8 us  [extended(): lax.ppermute(lax.slice_in_dim(block, 0, width, axis=dim), axis, backward)]
    ppermute x6, waiting for transfers between devices: 4.47 us -> 10 us  [extended(): lax.ppermute(lax.slice_in_dim(block, block.shape[dim] - width, None, axis...]
    ppermute x6, waiting for transfers between devices: 0.13 us -> 4.84 us  [extended(): lax.ppermute(lax.slice_in_dim(block, 0, width, axis=dim), axis, backward)]
    unnamed x66 -> x38, local copies, waits for them, and re-layouts: 12.6 us -> 8.74 us
    dot_general x1, matrix products: 1.15 us -> 0.23 us  [per_device(): jnp.einsum('oi,oxzy->ixzy', w_out, head_grad, preferred_element_type=jnp....]
    ppermute x6, starting transfers between devices: 4.7 us -> 5.5 us  [butterfly_sum(): value = value + lax.ppermute(value, axis, pairs)]
  transfers between devices with their start and end apart: 20 -> 20, of which waited for: 9 -> 13; matrix products, arithmetic and copies ran while one was open for 35% -> 27% of each run, Pallas kernels for 0% -> 0%
where the time goes in v6:
time: 77.1 us; the launch traced here: 76.9 us
  waiting for transfers between devices  28.2 us (37%)
  starting transfers between devices  19.4 us (25%)
  local copies, waits for them, and re-layouts  17.8 us (23%)
  matrix products  6.2 us (8%)
  other arithmetic  3.98 us (5%)
  between operations  1.32 us (2%)
    ppermute x6, waiting for transfers between devices, butterfly_sum(): value = value + lax.ppermute(value, axis, pairs)  13.1 us
    ppermute x6, starting transfers between devices, extended(): lax.ppermute(lax.slice_in_dim(block, 0, width, axis=dim), axis, backward)  10.8 us
    ppermute x6, waiting for transfers between devices, extended(): lax.ppermute(lax.slice_in_dim(block, block.shape[dim] - width, None, axis...  10 us
    unnamed x38, local copies, waits for them, and re-layouts  8.74 us
    ppermute x6, starting transfers between devices, butterfly_sum(): value = value + lax.ppermute(value, axis, pairs)  5.5 us
    ppermute x6, waiting for transfers between devices, extended(): lax.ppermute(lax.slice_in_dim(block, 0, width, axis=dim), axis, backward)  4.84 us
    conv_general_dilated x2, matrix products, spread_local(): lax.conv_general_dilated(padded[None], kernel, (1, 1, 1), 'VALID', dimens...  3.49 us
    ppermute x6, starting transfers between devices, extended(): lax.ppermute(lax.slice_in_dim(block, block.shape[dim] - width, None, axis...  3.02 us
  transfers between devices with their start and end apart: 20, of which 13 were waited for; matrix products, arithmetic and copies ran while one was open for 27% of the time, Pallas kernels for 0%

profile of v6, /device:TPU:0, one launch (start us, length us, event | category | flops | bytes accessed | tf_op | source)
XLA Modules:
  0.0 76.9 jit_solution(251662020937232872)
XLA Ops:
  0.7 1.1 %fusion.58 = bf16[32,2,8,128]{3,0,2,1:T(8,128)(2,1)S(1)} fusion(bf16[32,2,8,128]{3,2,1,0:T(8,128)(2,1)} %param.11), kind=kLoop, calls=%fused_computation.72 | loop fusion | flops 393216 | bytes 262144 | tf_op jit(solution)/shard_map/convert_element_type | solution.py:119
  5.8 2.6 %collective-permute-start.1 = (f32[2,2,128]{2,1,0:T(2,128)S(1)}, f32[2,2,128]{2,1,0:T(2,128)S(1)}, u32[]{:S(2)}, u32[]{:S(2)}) collective-permute-start(f32[2,2,128]{2,1,0:T(2,128)S(1)} %fusion.112), channel_id=1, source_target_pairs={{0,2},{1,3},{2,0},{3,1},{4,6},{5,7},{6,4},{7,5},{8,10},{9,11},{10,... | collective-permute-start | bytes 6152 | tf_op jit(solution)/shard_map/ppermute | solution.py:32
  8.4 4.6 %collective-permute-start.11 = (bf16[2,32,1,8,128]{4,1,3,2,0:T(8,128)(2,1)S(1)}, bf16[2,32,1,8,128]{4,1,3,2,0:T(8,128)(2,1)S(1)}, u32[]{:S(2)}, u32[]{:S(2)}) collective-permute-start(bf16[2,32,1,8,128]{4,1,3,2,0:T(8,128)(2,1)S(1)} %get-tuple-element.26), channel_id=1, source_target_pairs={{4,0},{8,4},{12,8},{16,12},{20,16},{24,20},{28,24},{0,28},{5,1},{9... | collective-permute-start | bytes 393224 | tf_op jit(solution)/shard_map/ppermute | solution.py:18
  13.8 4.7 %collective-permute-start.3 = (bf16[32,1,8,128]{3,0,2,1:T(8,128)(2,1)S(1)}, bf16[32,1,8,128]{3,0,2,1:T(8,128)(2,1)S(1)}, u32[]{:S(2)}, u32[]{:S(2)}) collective-permute-start(bf16[32,1,8,128]{3,0,2,1:T(8,128)(2,1)S(1)} %get-tuple-element.44), channel_id=1, source_target_pairs={{4,0},{8,4},{12,8},{16,12},{20,16},{24,20},{28,24},{0,28},{5,1},{9... | collective-permute-start | bytes 196616 | tf_op jit(solution)/shard_map/ppermute | solution.py:18
  18.7 1.8 %collective-permute-done.3 = bf16[32,1,8,128]{3,0,2,1:T(8,128)(2,1)S(1)} collective-permute-done((bf16[32,1,8,128]{3,0,2,1:T(8,128)(2,1)S(1)}, bf16[32,1,8,128]{3,0,2,1:T(8,128)(2,1)S(1)}, u32[]{:S(2)}, u32[]{:S(2)}) %collective-permute-start.3) | collective-permute-done | bytes 65568 | tf_op jit(solution)/shard_map/ppermute | solution.py:18
  20.5 5.1 %collective-permute-done.2 = bf16[32,1,8,128]{3,0,2,1:T(8,128)(2,1)S(1)} collective-permute-done((bf16[32,1,8,128]{3,0,2,1:T(8,128)(2,1)S(1)}, bf16[32,1,8,128]{3,0,2,1:T(8,128)(2,1)S(1)}, u32[]{:S(2)}, u32[]{:S(2)}) %collective-permute-start.2) | collective-permute-done | bytes 65568 | tf_op jit(solution)/shard_map/ppermute | solution.py:15
  26.3 1.1 %collective-permute-done.5 = bf16[32,4,1,128]{3,0,2,1:T(8,128)(2,1)S(1)} collective-permute-done((bf16[32,4,1,128]{3,0,2,1:T(8,128)(2,1)S(1)}, bf16[32,4,1,128]{3,0,2,1:T(8,128)(2,1)S(1)}, u32[]{:S(2)}, u32[]{:S(2)}) %collective-permute-start.5) | collective-permute-done | bytes 32800 | tf_op jit(solution)/shard_map/ppermute | solution.py:18
  27.4 1.6 %collective-permute-done.4 = bf16[32,4,1,128]{3,0,2,1:T(8,128)(2,1)S(1)} collective-permute-done((bf16[32,4,1,128]{3,0,2,1:T(8,128)(2,1)S(1)}, bf16[32,4,1,128]{3,0,2,1:T(8,128)(2,1)S(1)}, u32[]{:S(2)}, u32[]{:S(2)}) %collective-permute-start.4) | collective-permute-done | bytes 32800 | tf_op jit(solution)/shard_map/ppermute | solution.py:15
  29.6 2.1 %copy.69 = bf16[32,4,10,1,130]{0,1,4,2,3:T(4,128)(2,1)S(1)} copy(bf16[32,4,10,1,130]{4,0,2,1,3:T(8,128)(2,1)S(1)} %maximum_bitcast_fusion) | data formatting | bytes 665600
  33.1 1.8 %fusion.19 = f32[2,8,8,17,32]{4,2,3,1,0:T(8,128)S(1)} fusion(bf16[3,3,3,32,32]{4,3,2,1,0:T(8,128)(2,1)S(1)} %copy-done, bf16[32,4,10,1,7,2]{0,4,5,2,1,3:T(8,128)(2,1)S(1)} %slice.250, bf16[32,4,10,1,8,17]{0,4,5,2,1,3:T(8,128)(2,1)S(1)} %copy.46, pred[8,17]{0,1:T(8,128)(4,1)S(1)} %copy-done.7), kind=kOutput, calls=%fused_computation.16 | convolution fusion | flops 121561088 | bytes 717960 | tf_op jit(solution)/shard_map/conv_general_dilated | solution.py:83
  37.1 2.0 %collective-permute-start.6 = (bf16[32,1,8,128]{3,0,2,1:T(8,128)(2,1)}, bf16[32,1,8,128]{3,0,2,1:T(8,128)(2,1)S(1)}, u32[]{:S(2)}, u32[]{:S(2)}) collective-permute-start(bf16[32,1,8,128]{3,0,2,1:T(8,128)(2,1)} %get-tuple-element.41), channel_id=1, source_target_pairs={{0,4},{4,8},{8,12},{12,16},{16,20},{20,24},{24,28},{28,0},{1,5},{5... | collective-permute-start | bytes 196616 | tf_op jit(solution)/shard_map/ppermute | solution.py:15
  40.0 1.6 %collective-permute-done.13 = bf16[2,32,4,1,128]{4,1,3,2,0:T(8,128)(2,1)S(1)} collective-permute-done((bf16[2,32,4,1,128]{4,1,3,2,0:T(8,128)(2,1)S(1)}, bf16[2,32,4,1,128]{4,1,3,2,0:T(8,128)(2,1)S(1)}, u32[]{:S(2)}, u32[]{:S(2)}) %collective-permute-start.13) | collective-permute-done | bytes 65568 | tf_op jit(solution)/shard_map/ppermute | solution.py:18
  41.6 1.6 %collective-permute-done.12 = bf16[2,32,4,1,128]{4,1,3,2,0:T(8,128)(2,1)S(1)} collective-permute-done((bf16[2,32,4,1,128]{4,1,3,2,0:T(8,128)(2,1)S(1)}, bf16[2,32,4,1,128]{4,1,3,2,0:T(8,128)(2,1)S(1)}, u32[]{:S(2)}, u32[]{:S(2)}) %collective-permute-start.12) | collective-permute-done | bytes 65568 | tf_op jit(solution)/shard_map/ppermute | solution.py:15
  46.5 1.0 %concatenate.63 = f32[55395]{0:T(1024)S(1)} concatenate(f32[27648]{0:T(1024)S(1)} %mul.113, f32[27648]{0:T(1024)S(1)} %mul.117, f32[96]{0:T(128)S(1)} %reshape.93, f32[3]{0:T(128)S(1)} %broadcast_multiply_fusion), dimensions={0} | concatenate | bytes 443160 | tf_op jit(solution)/shard_map/concatenate | solution.py:55
  47.7 1.3 %collective-permute-start.9 = (bf16[32,4,1,128]{3,0,2,1:T(8,128)(2,1)S(1)}, bf16[32,4,1,128]{3,0,2,1:T(8,128)(2,1)S(1)}, u32[]{:S(2)}, u32[]{:S(2)}) collective-permute-start(bf16[32,4,1,128]{3,0,2,1:T(8,128)(2,1)S(1)} %get-tuple-element.28), channel_id=1, source_target_pairs={{1,0},{2,1},{3,2},{0,3},{5,4},{6,5},{7,6},{4,7},{9,8},{10,9},{11,1... | collective-permute-start | bytes 98312 | tf_op jit(solution)/shard_map/ppermute | solution.py:18
  49.0 1.2 %collective-permute-start.15 = (f32[224,128]{1,0:T(8,128)S(1)}, f32[224,128]{1,0:T(8,128)S(1)}, u32[]{:S(2)}, u32[]{:S(2)}) collective-permute-start(f32[224,128]{1,0:T(8,128)S(1)} %select_add_fusion), channel_id=1, source_target_pairs={{0,2},{1,3},{2,0},{3,1},{4,6},{5,7},{6,4},{7,5},{8,10},{9,11},{10,... | collective-permute-start | bytes 344072 | tf_op jit(solution)/shard_map/ppermute | solution.py:32
  50.6 1.7 %collective-permute-done.8 = bf16[32,4,1,128]{3,0,2,1:T(8,128)(2,1)S(1)} collective-permute-done((bf16[32,4,1,128]{3,0,2,1:T(8,128)(2,1)S(1)}, bf16[32,4,1,128]{3,0,2,1:T(8,128)(2,1)S(1)}, u32[]{:S(2)}, u32[]{:S(2)}) %collective-permute-start.8) | collective-permute-done | bytes 32800 | tf_op jit(solution)/shard_map/ppermute | solution.py:15
  52.4 2.7 %collective-permute-done.15 = f32[224,128]{1,0:T(8,128)S(1)} collective-permute-done((f32[224,128]{1,0:T(8,128)S(1)}, f32[224,128]{1,0:T(8,128)S(1)}, u32[]{:S(2)}, u32[]{:S(2)}) %collective-permute-start.15) | collective-permute-done | bytes 114720 | tf_op jit(solution)/shard_map/ppermute | solution.py:32
  55.5 4.8 %collective-permute-done.16 = f32[224,128]{1,0:T(8,128)S(1)} collective-permute-done((f32[224,128]{1,0:T(8,128)S(1)}, f32[224,128]{1,0:T(8,128)S(1)}, u32[]{:S(2)}, u32[]{:S(2)}) %collective-permute-start.16) | collective-permute-done | bytes 114720 | tf_op jit(solution)/shard_map/ppermute | solution.py:32
  60.8 2.1 %copy.70 = bf16[32,4,10,1,130]{0,1,4,2,3:T(4,128)(2,1)S(1)} copy(bf16[32,4,10,1,130]{4,0,2,1,3:T(8,128)(2,1)S(1)} %maximum_bitcast_fusion.1) | data formatting | bytes 665600
  63.9 1.3 %collective-permute-done.17 = f32[224,128]{1,0:T(8,128)S(1)} collective-permute-done((f32[224,128]{1,0:T(8,128)S(1)}, f32[224,128]{1,0:T(8,128)S(1)}, u32[]{:S(2)}, u32[]{:S(2)}) %collective-permute-start.17) | collective-permute-done | bytes 114720 | tf_op jit(solution)/shard_map/ppermute | solution.py:32
  66.1 1.7 %fusion.22 = bf16[2,8,8,17,32]{4,2,3,1,0:T(8,128)(2,1)S(1)} fusion(bf16[3,3,3,32,32]{4,3,2,1,0:T(8,128)(2,1)S(1)} %copy-done.6, bf16[32,4,10,1,7,2]{0,4,5,2,1,3:T(8,128)(2,1)S(1)} %slice.256, bf16[32,4,10,1,8,17]{0,4,5,2,1,3:T(8,128)(2,1)S(1)} %copy.52, pred[8,17]{0,1:T(8,128)(4,1)S(1)} %copy-done.7), kind=kOutput, calls=%fused_computation.17 | convolution fusion | flops 121630720 | bytes 578696 | tf_op jit(solution)/shard_map/conv_general_dilated | solution.py:83
  67.9 4.3 %collective-permute-done.18 = f32[224,128]{1,0:T(8,128)S(1)} collective-permute-done((f32[224,128]{1,0:T(8,128)S(1)}, f32[224,128]{1,0:T(8,128)S(1)}, u32[]{:S(2)}, u32[]{:S(2)}) %collective-permute-start.18) | collective-permute-done | bytes 114720 | tf_op jit(solution)/shard_map/ppermute | solution.py:32
  72.3 1.0 %copy.61 = bf16[32,2,8,128]{3,2,1,0:T(8,128)(2,1)} copy(bf16[32,2,8,128]{0,2,3,1:T(8,128)(2,1)S(1)} %slice_bitcast_fusion) | data formatting | bytes 262144
  (129 shorter events, 20.8 us)
Async XLA Ops:
  0.6 32.1 %copy-start = (bf16[3,3,3,32,32]{4,3,2,1,0:T(8,128)(2,1)S(1)}, bf16[3,3,3,32,32]{4,3,2,1,0:T(8,128)(2,1)}, u32[]{:S(2)}) copy-start(bf16[3,3,3,32,32]{4,3,2,1,0:T(8,128)(2,1)} %param.13) | copy-start | bytes 165892
  0.6 12.6 %copy-start.2 = (bf16[32,2,8,128]{3,2,1,0:T(8,128)(2,1)S(1)}, bf16[32,2,8,128]{3,2,1,0:T(8,128)(2,1)}, u32[]{:S(2)}) copy-start(bf16[32,2,8,128]{3,2,1,0:T(8,128)(2,1)} %param.11) | copy-start | bytes 393220
  0.7 12.6 %copy-start.3 = (bf16[3,32]{1,0:T(4,128)(2,1)S(1)}, bf16[3,32]{1,0:T(4,128)(2,1)}, u32[]{:S(2)}) copy-start(bf16[3,32]{1,0:T(4,128)(2,1)} %param.14) | copy-start | bytes 580
  0.7 12.4 %copy-start.4 = (f32[2,128]{1,0:T(2,128)S(1)}, f32[2,128]{1,0:T(2,128)}, u32[]{:S(2)}) copy-start(f32[2,128]{1,0:T(2,128)} %param.16) | copy-start | bytes 3076
  3.4 2.4 %collective-permute-start = (f32[2,2,128]{2,1,0:T(2,128)S(1)}, f32[2,2,128]{2,1,0:T(2,128)S(1)}, u32[]{:S(2)}, u32[]{:S(2)}) collective-permute-start(f32[2,2,128]{2,1,0:T(2,128)S(1)} %pad_maximum_fusion.16), channel_id=1, source_target_pairs={{0,1},{1,0},{2,3},{3,2},{4,5},{5,4},{6,7},{7,6},{8,9},{9,8},{10,11... | collective-permute-start | bytes 6152 | tf_op jit(solution)/shard_map/ppermute | solution.py:32
  5.8 7.2 %collective-permute-start.1 = (f32[2,2,128]{2,1,0:T(2,128)S(1)}, f32[2,2,128]{2,1,0:T(2,128)S(1)}, u32[]{:S(2)}, u32[]{:S(2)}) collective-permute-start(f32[2,2,128]{2,1,0:T(2,128)S(1)} %fusion.112), channel_id=1, source_target_pairs={{0,2},{1,3},{2,0},{3,1},{4,6},{5,7},{6,4},{7,5},{8,10},{9,11},{10,... | collective-permute-start | bytes 6152 | tf_op jit(solution)/shard_map/ppermute | solution.py:32
  8.4 30.9 %collective-permute-start.11 = (bf16[2,32,1,8,128]{4,1,3,2,0:T(8,128)(2,1)S(1)}, bf16[2,32,1,8,128]{4,1,3,2,0:T(8,128)(2,1)S(1)}, u32[]{:S(2)}, u32[]{:S(2)}) collective-permute-start(bf16[2,32,1,8,128]{4,1,3,2,0:T(8,128)(2,1)S(1)} %get-tuple-element.26), channel_id=1, source_target_pairs={{4,0},{8,4},{12,8},{16,12},{20,16},{24,20},{28,24},{0,28},{5,1},{9... | collective-permute-start | bytes 393224 | tf_op jit(solution)/shard_map/ppermute | solution.py:18
  13.0 26.3 %collective-permute-start.10 = (bf16[2,32,1,8,128]{4,1,3,2,0:T(8,128)(2,1)S(1)}, bf16[2,32,1,8,128]{4,1,3,2,0:T(8,128)(2,1)S(1)}, u32[]{:S(2)}, u32[]{:S(2)}) collective-permute-start(bf16[2,32,1,8,128]{4,1,3,2,0:T(8,128)(2,1)S(1)} %get-tuple-element.25), channel_id=1, source_target_pairs={{0,4},{4,8},{8,12},{12,16},{16,20},{20,24},{24,28},{28,0},{1,5},{5... | collective-permute-start | bytes 393224 | tf_op jit(solution)/shard_map/ppermute | solution.py:15
  13.8 6.6 %collective-permute-start.3 = (bf16[32,1,8,128]{3,0,2,1:T(8,128)(2,1)S(1)}, bf16[32,1,8,128]{3,0,2,1:T(8,128)(2,1)S(1)}, u32[]{:S(2)}, u32[]{:S(2)}) collective-permute-start(bf16[32,1,8,128]{3,0,2,1:T(8,128)(2,1)S(1)} %get-tuple-element.44), channel_id=1, source_target_pairs={{4,0},{8,4},{12,8},{16,12},{20,16},{24,20},{28,24},{0,28},{5,1},{9... | collective-permute-start | bytes 196616 | tf_op jit(solution)/shard_map/ppermute | solution.py:18
  18.6 7.0 %collective-permute-start.2 = (bf16[32,1,8,128]{3,0,2,1:T(8,128)(2,1)S(1)}, bf16[32,1,8,128]{3,0,2,1:T(8,128)(2,1)S(1)}, u32[]{:S(2)}, u32[]{:S(2)}) collective-permute-start(bf16[32,1,8,128]{3,0,2,1:T(8,128)(2,1)S(1)} %get-tuple-element.43), channel_id=1, source_target_pairs={{0,4},{4,8},{8,12},{12,16},{16,20},{20,24},{24,28},{28,0},{1,5},{5... | collective-permute-start | bytes 196616 | tf_op jit(solution)/shard_map/ppermute | solution.py:15
  25.6 1.8 %collective-permute-start.5 = (bf16[32,4,1,128]{3,0,2,1:T(8,128)(2,1)S(1)}, bf16[32,4,1,128]{3,0,2,1:T(8,128)(2,1)S(1)}, u32[]{:S(2)}, u32[]{:S(2)}) collective-permute-start(bf16[32,4,1,128]{3,0,2,1:T(8,128)(2,1)S(1)} %get-tuple-element.30), channel_id=1, source_target_pairs={{1,0},{2,1},{3,2},{0,3},{5,4},{6,5},{7,6},{4,7},{9,8},{10,9},{11,1... | collective-permute-start | bytes 98312 | tf_op jit(solution)/shard_map/ppermute | solution.py:18
  25.6 3.4 %collective-permute-start.4 = (bf16[32,4,1,128]{3,0,2,1:T(8,128)(2,1)S(1)}, bf16[32,4,1,128]{3,0,2,1:T(8,128)(2,1)S(1)}, u32[]{:S(2)}, u32[]{:S(2)}) collective-permute-start(bf16[32,4,1,128]{3,0,2,1:T(8,128)(2,1)S(1)} %get-tuple-element.29), channel_id=1, source_target_pairs={{0,1},{1,2},{2,3},{3,0},{4,5},{5,6},{6,7},{7,4},{8,9},{9,10},{10,1... | collective-permute-start | bytes 98312 | tf_op jit(solution)/shard_map/ppermute | solution.py:15
  37.1 10.5 %collective-permute-start.7 = (bf16[32,1,8,128]{3,0,2,1:T(8,128)(2,1)}, bf16[32,1,8,128]{3,0,2,1:T(8,128)(2,1)S(1)}, u32[]{:S(2)}, u32[]{:S(2)}) collective-permute-start(bf16[32,1,8,128]{3,0,2,1:T(8,128)(2,1)} %get-tuple-element.42), channel_id=1, source_target_pairs={{4,0},{8,4},{12,8},{16,12},{20,16},{24,20},{28,24},{0,28},{5,1},{9... | collective-permute-start | bytes 196616 | tf_op jit(solution)/shard_map/ppermute | solution.py:18
  37.1 10.5 %collective-permute-start.6 = (bf16[32,1,8,128]{3,0,2,1:T(8,128)(2,1)}, bf16[32,1,8,128]{3,0,2,1:T(8,128)(2,1)S(1)}, u32[]{:S(2)}, u32[]{:S(2)}) collective-permute-start(bf16[32,1,8,128]{3,0,2,1:T(8,128)(2,1)} %get-tuple-element.41), channel_id=1, source_target_pairs={{0,4},{4,8},{8,12},{12,16},{16,20},{20,24},{24,28},{28,0},{1,5},{5... | collective-permute-start | bytes 196616 | tf_op jit(solution)/shard_map/ppermute | solution.py:15
  39.3 2.3 %collective-permute-start.13 = (bf16[2,32,4,1,128]{4,1,3,2,0:T(8,128)(2,1)S(1)}, bf16[2,32,4,1,128]{4,1,3,2,0:T(8,128)(2,1)S(1)}, u32[]{:S(2)}, u32[]{:S(2)}) collective-permute-start(bf16[2,32,4,1,128]{4,1,3,2,0:T(8,128)(2,1)S(1)} %get-tuple-element.20), channel_id=1, source_target_pairs={{1,0},{2,1},{3,2},{0,3},{5,4},{6,5},{7,6},{4,7},{9,8},{10,9},{11,1... | collective-permute-start | bytes 196616 | tf_op jit(solution)/shard_map/ppermute | solution.py:18
  39.4 3.8 %collective-permute-start.12 = (bf16[2,32,4,1,128]{4,1,3,2,0:T(8,128)(2,1)S(1)}, bf16[2,32,4,1,128]{4,1,3,2,0:T(8,128)(2,1)S(1)}, u32[]{:S(2)}, u32[]{:S(2)}) collective-permute-start(bf16[2,32,4,1,128]{4,1,3,2,0:T(8,128)(2,1)S(1)} %get-tuple-element.19), channel_id=1, source_target_pairs={{0,1},{1,2},{2,3},{3,0},{4,5},{5,6},{6,7},{7,4},{8,9},{9,10},{10,1... | collective-permute-start | bytes 196616 | tf_op jit(solution)/shard_map/ppermute | solution.py:15
  47.5 1.4 %collective-permute-start.14 = (f32[224,128]{1,0:T(8,128)S(1)}, f32[224,128]{1,0:T(8,128)S(1)}, u32[]{:S(2)}, u32[]{:S(2)}) collective-permute-start(f32[224,128]{1,0:T(8,128)S(1)} %fusion.81), channel_id=1, source_target_pairs={{0,1},{1,0},{2,3},{3,2},{4,5},{5,4},{6,7},{7,6},{8,9},{9,8},{10,11... | collective-permute-start | bytes 344072 | tf_op jit(solution)/shard_map/ppermute | solution.py:46
  47.7 2.9 %collective-permute-start.9 = (bf16[32,4,1,128]{3,0,2,1:T(8,128)(2,1)S(1)}, bf16[32,4,1,128]{3,0,2,1:T(8,128)(2,1)S(1)}, u32[]{:S(2)}, u32[]{:S(2)}) collective-permute-start(bf16[32,4,1,128]{3,0,2,1:T(8,128)(2,1)S(1)} %get-tuple-element.28), channel_id=1, source_target_pairs={{1,0},{2,1},{3,2},{0,3},{5,4},{6,5},{7,6},{4,7},{9,8},{10,9},{11,1... | collective-permute-start | bytes 98312 | tf_op jit(solution)/shard_map/ppermute | solution.py:18
  49.0 3.3 %collective-permute-start.8 = (bf16[32,4,1,128]{3,0,2,1:T(8,128)(2,1)S(1)}, bf16[32,4,1,128]{3,0,2,1:T(8,128)(2,1)S(1)}, u32[]{:S(2)}, u32[]{:S(2)}) collective-permute-start(bf16[32,4,1,128]{3,0,2,1:T(8,128)(2,1)S(1)} %get-tuple-element.27), channel_id=1, source_target_pairs={{0,1},{1,2},{2,3},{3,0},{4,5},{5,6},{6,7},{7,4},{8,9},{9,10},{10,1... | collective-permute-start | bytes 98312 | tf_op jit(solution)/shard_map/ppermute | solution.py:15
  49.0 6.1 %collective-permute-start.15 = (f32[224,128]{1,0:T(8,128)S(1)}, f32[224,128]{1,0:T(8,128)S(1)}, u32[]{:S(2)}, u32[]{:S(2)}) collective-permute-start(f32[224,128]{1,0:T(8,128)S(1)} %select_add_fusion), channel_id=1, source_target_pairs={{0,2},{1,3},{2,0},{3,1},{4,6},{5,7},{6,4},{7,5},{8,10},{9,11},{10,... | collective-permute-start | bytes 344072 | tf_op jit(solution)/shard_map/ppermute | solution.py:32
  55.1 5.2 %collective-permute-start.16 = (f32[224,128]{1,0:T(8,128)S(1)}, f32[224,128]{1,0:T(8,128)S(1)}, u32[]{:S(2)}, u32[]{:S(2)}) collective-permute-start(f32[224,128]{1,0:T(8,128)S(1)} %add.91), channel_id=1, source_target_pairs={{0,4},{4,0},{8,12},{12,8},{16,20},{20,16},{24,28},{28,24},{1,5},{5... | collective-permute-start | bytes 344072 | tf_op jit(solution)/shard_map/ppermute | solution.py:32
  60.3 4.9 %collective-permute-start.17 = (f32[224,128]{1,0:T(8,128)S(1)}, f32[224,128]{1,0:T(8,128)S(1)}, u32[]{:S(2)}, u32[]{:S(2)}) collective-permute-start(f32[224,128]{1,0:T(8,128)S(1)} %add.92), channel_id=1, source_target_pairs={{0,8},{4,12},{8,0},{12,4},{16,24},{20,28},{24,16},{28,20},{1,9},{5... | collective-permute-start | bytes 344072 | tf_op jit(solution)/shard_map/ppermute | solution.py:32
  65.2 7.0 %collective-permute-start.18 = (f32[224,128]{1,0:T(8,128)S(1)}, f32[224,128]{1,0:T(8,128)S(1)}, u32[]{:S(2)}, u32[]{:S(2)}) collective-permute-start(f32[224,128]{1,0:T(8,128)S(1)} %add.93), channel_id=1, source_target_pairs={{0,16},{4,20},{8,24},{12,28},{16,0},{20,4},{24,8},{28,12},{1,17},{... | collective-permute-start | bytes 344072 | tf_op jit(solution)/shard_map/ppermute | solution.py:32
  72.2 1.4 %collective-permute-start.19 = (f32[224,128]{1,0:T(8,128)S(1)}, f32[224,128]{1,0:T(8,128)S(1)}, u32[]{:S(2)}, u32[]{:S(2)}) collective-permute-start(f32[224,128]{1,0:T(8,128)S(1)} %add.94), channel_id=1, source_target_pairs={{0,1},{1,0},{2,3},{3,2},{4,5},{5,4},{6,7},{7,6},{8,9},{9,8},{10,11... | collective-permute-start | bytes 344072 | tf_op jit(solution)/shard_map/ppermute | solution.py:48
  (4 other events, 16.5 us)

commit v7 on v6

--- a/solution.py
+++ b/solution.py
@@ -78,16 +78,21 @@
     return jnp.concatenate((field[..., -1:], field, field[..., :1]), axis=-1)
 
 
-def spread_local(weight, padded, shape):
-    kernel = jnp.transpose(weight[::-1, ::-1, ::-1], (4, 3, 0, 1, 2))
-    return lax.conv_general_dilated(
-        padded[None],
-        kernel,
-        (1, 1, 1),
-        "VALID",
-        dimension_numbers=("NCDHW", "OIDHW", "NCDHW"),
+def spread_local(weight, extended_field, shape):
+    windows = jnp.stack(
+        [
+            extended_field[:, 2 - tap_x : 2 - tap_x + shape[1], 2 - tap_z : 2 - tap_z + shape[2]]
+            for tap_x in range(3)
+            for tap_z in range(3)
+        ]
+    )
+    per_shift = jnp.einsum(
+        "toxzy,tsoi->sixzy",
+        windows,
+        weight.reshape(9, 3, shape[0], shape[0]),
         preferred_element_type=jnp.float32,
-    )[0]
+    )
+    return sum(jnp.roll(per_shift[tap_y], tap_y - 1, axis=3) for tap_y in range(3))
 
 
 def taps_from_inputs(grad_field, extended_inputs):
@@ -145,10 +150,10 @@
     grad_bias = jnp.sum(head_grad.astype(jnp.float32), axis=(1, 2, 3)) * norm_factor
     back_second = jnp.einsum("oi,oxzy->ixzy", w_out, head_grad, preferred_element_type=jnp.float32)
     grad_second_pre = (back_second * silu_slope(second_wide)).astype(jnp.bfloat16)
-    second_padded = wrap_columns(extended(grad_second_pre, (("sky", 1), ("los", 2)), 1))
+    second_padded = extended(grad_second_pre, (("sky", 1), ("los", 2)), 1)
     back_first = spread_local(w_second, second_padded, shape)
     grad_first_pre = (back_first * silu_slope(first_wide)).astype(jnp.bfloat16)
-    first_padded = wrap_columns(extended(grad_first_pre, (("sky", 1), ("los", 2)), 1))
+    first_padded = extended(grad_first_pre, (("sky", 1), ("los", 2)), 1)
     grad_features = spread_local(w_first, first_padded, shape).astype(jnp.bfloat16)
     saved_padded = extended(jnp.stack((features, pre_first)), (("sky", 2), ("los", 3)), 1)
     hidden_padded = jax.nn.silu(saved_padded[1].astype(jnp.float32)).astype(jnp.bfloat16)

time: 77.1 us -> 72.5 us (0.940)
  local copies, waits for them, and re-layouts: 17.8 us -> 10.2 us
  waiting for transfers between devices: 28.2 us -> 33.5 us
  matrix products: 6.2 us -> 3.64 us
    ppermute x6, waiting for transfers between devices: 13.1 us -> 20 us  [butterfly_sum(): value = value + lax.ppermute(value, axis, pairs)]
    unnamed x38 -> x45, local copies, waits for them, and re-layouts: 8.74 us -> 3.73 us
    conv_general_dilated x2 -> x0, matrix products: 3.49 us -> none  [spread_local(): lax.conv_general_dilated(padded[None], kernel, (1, 1, 1), 'VALID', dimens...]
    ppermute x6, starting transfers between devices: 10.8 us -> 14.1 us  [extended(): lax.ppermute(lax.slice_in_dim(block, 0, width, axis=dim), axis, backward)]
    ppermute x6, waiting for transfers between devices: 4.84 us -> 2.89 us  [extended(): lax.ppermute(lax.slice_in_dim(block, 0, width, axis=dim), axis, backward)]
    ppermute x6, starting transfers between devices: 5.5 us -> 3.68 us  [butterfly_sum(): value = value + lax.ppermute(value, axis, pairs)]
    broadcast_in_dim x2 -> x0, local copies, waits for them, and re-layouts: 1.41 us -> none  [spread_local(): padded[None]]
    ppermute x1, waiting for transfers between devices: 0.01 us -> 1.03 us  [split_sum(): keep = keep + lax.ppermute(send, first, pairs)]
  transfers between devices with their start and end apart: 20 -> 20, of which waited for: 13 -> 11; matrix products, arithmetic and copies ran while one was open for 27% -> 15% of each run, Pallas kernels for 0% -> 0%
where the time goes in v7:
time: 72.5 us; the launch traced here: 72.3 us
  waiting for transfers between devices  33.5 us (46%)
  starting transfers between devices  20.1 us (28%)
  local copies, waits for them, and re-layouts  10.2 us (14%)
  matrix products  3.64 us (5%)
  other arithmetic  3.56 us (5%)
  between operations  1.42 us (2%)
    ppermute x6, waiting for transfers between devices, butterfly_sum(): value = value + lax.ppermute(value, axis, pairs)  20 us
    ppermute x6, starting transfers between devices, extended(): lax.ppermute(lax.slice_in_dim(block, 0, width, axis=dim), axis, backward)  14.1 us
    ppermute x6, waiting for transfers between devices, extended(): lax.ppermute(lax.slice_in_dim(block, block.shape[dim] - width, None, axis...  9.22 us
    unnamed x45, local copies, waits for them, and re-layouts  3.73 us
    ppermute x6, starting transfers between devices, butterfly_sum(): value = value + lax.ppermute(value, axis, pairs)  3.68 us
    ppermute x6, waiting for transfers between devices, extended(): lax.ppermute(lax.slice_in_dim(block, 0, width, axis=dim), axis, backward)  2.89 us
    ppermute x6, starting transfers between devices, extended(): lax.ppermute(lax.slice_in_dim(block, block.shape[dim] - width, None, axis...  2.15 us
    reshape x2, local copies, waits for them, and re-layouts, unpack_rows(): parts.append(flat[start:start + size].reshape(shape))  1.85 us
  transfers between devices with their start and end apart: 20, of which 11 were waited for; matrix products, arithmetic and copies ran while one was open for 15% of the time, Pallas kernels for 0%

profile of v7, /device:TPU:0, one launch (start us, length us, event | category | flops | bytes accessed | tf_op | source)
XLA Modules:
  0.0 72.3 jit_solution(16125119319170024972)
XLA Ops:
  0.7 1.1 %fusion.34 = bf16[32,2,8,128]{3,0,2,1:T(8,128)(2,1)S(1)} fusion(bf16[32,2,8,128]{3,2,1,0:T(8,128)(2,1)} %param.11), kind=kLoop, calls=%fused_computation.56 | loop fusion | flops 393216 | bytes 262144 | tf_op jit(solution)/shard_map/convert_element_type | solution.py:124
  1.8 0.8 %fusion.105 = f32[2,8,128,3]{2,3,1,0:T(4,128)S(1)} fusion(bf16[32,2,8,128]{3,0,2,1:T(8,128)(2,1)S(1)} %fusion.34, bf16[3,32]{1,0:T(4,128)(2,1)} %param.14), kind=kOutput, calls=%fused_computation.207 | convolution fusion | flops 393216 | bytes 155840 | tf_op jit(solution)/shard_map/oi,ixzy->oxzy/dot_general | solution.py:125
  3.9 0.9 %copy.103 = bf16[32,2,8,128]{3,0,2,1:T(8,128)(2,1)S(1)} copy(bf16[32,2,8,128]{3,2,1,0:T(8,128)(2,1)} %param.9) | data formatting | bytes 262144 | tf_op args[0]
  4.8 0.9 %copy.104 = bf16[32,2,8,128]{3,0,2,1:T(8,128)(2,1)S(1)} copy(bf16[32,2,8,128]{3,2,1,0:T(8,128)(2,1)} %param.10) | data formatting | bytes 262144 | tf_op args[1]
  5.8 2.6 %collective-permute-start.1 = (f32[2,2,128]{2,1,0:T(2,128)S(1)}, f32[2,2,128]{2,1,0:T(2,128)S(1)}, u32[]{:S(2)}, u32[]{:S(2)}) collective-permute-start(f32[2,2,128]{2,1,0:T(2,128)S(1)} %fusion.109), channel_id=1, source_target_pairs={{0,2},{1,3},{2,0},{3,1},{4,6},{5,7},{6,4},{7,5},{8,10},{9,11},{10,... | collective-permute-start | bytes 6152 | tf_op jit(solution)/shard_map/ppermute | solution.py:32
  8.4 4.6 %collective-permute-start.11 = (bf16[2,32,1,8,128]{4,1,3,2,0:T(8,128)(2,1)S(1)}, bf16[2,32,1,8,128]{4,1,3,2,0:T(8,128)(2,1)S(1)}, u32[]{:S(2)}, u32[]{:S(2)}) collective-permute-start(bf16[2,32,1,8,128]{4,1,3,2,0:T(8,128)(2,1)S(1)} %get-tuple-element.31), channel_id=1, source_target_pairs={{4,0},{8,4},{12,8},{16,12},{20,16},{24,20},{28,24},{0,28},{5,1},{9... | collective-permute-start | bytes 393224 | tf_op jit(solution)/shard_map/ppermute | solution.py:18
  13.8 4.7 %collective-permute-start.3 = (bf16[32,1,8,128]{3,0,2,1:T(8,128)(2,1)S(1)}, bf16[32,1,8,128]{3,0,2,1:T(8,128)(2,1)S(1)}, u32[]{:S(2)}, u32[]{:S(2)}) collective-permute-start(bf16[32,1,8,128]{3,0,2,1:T(8,128)(2,1)S(1)} %get-tuple-element.53), channel_id=1, source_target_pairs={{4,0},{8,4},{12,8},{16,12},{20,16},{24,20},{28,24},{0,28},{5,1},{9... | collective-permute-start | bytes 196616 | tf_op jit(solution)/shard_map/ppermute | solution.py:18
  18.7 1.8 %collective-permute-done.3 = bf16[32,1,8,128]{3,0,2,1:T(8,128)(2,1)S(1)} collective-permute-done((bf16[32,1,8,128]{3,0,2,1:T(8,128)(2,1)S(1)}, bf16[32,1,8,128]{3,0,2,1:T(8,128)(2,1)S(1)}, u32[]{:S(2)}, u32[]{:S(2)}) %collective-permute-start.3) | collective-permute-done | bytes 65568 | tf_op jit(solution)/shard_map/ppermute | solution.py:18
  20.5 5.1 %collective-permute-done.2 = bf16[32,1,8,128]{3,0,2,1:T(8,128)(2,1)S(1)} collective-permute-done((bf16[32,1,8,128]{3,0,2,1:T(8,128)(2,1)S(1)}, bf16[32,1,8,128]{3,0,2,1:T(8,128)(2,1)S(1)}, u32[]{:S(2)}, u32[]{:S(2)}) %collective-permute-start.2) | collective-permute-done | bytes 65568 | tf_op jit(solution)/shard_map/ppermute | solution.py:15
  25.6 1.7 %collective-permute-start.4 = (bf16[32,4,1,128]{3,0,2,1:T(8,128)(2,1)S(1)}, bf16[32,4,1,128]{3,0,2,1:T(8,128)(2,1)S(1)}, u32[]{:S(2)}, u32[]{:S(2)}) collective-permute-start(bf16[32,4,1,128]{3,0,2,1:T(8,128)(2,1)S(1)} %get-tuple-element.39), channel_id=1, source_target_pairs={{1,0},{2,1},{3,2},{0,3},{5,4},{6,5},{7,6},{4,7},{9,8},{10,9},{11,1... | collective-permute-start | bytes 98312 | tf_op jit(solution)/shard_map/ppermute | solution.py:18
  27.5 1.4 %collective-permute-done.5 = bf16[32,4,1,128]{3,0,2,1:T(8,128)(2,1)S(1)} collective-permute-done((bf16[32,4,1,128]{3,0,2,1:T(8,128)(2,1)S(1)}, bf16[32,4,1,128]{3,0,2,1:T(8,128)(2,1)S(1)}, u32[]{:S(2)}, u32[]{:S(2)}) %collective-permute-start.5) | collective-permute-done | bytes 32800 | tf_op jit(solution)/shard_map/ppermute | solution.py:15
  31.2 2.0 %collective-permute-start.6 = (bf16[32,1,8,128]{3,0,2,1:T(8,128)(2,1)S(1)}, bf16[32,1,8,128]{3,0,2,1:T(8,128)(2,1)S(1)}, u32[]{:S(2)}, u32[]{:S(2)}) collective-permute-start(bf16[32,1,8,128]{3,0,2,1:T(8,128)(2,1)S(1)} %get-tuple-element.50), channel_id=1, source_target_pairs={{0,4},{4,8},{8,12},{12,16},{16,20},{20,24},{24,28},{28,0},{1,5},{5... | collective-permute-start | bytes 196616 | tf_op jit(solution)/shard_map/ppermute | solution.py:15
  33.5 1.2 %collective-permute-start.13 = (bf16[2,32,4,1,128]{4,1,3,2,0:T(8,128)(2,1)S(1)}, bf16[2,32,4,1,128]{4,1,3,2,0:T(8,128)(2,1)S(1)}, u32[]{:S(2)}, u32[]{:S(2)}) collective-permute-start(bf16[2,32,4,1,128]{4,1,3,2,0:T(8,128)(2,1)S(1)} %get-tuple-element.29), channel_id=1, source_target_pairs={{1,0},{2,1},{3,2},{0,3},{5,4},{6,5},{7,6},{4,7},{9,8},{10,9},{11,1... | collective-permute-start | bytes 196616 | tf_op jit(solution)/shard_map/ppermute | solution.py:18
  34.7 1.1 %collective-permute-done.7 = bf16[32,1,8,128]{3,0,2,1:T(8,128)(2,1)S(1)} collective-permute-done((bf16[32,1,8,128]{3,0,2,1:T(8,128)(2,1)S(1)}, bf16[32,1,8,128]{3,0,2,1:T(8,128)(2,1)S(1)}, u32[]{:S(2)}, u32[]{:S(2)}) %collective-permute-start.7) | collective-permute-done | bytes 65568 | tf_op jit(solution)/shard_map/ppermute | solution.py:18
  35.8 2.8 %collective-permute-done.6 = bf16[32,1,8,128]{3,0,2,1:T(8,128)(2,1)S(1)} collective-permute-done((bf16[32,1,8,128]{3,0,2,1:T(8,128)(2,1)S(1)}, bf16[32,1,8,128]{3,0,2,1:T(8,128)(2,1)S(1)}, u32[]{:S(2)}, u32[]{:S(2)}) %collective-permute-start.6) | collective-permute-done | bytes 65568 | tf_op jit(solution)/shard_map/ppermute | solution.py:15
  38.6 1.7 %collective-permute-start.8 = (bf16[32,4,1,128]{3,0,2,1:T(8,128)(2,1)S(1)}, bf16[32,4,1,128]{3,0,2,1:T(8,128)(2,1)S(1)}, u32[]{:S(2)}, u32[]{:S(2)}) collective-permute-start(bf16[32,4,1,128]{3,0,2,1:T(8,128)(2,1)S(1)} %get-tuple-element.35), channel_id=1, source_target_pairs={{1,0},{2,1},{3,2},{0,3},{5,4},{6,5},{7,6},{4,7},{9,8},{10,9},{11,1... | collective-permute-start | bytes 98312 | tf_op jit(solution)/shard_map/ppermute | solution.py:18
  43.7 1.0 %concatenate.107 = f32[55395]{0:T(1024)S(1)} concatenate(f32[27648]{0:T(1024)S(1)} %mul.113, f32[27648]{0:T(1024)S(1)} %mul.117, f32[96]{0:T(128)S(1)} %reshape.100, f32[3]{0:T(128)S(1)} %broadcast_multiply_fusion), dimensions={0} | concatenate | bytes 443160 | tf_op jit(solution)/shard_map/concatenate | solution.py:55
  45.1 1.0 %collective-permute-done.14 = f32[224,128]{1,0:T(8,128)S(1)} collective-permute-done((f32[224,128]{1,0:T(8,128)S(1)}, f32[224,128]{1,0:T(8,128)S(1)}, u32[]{:S(2)}, u32[]{:S(2)}) %collective-permute-start.14) | collective-permute-done | bytes 114720 | tf_op jit(solution)/shard_map/ppermute | solution.py:46
  46.6 4.9 %collective-permute-done.15 = f32[224,128]{1,0:T(8,128)S(1)} collective-permute-done((f32[224,128]{1,0:T(8,128)S(1)}, f32[224,128]{1,0:T(8,128)S(1)}, u32[]{:S(2)}, u32[]{:S(2)}) %collective-permute-start.15) | collective-permute-done | bytes 114720 | tf_op jit(solution)/shard_map/ppermute | solution.py:32
  51.5 4.8 %collective-permute-done.16 = f32[224,128]{1,0:T(8,128)S(1)} collective-permute-done((f32[224,128]{1,0:T(8,128)S(1)}, f32[224,128]{1,0:T(8,128)S(1)}, u32[]{:S(2)}, u32[]{:S(2)}) %collective-permute-start.16) | collective-permute-done | bytes 114720 | tf_op jit(solution)/shard_map/ppermute | solution.py:32
  56.9 4.3 %collective-permute-done.17 = f32[224,128]{1,0:T(8,128)S(1)} collective-permute-done((f32[224,128]{1,0:T(8,128)S(1)}, f32[224,128]{1,0:T(8,128)S(1)}, u32[]{:S(2)}, u32[]{:S(2)}) %collective-permute-start.17) | collective-permute-done | bytes 114720 | tf_op jit(solution)/shard_map/ppermute | solution.py:32
  61.6 6.0 %collective-permute-done.18 = f32[224,128]{1,0:T(8,128)S(1)} collective-permute-done((f32[224,128]{1,0:T(8,128)S(1)}, f32[224,128]{1,0:T(8,128)S(1)}, u32[]{:S(2)}, u32[]{:S(2)}) %collective-permute-start.18) | collective-permute-done | bytes 114720 | tf_op jit(solution)/shard_map/ppermute | solution.py:32
  69.3 0.9 %reshape.101 = f32[3,3,3,32,32]{4,3,2,1,0:T(8,128)} reshape(f32[216,128]{1,0:T(8,128)S(1)} %get-tuple-element.41) | data formatting | bytes 221184 | tf_op jit(solution)/shard_map/reshape | solution.py:67
  70.2 0.9 %reshape.102 = f32[3,3,3,32,32]{4,3,2,1,0:T(8,128)} reshape(f32[216,128]{1,0:T(8,128)S(1)} %get-tuple-element.40) | data formatting | bytes 221184 | tf_op jit(solution)/shard_map/reshape | solution.py:67
  (135 shorter events, 12.6 us)
Async XLA Ops:
  0.6 28.6 %copy-start = (bf16[3,3,3,32,32]{4,3,2,1,0:T(8,128)(2,1)S(1)}, bf16[3,3,3,32,32]{4,3,2,1,0:T(8,128)(2,1)}, u32[]{:S(2)}) copy-start(bf16[3,3,3,32,32]{4,3,2,1,0:T(8,128)(2,1)} %param.13) | copy-start | bytes 165892
  0.6 12.6 %copy-start.3 = (bf16[32,2,8,128]{3,2,1,0:T(8,128)(2,1)S(1)}, bf16[32,2,8,128]{3,2,1,0:T(8,128)(2,1)}, u32[]{:S(2)}) copy-start(bf16[32,2,8,128]{3,2,1,0:T(8,128)(2,1)} %param.11) | copy-start | bytes 393220
  0.7 12.6 %copy-start.4 = (bf16[3,32]{1,0:T(4,128)(2,1)S(1)}, bf16[3,32]{1,0:T(4,128)(2,1)}, u32[]{:S(2)}) copy-start(bf16[3,32]{1,0:T(4,128)(2,1)} %param.14) | copy-start | bytes 580
  0.7 12.4 %copy-start.5 = (f32[2,128]{1,0:T(2,128)S(1)}, f32[2,128]{1,0:T(2,128)}, u32[]{:S(2)}) copy-start(f32[2,128]{1,0:T(2,128)} %param.16) | copy-start | bytes 3076
  3.4 2.4 %collective-permute-start = (f32[2,2,128]{2,1,0:T(2,128)S(1)}, f32[2,2,128]{2,1,0:T(2,128)S(1)}, u32[]{:S(2)}, u32[]{:S(2)}) collective-permute-start(f32[2,2,128]{2,1,0:T(2,128)S(1)} %pad_maximum_fusion.20), channel_id=1, source_target_pairs={{0,1},{1,0},{2,3},{3,2},{4,5},{5,4},{6,7},{7,6},{8,9},{9,8},{10,11... | collective-permute-start | bytes 6152 | tf_op jit(solution)/shard_map/ppermute | solution.py:32
  5.8 7.2 %collective-permute-start.1 = (f32[2,2,128]{2,1,0:T(2,128)S(1)}, f32[2,2,128]{2,1,0:T(2,128)S(1)}, u32[]{:S(2)}, u32[]{:S(2)}) collective-permute-start(f32[2,2,128]{2,1,0:T(2,128)S(1)} %fusion.109), channel_id=1, source_target_pairs={{0,2},{1,3},{2,0},{3,1},{4,6},{5,7},{6,4},{7,5},{8,10},{9,11},{10,... | collective-permute-start | bytes 6152 | tf_op jit(solution)/shard_map/ppermute | solution.py:32
  8.4 25.0 %collective-permute-start.11 = (bf16[2,32,1,8,128]{4,1,3,2,0:T(8,128)(2,1)S(1)}, bf16[2,32,1,8,128]{4,1,3,2,0:T(8,128)(2,1)S(1)}, u32[]{:S(2)}, u32[]{:S(2)}) collective-permute-start(bf16[2,32,1,8,128]{4,1,3,2,0:T(8,128)(2,1)S(1)} %get-tuple-element.31), channel_id=1, source_target_pairs={{4,0},{8,4},{12,8},{16,12},{20,16},{24,20},{28,24},{0,28},{5,1},{9... | collective-permute-start | bytes 393224 | tf_op jit(solution)/shard_map/ppermute | solution.py:18
  13.0 20.4 %collective-permute-start.10 = (bf16[2,32,1,8,128]{4,1,3,2,0:T(8,128)(2,1)S(1)}, bf16[2,32,1,8,128]{4,1,3,2,0:T(8,128)(2,1)S(1)}, u32[]{:S(2)}, u32[]{:S(2)}) collective-permute-start(bf16[2,32,1,8,128]{4,1,3,2,0:T(8,128)(2,1)S(1)} %get-tuple-element.30), channel_id=1, source_target_pairs={{0,4},{4,8},{8,12},{12,16},{16,20},{20,24},{24,28},{28,0},{1,5},{5... | collective-permute-start | bytes 393224 | tf_op jit(solution)/shard_map/ppermute | solution.py:15
  13.8 6.6 %collective-permute-start.3 = (bf16[32,1,8,128]{3,0,2,1:T(8,128)(2,1)S(1)}, bf16[32,1,8,128]{3,0,2,1:T(8,128)(2,1)S(1)}, u32[]{:S(2)}, u32[]{:S(2)}) collective-permute-start(bf16[32,1,8,128]{3,0,2,1:T(8,128)(2,1)S(1)} %get-tuple-element.53), channel_id=1, source_target_pairs={{4,0},{8,4},{12,8},{16,12},{20,16},{24,20},{28,24},{0,28},{5,1},{9... | collective-permute-start | bytes 196616 | tf_op jit(solution)/shard_map/ppermute | solution.py:18
  18.6 7.0 %collective-permute-start.2 = (bf16[32,1,8,128]{3,0,2,1:T(8,128)(2,1)S(1)}, bf16[32,1,8,128]{3,0,2,1:T(8,128)(2,1)S(1)}, u32[]{:S(2)}, u32[]{:S(2)}) collective-permute-start(bf16[32,1,8,128]{3,0,2,1:T(8,128)(2,1)S(1)} %get-tuple-element.52), channel_id=1, source_target_pairs={{0,4},{4,8},{8,12},{12,16},{16,20},{20,24},{24,28},{28,0},{1,5},{5... | collective-permute-start | bytes 196616 | tf_op jit(solution)/shard_map/ppermute | solution.py:15
  25.6 3.4 %collective-permute-start.5 = (bf16[32,4,1,128]{3,0,2,1:T(8,128)(2,1)S(1)}, bf16[32,4,1,128]{3,0,2,1:T(8,128)(2,1)S(1)}, u32[]{:S(2)}, u32[]{:S(2)}) collective-permute-start(bf16[32,4,1,128]{3,0,2,1:T(8,128)(2,1)S(1)} %get-tuple-element.38), channel_id=1, source_target_pairs={{0,1},{1,2},{2,3},{3,0},{4,5},{5,6},{6,7},{7,4},{8,9},{9,10},{10,1... | collective-permute-start | bytes 98312 | tf_op jit(solution)/shard_map/ppermute | solution.py:15
  25.6 3.3 %collective-permute-start.4 = (bf16[32,4,1,128]{3,0,2,1:T(8,128)(2,1)S(1)}, bf16[32,4,1,128]{3,0,2,1:T(8,128)(2,1)S(1)}, u32[]{:S(2)}, u32[]{:S(2)}) collective-permute-start(bf16[32,4,1,128]{3,0,2,1:T(8,128)(2,1)S(1)} %get-tuple-element.39), channel_id=1, source_target_pairs={{1,0},{2,1},{3,2},{0,3},{5,4},{6,5},{7,6},{4,7},{9,8},{10,9},{11,1... | collective-permute-start | bytes 98312 | tf_op jit(solution)/shard_map/ppermute | solution.py:18
  31.1 4.7 %collective-permute-start.7 = (bf16[32,1,8,128]{3,0,2,1:T(8,128)(2,1)S(1)}, bf16[32,1,8,128]{3,0,2,1:T(8,128)(2,1)S(1)}, u32[]{:S(2)}, u32[]{:S(2)}) collective-permute-start(bf16[32,1,8,128]{3,0,2,1:T(8,128)(2,1)S(1)} %get-tuple-element.51), channel_id=1, source_target_pairs={{4,0},{8,4},{12,8},{16,12},{20,16},{24,20},{28,24},{0,28},{5,1},{9... | collective-permute-start | bytes 196616 | tf_op jit(solution)/shard_map/ppermute | solution.py:18
  31.2 7.4 %collective-permute-start.6 = (bf16[32,1,8,128]{3,0,2,1:T(8,128)(2,1)S(1)}, bf16[32,1,8,128]{3,0,2,1:T(8,128)(2,1)S(1)}, u32[]{:S(2)}, u32[]{:S(2)}) collective-permute-start(bf16[32,1,8,128]{3,0,2,1:T(8,128)(2,1)S(1)} %get-tuple-element.50), channel_id=1, source_target_pairs={{0,4},{4,8},{8,12},{12,16},{16,20},{20,24},{24,28},{28,0},{1,5},{5... | collective-permute-start | bytes 196616 | tf_op jit(solution)/shard_map/ppermute | solution.py:15
  33.5 6.9 %collective-permute-start.13 = (bf16[2,32,4,1,128]{4,1,3,2,0:T(8,128)(2,1)S(1)}, bf16[2,32,4,1,128]{4,1,3,2,0:T(8,128)(2,1)S(1)}, u32[]{:S(2)}, u32[]{:S(2)}) collective-permute-start(bf16[2,32,4,1,128]{4,1,3,2,0:T(8,128)(2,1)S(1)} %get-tuple-element.29), channel_id=1, source_target_pairs={{1,0},{2,1},{3,2},{0,3},{5,4},{6,5},{7,6},{4,7},{9,8},{10,9},{11,1... | collective-permute-start | bytes 196616 | tf_op jit(solution)/shard_map/ppermute | solution.py:18
  34.7 5.7 %collective-permute-start.12 = (bf16[2,32,4,1,128]{4,1,3,2,0:T(8,128)(2,1)S(1)}, bf16[2,32,4,1,128]{4,1,3,2,0:T(8,128)(2,1)S(1)}, u32[]{:S(2)}, u32[]{:S(2)}) collective-permute-start(bf16[2,32,4,1,128]{4,1,3,2,0:T(8,128)(2,1)S(1)} %get-tuple-element.28), channel_id=1, source_target_pairs={{0,1},{1,2},{2,3},{3,0},{4,5},{5,6},{6,7},{7,4},{8,9},{9,10},{10,1... | collective-permute-start | bytes 196616 | tf_op jit(solution)/shard_map/ppermute | solution.py:15
  38.6 6.2 %collective-permute-start.9 = (bf16[32,4,1,128]{3,0,2,1:T(8,128)(2,1)S(1)}, bf16[32,4,1,128]{3,0,2,1:T(8,128)(2,1)S(1)}, u32[]{:S(2)}, u32[]{:S(2)}) collective-permute-start(bf16[32,4,1,128]{3,0,2,1:T(8,128)(2,1)S(1)} %get-tuple-element.34), channel_id=1, source_target_pairs={{0,1},{1,2},{2,3},{3,0},{4,5},{5,6},{6,7},{7,4},{8,9},{9,10},{10,1... | collective-permute-start | bytes 98312 | tf_op jit(solution)/shard_map/ppermute | solution.py:15
  38.6 6.2 %collective-permute-start.8 = (bf16[32,4,1,128]{3,0,2,1:T(8,128)(2,1)S(1)}, bf16[32,4,1,128]{3,0,2,1:T(8,128)(2,1)S(1)}, u32[]{:S(2)}, u32[]{:S(2)}) collective-permute-start(bf16[32,4,1,128]{3,0,2,1:T(8,128)(2,1)S(1)} %get-tuple-element.35), channel_id=1, source_target_pairs={{1,0},{2,1},{3,2},{0,3},{5,4},{6,5},{7,6},{4,7},{9,8},{10,9},{11,1... | collective-permute-start | bytes 98312 | tf_op jit(solution)/shard_map/ppermute | solution.py:18
  44.7 1.4 %collective-permute-start.14 = (f32[224,128]{1,0:T(8,128)S(1)}, f32[224,128]{1,0:T(8,128)S(1)}, u32[]{:S(2)}, u32[]{:S(2)}) collective-permute-start(f32[224,128]{1,0:T(8,128)S(1)} %fusion.84), channel_id=1, source_target_pairs={{0,1},{1,0},{2,3},{3,2},{4,5},{5,4},{6,7},{7,6},{8,9},{9,8},{10,11... | collective-permute-start | bytes 344072 | tf_op jit(solution)/shard_map/ppermute | solution.py:46
  46.2 5.3 %collective-permute-start.15 = (f32[224,128]{1,0:T(8,128)S(1)}, f32[224,128]{1,0:T(8,128)S(1)}, u32[]{:S(2)}, u32[]{:S(2)}) collective-permute-start(f32[224,128]{1,0:T(8,128)S(1)} %select_add_fusion), channel_id=1, source_target_pairs={{0,2},{1,3},{2,0},{3,1},{4,6},{5,7},{6,4},{7,5},{8,10},{9,11},{10,... | collective-permute-start | bytes 344072 | tf_op jit(solution)/shard_map/ppermute | solution.py:32
  51.4 4.9 %collective-permute-start.16 = (f32[224,128]{1,0:T(8,128)S(1)}, f32[224,128]{1,0:T(8,128)S(1)}, u32[]{:S(2)}, u32[]{:S(2)}) collective-permute-start(f32[224,128]{1,0:T(8,128)S(1)} %add.107), channel_id=1, source_target_pairs={{0,4},{4,0},{8,12},{12,8},{16,20},{20,16},{24,28},{28,24},{1,5},{5... | collective-permute-start | bytes 344072 | tf_op jit(solution)/shard_map/ppermute | solution.py:32
  56.3 4.9 %collective-permute-start.17 = (f32[224,128]{1,0:T(8,128)S(1)}, f32[224,128]{1,0:T(8,128)S(1)}, u32[]{:S(2)}, u32[]{:S(2)}) collective-permute-start(f32[224,128]{1,0:T(8,128)S(1)} %add.108), channel_id=1, source_target_pairs={{0,8},{4,12},{8,0},{12,4},{16,24},{20,28},{24,16},{28,20},{1,9},{5... | collective-permute-start | bytes 344072 | tf_op jit(solution)/shard_map/ppermute | solution.py:32
  61.2 6.4 %collective-permute-start.18 = (f32[224,128]{1,0:T(8,128)S(1)}, f32[224,128]{1,0:T(8,128)S(1)}, u32[]{:S(2)}, u32[]{:S(2)}) collective-permute-start(f32[224,128]{1,0:T(8,128)S(1)} %add.109), channel_id=1, source_target_pairs={{0,16},{4,20},{8,24},{12,28},{16,0},{20,4},{24,8},{28,12},{1,17},{... | collective-permute-start | bytes 344072 | tf_op jit(solution)/shard_map/ppermute | solution.py:32
  67.6 1.4 %collective-permute-start.19 = (f32[224,128]{1,0:T(8,128)S(1)}, f32[224,128]{1,0:T(8,128)S(1)}, u32[]{:S(2)}, u32[]{:S(2)}) collective-permute-start(f32[224,128]{1,0:T(8,128)S(1)} %add.110), channel_id=1, source_target_pairs={{0,1},{1,0},{2,3},{3,2},{4,5},{5,4},{6,7},{7,6},{8,9},{9,8},{10,11... | collective-permute-start | bytes 344072 | tf_op jit(solution)/shard_map/ppermute | solution.py:48
  (3 other events, 24.6 us)

commit v8 on v7

--- a/solution.py
+++ b/solution.py
@@ -35,17 +35,23 @@
 
 
 def split_sum(value, axes):
-    first = axes[0]
-    if lax.axis_size(first) % 2:
-        return butterfly_sum(value, axes)
+    sizes = [lax.axis_size(axis) for axis in axes]
+    total = math.prod(sizes)
+    if total & (total - 1) or sizes[0] % 2:
+        return lax.psum(value, axes)
     half = value.shape[0] // 2
-    pairs = [(i, i ^ 1) for i in range(lax.axis_size(first))]
-    upper = lax.axis_index(first) % 2 == 1
+    upper = lax.axis_index(axes[0]) % 2 == 1
     keep = jnp.where(upper, value[half:], value[:half])
     send = jnp.where(upper, value[:half], value[half:])
-    keep = keep + lax.ppermute(send, first, pairs)
-    keep = butterfly_sum(keep, axes, skip=1)
-    other = lax.ppermute(keep, first, pairs)
+    index_axes = tuple(reversed(axes))
+    partner = [(i, i ^ 1) for i in range(total)]
+    keep = keep + lax.ppermute(send, index_axes, partner)
+    bits = [1 << b for b in range(1, total.bit_length() - 1)]
+    turned = bits[len(bits) // 2 :] + bits[: len(bits) // 2]
+    for lower_bit, upper_bit in zip(bits, turned):
+        pairs = [(i, i ^ (upper_bit if i & 1 else lower_bit)) for i in range(total)]
+        keep = keep + lax.ppermute(keep, index_axes, pairs)
+    other = lax.ppermute(keep, index_axes, partner)
     return jnp.where(
         upper, jnp.concatenate((other, keep)), jnp.concatenate((keep, other))
     )

time: 72.5 us -> 72.1 us (level)
    ppermute x6 -> x2, waiting for transfers between devices: 20 us -> 0.01 us  [butterfly_sum(): value = value + lax.ppermute(value, axis, pairs)]
    ppermute x2 -> x6, waiting for transfers between devices: 1.42 us -> 21 us  [the longest x4 19.5 us: split_sum(): keep = keep + lax.ppermute(keep, index_axes, pairs)]
    ppermute x6 -> x2, starting transfers between devices: 3.68 us -> 3.09 us  [butterfly_sum(): value = value + lax.ppermute(value, axis, pairs)]
where the time goes in v8:
time: 72.1 us; the launch traced here: 71.9 us
  waiting for transfers between devices  33.1 us (46%)
  starting transfers between devices  20.1 us (28%)
  local copies, waits for them, and re-layouts  10.2 us (14%)
  matrix products  3.64 us (5%)
  other arithmetic  3.56 us (5%)
  between operations  1.42 us (2%)
    ppermute x4, waiting for transfers between devices, split_sum(): keep = keep + lax.ppermute(keep, index_axes, pairs)  19.5 us
    ppermute x6, starting transfers between devices, extended(): lax.ppermute(lax.slice_in_dim(block, 0, width, axis=dim), axis, backward)  14.1 us
    ppermute x6, waiting for transfers between devices, extended(): lax.ppermute(lax.slice_in_dim(block, block.shape[dim] - width, None, axis...  9.22 us
    unnamed x45, local copies, waits for them, and re-layouts  3.73 us
    ppermute x2, starting transfers between devices, butterfly_sum(): value = value + lax.ppermute(value, axis, pairs)  3.09 us
    ppermute x6, waiting for transfers between devices, extended(): lax.ppermute(lax.slice_in_dim(block, 0, width, axis=dim), axis, backward)  2.89 us
    ppermute x6, starting transfers between devices, extended(): lax.ppermute(lax.slice_in_dim(block, block.shape[dim] - width, None, axis...  2.15 us
    reshape x2, local copies, waits for them, and re-layouts, unpack_rows(): parts.append(flat[start:start + size].reshape(shape))  1.85 us
  transfers between devices with their start and end apart: 20, of which 11 were waited for; matrix products, arithmetic and copies ran while one was open for 15% of the time, Pallas kernels for 0%

profile of v8, /device:TPU:0, one launch (start us, length us, event | category | flops | bytes accessed | tf_op | source)
XLA Modules:
  0.0 71.9 jit_solution(12290655831741639435)
XLA Ops:
  0.7 1.1 %fusion.34 = bf16[32,2,8,128]{3,0,2,1:T(8,128)(2,1)S(1)} fusion(bf16[32,2,8,128]{3,2,1,0:T(8,128)(2,1)} %param.11), kind=kLoop, calls=%fused_computation.56 | loop fusion | flops 393216 | bytes 262144 | tf_op jit(solution)/shard_map/convert_element_type | solution.py:130
  1.8 0.8 %fusion.105 = f32[2,8,128,3]{2,3,1,0:T(4,128)S(1)} fusion(bf16[32,2,8,128]{3,0,2,1:T(8,128)(2,1)S(1)} %fusion.34, bf16[3,32]{1,0:T(4,128)(2,1)} %param.14), kind=kOutput, calls=%fused_computation.207 | convolution fusion | flops 393216 | bytes 155840 | tf_op jit(solution)/shard_map/oi,ixzy->oxzy/dot_general | solution.py:131
  3.9 0.9 %copy.103 = bf16[32,2,8,128]{3,0,2,1:T(8,128)(2,1)S(1)} copy(bf16[32,2,8,128]{3,2,1,0:T(8,128)(2,1)} %param.9) | data formatting | bytes 262144 | tf_op args[0]
  4.8 0.9 %copy.104 = bf16[32,2,8,128]{3,0,2,1:T(8,128)(2,1)S(1)} copy(bf16[32,2,8,128]{3,2,1,0:T(8,128)(2,1)} %param.10) | data formatting | bytes 262144 | tf_op args[1]
  5.8 2.6 %collective-permute-start.1 = (f32[2,2,128]{2,1,0:T(2,128)S(1)}, f32[2,2,128]{2,1,0:T(2,128)S(1)}, u32[]{:S(2)}, u32[]{:S(2)}) collective-permute-start(f32[2,2,128]{2,1,0:T(2,128)S(1)} %fusion.109), channel_id=1, source_target_pairs={{0,2},{1,3},{2,0},{3,1},{4,6},{5,7},{6,4},{7,5},{8,10},{9,11},{10,... | collective-permute-start | bytes 6152 | tf_op jit(solution)/shard_map/ppermute | solution.py:32
  8.4 4.6 %collective-permute-start.11 = (bf16[2,32,1,8,128]{4,1,3,2,0:T(8,128)(2,1)S(1)}, bf16[2,32,1,8,128]{4,1,3,2,0:T(8,128)(2,1)S(1)}, u32[]{:S(2)}, u32[]{:S(2)}) collective-permute-start(bf16[2,32,1,8,128]{4,1,3,2,0:T(8,128)(2,1)S(1)} %get-tuple-element.31), channel_id=1, source_target_pairs={{4,0},{8,4},{12,8},{16,12},{20,16},{24,20},{28,24},{0,28},{5,1},{9... | collective-permute-start | bytes 393224 | tf_op jit(solution)/shard_map/ppermute | solution.py:18
  13.8 4.7 %collective-permute-start.3 = (bf16[32,1,8,128]{3,0,2,1:T(8,128)(2,1)S(1)}, bf16[32,1,8,128]{3,0,2,1:T(8,128)(2,1)S(1)}, u32[]{:S(2)}, u32[]{:S(2)}) collective-permute-start(bf16[32,1,8,128]{3,0,2,1:T(8,128)(2,1)S(1)} %get-tuple-element.53), channel_id=1, source_target_pairs={{4,0},{8,4},{12,8},{16,12},{20,16},{24,20},{28,24},{0,28},{5,1},{9... | collective-permute-start | bytes 196616 | tf_op jit(solution)/shard_map/ppermute | solution.py:18
  18.7 1.8 %collective-permute-done.3 = bf16[32,1,8,128]{3,0,2,1:T(8,128)(2,1)S(1)} collective-permute-done((bf16[32,1,8,128]{3,0,2,1:T(8,128)(2,1)S(1)}, bf16[32,1,8,128]{3,0,2,1:T(8,128)(2,1)S(1)}, u32[]{:S(2)}, u32[]{:S(2)}) %collective-permute-start.3) | collective-permute-done | bytes 65568 | tf_op jit(solution)/shard_map/ppermute | solution.py:18
  20.5 5.1 %collective-permute-done.2 = bf16[32,1,8,128]{3,0,2,1:T(8,128)(2,1)S(1)} collective-permute-done((bf16[32,1,8,128]{3,0,2,1:T(8,128)(2,1)S(1)}, bf16[32,1,8,128]{3,0,2,1:T(8,128)(2,1)S(1)}, u32[]{:S(2)}, u32[]{:S(2)}) %collective-permute-start.2) | collective-permute-done | bytes 65568 | tf_op jit(solution)/shard_map/ppermute | solution.py:15
  25.6 1.7 %collective-permute-start.4 = (bf16[32,4,1,128]{3,0,2,1:T(8,128)(2,1)S(1)}, bf16[32,4,1,128]{3,0,2,1:T(8,128)(2,1)S(1)}, u32[]{:S(2)}, u32[]{:S(2)}) collective-permute-start(bf16[32,4,1,128]{3,0,2,1:T(8,128)(2,1)S(1)} %get-tuple-element.39), channel_id=1, source_target_pairs={{1,0},{2,1},{3,2},{0,3},{5,4},{6,5},{7,6},{4,7},{9,8},{10,9},{11,1... | collective-permute-start | bytes 98312 | tf_op jit(solution)/shard_map/ppermute | solution.py:18
  27.5 1.4 %collective-permute-done.5 = bf16[32,4,1,128]{3,0,2,1:T(8,128)(2,1)S(1)} collective-permute-done((bf16[32,4,1,128]{3,0,2,1:T(8,128)(2,1)S(1)}, bf16[32,4,1,128]{3,0,2,1:T(8,128)(2,1)S(1)}, u32[]{:S(2)}, u32[]{:S(2)}) %collective-permute-start.5) | collective-permute-done | bytes 32800 | tf_op jit(solution)/shard_map/ppermute | solution.py:15
  31.2 2.0 %collective-permute-start.6 = (bf16[32,1,8,128]{3,0,2,1:T(8,128)(2,1)S(1)}, bf16[32,1,8,128]{3,0,2,1:T(8,128)(2,1)S(1)}, u32[]{:S(2)}, u32[]{:S(2)}) collective-permute-start(bf16[32,1,8,128]{3,0,2,1:T(8,128)(2,1)S(1)} %get-tuple-element.50), channel_id=1, source_target_pairs={{0,4},{4,8},{8,12},{12,16},{16,20},{20,24},{24,28},{28,0},{1,5},{5... | collective-permute-start | bytes 196616 | tf_op jit(solution)/shard_map/ppermute | solution.py:15
  33.5 1.2 %collective-permute-start.13 = (bf16[2,32,4,1,128]{4,1,3,2,0:T(8,128)(2,1)S(1)}, bf16[2,32,4,1,128]{4,1,3,2,0:T(8,128)(2,1)S(1)}, u32[]{:S(2)}, u32[]{:S(2)}) collective-permute-start(bf16[2,32,4,1,128]{4,1,3,2,0:T(8,128)(2,1)S(1)} %get-tuple-element.29), channel_id=1, source_target_pairs={{1,0},{2,1},{3,2},{0,3},{5,4},{6,5},{7,6},{4,7},{9,8},{10,9},{11,1... | collective-permute-start | bytes 196616 | tf_op jit(solution)/shard_map/ppermute | solution.py:18
  34.7 1.1 %collective-permute-done.7 = bf16[32,1,8,128]{3,0,2,1:T(8,128)(2,1)S(1)} collective-permute-done((bf16[32,1,8,128]{3,0,2,1:T(8,128)(2,1)S(1)}, bf16[32,1,8,128]{3,0,2,1:T(8,128)(2,1)S(1)}, u32[]{:S(2)}, u32[]{:S(2)}) %collective-permute-start.7) | collective-permute-done | bytes 65568 | tf_op jit(solution)/shard_map/ppermute | solution.py:18
  35.8 2.8 %collective-permute-done.6 = bf16[32,1,8,128]{3,0,2,1:T(8,128)(2,1)S(1)} collective-permute-done((bf16[32,1,8,128]{3,0,2,1:T(8,128)(2,1)S(1)}, bf16[32,1,8,128]{3,0,2,1:T(8,128)(2,1)S(1)}, u32[]{:S(2)}, u32[]{:S(2)}) %collective-permute-start.6) | collective-permute-done | bytes 65568 | tf_op jit(solution)/shard_map/ppermute | solution.py:15
  38.6 1.7 %collective-permute-start.8 = (bf16[32,4,1,128]{3,0,2,1:T(8,128)(2,1)S(1)}, bf16[32,4,1,128]{3,0,2,1:T(8,128)(2,1)S(1)}, u32[]{:S(2)}, u32[]{:S(2)}) collective-permute-start(bf16[32,4,1,128]{3,0,2,1:T(8,128)(2,1)S(1)} %get-tuple-element.35), channel_id=1, source_target_pairs={{1,0},{2,1},{3,2},{0,3},{5,4},{6,5},{7,6},{4,7},{9,8},{10,9},{11,1... | collective-permute-start | bytes 98312 | tf_op jit(solution)/shard_map/ppermute | solution.py:18
  43.7 1.0 %concatenate.107 = f32[55395]{0:T(1024)S(1)} concatenate(f32[27648]{0:T(1024)S(1)} %mul.113, f32[27648]{0:T(1024)S(1)} %mul.117, f32[96]{0:T(128)S(1)} %reshape.100, f32[3]{0:T(128)S(1)} %broadcast_multiply_fusion), dimensions={0} | concatenate | bytes 443160 | tf_op jit(solution)/shard_map/concatenate | solution.py:61
  45.1 1.0 %collective-permute-done.14 = f32[224,128]{1,0:T(8,128)S(1)} collective-permute-done((f32[224,128]{1,0:T(8,128)S(1)}, f32[224,128]{1,0:T(8,128)S(1)}, u32[]{:S(2)}, u32[]{:S(2)}) %collective-permute-start.14) | collective-permute-done | bytes 114720 | tf_op jit(solution)/shard_map/ppermute | solution.py:48
  46.6 4.5 %collective-permute-done.15 = f32[224,128]{1,0:T(8,128)S(1)} collective-permute-done((f32[224,128]{1,0:T(8,128)S(1)}, f32[224,128]{1,0:T(8,128)S(1)}, u32[]{:S(2)}, u32[]{:S(2)}) %collective-permute-start.15) | collective-permute-done | bytes 114720 | tf_op jit(solution)/shard_map/ppermute | solution.py:53
  51.1 4.8 %collective-permute-done.16 = f32[224,128]{1,0:T(8,128)S(1)} collective-permute-done((f32[224,128]{1,0:T(8,128)S(1)}, f32[224,128]{1,0:T(8,128)S(1)}, u32[]{:S(2)}, u32[]{:S(2)}) %collective-permute-start.16) | collective-permute-done | bytes 114720 | tf_op jit(solution)/shard_map/ppermute | solution.py:53
  56.5 4.3 %collective-permute-done.17 = f32[224,128]{1,0:T(8,128)S(1)} collective-permute-done((f32[224,128]{1,0:T(8,128)S(1)}, f32[224,128]{1,0:T(8,128)S(1)}, u32[]{:S(2)}, u32[]{:S(2)}) %collective-permute-start.17) | collective-permute-done | bytes 114720 | tf_op jit(solution)/shard_map/ppermute | solution.py:53
  61.2 6.0 %collective-permute-done.18 = f32[224,128]{1,0:T(8,128)S(1)} collective-permute-done((f32[224,128]{1,0:T(8,128)S(1)}, f32[224,128]{1,0:T(8,128)S(1)}, u32[]{:S(2)}, u32[]{:S(2)}) %collective-permute-start.18) | collective-permute-done | bytes 114720 | tf_op jit(solution)/shard_map/ppermute | solution.py:53
  68.9 0.9 %reshape.101 = f32[3,3,3,32,32]{4,3,2,1,0:T(8,128)} reshape(f32[216,128]{1,0:T(8,128)S(1)} %get-tuple-element.41) | data formatting | bytes 221184 | tf_op jit(solution)/shard_map/reshape | solution.py:73
  69.8 0.9 %reshape.102 = f32[3,3,3,32,32]{4,3,2,1,0:T(8,128)} reshape(f32[216,128]{1,0:T(8,128)S(1)} %get-tuple-element.40) | data formatting | bytes 221184 | tf_op jit(solution)/shard_map/reshape | solution.py:73
  (135 shorter events, 12.6 us)
Async XLA Ops:
  0.6 28.6 %copy-start = (bf16[3,3,3,32,32]{4,3,2,1,0:T(8,128)(2,1)S(1)}, bf16[3,3,3,32,32]{4,3,2,1,0:T(8,128)(2,1)}, u32[]{:S(2)}) copy-start(bf16[3,3,3,32,32]{4,3,2,1,0:T(8,128)(2,1)} %param.13) | copy-start | bytes 165892
  0.6 12.6 %copy-start.3 = (bf16[32,2,8,128]{3,2,1,0:T(8,128)(2,1)S(1)}, bf16[32,2,8,128]{3,2,1,0:T(8,128)(2,1)}, u32[]{:S(2)}) copy-start(bf16[32,2,8,128]{3,2,1,0:T(8,128)(2,1)} %param.11) | copy-start | bytes 393220
  0.7 12.6 %copy-start.4 = (bf16[3,32]{1,0:T(4,128)(2,1)S(1)}, bf16[3,32]{1,0:T(4,128)(2,1)}, u32[]{:S(2)}) copy-start(bf16[3,32]{1,0:T(4,128)(2,1)} %param.14) | copy-start | bytes 580
  0.7 12.4 %copy-start.5 = (f32[2,128]{1,0:T(2,128)S(1)}, f32[2,128]{1,0:T(2,128)}, u32[]{:S(2)}) copy-start(f32[2,128]{1,0:T(2,128)} %param.16) | copy-start | bytes 3076
  3.4 2.4 %collective-permute-start = (f32[2,2,128]{2,1,0:T(2,128)S(1)}, f32[2,2,128]{2,1,0:T(2,128)S(1)}, u32[]{:S(2)}, u32[]{:S(2)}) collective-permute-start(f32[2,2,128]{2,1,0:T(2,128)S(1)} %pad_maximum_fusion.20), channel_id=1, source_target_pairs={{0,1},{1,0},{2,3},{3,2},{4,5},{5,4},{6,7},{7,6},{8,9},{9,8},{10,11... | collective-permute-start | bytes 6152 | tf_op jit(solution)/shard_map/ppermute | solution.py:32
  5.8 7.2 %collective-permute-start.1 = (f32[2,2,128]{2,1,0:T(2,128)S(1)}, f32[2,2,128]{2,1,0:T(2,128)S(1)}, u32[]{:S(2)}, u32[]{:S(2)}) collective-permute-start(f32[2,2,128]{2,1,0:T(2,128)S(1)} %fusion.109), channel_id=1, source_target_pairs={{0,2},{1,3},{2,0},{3,1},{4,6},{5,7},{6,4},{7,5},{8,10},{9,11},{10,... | collective-permute-start | bytes 6152 | tf_op jit(solution)/shard_map/ppermute | solution.py:32
  8.4 25.0 %collective-permute-start.11 = (bf16[2,32,1,8,128]{4,1,3,2,0:T(8,128)(2,1)S(1)}, bf16[2,32,1,8,128]{4,1,3,2,0:T(8,128)(2,1)S(1)}, u32[]{:S(2)}, u32[]{:S(2)}) collective-permute-start(bf16[2,32,1,8,128]{4,1,3,2,0:T(8,128)(2,1)S(1)} %get-tuple-element.31), channel_id=1, source_target_pairs={{4,0},{8,4},{12,8},{16,12},{20,16},{24,20},{28,24},{0,28},{5,1},{9... | collective-permute-start | bytes 393224 | tf_op jit(solution)/shard_map/ppermute | solution.py:18
  13.0 20.4 %collective-permute-start.10 = (bf16[2,32,1,8,128]{4,1,3,2,0:T(8,128)(2,1)S(1)}, bf16[2,32,1,8,128]{4,1,3,2,0:T(8,128)(2,1)S(1)}, u32[]{:S(2)}, u32[]{:S(2)}) collective-permute-start(bf16[2,32,1,8,128]{4,1,3,2,0:T(8,128)(2,1)S(1)} %get-tuple-element.30), channel_id=1, source_target_pairs={{0,4},{4,8},{8,12},{12,16},{16,20},{20,24},{24,28},{28,0},{1,5},{5... | collective-permute-start | bytes 393224 | tf_op jit(solution)/shard_map/ppermute | solution.py:15
  13.8 6.6 %collective-permute-start.3 = (bf16[32,1,8,128]{3,0,2,1:T(8,128)(2,1)S(1)}, bf16[32,1,8,128]{3,0,2,1:T(8,128)(2,1)S(1)}, u32[]{:S(2)}, u32[]{:S(2)}) collective-permute-start(bf16[32,1,8,128]{3,0,2,1:T(8,128)(2,1)S(1)} %get-tuple-element.53), channel_id=1, source_target_pairs={{4,0},{8,4},{12,8},{16,12},{20,16},{24,20},{28,24},{0,28},{5,1},{9... | collective-permute-start | bytes 196616 | tf_op jit(solution)/shard_map/ppermute | solution.py:18
  18.6 7.0 %collective-permute-start.2 = (bf16[32,1,8,128]{3,0,2,1:T(8,128)(2,1)S(1)}, bf16[32,1,8,128]{3,0,2,1:T(8,128)(2,1)S(1)}, u32[]{:S(2)}, u32[]{:S(2)}) collective-permute-start(bf16[32,1,8,128]{3,0,2,1:T(8,128)(2,1)S(1)} %get-tuple-element.52), channel_id=1, source_target_pairs={{0,4},{4,8},{8,12},{12,16},{16,20},{20,24},{24,28},{28,0},{1,5},{5... | collective-permute-start | bytes 196616 | tf_op jit(solution)/shard_map/ppermute | solution.py:15
  25.6 3.4 %collective-permute-start.5 = (bf16[32,4,1,128]{3,0,2,1:T(8,128)(2,1)S(1)}, bf16[32,4,1,128]{3,0,2,1:T(8,128)(2,1)S(1)}, u32[]{:S(2)}, u32[]{:S(2)}) collective-permute-start(bf16[32,4,1,128]{3,0,2,1:T(8,128)(2,1)S(1)} %get-tuple-element.38), channel_id=1, source_target_pairs={{0,1},{1,2},{2,3},{3,0},{4,5},{5,6},{6,7},{7,4},{8,9},{9,10},{10,1... | collective-permute-start | bytes 98312 | tf_op jit(solution)/shard_map/ppermute | solution.py:15
  25.6 3.3 %collective-permute-start.4 = (bf16[32,4,1,128]{3,0,2,1:T(8,128)(2,1)S(1)}, bf16[32,4,1,128]{3,0,2,1:T(8,128)(2,1)S(1)}, u32[]{:S(2)}, u32[]{:S(2)}) collective-permute-start(bf16[32,4,1,128]{3,0,2,1:T(8,128)(2,1)S(1)} %get-tuple-element.39), channel_id=1, source_target_pairs={{1,0},{2,1},{3,2},{0,3},{5,4},{6,5},{7,6},{4,7},{9,8},{10,9},{11,1... | collective-permute-start | bytes 98312 | tf_op jit(solution)/shard_map/ppermute | solution.py:18
  31.1 4.7 %collective-permute-start.7 = (bf16[32,1,8,128]{3,0,2,1:T(8,128)(2,1)S(1)}, bf16[32,1,8,128]{3,0,2,1:T(8,128)(2,1)S(1)}, u32[]{:S(2)}, u32[]{:S(2)}) collective-permute-start(bf16[32,1,8,128]{3,0,2,1:T(8,128)(2,1)S(1)} %get-tuple-element.51), channel_id=1, source_target_pairs={{4,0},{8,4},{12,8},{16,12},{20,16},{24,20},{28,24},{0,28},{5,1},{9... | collective-permute-start | bytes 196616 | tf_op jit(solution)/shard_map/ppermute | solution.py:18
  31.2 7.4 %collective-permute-start.6 = (bf16[32,1,8,128]{3,0,2,1:T(8,128)(2,1)S(1)}, bf16[32,1,8,128]{3,0,2,1:T(8,128)(2,1)S(1)}, u32[]{:S(2)}, u32[]{:S(2)}) collective-permute-start(bf16[32,1,8,128]{3,0,2,1:T(8,128)(2,1)S(1)} %get-tuple-element.50), channel_id=1, source_target_pairs={{0,4},{4,8},{8,12},{12,16},{16,20},{20,24},{24,28},{28,0},{1,5},{5... | collective-permute-start | bytes 196616 | tf_op jit(solution)/shard_map/ppermute | solution.py:15
  33.5 6.9 %collective-permute-start.13 = (bf16[2,32,4,1,128]{4,1,3,2,0:T(8,128)(2,1)S(1)}, bf16[2,32,4,1,128]{4,1,3,2,0:T(8,128)(2,1)S(1)}, u32[]{:S(2)}, u32[]{:S(2)}) collective-permute-start(bf16[2,32,4,1,128]{4,1,3,2,0:T(8,128)(2,1)S(1)} %get-tuple-element.29), channel_id=1, source_target_pairs={{1,0},{2,1},{3,2},{0,3},{5,4},{6,5},{7,6},{4,7},{9,8},{10,9},{11,1... | collective-permute-start | bytes 196616 | tf_op jit(solution)/shard_map/ppermute | solution.py:18
  34.7 5.7 %collective-permute-start.12 = (bf16[2,32,4,1,128]{4,1,3,2,0:T(8,128)(2,1)S(1)}, bf16[2,32,4,1,128]{4,1,3,2,0:T(8,128)(2,1)S(1)}, u32[]{:S(2)}, u32[]{:S(2)}) collective-permute-start(bf16[2,32,4,1,128]{4,1,3,2,0:T(8,128)(2,1)S(1)} %get-tuple-element.28), channel_id=1, source_target_pairs={{0,1},{1,2},{2,3},{3,0},{4,5},{5,6},{6,7},{7,4},{8,9},{9,10},{10,1... | collective-permute-start | bytes 196616 | tf_op jit(solution)/shard_map/ppermute | solution.py:15
  38.6 6.2 %collective-permute-start.9 = (bf16[32,4,1,128]{3,0,2,1:T(8,128)(2,1)S(1)}, bf16[32,4,1,128]{3,0,2,1:T(8,128)(2,1)S(1)}, u32[]{:S(2)}, u32[]{:S(2)}) collective-permute-start(bf16[32,4,1,128]{3,0,2,1:T(8,128)(2,1)S(1)} %get-tuple-element.34), channel_id=1, source_target_pairs={{0,1},{1,2},{2,3},{3,0},{4,5},{5,6},{6,7},{7,4},{8,9},{9,10},{10,1... | collective-permute-start | bytes 98312 | tf_op jit(solution)/shard_map/ppermute | solution.py:15
  38.6 6.2 %collective-permute-start.8 = (bf16[32,4,1,128]{3,0,2,1:T(8,128)(2,1)S(1)}, bf16[32,4,1,128]{3,0,2,1:T(8,128)(2,1)S(1)}, u32[]{:S(2)}, u32[]{:S(2)}) collective-permute-start(bf16[32,4,1,128]{3,0,2,1:T(8,128)(2,1)S(1)} %get-tuple-element.35), channel_id=1, source_target_pairs={{1,0},{2,1},{3,2},{0,3},{5,4},{6,5},{7,6},{4,7},{9,8},{10,9},{11,1... | collective-permute-start | bytes 98312 | tf_op jit(solution)/shard_map/ppermute | solution.py:18
  44.7 1.4 %collective-permute-start.14 = (f32[224,128]{1,0:T(8,128)S(1)}, f32[224,128]{1,0:T(8,128)S(1)}, u32[]{:S(2)}, u32[]{:S(2)}) collective-permute-start(f32[224,128]{1,0:T(8,128)S(1)} %fusion.84), channel_id=1, source_target_pairs={{0,1},{1,0},{2,3},{3,2},{4,5},{5,4},{6,7},{7,6},{8,9},{9,8},{10,11... | collective-permute-start | bytes 344072 | tf_op jit(solution)/shard_map/ppermute | solution.py:48
  46.2 4.9 %collective-permute-start.15 = (f32[224,128]{1,0:T(8,128)S(1)}, f32[224,128]{1,0:T(8,128)S(1)}, u32[]{:S(2)}, u32[]{:S(2)}) collective-permute-start(f32[224,128]{1,0:T(8,128)S(1)} %select_add_fusion), channel_id=1, source_target_pairs={{0,2},{1,9},{2,0},{3,11},{4,6},{5,13},{6,4},{7,15},{8,10},{9,1},{1... | collective-permute-start | bytes 344072 | tf_op jit(solution)/shard_map/ppermute | solution.py:53
  51.0 4.9 %collective-permute-start.16 = (f32[224,128]{1,0:T(8,128)S(1)}, f32[224,128]{1,0:T(8,128)S(1)}, u32[]{:S(2)}, u32[]{:S(2)}) collective-permute-start(f32[224,128]{1,0:T(8,128)S(1)} %add.107), channel_id=1, source_target_pairs={{0,4},{1,17},{2,6},{3,19},{4,0},{5,21},{6,2},{7,23},{8,12},{9,25},... | collective-permute-start | bytes 344072 | tf_op jit(solution)/shard_map/ppermute | solution.py:53
  55.9 4.9 %collective-permute-start.17 = (f32[224,128]{1,0:T(8,128)S(1)}, f32[224,128]{1,0:T(8,128)S(1)}, u32[]{:S(2)}, u32[]{:S(2)}) collective-permute-start(f32[224,128]{1,0:T(8,128)S(1)} %add.108), channel_id=1, source_target_pairs={{0,8},{1,3},{2,10},{3,1},{4,12},{5,7},{6,14},{7,5},{8,0},{9,11},{1... | collective-permute-start | bytes 344072 | tf_op jit(solution)/shard_map/ppermute | solution.py:53
  60.8 6.4 %collective-permute-start.18 = (f32[224,128]{1,0:T(8,128)S(1)}, f32[224,128]{1,0:T(8,128)S(1)}, u32[]{:S(2)}, u32[]{:S(2)}) collective-permute-start(f32[224,128]{1,0:T(8,128)S(1)} %add.109), channel_id=1, source_target_pairs={{0,16},{1,5},{2,18},{3,7},{4,20},{5,1},{6,22},{7,3},{8,24},{9,13},... | collective-permute-start | bytes 344072 | tf_op jit(solution)/shard_map/ppermute | solution.py:53
  67.2 1.4 %collective-permute-start.19 = (f32[224,128]{1,0:T(8,128)S(1)}, f32[224,128]{1,0:T(8,128)S(1)}, u32[]{:S(2)}, u32[]{:S(2)}) collective-permute-start(f32[224,128]{1,0:T(8,128)S(1)} %add.110), channel_id=1, source_target_pairs={{0,1},{1,0},{2,3},{3,2},{4,5},{5,4},{6,7},{7,6},{8,9},{9,8},{10,11... | collective-permute-start | bytes 344072 | tf_op jit(solution)/shard_map/ppermute | solution.py:54
  (3 other events, 24.2 us)

commit v9 on v8

--- a/solution.py
+++ b/solution.py
@@ -101,20 +101,20 @@
     return sum(jnp.roll(per_shift[tap_y], tap_y - 1, axis=3) for tap_y in range(3))
 
 
-def taps_from_inputs(grad_field, extended_inputs):
-    shape = grad_field.shape
-    rolled = jnp.stack([jnp.roll(grad_field, tap_y - 1, axis=3) for tap_y in range(3)])
+def taps_from_halo(extended_grad, inputs):
+    shape = inputs.shape
     windows = jnp.stack(
         [
-            extended_inputs[:, tap_x : tap_x + shape[1], tap_z : tap_z + shape[2]]
+            extended_grad[:, 2 - tap_x : 2 - tap_x + shape[1], 2 - tap_z : 2 - tap_z + shape[2]]
             for tap_x in range(3)
             for tap_z in range(3)
         ]
     )
+    rolled = jnp.stack([jnp.roll(inputs, 1 - tap_y, axis=3) for tap_y in range(3)])
     taps = jnp.einsum(
-        "soxzy,tixzy->tsoi", rolled, windows, preferred_element_type=jnp.float32
+        "toxzy,sixzy->tsoi", windows, rolled, preferred_element_type=jnp.float32
     )
-    return taps.reshape(3, 3, 3, shape[0], extended_inputs.shape[0])
+    return taps.reshape(3, 3, 3, extended_grad.shape[0], shape[0])
 
 
 def per_device(
@@ -161,10 +161,9 @@
     grad_first_pre = (back_first * silu_slope(first_wide)).astype(jnp.bfloat16)
     first_padded = extended(grad_first_pre, (("sky", 1), ("los", 2)), 1)
     grad_features = spread_local(w_first, first_padded, shape).astype(jnp.bfloat16)
-    saved_padded = extended(jnp.stack((features, pre_first)), (("sky", 2), ("los", 3)), 1)
-    hidden_padded = jax.nn.silu(saved_padded[1].astype(jnp.float32)).astype(jnp.bfloat16)
-    grad_second = taps_from_inputs(grad_second_pre, hidden_padded)
-    grad_first = taps_from_inputs(grad_first_pre, saved_padded[0])
+    hidden_first = jax.nn.silu(first_wide).astype(jnp.bfloat16)
+    grad_second = taps_from_halo(second_padded, hidden_first)
+    grad_first = taps_from_halo(first_padded, features)
     reduced = (grad_first * norm_factor, grad_second * norm_factor, grad_out, grad_bias)
     reduced_shapes = [part.shape for part in reduced]
     grad_first, grad_second, grad_out, grad_bias = unpack_rows(

time: 72.1 us -> 66 us (0.915)
  waiting for transfers between devices: 33.1 us -> 26.8 us
  starting transfers between devices: 20.1 us -> 21.3 us
  local copies, waits for them, and re-layouts: 10.2 us -> 9.07 us
    ppermute x6 -> x4, starting transfers between devices: 14.1 us -> 9.24 us  [extended(): lax.ppermute(lax.slice_in_dim(block, 0, width, axis=dim), axis, backward)]
    ppermute x6 -> x4, waiting for transfers between devices: 9.22 us -> 5.62 us  [extended(): lax.ppermute(lax.slice_in_dim(block, block.shape[dim] - width, None, axis...]
    ppermute x6 -> x4, waiting for transfers between devices: 2.89 us -> 0.01 us  [extended(): lax.ppermute(lax.slice_in_dim(block, 0, width, axis=dim), axis, backward)]
    ppermute x6 -> x4, starting transfers between devices: 2.15 us -> 4.39 us  [extended(): lax.ppermute(lax.slice_in_dim(block, block.shape[dim] - width, None, axis...]
    ppermute x1, starting transfers between devices: 0.07 us -> 2.29 us  [split_sum(): keep = keep + lax.ppermute(send, index_axes, partner)]
    unnamed x45 -> x34, local copies, waits for them, and re-layouts: 3.73 us -> 1.74 us
    ppermute x4, starting transfers between devices: 0.59 us -> 2.24 us  [split_sum(): keep = keep + lax.ppermute(keep, index_axes, pairs)]
    ppermute x2, waiting for transfers between devices: 0.01 us -> 1.35 us  [butterfly_sum(): value = value + lax.ppermute(value, axis, pairs)]
  transfers between devices with their start and end apart: 20 -> 16, of which waited for: 11 -> 10; matrix products, arithmetic and copies ran while one was open for 15% -> 8% of each run, Pallas kernels for 0% -> 0%
where the time goes in v9:
time: 66 us; the launch traced here: 65.8 us
  waiting for transfers between devices  26.8 us (41%)
  starting transfers between devices  21.3 us (32%)
  local copies, waits for them, and re-layouts  9.07 us (14%)
  matrix products  4.24 us (6%)
  other arithmetic  3.11 us (5%)
  between operations  1.24 us (2%)
    ppermute x4, waiting for transfers between devices, split_sum(): keep = keep + lax.ppermute(keep, index_axes, pairs)  18.5 us
    ppermute x4, starting transfers between devices, extended(): lax.ppermute(lax.slice_in_dim(block, 0, width, axis=dim), axis, backward)  9.24 us
    ppermute x4, waiting for transfers between devices, extended(): lax.ppermute(lax.slice_in_dim(block, block.shape[dim] - width, None, axis...  5.62 us
    ppermute x4, starting transfers between devices, extended(): lax.ppermute(lax.slice_in_dim(block, block.shape[dim] - width, None, axis...  4.39 us
    ppermute x2, starting transfers between devices, butterfly_sum(): value = value + lax.ppermute(value, axis, pairs)  3.09 us
    ppermute x1, starting transfers between devices, split_sum(): keep = keep + lax.ppermute(send, index_axes, partner)  2.29 us
    ppermute x4, starting transfers between devices, split_sum(): keep = keep + lax.ppermute(keep, index_axes, pairs)  2.24 us
    dot_general x2, matrix products, taps_from_halo(): jnp.einsum('toxzy,sixzy->tsoi', windows, rolled, preferred_element_type=j...  2.13 us
  transfers between devices with their start and end apart: 16, of which 10 were waited for; matrix products, arithmetic and copies ran while one was open for 8% of the time, Pallas kernels for 0%

profile of v9, /device:TPU:0, one launch (start us, length us, event | category | flops | bytes accessed | tf_op | source)
XLA Modules:
  0.0 65.8 jit_solution(17320967528499350962)
XLA Ops:
  0.7 1.0 %fusion.22 = bf16[32,2,8,128]{3,0,2,1:T(8,128)(2,1)S(1)} fusion(bf16[32,2,8,128]{3,2,1,0:T(8,128)(2,1)} %param.11), kind=kLoop, calls=%fused_computation.40 | loop fusion | flops 393216 | bytes 262144 | tf_op jit(solution)/shard_map/convert_element_type | solution.py:130
  3.8 1.1 %fusion.92 = (bf16[32,2,8,127]{3,2,1,0:T(8,128)(2,1)S(1)}, bf16[32,2,8,127]{3,2,1,0:T(8,128)(2,1)S(1)}) fusion(bf16[32,2,8,128]{3,2,1,0:T(8,128)(2,1)} %param.9), kind=kLoop, calls=%fused_computation.167 | loop fusion | bytes 520192 | tf_op jit(solution)/shard_map/jit(_roll_static)/slice | solution.py:113
  5.3 2.6 %collective-permute-start.1 = (f32[2,2,128]{2,1,0:T(2,128)S(1)}, f32[2,2,128]{2,1,0:T(2,128)S(1)}, u32[]{:S(2)}, u32[]{:S(2)}) collective-permute-start(f32[2,2,128]{2,1,0:T(2,128)S(1)} %fusion.87), channel_id=1, source_target_pairs={{0,2},{1,3},{2,0},{3,1},{4,6},{5,7},{6,4},{7,5},{8,10},{9,11},{10,... | collective-permute-start | bytes 6152 | tf_op jit(solution)/shard_map/ppermute | solution.py:32
  8.1 1.4 %collective-permute-done.1 = f32[2,2,128]{2,1,0:T(2,128)S(1)} collective-permute-done((f32[2,2,128]{2,1,0:T(2,128)S(1)}, f32[2,2,128]{2,1,0:T(2,128)S(1)}, u32[]{:S(2)}, u32[]{:S(2)}) %collective-permute-start.1) | collective-permute-done | bytes 2080 | tf_op jit(solution)/shard_map/ppermute | solution.py:32
  9.9 2.1 %collective-permute-start.2 = (bf16[32,1,8,128]{3,0,2,1:T(8,128)(2,1)S(1)}, bf16[32,1,8,128]{3,0,2,1:T(8,128)(2,1)S(1)}, u32[]{:S(2)}, u32[]{:S(2)}) collective-permute-start(bf16[32,1,8,128]{3,0,2,1:T(8,128)(2,1)S(1)} %get-tuple-element.50), channel_id=1, source_target_pairs={{0,4},{4,8},{8,12},{12,16},{16,20},{20,24},{24,28},{28,0},{1,5},{5... | collective-permute-start | bytes 196616 | tf_op jit(solution)/shard_map/ppermute | solution.py:15
  12.0 3.1 %collective-permute-start.3 = (bf16[32,1,8,128]{3,0,2,1:T(8,128)(2,1)S(1)}, bf16[32,1,8,128]{3,0,2,1:T(8,128)(2,1)S(1)}, u32[]{:S(2)}, u32[]{:S(2)}) collective-permute-start(bf16[32,1,8,128]{3,0,2,1:T(8,128)(2,1)S(1)} %get-tuple-element.51), channel_id=1, source_target_pairs={{4,0},{8,4},{12,8},{16,12},{20,16},{24,20},{28,24},{0,28},{5,1},{9... | collective-permute-start | bytes 196616 | tf_op jit(solution)/shard_map/ppermute | solution.py:18
  15.2 2.1 %collective-permute-done.2 = bf16[32,1,8,128]{3,0,2,1:T(8,128)(2,1)S(1)} collective-permute-done((bf16[32,1,8,128]{3,0,2,1:T(8,128)(2,1)S(1)}, bf16[32,1,8,128]{3,0,2,1:T(8,128)(2,1)S(1)}, u32[]{:S(2)}, u32[]{:S(2)}) %collective-permute-start.2) | collective-permute-done | bytes 65568 | tf_op jit(solution)/shard_map/ppermute | solution.py:15
  17.4 1.7 %collective-permute-start.4 = (bf16[32,4,1,128]{3,0,2,1:T(8,128)(2,1)S(1)}, bf16[32,4,1,128]{3,0,2,1:T(8,128)(2,1)S(1)}, u32[]{:S(2)}, u32[]{:S(2)}) collective-permute-start(bf16[32,4,1,128]{3,0,2,1:T(8,128)(2,1)S(1)} %get-tuple-element.35), channel_id=1, source_target_pairs={{1,0},{2,1},{3,2},{0,3},{5,4},{6,5},{7,6},{4,7},{9,8},{10,9},{11,1... | collective-permute-start | bytes 98312 | tf_op jit(solution)/shard_map/ppermute | solution.py:18
  19.2 1.5 %collective-permute-done.5 = bf16[32,4,1,128]{3,0,2,1:T(8,128)(2,1)S(1)} collective-permute-done((bf16[32,4,1,128]{3,0,2,1:T(8,128)(2,1)S(1)}, bf16[32,4,1,128]{3,0,2,1:T(8,128)(2,1)S(1)}, u32[]{:S(2)}, u32[]{:S(2)}) %collective-permute-start.5) | collective-permute-done | bytes 32800 | tf_op jit(solution)/shard_map/ppermute | solution.py:15
  22.9 1.4 %collective-permute-start.6 = (bf16[32,1,8,128]{3,0,2,1:T(8,128)(2,1)S(1)}, bf16[32,1,8,128]{3,0,2,1:T(8,128)(2,1)S(1)}, u32[]{:S(2)}, u32[]{:S(2)}) collective-permute-start(bf16[32,1,8,128]{3,0,2,1:T(8,128)(2,1)S(1)} %get-tuple-element.48), channel_id=1, source_target_pairs={{0,4},{4,8},{8,12},{12,16},{16,20},{20,24},{24,28},{28,0},{1,5},{5... | collective-permute-start | bytes 196616 | tf_op jit(solution)/shard_map/ppermute | solution.py:15
  24.3 3.5 %collective-permute-start.7 = (bf16[32,1,8,128]{3,0,2,1:T(8,128)(2,1)S(1)}, bf16[32,1,8,128]{3,0,2,1:T(8,128)(2,1)S(1)}, u32[]{:S(2)}, u32[]{:S(2)}) collective-permute-start(bf16[32,1,8,128]{3,0,2,1:T(8,128)(2,1)S(1)} %get-tuple-element.49), channel_id=1, source_target_pairs={{4,0},{8,4},{12,8},{16,12},{20,16},{24,20},{28,24},{0,28},{5,1},{9... | collective-permute-start | bytes 196616 | tf_op jit(solution)/shard_map/ppermute | solution.py:18
  27.9 2.0 %collective-permute-done.6 = bf16[32,1,8,128]{3,0,2,1:T(8,128)(2,1)S(1)} collective-permute-done((bf16[32,1,8,128]{3,0,2,1:T(8,128)(2,1)S(1)}, bf16[32,1,8,128]{3,0,2,1:T(8,128)(2,1)S(1)}, u32[]{:S(2)}, u32[]{:S(2)}) %collective-permute-start.6) | collective-permute-done | bytes 65568 | tf_op jit(solution)/shard_map/ppermute | solution.py:15
  30.8 0.9 %collective-permute-start.8 = (bf16[32,4,1,128]{3,0,2,1:T(8,128)(2,1)S(1)}, bf16[32,4,1,128]{3,0,2,1:T(8,128)(2,1)S(1)}, u32[]{:S(2)}, u32[]{:S(2)}) collective-permute-start(bf16[32,4,1,128]{3,0,2,1:T(8,128)(2,1)S(1)} %get-tuple-element.31), channel_id=1, source_target_pairs={{1,0},{2,1},{3,2},{0,3},{5,4},{6,5},{7,6},{4,7},{9,8},{10,9},{11,1... | collective-permute-start | bytes 98312 | tf_op jit(solution)/shard_map/ppermute | solution.py:18
  31.7 1.1 %fusion.1 = f32[9,3,32,32]{2,3,0,1:T(8,128)S(1)} fusion(bf16[9,32,2,8,128]{4,1,3,2,0:T(8,128)(2,1)S(1)} %fusion.50, bf16[1,32,2,8,128]{4,1,3,2,0:T(8,128)(2,1)S(1)} %maximum_bitcast_fusion.7, bf16[1,32,2,8,128]{4,1,3,2,0:T(8,128)(2,1)S(1)} %bitcast.257, bf16[1,32,2,8,128]{4,1,3,2,0:T(8,128)(2,1)S(1)} %maximum_bitcast_fusion.6), kind=kOutput, calls=%fused_computation.4 | convolution fusion | flops 114453504 | bytes 1683456 | tf_op jit(solution)/shard_map/toxzy,sixzy->tsoi/dot_general | solution.py:114
  33.6 1.1 %fusion.3 = f32[9,3,32,32]{2,3,0,1:T(8,128)S(1)} fusion(bf16[1,32,2,8,128]{4,1,3,2,0:T(8,128)(2,1)S(1)} %get-tuple-element.60, bf16[1,32,2,8,128]{4,1,3,2,0:T(8,128)(2,1)S(1)} %bitcast.264, bf16[1,32,2,8,128]{4,1,3,2,0:T(8,128)(2,1)S(1)} %get-tuple-element.59, bf16[9,32,2,8,128]{4,1,3,2,0:T(8,128)(2,1)S(1)} %fusion.40), kind=kOutput, calls=%fused_computation.7 | convolution fusion | flops 114453504 | bytes 1683456 | tf_op jit(solution)/shard_map/toxzy,sixzy->tsoi/dot_general | solution.py:114
  35.2 1.0 %concatenate.99 = f32[55395]{0:T(1024)S(1)} concatenate(f32[27648]{0:T(1024)S(1)} %mul.112, f32[27648]{0:T(1024)S(1)} %mul.116, f32[96]{0:T(128)S(1)} %reshape.98, f32[3]{0:T(128)S(1)} %broadcast_multiply_fusion), dimensions={0} | concatenate | bytes 443160 | tf_op jit(solution)/shard_map/concatenate | solution.py:61
  36.2 2.3 %collective-permute-start.10 = (f32[224,128]{1,0:T(8,128)S(1)}, f32[224,128]{1,0:T(8,128)S(1)}, u32[]{:S(2)}, u32[]{:S(2)}) collective-permute-start(f32[224,128]{1,0:T(8,128)S(1)} %fusion.61), channel_id=1, source_target_pairs={{0,1},{1,0},{2,3},{3,2},{4,5},{5,4},{6,7},{7,6},{8,9},{9,8},{10,11... | collective-permute-start | bytes 344072 | tf_op jit(solution)/shard_map/ppermute | solution.py:48
  38.5 1.0 %collective-permute-done.10 = f32[224,128]{1,0:T(8,128)S(1)} collective-permute-done((f32[224,128]{1,0:T(8,128)S(1)}, f32[224,128]{1,0:T(8,128)S(1)}, u32[]{:S(2)}, u32[]{:S(2)}) %collective-permute-start.10) | collective-permute-done | bytes 114720 | tf_op jit(solution)/shard_map/ppermute | solution.py:48
  39.9 4.4 %collective-permute-done.11 = f32[224,128]{1,0:T(8,128)S(1)} collective-permute-done((f32[224,128]{1,0:T(8,128)S(1)}, f32[224,128]{1,0:T(8,128)S(1)}, u32[]{:S(2)}, u32[]{:S(2)}) %collective-permute-start.11) | collective-permute-done | bytes 114720 | tf_op jit(solution)/shard_map/ppermute | solution.py:53
  44.4 4.8 %collective-permute-done.12 = f32[224,128]{1,0:T(8,128)S(1)} collective-permute-done((f32[224,128]{1,0:T(8,128)S(1)}, f32[224,128]{1,0:T(8,128)S(1)}, u32[]{:S(2)}, u32[]{:S(2)}) %collective-permute-start.12) | collective-permute-done | bytes 114720 | tf_op jit(solution)/shard_map/ppermute | solution.py:53
  49.8 4.3 %collective-permute-done.13 = f32[224,128]{1,0:T(8,128)S(1)} collective-permute-done((f32[224,128]{1,0:T(8,128)S(1)}, f32[224,128]{1,0:T(8,128)S(1)}, u32[]{:S(2)}, u32[]{:S(2)}) %collective-permute-start.13) | collective-permute-done | bytes 114720 | tf_op jit(solution)/shard_map/ppermute | solution.py:53
  54.1 1.7 %collective-permute-start.14 = (f32[224,128]{1,0:T(8,128)S(1)}, f32[224,128]{1,0:T(8,128)S(1)}, u32[]{:S(2)}, u32[]{:S(2)}) collective-permute-start(f32[224,128]{1,0:T(8,128)S(1)} %add.105), channel_id=1, source_target_pairs={{0,16},{1,5},{2,18},{3,7},{4,20},{5,1},{6,22},{7,3},{8,24},{9,13},... | collective-permute-start | bytes 344072 | tf_op jit(solution)/shard_map/ppermute | solution.py:53
  56.1 5.0 %collective-permute-done.14 = f32[224,128]{1,0:T(8,128)S(1)} collective-permute-done((f32[224,128]{1,0:T(8,128)S(1)}, f32[224,128]{1,0:T(8,128)S(1)}, u32[]{:S(2)}, u32[]{:S(2)}) %collective-permute-start.14) | collective-permute-done | bytes 114720 | tf_op jit(solution)/shard_map/ppermute | solution.py:53
  63.4 0.9 %reshape.100 = f32[3,3,3,32,32]{4,3,2,1,0:T(8,128)} reshape(f32[216,128]{1,0:T(8,128)S(1)} %get-tuple-element.36) | data formatting | bytes 221184 | tf_op jit(solution)/shard_map/reshape | solution.py:73
  (108 shorter events, 12.8 us)
Async XLA Ops:
  0.6 20.4 %copy-start = (bf16[3,3,3,32,32]{4,3,2,1,0:T(8,128)(2,1)S(1)}, bf16[3,3,3,32,32]{4,3,2,1,0:T(8,128)(2,1)}, u32[]{:S(2)}) copy-start(bf16[3,3,3,32,32]{4,3,2,1,0:T(8,128)(2,1)} %param.13) | copy-start | bytes 165892
  0.6 4.3 %copy-start.1 = (bf16[32,2,8,128]{3,2,1,0:T(8,128)(2,1)S(1)}, bf16[32,2,8,128]{3,2,1,0:T(8,128)(2,1)}, u32[]{:S(2)}) copy-start(bf16[32,2,8,128]{3,2,1,0:T(8,128)(2,1)} %param.9) | copy-start | bytes 393220
  3.3 2.0 %collective-permute-start = (f32[2,2,128]{2,1,0:T(2,128)S(1)}, f32[2,2,128]{2,1,0:T(2,128)S(1)}, u32[]{:S(2)}, u32[]{:S(2)}) collective-permute-start(f32[2,2,128]{2,1,0:T(2,128)S(1)} %pad_maximum_fusion.14), channel_id=1, source_target_pairs={{0,1},{1,0},{2,3},{3,2},{4,5},{5,4},{6,7},{7,6},{8,9},{9,8},{10,11... | collective-permute-start | bytes 6152 | tf_op jit(solution)/shard_map/ppermute | solution.py:32
  5.0 4.4 %copy-start.6 = (f32[2,128]{1,0:T(2,128)S(1)}, f32[2,128]{1,0:T(2,128)}, u32[]{:S(2)}) copy-start(f32[2,128]{1,0:T(2,128)} %param.16) | copy-start | bytes 3076
  5.1 4.4 %copy-start.7 = (f32[2,128]{1,0:T(2,128)S(1)}, f32[2,128]{1,0:T(2,128)}, u32[]{:S(2)}) copy-start(f32[2,128]{1,0:T(2,128)} %param.17) | copy-start | bytes 3076
  5.1 4.5 %copy-start.3 = (bf16[32,2,8,128]{3,2,1,0:T(8,128)(2,1)S(1)}, bf16[32,2,8,128]{3,2,1,0:T(8,128)(2,1)}, u32[]{:S(2)}) copy-start(bf16[32,2,8,128]{3,2,1,0:T(8,128)(2,1)} %param.11) | copy-start | bytes 393220
  5.1 4.5 %copy-start.5 = (bf16[3,32]{1,0:T(4,128)(2,1)S(1)}, bf16[3,32]{1,0:T(4,128)(2,1)}, u32[]{:S(2)}) copy-start(bf16[3,32]{1,0:T(4,128)(2,1)} %param.14) | copy-start | bytes 580
  5.3 4.1 %collective-permute-start.1 = (f32[2,2,128]{2,1,0:T(2,128)S(1)}, f32[2,2,128]{2,1,0:T(2,128)S(1)}, u32[]{:S(2)}, u32[]{:S(2)}) collective-permute-start(f32[2,2,128]{2,1,0:T(2,128)S(1)} %fusion.87), channel_id=1, source_target_pairs={{0,2},{1,3},{2,0},{3,1},{4,6},{5,7},{6,4},{7,5},{8,10},{9,11},{10,... | collective-permute-start | bytes 6152 | tf_op jit(solution)/shard_map/ppermute | solution.py:32
  9.9 7.4 %collective-permute-start.2 = (bf16[32,1,8,128]{3,0,2,1:T(8,128)(2,1)S(1)}, bf16[32,1,8,128]{3,0,2,1:T(8,128)(2,1)S(1)}, u32[]{:S(2)}, u32[]{:S(2)}) collective-permute-start(bf16[32,1,8,128]{3,0,2,1:T(8,128)(2,1)S(1)} %get-tuple-element.50), channel_id=1, source_target_pairs={{0,4},{4,8},{8,12},{12,16},{16,20},{20,24},{24,28},{28,0},{1,5},{5... | collective-permute-start | bytes 196616 | tf_op jit(solution)/shard_map/ppermute | solution.py:15
  12.0 5.3 %collective-permute-start.3 = (bf16[32,1,8,128]{3,0,2,1:T(8,128)(2,1)S(1)}, bf16[32,1,8,128]{3,0,2,1:T(8,128)(2,1)S(1)}, u32[]{:S(2)}, u32[]{:S(2)}) collective-permute-start(bf16[32,1,8,128]{3,0,2,1:T(8,128)(2,1)S(1)} %get-tuple-element.51), channel_id=1, source_target_pairs={{4,0},{8,4},{12,8},{16,12},{20,16},{24,20},{28,24},{0,28},{5,1},{9... | collective-permute-start | bytes 196616 | tf_op jit(solution)/shard_map/ppermute | solution.py:18
  17.3 3.4 %collective-permute-start.5 = (bf16[32,4,1,128]{3,0,2,1:T(8,128)(2,1)S(1)}, bf16[32,4,1,128]{3,0,2,1:T(8,128)(2,1)S(1)}, u32[]{:S(2)}, u32[]{:S(2)}) collective-permute-start(bf16[32,4,1,128]{3,0,2,1:T(8,128)(2,1)S(1)} %get-tuple-element.34), channel_id=1, source_target_pairs={{0,1},{1,2},{2,3},{3,0},{4,5},{5,6},{6,7},{7,4},{8,9},{9,10},{10,1... | collective-permute-start | bytes 98312 | tf_op jit(solution)/shard_map/ppermute | solution.py:15
  17.4 3.3 %collective-permute-start.4 = (bf16[32,4,1,128]{3,0,2,1:T(8,128)(2,1)S(1)}, bf16[32,4,1,128]{3,0,2,1:T(8,128)(2,1)S(1)}, u32[]{:S(2)}, u32[]{:S(2)}) collective-permute-start(bf16[32,4,1,128]{3,0,2,1:T(8,128)(2,1)S(1)} %get-tuple-element.35), channel_id=1, source_target_pairs={{1,0},{2,1},{3,2},{0,3},{5,4},{6,5},{7,6},{4,7},{9,8},{10,9},{11,1... | collective-permute-start | bytes 98312 | tf_op jit(solution)/shard_map/ppermute | solution.py:18
  21.5 0.9 %copy-start.4 = (bf16[32,2,8,128]{3,2,1,0:T(8,128)(2,1)S(1)}, bf16[32,2,8,128]{3,2,1,0:T(8,128)(2,1)}, u32[]{:S(2)}) copy-start(bf16[32,2,8,128]{3,2,1,0:T(8,128)(2,1)} %param.10) | copy-start | bytes 393220
  22.9 7.1 %collective-permute-start.6 = (bf16[32,1,8,128]{3,0,2,1:T(8,128)(2,1)S(1)}, bf16[32,1,8,128]{3,0,2,1:T(8,128)(2,1)S(1)}, u32[]{:S(2)}, u32[]{:S(2)}) collective-permute-start(bf16[32,1,8,128]{3,0,2,1:T(8,128)(2,1)S(1)} %get-tuple-element.48), channel_id=1, source_target_pairs={{0,4},{4,8},{8,12},{12,16},{16,20},{20,24},{24,28},{28,0},{1,5},{5... | collective-permute-start | bytes 196616 | tf_op jit(solution)/shard_map/ppermute | solution.py:15
  24.3 5.7 %collective-permute-start.7 = (bf16[32,1,8,128]{3,0,2,1:T(8,128)(2,1)S(1)}, bf16[32,1,8,128]{3,0,2,1:T(8,128)(2,1)S(1)}, u32[]{:S(2)}, u32[]{:S(2)}) collective-permute-start(bf16[32,1,8,128]{3,0,2,1:T(8,128)(2,1)S(1)} %get-tuple-element.49), channel_id=1, source_target_pairs={{4,0},{8,4},{12,8},{16,12},{20,16},{24,20},{28,24},{0,28},{5,1},{9... | collective-permute-start | bytes 196616 | tf_op jit(solution)/shard_map/ppermute | solution.py:18
  29.9 3.4 %collective-permute-start.9 = (bf16[32,4,1,128]{3,0,2,1:T(8,128)(2,1)S(1)}, bf16[32,4,1,128]{3,0,2,1:T(8,128)(2,1)S(1)}, u32[]{:S(2)}, u32[]{:S(2)}) collective-permute-start(bf16[32,4,1,128]{3,0,2,1:T(8,128)(2,1)S(1)} %get-tuple-element.30), channel_id=1, source_target_pairs={{0,1},{1,2},{2,3},{3,0},{4,5},{5,6},{6,7},{7,4},{8,9},{9,10},{10,1... | collective-permute-start | bytes 98312 | tf_op jit(solution)/shard_map/ppermute | solution.py:15
  30.8 2.5 %collective-permute-start.8 = (bf16[32,4,1,128]{3,0,2,1:T(8,128)(2,1)S(1)}, bf16[32,4,1,128]{3,0,2,1:T(8,128)(2,1)S(1)}, u32[]{:S(2)}, u32[]{:S(2)}) collective-permute-start(bf16[32,4,1,128]{3,0,2,1:T(8,128)(2,1)S(1)} %get-tuple-element.31), channel_id=1, source_target_pairs={{1,0},{2,1},{3,2},{0,3},{5,4},{6,5},{7,6},{4,7},{9,8},{10,9},{11,1... | collective-permute-start | bytes 98312 | tf_op jit(solution)/shard_map/ppermute | solution.py:18
  35.2 14.1 %copy-start.2 = (bf16[3,3,3,32,32]{4,3,2,1,0:T(8,128)(2,1)S(1)}, bf16[3,3,3,32,32]{4,3,2,1,0:T(8,128)(2,1)}, u32[]{:S(2)}) copy-start(bf16[3,3,3,32,32]{4,3,2,1,0:T(8,128)(2,1)} %param.12) | copy-start | bytes 165892
  36.2 3.3 %collective-permute-start.10 = (f32[224,128]{1,0:T(8,128)S(1)}, f32[224,128]{1,0:T(8,128)S(1)}, u32[]{:S(2)}, u32[]{:S(2)}) collective-permute-start(f32[224,128]{1,0:T(8,128)S(1)} %fusion.61), channel_id=1, source_target_pairs={{0,1},{1,0},{2,3},{3,2},{4,5},{5,4},{6,7},{7,6},{8,9},{9,8},{10,11... | collective-permute-start | bytes 344072 | tf_op jit(solution)/shard_map/ppermute | solution.py:48
  39.5 4.9 %collective-permute-start.11 = (f32[224,128]{1,0:T(8,128)S(1)}, f32[224,128]{1,0:T(8,128)S(1)}, u32[]{:S(2)}, u32[]{:S(2)}) collective-permute-start(f32[224,128]{1,0:T(8,128)S(1)} %select_add_fusion), channel_id=1, source_target_pairs={{0,2},{1,9},{2,0},{3,11},{4,6},{5,13},{6,4},{7,15},{8,10},{9,1},{1... | collective-permute-start | bytes 344072 | tf_op jit(solution)/shard_map/ppermute | solution.py:53
  44.4 4.9 %collective-permute-start.12 = (f32[224,128]{1,0:T(8,128)S(1)}, f32[224,128]{1,0:T(8,128)S(1)}, u32[]{:S(2)}, u32[]{:S(2)}) collective-permute-start(f32[224,128]{1,0:T(8,128)S(1)} %add.103), channel_id=1, source_target_pairs={{0,4},{1,17},{2,6},{3,19},{4,0},{5,21},{6,2},{7,23},{8,12},{9,25},... | collective-permute-start | bytes 344072 | tf_op jit(solution)/shard_map/ppermute | solution.py:53
  49.2 4.9 %collective-permute-start.13 = (f32[224,128]{1,0:T(8,128)S(1)}, f32[224,128]{1,0:T(8,128)S(1)}, u32[]{:S(2)}, u32[]{:S(2)}) collective-permute-start(f32[224,128]{1,0:T(8,128)S(1)} %add.104), channel_id=1, source_target_pairs={{0,8},{1,3},{2,10},{3,1},{4,12},{5,7},{6,14},{7,5},{8,0},{9,11},{1... | collective-permute-start | bytes 344072 | tf_op jit(solution)/shard_map/ppermute | solution.py:53
  54.1 7.0 %collective-permute-start.14 = (f32[224,128]{1,0:T(8,128)S(1)}, f32[224,128]{1,0:T(8,128)S(1)}, u32[]{:S(2)}, u32[]{:S(2)}) collective-permute-start(f32[224,128]{1,0:T(8,128)S(1)} %add.105), channel_id=1, source_target_pairs={{0,16},{1,5},{2,18},{3,7},{4,20},{5,1},{6,22},{7,3},{8,24},{9,13},... | collective-permute-start | bytes 344072 | tf_op jit(solution)/shard_map/ppermute | solution.py:53
  61.1 1.4 %collective-permute-start.15 = (f32[224,128]{1,0:T(8,128)S(1)}, f32[224,128]{1,0:T(8,128)S(1)}, u32[]{:S(2)}, u32[]{:S(2)}) collective-permute-start(f32[224,128]{1,0:T(8,128)S(1)} %add.106), channel_id=1, source_target_pairs={{0,1},{1,0},{2,3},{3,2},{4,5},{5,4},{6,7},{7,6},{8,9},{9,8},{10,11... | collective-permute-start | bytes 344072 | tf_op jit(solution)/shard_map/ppermute | solution.py:54

commit v10 on v9

--- a/solution.py
+++ b/solution.py
@@ -156,10 +156,12 @@
     grad_bias = jnp.sum(head_grad.astype(jnp.float32), axis=(1, 2, 3)) * norm_factor
     back_second = jnp.einsum("oi,oxzy->ixzy", w_out, head_grad, preferred_element_type=jnp.float32)
     grad_second_pre = (back_second * silu_slope(second_wide)).astype(jnp.bfloat16)
-    second_padded = extended(grad_second_pre, (("sky", 1), ("los", 2)), 1)
-    back_first = spread_local(w_second, second_padded, shape)
-    grad_first_pre = (back_first * silu_slope(first_wide)).astype(jnp.bfloat16)
-    first_padded = extended(grad_first_pre, (("sky", 1), ("los", 2)), 1)
+    both_wide = extended(jnp.stack((grad_second_pre, pre_first)), (("sky", 2), ("los", 3)), 2)
+    second_padded = both_wide[0, :, 1:-1, 1:-1]
+    first_around = both_wide[1, :, 1:-1, 1:-1].astype(jnp.float32)
+    around_shape = first_around.shape
+    back_first = spread_local(w_second, both_wide[0], around_shape)
+    first_padded = (back_first * silu_slope(first_around)).astype(jnp.bfloat16)
     grad_features = spread_local(w_first, first_padded, shape).astype(jnp.bfloat16)
     hidden_first = jax.nn.silu(first_wide).astype(jnp.bfloat16)
     grad_second = taps_from_halo(second_padded, hidden_first)

time: 66 us -> 67.7 us (1.026)
  waiting for transfers between devices: 26.8 us -> 36.2 us
  starting transfers between devices: 21.3 us -> 12.5 us
    ppermute x4 -> x2, waiting for transfers between devices: 0.01 us -> 8.45 us  [extended(): lax.ppermute(lax.slice_in_dim(block, 0, width, axis=dim), axis, backward)]
    ppermute x4 -> x2, starting transfers between devices: 9.24 us -> 5.19 us  [extended(): lax.ppermute(lax.slice_in_dim(block, 0, width, axis=dim), axis, backward)]
    ppermute x4 -> x2, starting transfers between devices: 4.39 us -> 0.5 us  [extended(): lax.ppermute(lax.slice_in_dim(block, block.shape[dim] - width, None, axis...]
    ppermute x4 -> x2, waiting for transfers between devices: 5.62 us -> 7.81 us  [extended(): lax.ppermute(lax.slice_in_dim(block, block.shape[dim] - width, None, axis...]
    ppermute x1, starting transfers between devices: 2.29 us -> 0.16 us  [split_sum(): keep = keep + lax.ppermute(send, index_axes, partner)]
    ppermute x4, waiting for transfers between devices: 18.5 us -> 16.9 us  [split_sum(): keep = keep + lax.ppermute(keep, index_axes, pairs)]
    ppermute x4, starting transfers between devices: 2.24 us -> 3.48 us  [split_sum(): keep = keep + lax.ppermute(keep, index_axes, pairs)]
    unnamed x34 -> x47, local copies, waits for them, and re-layouts: 1.74 us -> 1.63 us
  transfers between devices with their start and end apart: 16 -> 12, of which waited for: 10 -> 11; matrix products, arithmetic and copies ran while one was open for 8% -> 6% of each run, Pallas kernels for 0% -> 0%
where the time goes in v10:
time: 67.7 us; the launch traced here: 67.6 us
  waiting for transfers between devices  36.2 us (53%)
  starting transfers between devices  12.5 us (18%)
  local copies, waits for them, and re-layouts  9.31 us (14%)
  matrix products  4.66 us (7%)
  other arithmetic  3.61 us (5%)
  between operations  1.29 us (2%)
    ppermute x4, waiting for transfers between devices, split_sum(): keep = keep + lax.ppermute(keep, index_axes, pairs)  16.9 us
    ppermute x2, waiting for transfers between devices, extended(): lax.ppermute(lax.slice_in_dim(block, 0, width, axis=dim), axis, backward)  8.45 us
    ppermute x2, waiting for transfers between devices, extended(): lax.ppermute(lax.slice_in_dim(block, block.shape[dim] - width, None, axis...  7.81 us
    ppermute x2, starting transfers between devices, extended(): lax.ppermute(lax.slice_in_dim(block, 0, width, axis=dim), axis, backward)  5.19 us
    ppermute x4, starting transfers between devices, split_sum(): keep = keep + lax.ppermute(keep, index_axes, pairs)  3.48 us
    ppermute x2, starting transfers between devices, butterfly_sum(): value = value + lax.ppermute(value, axis, pairs)  3.09 us
    dot_general x2, matrix products, taps_from_halo(): jnp.einsum('toxzy,sixzy->tsoi', windows, rolled, preferred_element_type=j...  2.13 us
    reshape x2, local copies, waits for them, and re-layouts, unpack_rows(): parts.append(flat[start:start + size].reshape(shape))  1.85 us
  transfers between devices with their start and end apart: 12, of which 11 were waited for; matrix products, arithmetic and copies ran while one was open for 6% of the time, Pallas kernels for 0%

profile of v10, /device:TPU:0, one launch (start us, length us, event | category | flops | bytes accessed | tf_op | source)
XLA Modules:
  0.0 67.6 jit_solution(15916337650824823267)
XLA Ops:
  0.7 1.0 %fusion.49 = bf16[32,2,8,128]{3,0,2,1:T(8,128)(2,1)S(1)} fusion(bf16[32,2,8,128]{3,2,1,0:T(8,128)(2,1)} %param.11), kind=kLoop, calls=%fused_computation.77 | loop fusion | flops 393216 | bytes 262144 | tf_op jit(solution)/shard_map/convert_element_type | solution.py:130
  1.7 0.8 %fusion.97 = f32[2,8,128,3]{2,3,1,0:T(4,128)S(1)} fusion(bf16[32,2,8,128]{3,0,2,1:T(8,128)(2,1)S(1)} %fusion.49, bf16[3,32]{1,0:T(4,128)(2,1)} %param.14), kind=kOutput, calls=%fused_computation.175 | convolution fusion | flops 393216 | bytes 155840 | tf_op jit(solution)/shard_map/oi,ixzy->oxzy/dot_general | solution.py:131
  2.5 0.7 %fusion.77 = f32[3,2,8,128]{3,2,1,0:T(8,128)S(1)} fusion(f32[2,8,128,3]{2,3,1,0:T(4,128)S(1)} %fusion.97, f32[3]{0:T(128)} %param.15), kind=kLoop, calls=%fused_computation.141 | loop fusion | flops 6144 | bytes 49164 | tf_op jit(solution)/shard_map/add | solution.py:134
  3.8 1.1 %fusion.107 = (bf16[32,2,8,127]{3,2,1,0:T(8,128)(2,1)S(1)}, bf16[32,2,8,127]{3,2,1,0:T(8,128)(2,1)S(1)}) fusion(bf16[32,2,8,128]{3,2,1,0:T(8,128)(2,1)} %param.9), kind=kLoop, calls=%fused_computation.189 | loop fusion | bytes 520192 | tf_op jit(solution)/shard_map/jit(_roll_static)/slice | solution.py:113
  5.7 2.6 %collective-permute-start.1 = (f32[2,2,128]{2,1,0:T(2,128)S(1)}, f32[2,2,128]{2,1,0:T(2,128)S(1)}, u32[]{:S(2)}, u32[]{:S(2)}) collective-permute-start(f32[2,2,128]{2,1,0:T(2,128)S(1)} %fusion.102), channel_id=1, source_target_pairs={{0,2},{1,3},{2,0},{3,1},{4,6},{5,7},{6,4},{7,5},{8,10},{9,11},{10,... | collective-permute-start | bytes 6152 | tf_op jit(solution)/shard_map/ppermute | solution.py:32
  8.5 1.4 %collective-permute-done.1 = f32[2,2,128]{2,1,0:T(2,128)S(1)} collective-permute-done((f32[2,2,128]{2,1,0:T(2,128)S(1)}, f32[2,2,128]{2,1,0:T(2,128)S(1)}, u32[]{:S(2)}, u32[]{:S(2)}) %collective-permute-start.1) | collective-permute-done | bytes 2080 | tf_op jit(solution)/shard_map/ppermute | solution.py:32
  10.3 5.1 %collective-permute-start.3 = (bf16[2,32,2,8,128]{4,1,3,2,0:T(8,128)(2,1)S(1)}, bf16[2,32,2,8,128]{4,1,3,2,0:T(8,128)(2,1)S(1)}, u32[]{:S(2)}, u32[]{:S(2)}) collective-permute-start(bf16[2,32,2,8,128]{4,1,3,2,0:T(8,128)(2,1)S(1)} %pad_maximum_fusion.1), channel_id=1, source_target_pairs={{4,0},{8,4},{12,8},{16,12},{20,16},{24,20},{28,24},{0,28},{5,1},{9... | collective-permute-start | bytes 786440 | tf_op jit(solution)/shard_map/ppermute | solution.py:18
  15.9 4.6 %collective-permute-done.3 = bf16[2,32,2,8,128]{4,1,3,2,0:T(8,128)(2,1)S(1)} collective-permute-done((bf16[2,32,2,8,128]{4,1,3,2,0:T(8,128)(2,1)S(1)}, bf16[2,32,2,8,128]{4,1,3,2,0:T(8,128)(2,1)S(1)}, u32[]{:S(2)}, u32[]{:S(2)}) %collective-permute-start.3) | collective-permute-done | bytes 262176 | tf_op jit(solution)/shard_map/ppermute | solution.py:18
  20.5 4.9 %collective-permute-done.2 = bf16[2,32,2,8,128]{4,1,3,2,0:T(8,128)(2,1)S(1)} collective-permute-done((bf16[2,32,2,8,128]{4,1,3,2,0:T(8,128)(2,1)S(1)}, bf16[2,32,2,8,128]{4,1,3,2,0:T(8,128)(2,1)S(1)}, u32[]{:S(2)}, u32[]{:S(2)}) %collective-permute-start.2) | collective-permute-done | bytes 262176 | tf_op jit(solution)/shard_map/ppermute | solution.py:15
  26.0 3.8 %collective-permute-done.5 = bf16[2,32,6,2,128]{4,1,3,2,0:T(8,128)(2,1)S(1)} collective-permute-done((bf16[2,32,6,2,128]{4,1,3,2,0:T(8,128)(2,1)S(1)}, bf16[2,32,6,2,128]{4,1,3,2,0:T(8,128)(2,1)S(1)}, u32[]{:S(2)}, u32[]{:S(2)}) %collective-permute-start.5) | collective-permute-done | bytes 196640 | tf_op jit(solution)/shard_map/ppermute | solution.py:18
  29.8 2.9 %collective-permute-done.4 = bf16[2,32,6,2,128]{4,1,3,2,0:T(8,128)(2,1)S(1)} collective-permute-done((bf16[2,32,6,2,128]{4,1,3,2,0:T(8,128)(2,1)S(1)}, bf16[2,32,6,2,128]{4,1,3,2,0:T(8,128)(2,1)S(1)}, u32[]{:S(2)}, u32[]{:S(2)}) %collective-permute-start.4) | collective-permute-done | bytes 196640 | tf_op jit(solution)/shard_map/ppermute | solution.py:15
  33.1 1.1 %fusion.7 = f32[9,3,32,32]{2,3,0,1:T(8,128)S(1)} fusion(bf16[9,32,2,8,128]{4,1,3,2,0:T(8,128)(2,1)S(1)} %fusion.57, bf16[1,32,2,8,128]{4,1,3,2,0:T(8,128)(2,1)S(1)} %get-tuple-element.50, bf16[1,32,2,8,128]{4,1,3,2,0:T(8,128)(2,1)S(1)} %fusion.110, bf16[1,32,2,8,128]{4,1,3,2,0:T(8,128)(2,1)S(1)} %get-tuple-element.49), kind=kOutput, calls=%fused_computation.7 | convolution fusion | flops 114453504 | bytes 1683456 | tf_op jit(solution)/shard_map/toxzy,sixzy->tsoi/dot_general | solution.py:114
  35.3 0.9 %fusion.3 = f32[3,32,4,10,128]{4,1,3,2,0:T(8,128)S(1)} fusion(bf16[9,32,4,10,128]{4,1,3,2,0:T(8,128)(2,1)S(1)} %fusion.33, bf16[9,3,32,32,1,1]{3,2,1,0,5,4:T(8,128)(2,1)S(1)} %bitcast.315), kind=kOutput, calls=%fused_computation.3 | convolution fusion | flops 283115520 | bytes 4970496 | tf_op jit(solution)/shard_map/toxzy,tsoi->sixzy/dot_general | solution.py:95
  37.6 1.1 %fusion.9 = f32[9,3,32,32]{2,3,0,1:T(8,128)S(1)} fusion(bf16[1,32,2,8,128]{4,1,3,2,0:T(8,128)(2,1)S(1)} %get-tuple-element.48, bf16[1,32,2,8,128]{4,1,3,2,0:T(8,128)(2,1)S(1)} %bitcast.327, bf16[1,32,2,8,128]{4,1,3,2,0:T(8,128)(2,1)S(1)} %get-tuple-element.47, bf16[9,32,2,8,128]{4,1,3,2,0:T(8,128)(2,1)S(1)} %fusion.66), kind=kOutput, calls=%fused_computation.10 | convolution fusion | flops 114453504 | bytes 1683456 | tf_op jit(solution)/shard_map/toxzy,sixzy->tsoi/dot_general | solution.py:114
  39.2 1.0 %concatenate.59 = f32[55395]{0:T(1024)S(1)} concatenate(f32[27648]{0:T(1024)S(1)} %mul.112, f32[27648]{0:T(1024)S(1)} %mul.116, f32[96]{0:T(128)S(1)} %reshape.100, f32[3]{0:T(128)S(1)} %broadcast_multiply_fusion), dimensions={0} | concatenate | bytes 443160 | tf_op jit(solution)/shard_map/concatenate | solution.py:61
  40.3 1.2 %collective-permute-done.6 = f32[224,128]{1,0:T(8,128)S(1)} collective-permute-done((f32[224,128]{1,0:T(8,128)S(1)}, f32[224,128]{1,0:T(8,128)S(1)}, u32[]{:S(2)}, u32[]{:S(2)}) %collective-permute-start.6) | collective-permute-done | bytes 114720 | tf_op jit(solution)/shard_map/ppermute | solution.py:48
  42.2 4.3 %collective-permute-done.7 = f32[224,128]{1,0:T(8,128)S(1)} collective-permute-done((f32[224,128]{1,0:T(8,128)S(1)}, f32[224,128]{1,0:T(8,128)S(1)}, u32[]{:S(2)}, u32[]{:S(2)}) %collective-permute-start.7) | collective-permute-done | bytes 114720 | tf_op jit(solution)/shard_map/ppermute | solution.py:53
  46.5 1.3 %collective-permute-start.8 = (f32[224,128]{1,0:T(8,128)S(1)}, f32[224,128]{1,0:T(8,128)S(1)}, u32[]{:S(2)}, u32[]{:S(2)}) collective-permute-start(f32[224,128]{1,0:T(8,128)S(1)} %add.106), channel_id=1, source_target_pairs={{0,4},{1,17},{2,6},{3,19},{4,0},{5,21},{6,2},{7,23},{8,12},{9,25},... | collective-permute-start | bytes 344072 | tf_op jit(solution)/shard_map/ppermute | solution.py:53
  47.7 3.6 %collective-permute-done.8 = f32[224,128]{1,0:T(8,128)S(1)} collective-permute-done((f32[224,128]{1,0:T(8,128)S(1)}, f32[224,128]{1,0:T(8,128)S(1)}, u32[]{:S(2)}, u32[]{:S(2)}) %collective-permute-start.8) | collective-permute-done | bytes 114720 | tf_op jit(solution)/shard_map/ppermute | solution.py:53
  52.1 4.1 %collective-permute-done.9 = f32[224,128]{1,0:T(8,128)S(1)} collective-permute-done((f32[224,128]{1,0:T(8,128)S(1)}, f32[224,128]{1,0:T(8,128)S(1)}, u32[]{:S(2)}, u32[]{:S(2)}) %collective-permute-start.9) | collective-permute-done | bytes 114720 | tf_op jit(solution)/shard_map/ppermute | solution.py:53
  56.2 1.3 %collective-permute-start.10 = (f32[224,128]{1,0:T(8,128)S(1)}, f32[224,128]{1,0:T(8,128)S(1)}, u32[]{:S(2)}, u32[]{:S(2)}) collective-permute-start(f32[224,128]{1,0:T(8,128)S(1)} %add.108), channel_id=1, source_target_pairs={{0,16},{1,5},{2,18},{3,7},{4,20},{5,1},{6,22},{7,3},{8,24},{9,13},... | collective-permute-start | bytes 344072 | tf_op jit(solution)/shard_map/ppermute | solution.py:53
  57.8 5.0 %collective-permute-done.10 = f32[224,128]{1,0:T(8,128)S(1)} collective-permute-done((f32[224,128]{1,0:T(8,128)S(1)}, f32[224,128]{1,0:T(8,128)S(1)}, u32[]{:S(2)}, u32[]{:S(2)}) %collective-permute-start.10) | collective-permute-done | bytes 114720 | tf_op jit(solution)/shard_map/ppermute | solution.py:53
  64.5 0.9 %reshape.101 = f32[3,3,3,32,32]{4,3,2,1,0:T(8,128)} reshape(f32[216,128]{1,0:T(8,128)S(1)} %get-tuple-element.31) | data formatting | bytes 221184 | tf_op jit(solution)/shard_map/reshape | solution.py:73
  65.5 0.9 %reshape.102 = f32[3,3,3,32,32]{4,3,2,1,0:T(8,128)} reshape(f32[216,128]{1,0:T(8,128)S(1)} %get-tuple-element.30) | data formatting | bytes 221184 | tf_op jit(solution)/shard_map/reshape | solution.py:73
  (110 shorter events, 10.7 us)
Async XLA Ops:
  0.6 34.7 %copy-start = (bf16[3,3,3,32,32]{4,3,2,1,0:T(8,128)(2,1)S(1)}, bf16[3,3,3,32,32]{4,3,2,1,0:T(8,128)(2,1)}, u32[]{:S(2)}) copy-start(bf16[3,3,3,32,32]{4,3,2,1,0:T(8,128)(2,1)} %param.13) | copy-start | bytes 165892
  0.6 4.3 %copy-start.1 = (bf16[32,2,8,128]{3,2,1,0:T(8,128)(2,1)S(1)}, bf16[32,2,8,128]{3,2,1,0:T(8,128)(2,1)}, u32[]{:S(2)}) copy-start(bf16[32,2,8,128]{3,2,1,0:T(8,128)(2,1)} %param.9) | copy-start | bytes 393220
  0.7 4.4 %copy-start.2 = (bf16[32,2,8,128]{3,2,1,0:T(8,128)(2,1)S(1)}, bf16[32,2,8,128]{3,2,1,0:T(8,128)(2,1)}, u32[]{:S(2)}) copy-start(bf16[32,2,8,128]{3,2,1,0:T(8,128)(2,1)} %param.10) | copy-start | bytes 393220
  3.3 2.4 %collective-permute-start = (f32[2,2,128]{2,1,0:T(2,128)S(1)}, f32[2,2,128]{2,1,0:T(2,128)S(1)}, u32[]{:S(2)}, u32[]{:S(2)}) collective-permute-start(f32[2,2,128]{2,1,0:T(2,128)S(1)} %pad_maximum_fusion.8), channel_id=1, source_target_pairs={{0,1},{1,0},{2,3},{3,2},{4,5},{5,4},{6,7},{7,6},{8,9},{9,8},{10,11... | collective-permute-start | bytes 6152 | tf_op jit(solution)/shard_map/ppermute | solution.py:32
  5.4 4.5 %copy-start.6 = (f32[2,128]{1,0:T(2,128)S(1)}, f32[2,128]{1,0:T(2,128)}, u32[]{:S(2)}) copy-start(f32[2,128]{1,0:T(2,128)} %param.16) | copy-start | bytes 3076
  5.4 4.5 %copy-start.7 = (f32[2,128]{1,0:T(2,128)S(1)}, f32[2,128]{1,0:T(2,128)}, u32[]{:S(2)}) copy-start(f32[2,128]{1,0:T(2,128)} %param.17) | copy-start | bytes 3076
  5.4 4.6 %copy-start.4 = (bf16[32,2,8,128]{3,2,1,0:T(8,128)(2,1)S(1)}, bf16[32,2,8,128]{3,2,1,0:T(8,128)(2,1)}, u32[]{:S(2)}) copy-start(bf16[32,2,8,128]{3,2,1,0:T(8,128)(2,1)} %param.11) | copy-start | bytes 393220
  5.4 4.6 %copy-start.5 = (bf16[3,32]{1,0:T(4,128)(2,1)S(1)}, bf16[3,32]{1,0:T(4,128)(2,1)}, u32[]{:S(2)}) copy-start(bf16[3,32]{1,0:T(4,128)(2,1)} %param.14) | copy-start | bytes 580
  5.7 4.1 %collective-permute-start.1 = (f32[2,2,128]{2,1,0:T(2,128)S(1)}, f32[2,2,128]{2,1,0:T(2,128)S(1)}, u32[]{:S(2)}, u32[]{:S(2)}) collective-permute-start(f32[2,2,128]{2,1,0:T(2,128)S(1)} %fusion.102), channel_id=1, source_target_pairs={{0,2},{1,3},{2,0},{3,1},{4,6},{5,7},{6,4},{7,5},{8,10},{9,11},{10,... | collective-permute-start | bytes 6152 | tf_op jit(solution)/shard_map/ppermute | solution.py:32
  10.3 10.2 %collective-permute-start.3 = (bf16[2,32,2,8,128]{4,1,3,2,0:T(8,128)(2,1)S(1)}, bf16[2,32,2,8,128]{4,1,3,2,0:T(8,128)(2,1)S(1)}, u32[]{:S(2)}, u32[]{:S(2)}) collective-permute-start(bf16[2,32,2,8,128]{4,1,3,2,0:T(8,128)(2,1)S(1)} %pad_maximum_fusion.1), channel_id=1, source_target_pairs={{4,0},{8,4},{12,8},{16,12},{20,16},{24,20},{28,24},{0,28},{5,1},{9... | collective-permute-start | bytes 786440 | tf_op jit(solution)/shard_map/ppermute | solution.py:18
  15.4 10.0 %collective-permute-start.2 = (bf16[2,32,2,8,128]{4,1,3,2,0:T(8,128)(2,1)S(1)}, bf16[2,32,2,8,128]{4,1,3,2,0:T(8,128)(2,1)S(1)}, u32[]{:S(2)}, u32[]{:S(2)}) collective-permute-start(bf16[2,32,2,8,128]{4,1,3,2,0:T(8,128)(2,1)S(1)} %pad_maximum_fusion.1), channel_id=1, source_target_pairs={{0,4},{4,8},{8,12},{12,16},{16,20},{20,24},{24,28},{28,0},{1,5},{5... | collective-permute-start | bytes 786440 | tf_op jit(solution)/shard_map/ppermute | solution.py:15
  25.5 4.4 %collective-permute-start.5 = (bf16[2,32,6,2,128]{4,1,3,2,0:T(8,128)(2,1)S(1)}, bf16[2,32,6,2,128]{4,1,3,2,0:T(8,128)(2,1)S(1)}, u32[]{:S(2)}, u32[]{:S(2)}) collective-permute-start(bf16[2,32,6,2,128]{4,1,3,2,0:T(8,128)(2,1)S(1)} %get-tuple-element.29), channel_id=1, source_target_pairs={{1,0},{2,1},{3,2},{0,3},{5,4},{6,5},{7,6},{4,7},{9,8},{10,9},{11,1... | collective-permute-start | bytes 589832 | tf_op jit(solution)/shard_map/ppermute | solution.py:18
  25.5 7.2 %collective-permute-start.4 = (bf16[2,32,6,2,128]{4,1,3,2,0:T(8,128)(2,1)S(1)}, bf16[2,32,6,2,128]{4,1,3,2,0:T(8,128)(2,1)S(1)}, u32[]{:S(2)}, u32[]{:S(2)}) collective-permute-start(bf16[2,32,6,2,128]{4,1,3,2,0:T(8,128)(2,1)S(1)} %get-tuple-element.28), channel_id=1, source_target_pairs={{0,1},{1,2},{2,3},{3,0},{4,5},{5,6},{6,7},{7,4},{8,9},{9,10},{10,1... | collective-permute-start | bytes 589832 | tf_op jit(solution)/shard_map/ppermute | solution.py:15
  39.2 12.5 %copy-start.3 = (bf16[3,3,3,32,32]{4,3,2,1,0:T(8,128)(2,1)S(1)}, bf16[3,3,3,32,32]{4,3,2,1,0:T(8,128)(2,1)}, u32[]{:S(2)}) copy-start(bf16[3,3,3,32,32]{4,3,2,1,0:T(8,128)(2,1)} %param.12) | copy-start | bytes 165892
  40.2 1.4 %collective-permute-start.6 = (f32[224,128]{1,0:T(8,128)S(1)}, f32[224,128]{1,0:T(8,128)S(1)}, u32[]{:S(2)}, u32[]{:S(2)}) collective-permute-start(f32[224,128]{1,0:T(8,128)S(1)} %fusion.76), channel_id=1, source_target_pairs={{0,1},{1,0},{2,3},{3,2},{4,5},{5,4},{6,7},{7,6},{8,9},{9,8},{10,11... | collective-permute-start | bytes 344072 | tf_op jit(solution)/shard_map/ppermute | solution.py:48
  41.6 4.9 %collective-permute-start.7 = (f32[224,128]{1,0:T(8,128)S(1)}, f32[224,128]{1,0:T(8,128)S(1)}, u32[]{:S(2)}, u32[]{:S(2)}) collective-permute-start(f32[224,128]{1,0:T(8,128)S(1)} %select_add_fusion), channel_id=1, source_target_pairs={{0,2},{1,9},{2,0},{3,11},{4,6},{5,13},{6,4},{7,15},{8,10},{9,1},{1... | collective-permute-start | bytes 344072 | tf_op jit(solution)/shard_map/ppermute | solution.py:53
  46.5 4.9 %collective-permute-start.8 = (f32[224,128]{1,0:T(8,128)S(1)}, f32[224,128]{1,0:T(8,128)S(1)}, u32[]{:S(2)}, u32[]{:S(2)}) collective-permute-start(f32[224,128]{1,0:T(8,128)S(1)} %add.106), channel_id=1, source_target_pairs={{0,4},{1,17},{2,6},{3,19},{4,0},{5,21},{6,2},{7,23},{8,12},{9,25},... | collective-permute-start | bytes 344072 | tf_op jit(solution)/shard_map/ppermute | solution.py:53
  51.3 4.9 %collective-permute-start.9 = (f32[224,128]{1,0:T(8,128)S(1)}, f32[224,128]{1,0:T(8,128)S(1)}, u32[]{:S(2)}, u32[]{:S(2)}) collective-permute-start(f32[224,128]{1,0:T(8,128)S(1)} %add.107), channel_id=1, source_target_pairs={{0,8},{1,3},{2,10},{3,1},{4,12},{5,7},{6,14},{7,5},{8,0},{9,11},{1... | collective-permute-start | bytes 344072 | tf_op jit(solution)/shard_map/ppermute | solution.py:53
  56.2 6.6 %collective-permute-start.10 = (f32[224,128]{1,0:T(8,128)S(1)}, f32[224,128]{1,0:T(8,128)S(1)}, u32[]{:S(2)}, u32[]{:S(2)}) collective-permute-start(f32[224,128]{1,0:T(8,128)S(1)} %add.108), channel_id=1, source_target_pairs={{0,16},{1,5},{2,18},{3,7},{4,20},{5,1},{6,22},{7,3},{8,24},{9,13},... | collective-permute-start | bytes 344072 | tf_op jit(solution)/shard_map/ppermute | solution.py:53
  62.9 1.4 %collective-permute-start.11 = (f32[224,128]{1,0:T(8,128)S(1)}, f32[224,128]{1,0:T(8,128)S(1)}, u32[]{:S(2)}, u32[]{:S(2)}) collective-permute-start(f32[224,128]{1,0:T(8,128)S(1)} %add.109), channel_id=1, source_target_pairs={{0,1},{1,0},{2,3},{3,2},{4,5},{5,4},{6,7},{7,6},{8,9},{9,8},{10,11... | collective-permute-start | bytes 344072 | tf_op jit(solution)/shard_map/ppermute | solution.py:54

commit v11 on v9

--- a/solution.py
+++ b/solution.py
@@ -31,6 +31,24 @@
             pairs = [(i, i ^ step) for i in range(count)]
             value = value + lax.ppermute(value, axis, pairs)
             step *= 2
+    return value
+
+
+def quad_sum(value, axis):
+    count = lax.axis_size(axis)
+    if count & (count - 1):
+        return lax.psum(value, axis)
+    step = 1
+    while step < count:
+        if step * 2 >= count:
+            value = value + lax.ppermute(value, axis, [(i, i ^ step) for i in range(count)])
+            break
+        near, far, both = (
+            lax.ppermute(value, axis, [(i, i ^ mask) for i in range(count)])
+            for mask in (step, step * 2, step * 3)
+        )
+        value = (value + near) + (far + both)
+        step *= 4
     return value
 
 
@@ -137,7 +155,7 @@
     velocity = heads_raw[2]
     y_part = jnp.sum(pressure, axis=1) / depth_all
     k_part = -jnp.sum(density * velocity, axis=1) / depth_all
-    y_map, k_map = butterfly_sum(jnp.stack((y_part, k_part)), ("los",))
+    y_map, k_map = quad_sum(jnp.stack((y_part, k_part)), "los")
     y_resid = y_map - y_target
     k_resid = k_map - k_target
     y_resid = y_resid[:, None, :]

time: 66 us -> 65.2 us (0.988)
    ppermute x4, starting transfers between devices: 4.39 us -> 2.94 us  [extended(): lax.ppermute(lax.slice_in_dim(block, block.shape[dim] - width, None, axis...]
    ppermute x4, starting transfers between devices: 9.24 us -> 10.2 us  [extended(): lax.ppermute(lax.slice_in_dim(block, 0, width, axis=dim), axis, backward)]
    ppermute x1, starting transfers between devices: 2.29 us -> 1.45 us  [split_sum(): keep = keep + lax.ppermute(send, index_axes, partner)]
    ppermute x4, starting transfers between devices: 2.24 us -> 3.04 us  [split_sum(): keep = keep + lax.ppermute(keep, index_axes, pairs)]
    ppermute x4, waiting for transfers between devices: 18.5 us -> 17.7 us  [split_sum(): keep = keep + lax.ppermute(keep, index_axes, pairs)]
    ppermute x2 -> x3, waiting for transfers between devices: 1.35 us -> 1.16 us  [quad_sum(): lax.ppermute(value, axis, [(i, i ^ mask) for i in range(count)])]
    ppermute x2 -> x3, starting transfers between devices: 3.09 us -> 3.2 us  [quad_sum(): lax.ppermute(value, axis, [(i, i ^ mask) for i in range(count)])]
  transfers between devices with their start and end apart: 16 -> 17, of which waited for: 10 -> 10; matrix products, arithmetic and copies ran while one was open for 8% -> 8% of each run, Pallas kernels for 0% -> 0%
where the time goes in v11:
time: 65.2 us; the launch traced here: 65 us
  waiting for transfers between devices  26.5 us (41%)
  starting transfers between devices  20.9 us (32%)
  local copies, waits for them, and re-layouts  9.07 us (14%)
  matrix products  4.25 us (7%)
  other arithmetic  3.1 us (5%)
  between operations  1.23 us (2%)
    ppermute x4, waiting for transfers between devices, split_sum(): keep = keep + lax.ppermute(keep, index_axes, pairs)  17.7 us
    ppermute x4, starting transfers between devices, extended(): lax.ppermute(lax.slice_in_dim(block, 0, width, axis=dim), axis, backward)  10.2 us
    ppermute x4, waiting for transfers between devices, extended(): lax.ppermute(lax.slice_in_dim(block, block.shape[dim] - width, None, axis...  6.18 us
    ppermute x3, starting transfers between devices, quad_sum(): lax.ppermute(value, axis, [(i, i ^ mask) for i in range(count)])  3.2 us
    ppermute x4, starting transfers between devices, split_sum(): keep = keep + lax.ppermute(keep, index_axes, pairs)  3.04 us
    ppermute x4, starting transfers between devices, extended(): lax.ppermute(lax.slice_in_dim(block, block.shape[dim] - width, None, axis...  2.94 us
    dot_general x2, matrix products, taps_from_halo(): jnp.einsum('toxzy,sixzy->tsoi', windows, rolled, preferred_element_type=j...  2.13 us
    reshape x2, local copies, waits for them, and re-layouts, unpack_rows(): parts.append(flat[start:start + size].reshape(shape))  1.84 us
  transfers between devices with their start and end apart: 17, of which 10 were waited for; matrix products, arithmetic and copies ran while one was open for 8% of the time, Pallas kernels for 0%

profile of v11, /device:TPU:0, one launch (start us, length us, event | category | flops | bytes accessed | tf_op | source)
XLA Modules:
  0.0 65.0 jit_solution(12836119551926749901)
XLA Ops:
  0.7 1.0 %fusion.22 = bf16[32,2,8,128]{3,0,2,1:T(8,128)(2,1)S(1)} fusion(bf16[32,2,8,128]{3,2,1,0:T(8,128)(2,1)} %param.11), kind=kLoop, calls=%fused_computation.40 | loop fusion | flops 393216 | bytes 262144 | tf_op jit(solution)/shard_map/convert_element_type | solution.py:148
  3.3 3.0 %collective-permute-start.1 = (f32[2,2,128]{2,1,0:T(2,128)S(1)}, f32[2,2,128]{2,1,0:T(2,128)S(1)}, u32[]{:S(2)}, u32[]{:S(2)}) collective-permute-start(f32[2,2,128]{2,1,0:T(2,128)S(1)} %pad_maximum_fusion.14), channel_id=1, source_target_pairs={{0,2},{1,3},{2,0},{3,1},{4,6},{5,7},{6,4},{7,5},{8,10},{9,11},{10,... | collective-permute-start | bytes 6152 | tf_op jit(solution)/shard_map/ppermute | solution.py:47
  6.5 1.1 %fusion.91 = (bf16[32,2,8,127]{3,2,1,0:T(8,128)(2,1)S(1)}, bf16[32,2,8,127]{3,2,1,0:T(8,128)(2,1)S(1)}) fusion(bf16[32,2,8,128]{3,2,1,0:T(8,128)(2,1)} %param.9), kind=kLoop, calls=%fused_computation.167 | loop fusion | bytes 520192 | tf_op jit(solution)/shard_map/jit(_roll_static)/slice | solution.py:131
  8.2 1.2 %collective-permute-done.2 = f32[2,2,128]{2,1,0:T(2,128)S(1)} collective-permute-done((f32[2,2,128]{2,1,0:T(2,128)S(1)}, f32[2,2,128]{2,1,0:T(2,128)S(1)}, u32[]{:S(2)}, u32[]{:S(2)}) %collective-permute-start.2) | collective-permute-done | bytes 2080 | tf_op jit(solution)/shard_map/ppermute | solution.py:47
  9.8 1.6 %collective-permute-start.3 = (bf16[32,1,8,128]{3,0,2,1:T(8,128)(2,1)S(1)}, bf16[32,1,8,128]{3,0,2,1:T(8,128)(2,1)S(1)}, u32[]{:S(2)}, u32[]{:S(2)}) collective-permute-start(bf16[32,1,8,128]{3,0,2,1:T(8,128)(2,1)S(1)} %get-tuple-element.50), channel_id=1, source_target_pairs={{0,4},{4,8},{8,12},{12,16},{16,20},{20,24},{24,28},{28,0},{1,5},{5... | collective-permute-start | bytes 196616 | tf_op jit(solution)/shard_map/ppermute | solution.py:15
  11.3 3.2 %collective-permute-start.4 = (bf16[32,1,8,128]{3,0,2,1:T(8,128)(2,1)S(1)}, bf16[32,1,8,128]{3,0,2,1:T(8,128)(2,1)S(1)}, u32[]{:S(2)}, u32[]{:S(2)}) collective-permute-start(bf16[32,1,8,128]{3,0,2,1:T(8,128)(2,1)S(1)} %get-tuple-element.51), channel_id=1, source_target_pairs={{4,0},{8,4},{12,8},{16,12},{20,16},{24,20},{28,24},{0,28},{5,1},{9... | collective-permute-start | bytes 196616 | tf_op jit(solution)/shard_map/ppermute | solution.py:18
  14.7 2.2 %collective-permute-done.3 = bf16[32,1,8,128]{3,0,2,1:T(8,128)(2,1)S(1)} collective-permute-done((bf16[32,1,8,128]{3,0,2,1:T(8,128)(2,1)S(1)}, bf16[32,1,8,128]{3,0,2,1:T(8,128)(2,1)S(1)}, u32[]{:S(2)}, u32[]{:S(2)}) %collective-permute-start.3) | collective-permute-done | bytes 65568 | tf_op jit(solution)/shard_map/ppermute | solution.py:15
  17.0 1.7 %collective-permute-start.5 = (bf16[32,4,1,128]{3,0,2,1:T(8,128)(2,1)S(1)}, bf16[32,4,1,128]{3,0,2,1:T(8,128)(2,1)S(1)}, u32[]{:S(2)}, u32[]{:S(2)}) collective-permute-start(bf16[32,4,1,128]{3,0,2,1:T(8,128)(2,1)S(1)} %get-tuple-element.35), channel_id=1, source_target_pairs={{1,0},{2,1},{3,2},{0,3},{5,4},{6,5},{7,6},{4,7},{9,8},{10,9},{11,1... | collective-permute-start | bytes 98312 | tf_op jit(solution)/shard_map/ppermute | solution.py:18
  18.8 1.5 %collective-permute-done.6 = bf16[32,4,1,128]{3,0,2,1:T(8,128)(2,1)S(1)} collective-permute-done((bf16[32,4,1,128]{3,0,2,1:T(8,128)(2,1)S(1)}, bf16[32,4,1,128]{3,0,2,1:T(8,128)(2,1)S(1)}, u32[]{:S(2)}, u32[]{:S(2)}) %collective-permute-start.6) | collective-permute-done | bytes 32800 | tf_op jit(solution)/shard_map/ppermute | solution.py:15
  22.5 1.1 %collective-permute-start.7 = (bf16[32,1,8,128]{3,0,2,1:T(8,128)(2,1)S(1)}, bf16[32,1,8,128]{3,0,2,1:T(8,128)(2,1)S(1)}, u32[]{:S(2)}, u32[]{:S(2)}) collective-permute-start(bf16[32,1,8,128]{3,0,2,1:T(8,128)(2,1)S(1)} %get-tuple-element.48), channel_id=1, source_target_pairs={{0,4},{4,8},{8,12},{12,16},{16,20},{20,24},{24,28},{28,0},{1,5},{5... | collective-permute-start | bytes 196616 | tf_op jit(solution)/shard_map/ppermute | solution.py:15
  23.7 3.6 %collective-permute-start.8 = (bf16[32,1,8,128]{3,0,2,1:T(8,128)(2,1)S(1)}, bf16[32,1,8,128]{3,0,2,1:T(8,128)(2,1)S(1)}, u32[]{:S(2)}, u32[]{:S(2)}) collective-permute-start(bf16[32,1,8,128]{3,0,2,1:T(8,128)(2,1)S(1)} %get-tuple-element.49), channel_id=1, source_target_pairs={{4,0},{8,4},{12,8},{16,12},{20,16},{24,20},{28,24},{0,28},{5,1},{9... | collective-permute-start | bytes 196616 | tf_op jit(solution)/shard_map/ppermute | solution.py:18
  27.5 2.4 %collective-permute-done.7 = bf16[32,1,8,128]{3,0,2,1:T(8,128)(2,1)S(1)} collective-permute-done((bf16[32,1,8,128]{3,0,2,1:T(8,128)(2,1)S(1)}, bf16[32,1,8,128]{3,0,2,1:T(8,128)(2,1)S(1)}, u32[]{:S(2)}, u32[]{:S(2)}) %collective-permute-start.7) | collective-permute-done | bytes 65568 | tf_op jit(solution)/shard_map/ppermute | solution.py:15
  30.1 1.6 %collective-permute-start.9 = (bf16[32,4,1,128]{3,0,2,1:T(8,128)(2,1)S(1)}, bf16[32,4,1,128]{3,0,2,1:T(8,128)(2,1)S(1)}, u32[]{:S(2)}, u32[]{:S(2)}) collective-permute-start(bf16[32,4,1,128]{3,0,2,1:T(8,128)(2,1)S(1)} %get-tuple-element.31), channel_id=1, source_target_pairs={{1,0},{2,1},{3,2},{0,3},{5,4},{6,5},{7,6},{4,7},{9,8},{10,9},{11,1... | collective-permute-start | bytes 98312 | tf_op jit(solution)/shard_map/ppermute | solution.py:18
  31.8 1.1 %fusion.1 = f32[9,3,32,32]{2,3,0,1:T(8,128)S(1)} fusion(bf16[9,32,2,8,128]{4,1,3,2,0:T(8,128)(2,1)S(1)} %fusion.50, bf16[1,32,2,8,128]{4,1,3,2,0:T(8,128)(2,1)S(1)} %maximum_bitcast_fusion.7, bf16[1,32,2,8,128]{4,1,3,2,0:T(8,128)(2,1)S(1)} %bitcast.257, bf16[1,32,2,8,128]{4,1,3,2,0:T(8,128)(2,1)S(1)} %maximum_bitcast_fusion.6), kind=kOutput, calls=%fused_computation.4 | convolution fusion | flops 114453504 | bytes 1683456 | tf_op jit(solution)/shard_map/toxzy,sixzy->tsoi/dot_general | solution.py:132
  33.7 1.1 %fusion.3 = f32[9,3,32,32]{2,3,0,1:T(8,128)S(1)} fusion(bf16[1,32,2,8,128]{4,1,3,2,0:T(8,128)(2,1)S(1)} %get-tuple-element.60, bf16[1,32,2,8,128]{4,1,3,2,0:T(8,128)(2,1)S(1)} %bitcast.264, bf16[1,32,2,8,128]{4,1,3,2,0:T(8,128)(2,1)S(1)} %get-tuple-element.59, bf16[9,32,2,8,128]{4,1,3,2,0:T(8,128)(2,1)S(1)} %fusion.40), kind=kOutput, calls=%fused_computation.7 | convolution fusion | flops 114453504 | bytes 1683456 | tf_op jit(solution)/shard_map/toxzy,sixzy->tsoi/dot_general | solution.py:132
  35.2 1.0 %concatenate.99 = f32[55395]{0:T(1024)S(1)} concatenate(f32[27648]{0:T(1024)S(1)} %mul.112, f32[27648]{0:T(1024)S(1)} %mul.116, f32[96]{0:T(128)S(1)} %reshape.98, f32[3]{0:T(128)S(1)} %broadcast_multiply_fusion), dimensions={0} | concatenate | bytes 443160 | tf_op jit(solution)/shard_map/concatenate | solution.py:79
  36.2 1.4 %collective-permute-start.11 = (f32[224,128]{1,0:T(8,128)S(1)}, f32[224,128]{1,0:T(8,128)S(1)}, u32[]{:S(2)}, u32[]{:S(2)}) collective-permute-start(f32[224,128]{1,0:T(8,128)S(1)} %fusion.61), channel_id=1, source_target_pairs={{0,1},{1,0},{2,3},{3,2},{4,5},{5,4},{6,7},{7,6},{8,9},{9,8},{10,11... | collective-permute-start | bytes 344072 | tf_op jit(solution)/shard_map/ppermute | solution.py:66
  37.7 1.0 %collective-permute-done.11 = f32[224,128]{1,0:T(8,128)S(1)} collective-permute-done((f32[224,128]{1,0:T(8,128)S(1)}, f32[224,128]{1,0:T(8,128)S(1)}, u32[]{:S(2)}, u32[]{:S(2)}) %collective-permute-start.11) | collective-permute-done | bytes 114720 | tf_op jit(solution)/shard_map/ppermute | solution.py:66
  39.5 4.0 %collective-permute-done.12 = f32[224,128]{1,0:T(8,128)S(1)} collective-permute-done((f32[224,128]{1,0:T(8,128)S(1)}, f32[224,128]{1,0:T(8,128)S(1)}, u32[]{:S(2)}, u32[]{:S(2)}) %collective-permute-start.12) | collective-permute-done | bytes 114720 | tf_op jit(solution)/shard_map/ppermute | solution.py:71
  43.6 4.8 %collective-permute-done.13 = f32[224,128]{1,0:T(8,128)S(1)} collective-permute-done((f32[224,128]{1,0:T(8,128)S(1)}, f32[224,128]{1,0:T(8,128)S(1)}, u32[]{:S(2)}, u32[]{:S(2)}) %collective-permute-start.13) | collective-permute-done | bytes 114720 | tf_op jit(solution)/shard_map/ppermute | solution.py:71
  49.1 4.2 %collective-permute-done.14 = f32[224,128]{1,0:T(8,128)S(1)} collective-permute-done((f32[224,128]{1,0:T(8,128)S(1)}, f32[224,128]{1,0:T(8,128)S(1)}, u32[]{:S(2)}, u32[]{:S(2)}) %collective-permute-start.14) | collective-permute-done | bytes 114720 | tf_op jit(solution)/shard_map/ppermute | solution.py:71
  53.3 2.0 %collective-permute-start.15 = (f32[224,128]{1,0:T(8,128)S(1)}, f32[224,128]{1,0:T(8,128)S(1)}, u32[]{:S(2)}, u32[]{:S(2)}) collective-permute-start(f32[224,128]{1,0:T(8,128)S(1)} %add.109), channel_id=1, source_target_pairs={{0,16},{1,5},{2,18},{3,7},{4,20},{5,1},{6,22},{7,3},{8,24},{9,13},... | collective-permute-start | bytes 344072 | tf_op jit(solution)/shard_map/ppermute | solution.py:71
  55.6 4.7 %collective-permute-done.15 = f32[224,128]{1,0:T(8,128)S(1)} collective-permute-done((f32[224,128]{1,0:T(8,128)S(1)}, f32[224,128]{1,0:T(8,128)S(1)}, u32[]{:S(2)}, u32[]{:S(2)}) %collective-permute-start.15) | collective-permute-done | bytes 114720 | tf_op jit(solution)/shard_map/ppermute | solution.py:71
  62.6 0.9 %reshape.100 = f32[3,3,3,32,32]{4,3,2,1,0:T(8,128)} reshape(f32[216,128]{1,0:T(8,128)S(1)} %get-tuple-element.36) | data formatting | bytes 221184 | tf_op jit(solution)/shard_map/reshape | solution.py:91
  (109 shorter events, 12.3 us)
Async XLA Ops:
  0.6 20.0 %copy-start = (bf16[3,3,3,32,32]{4,3,2,1,0:T(8,128)(2,1)S(1)}, bf16[3,3,3,32,32]{4,3,2,1,0:T(8,128)(2,1)}, u32[]{:S(2)}) copy-start(bf16[3,3,3,32,32]{4,3,2,1,0:T(8,128)(2,1)} %param.13) | copy-start | bytes 165892
  0.6 7.0 %copy-start.1 = (bf16[32,2,8,128]{3,2,1,0:T(8,128)(2,1)S(1)}, bf16[32,2,8,128]{3,2,1,0:T(8,128)(2,1)}, u32[]{:S(2)}) copy-start(bf16[32,2,8,128]{3,2,1,0:T(8,128)(2,1)} %param.9) | copy-start | bytes 393220
  3.3 4.9 %collective-permute-start.1 = (f32[2,2,128]{2,1,0:T(2,128)S(1)}, f32[2,2,128]{2,1,0:T(2,128)S(1)}, u32[]{:S(2)}, u32[]{:S(2)}) collective-permute-start(f32[2,2,128]{2,1,0:T(2,128)S(1)} %pad_maximum_fusion.14), channel_id=1, source_target_pairs={{0,2},{1,3},{2,0},{3,1},{4,6},{5,7},{6,4},{7,5},{8,10},{9,11},{10,... | collective-permute-start | bytes 6152 | tf_op jit(solution)/shard_map/ppermute | solution.py:47
  6.3 3.0 %collective-permute-start.2 = (f32[2,2,128]{2,1,0:T(2,128)S(1)}, f32[2,2,128]{2,1,0:T(2,128)S(1)}, u32[]{:S(2)}, u32[]{:S(2)}) collective-permute-start(f32[2,2,128]{2,1,0:T(2,128)S(1)} %pad_maximum_fusion.14), channel_id=1, source_target_pairs={{0,3},{1,2},{2,1},{3,0},{4,7},{5,6},{6,5},{7,4},{8,11},{9,10},{10,... | collective-permute-start | bytes 6152 | tf_op jit(solution)/shard_map/ppermute | solution.py:47
  6.3 3.0 %collective-permute-start = (f32[2,2,128]{2,1,0:T(2,128)S(1)}, f32[2,2,128]{2,1,0:T(2,128)S(1)}, u32[]{:S(2)}, u32[]{:S(2)}) collective-permute-start(f32[2,2,128]{2,1,0:T(2,128)S(1)} %pad_maximum_fusion.14), channel_id=1, source_target_pairs={{0,1},{1,0},{2,3},{3,2},{4,5},{5,4},{6,7},{7,6},{8,9},{9,8},{10,11... | collective-permute-start | bytes 6152 | tf_op jit(solution)/shard_map/ppermute | solution.py:47
  7.7 1.6 %copy-start.6 = (f32[2,128]{1,0:T(2,128)S(1)}, f32[2,128]{1,0:T(2,128)}, u32[]{:S(2)}) copy-start(f32[2,128]{1,0:T(2,128)} %param.16) | copy-start | bytes 3076
  7.7 1.6 %copy-start.7 = (f32[2,128]{1,0:T(2,128)S(1)}, f32[2,128]{1,0:T(2,128)}, u32[]{:S(2)}) copy-start(f32[2,128]{1,0:T(2,128)} %param.17) | copy-start | bytes 3076
  7.7 1.8 %copy-start.3 = (bf16[32,2,8,128]{3,2,1,0:T(8,128)(2,1)S(1)}, bf16[32,2,8,128]{3,2,1,0:T(8,128)(2,1)}, u32[]{:S(2)}) copy-start(bf16[32,2,8,128]{3,2,1,0:T(8,128)(2,1)} %param.11) | copy-start | bytes 393220
  7.8 1.8 %copy-start.5 = (bf16[3,32]{1,0:T(4,128)(2,1)S(1)}, bf16[3,32]{1,0:T(4,128)(2,1)}, u32[]{:S(2)}) copy-start(bf16[3,32]{1,0:T(4,128)(2,1)} %param.14) | copy-start | bytes 580
  9.8 7.1 %collective-permute-start.3 = (bf16[32,1,8,128]{3,0,2,1:T(8,128)(2,1)S(1)}, bf16[32,1,8,128]{3,0,2,1:T(8,128)(2,1)S(1)}, u32[]{:S(2)}, u32[]{:S(2)}) collective-permute-start(bf16[32,1,8,128]{3,0,2,1:T(8,128)(2,1)S(1)} %get-tuple-element.50), channel_id=1, source_target_pairs={{0,4},{4,8},{8,12},{12,16},{16,20},{20,24},{24,28},{28,0},{1,5},{5... | collective-permute-start | bytes 196616 | tf_op jit(solution)/shard_map/ppermute | solution.py:15
  11.3 5.6 %collective-permute-start.4 = (bf16[32,1,8,128]{3,0,2,1:T(8,128)(2,1)S(1)}, bf16[32,1,8,128]{3,0,2,1:T(8,128)(2,1)S(1)}, u32[]{:S(2)}, u32[]{:S(2)}) collective-permute-start(bf16[32,1,8,128]{3,0,2,1:T(8,128)(2,1)S(1)} %get-tuple-element.51), channel_id=1, source_target_pairs={{4,0},{8,4},{12,8},{16,12},{20,16},{24,20},{28,24},{0,28},{5,1},{9... | collective-permute-start | bytes 196616 | tf_op jit(solution)/shard_map/ppermute | solution.py:18
  17.0 3.4 %collective-permute-start.6 = (bf16[32,4,1,128]{3,0,2,1:T(8,128)(2,1)S(1)}, bf16[32,4,1,128]{3,0,2,1:T(8,128)(2,1)S(1)}, u32[]{:S(2)}, u32[]{:S(2)}) collective-permute-start(bf16[32,4,1,128]{3,0,2,1:T(8,128)(2,1)S(1)} %get-tuple-element.34), channel_id=1, source_target_pairs={{0,1},{1,2},{2,3},{3,0},{4,5},{5,6},{6,7},{7,4},{8,9},{9,10},{10,1... | collective-permute-start | bytes 98312 | tf_op jit(solution)/shard_map/ppermute | solution.py:15
  17.0 3.3 %collective-permute-start.5 = (bf16[32,4,1,128]{3,0,2,1:T(8,128)(2,1)S(1)}, bf16[32,4,1,128]{3,0,2,1:T(8,128)(2,1)S(1)}, u32[]{:S(2)}, u32[]{:S(2)}) collective-permute-start(bf16[32,4,1,128]{3,0,2,1:T(8,128)(2,1)S(1)} %get-tuple-element.35), channel_id=1, source_target_pairs={{1,0},{2,1},{3,2},{0,3},{5,4},{6,5},{7,6},{4,7},{9,8},{10,9},{11,1... | collective-permute-start | bytes 98312 | tf_op jit(solution)/shard_map/ppermute | solution.py:18
  22.5 7.4 %collective-permute-start.7 = (bf16[32,1,8,128]{3,0,2,1:T(8,128)(2,1)S(1)}, bf16[32,1,8,128]{3,0,2,1:T(8,128)(2,1)S(1)}, u32[]{:S(2)}, u32[]{:S(2)}) collective-permute-start(bf16[32,1,8,128]{3,0,2,1:T(8,128)(2,1)S(1)} %get-tuple-element.48), channel_id=1, source_target_pairs={{0,4},{4,8},{8,12},{12,16},{16,20},{20,24},{24,28},{28,0},{1,5},{5... | collective-permute-start | bytes 196616 | tf_op jit(solution)/shard_map/ppermute | solution.py:15
  23.7 6.3 %collective-permute-start.8 = (bf16[32,1,8,128]{3,0,2,1:T(8,128)(2,1)S(1)}, bf16[32,1,8,128]{3,0,2,1:T(8,128)(2,1)S(1)}, u32[]{:S(2)}, u32[]{:S(2)}) collective-permute-start(bf16[32,1,8,128]{3,0,2,1:T(8,128)(2,1)S(1)} %get-tuple-element.49), channel_id=1, source_target_pairs={{4,0},{8,4},{12,8},{16,12},{20,16},{24,20},{28,24},{0,28},{5,1},{9... | collective-permute-start | bytes 196616 | tf_op jit(solution)/shard_map/ppermute | solution.py:18
  30.0 3.4 %collective-permute-start.10 = (bf16[32,4,1,128]{3,0,2,1:T(8,128)(2,1)S(1)}, bf16[32,4,1,128]{3,0,2,1:T(8,128)(2,1)S(1)}, u32[]{:S(2)}, u32[]{:S(2)}) collective-permute-start(bf16[32,4,1,128]{3,0,2,1:T(8,128)(2,1)S(1)} %get-tuple-element.30), channel_id=1, source_target_pairs={{0,1},{1,2},{2,3},{3,0},{4,5},{5,6},{6,7},{7,4},{8,9},{9,10},{10,1... | collective-permute-start | bytes 98312 | tf_op jit(solution)/shard_map/ppermute | solution.py:15
  30.1 3.2 %collective-permute-start.9 = (bf16[32,4,1,128]{3,0,2,1:T(8,128)(2,1)S(1)}, bf16[32,4,1,128]{3,0,2,1:T(8,128)(2,1)S(1)}, u32[]{:S(2)}, u32[]{:S(2)}) collective-permute-start(bf16[32,4,1,128]{3,0,2,1:T(8,128)(2,1)S(1)} %get-tuple-element.31), channel_id=1, source_target_pairs={{1,0},{2,1},{3,2},{0,3},{5,4},{6,5},{7,6},{4,7},{9,8},{10,9},{11,1... | collective-permute-start | bytes 98312 | tf_op jit(solution)/shard_map/ppermute | solution.py:18
  35.2 13.4 %copy-start.2 = (bf16[3,3,3,32,32]{4,3,2,1,0:T(8,128)(2,1)S(1)}, bf16[3,3,3,32,32]{4,3,2,1,0:T(8,128)(2,1)}, u32[]{:S(2)}) copy-start(bf16[3,3,3,32,32]{4,3,2,1,0:T(8,128)(2,1)} %param.12) | copy-start | bytes 165892
  36.2 2.4 %collective-permute-start.11 = (f32[224,128]{1,0:T(8,128)S(1)}, f32[224,128]{1,0:T(8,128)S(1)}, u32[]{:S(2)}, u32[]{:S(2)}) collective-permute-start(f32[224,128]{1,0:T(8,128)S(1)} %fusion.61), channel_id=1, source_target_pairs={{0,1},{1,0},{2,3},{3,2},{4,5},{5,4},{6,7},{7,6},{8,9},{9,8},{10,11... | collective-permute-start | bytes 344072 | tf_op jit(solution)/shard_map/ppermute | solution.py:66
  38.7 4.9 %collective-permute-start.12 = (f32[224,128]{1,0:T(8,128)S(1)}, f32[224,128]{1,0:T(8,128)S(1)}, u32[]{:S(2)}, u32[]{:S(2)}) collective-permute-start(f32[224,128]{1,0:T(8,128)S(1)} %select_add_fusion), channel_id=1, source_target_pairs={{0,2},{1,9},{2,0},{3,11},{4,6},{5,13},{6,4},{7,15},{8,10},{9,1},{1... | collective-permute-start | bytes 344072 | tf_op jit(solution)/shard_map/ppermute | solution.py:71
  43.6 4.9 %collective-permute-start.13 = (f32[224,128]{1,0:T(8,128)S(1)}, f32[224,128]{1,0:T(8,128)S(1)}, u32[]{:S(2)}, u32[]{:S(2)}) collective-permute-start(f32[224,128]{1,0:T(8,128)S(1)} %add.107), channel_id=1, source_target_pairs={{0,4},{1,17},{2,6},{3,19},{4,0},{5,21},{6,2},{7,23},{8,12},{9,25},... | collective-permute-start | bytes 344072 | tf_op jit(solution)/shard_map/ppermute | solution.py:71
  48.4 4.9 %collective-permute-start.14 = (f32[224,128]{1,0:T(8,128)S(1)}, f32[224,128]{1,0:T(8,128)S(1)}, u32[]{:S(2)}, u32[]{:S(2)}) collective-permute-start(f32[224,128]{1,0:T(8,128)S(1)} %add.108), channel_id=1, source_target_pairs={{0,8},{1,3},{2,10},{3,1},{4,12},{5,7},{6,14},{7,5},{8,0},{9,11},{1... | collective-permute-start | bytes 344072 | tf_op jit(solution)/shard_map/ppermute | solution.py:71
  53.3 7.0 %collective-permute-start.15 = (f32[224,128]{1,0:T(8,128)S(1)}, f32[224,128]{1,0:T(8,128)S(1)}, u32[]{:S(2)}, u32[]{:S(2)}) collective-permute-start(f32[224,128]{1,0:T(8,128)S(1)} %add.109), channel_id=1, source_target_pairs={{0,16},{1,5},{2,18},{3,7},{4,20},{5,1},{6,22},{7,3},{8,24},{9,13},... | collective-permute-start | bytes 344072 | tf_op jit(solution)/shard_map/ppermute | solution.py:71
  60.3 1.4 %collective-permute-start.16 = (f32[224,128]{1,0:T(8,128)S(1)}, f32[224,128]{1,0:T(8,128)S(1)}, u32[]{:S(2)}, u32[]{:S(2)}) collective-permute-start(f32[224,128]{1,0:T(8,128)S(1)} %add.110), channel_id=1, source_target_pairs={{0,1},{1,0},{2,3},{3,2},{4,5},{5,4},{6,7},{7,6},{8,9},{9,8},{10,11... | collective-permute-start | bytes 344072 | tf_op jit(solution)/shard_map/ppermute | solution.py:72
  (1 other events, 0.9 us)

commit v12 on v11

--- a/solution.py
+++ b/solution.py
@@ -75,21 +75,35 @@
     )
 
 
+def row_count(shape):
+    return -(-math.prod(shape) // 128)
+
+
 def pack_rows(parts):
-    flat = jnp.concatenate([part.reshape(-1) for part in parts])
-    rows = -(-flat.shape[0] // 2048) * 16
-    flat = jnp.pad(flat, (0, rows * 128 - flat.shape[0]))
-    return flat.reshape(rows, 128)
+    blocks = []
+    for part in parts:
+        size = math.prod(part.shape)
+        rows = row_count(part.shape)
+        flat = part.reshape(-1)
+        if rows * 128 != size:
+            flat = jnp.pad(flat, (0, rows * 128 - size))
+        blocks.append(flat.reshape(rows, 128))
+    total = sum(block.shape[0] for block in blocks)
+    blocks.append(jnp.zeros((-(-total // 16) * 16 - total, 128), jnp.float32))
+    return jnp.concatenate(blocks)
 
 
 def unpack_rows(packed, shapes):
-    flat = packed.reshape(-1)
     parts = []
     start = 0
     for shape in shapes:
         size = math.prod(shape)
-        parts.append(flat[start : start + size].reshape(shape))
-        start += size
+        rows = row_count(shape)
+        block = packed[start : start + rows]
+        if rows * 128 != size:
+            block = block.reshape(-1)[:size]
+        parts.append(block.reshape(shape))
+        start += rows
     return parts
 
 

time: 65.2 us -> 64.1 us (0.983)
  local copies, waits for them, and re-layouts: 9.07 us -> 7.66 us
    concatenate x1 -> x0, local copies, waits for them, and re-layouts: 0.98 us -> none  [pack_rows(): flat = jnp.concatenate([part.reshape(-1) for part in parts])]
    reshape x3 -> x6, local copies, waits for them, and re-layouts: 1.92 us -> 2.59 us  [the longest x3 2.5 us: unpack_rows(): parts.append(block.reshape(shape))]
  transfers between devices with their start and end apart: 17 -> 17, of which waited for: 10 -> 11; matrix products, arithmetic and copies ran while one was open for 8% -> 8% of each run, Pallas kernels for 0% -> 0%
where the time goes in v12:
time: 64.1 us; the launch traced here: 63.9 us
  waiting for transfers between devices  26.3 us (41%)
  starting transfers between devices  21.2 us (33%)
  local copies, waits for them, and re-layouts  7.66 us (12%)
  matrix products  4.26 us (7%)
  other arithmetic  3.26 us (5%)
  between operations  1.21 us (2%)
    ppermute x4, waiting for transfers between devices, split_sum(): keep = keep + lax.ppermute(keep, index_axes, pairs)  17.3 us
    ppermute x4, starting transfers between devices, extended(): lax.ppermute(lax.slice_in_dim(block, 0, width, axis=dim), axis, backward)  10.1 us
    ppermute x4, waiting for transfers between devices, extended(): lax.ppermute(lax.slice_in_dim(block, block.shape[dim] - width, None, axis...  6.5 us
    ppermute x4, starting transfers between devices, split_sum(): keep = keep + lax.ppermute(keep, index_axes, pairs)  3.44 us
    ppermute x3, starting transfers between devices, quad_sum(): lax.ppermute(value, axis, [(i, i ^ mask) for i in range(count)])  3.2 us
    ppermute x4, starting transfers between devices, extended(): lax.ppermute(lax.slice_in_dim(block, block.shape[dim] - width, None, axis...  3.01 us
    reshape x3, local copies, waits for them, and re-layouts, unpack_rows(): parts.append(block.reshape(shape))  2.5 us
    dot_general x2, matrix products, taps_from_halo(): jnp.einsum('toxzy,sixzy->tsoi', windows, rolled, preferred_element_type=j...  2.13 us
  transfers between devices with their start and end apart: 17, of which 11 were waited for; matrix products, arithmetic and copies ran while one was open for 8% of the time, Pallas kernels for 0%

profile of v12, /device:TPU:0, one launch (start us, length us, event | category | flops | bytes accessed | tf_op | source)
XLA Modules:
  0.0 63.9 jit_solution(3060652369397829424)
XLA Ops:
  0.7 1.0 %fusion.22 = bf16[32,2,8,128]{3,0,2,1:T(8,128)(2,1)S(1)} fusion(bf16[32,2,8,128]{3,2,1,0:T(8,128)(2,1)} %param.11), kind=kLoop, calls=%fused_computation.40 | loop fusion | flops 393216 | bytes 262144 | tf_op jit(solution)/shard_map/convert_element_type | solution.py:162
  3.3 3.0 %collective-permute-start.1 = (f32[2,2,128]{2,1,0:T(2,128)S(1)}, f32[2,2,128]{2,1,0:T(2,128)S(1)}, u32[]{:S(2)}, u32[]{:S(2)}) collective-permute-start(f32[2,2,128]{2,1,0:T(2,128)S(1)} %pad_maximum_fusion.16), channel_id=1, source_target_pairs={{0,2},{1,3},{2,0},{3,1},{4,6},{5,7},{6,4},{7,5},{8,10},{9,11},{10,... | collective-permute-start | bytes 6152 | tf_op jit(solution)/shard_map/ppermute | solution.py:47
  6.5 1.1 %fusion.89 = (bf16[32,2,8,127]{3,2,1,0:T(8,128)(2,1)S(1)}, bf16[32,2,8,127]{3,2,1,0:T(8,128)(2,1)S(1)}) fusion(bf16[32,2,8,128]{3,2,1,0:T(8,128)(2,1)} %param.9), kind=kLoop, calls=%fused_computation.171 | loop fusion | bytes 520192 | tf_op jit(solution)/shard_map/jit(_roll_static)/slice | solution.py:145
  8.2 1.1 %collective-permute-done.2 = f32[2,2,128]{2,1,0:T(2,128)S(1)} collective-permute-done((f32[2,2,128]{2,1,0:T(2,128)S(1)}, f32[2,2,128]{2,1,0:T(2,128)S(1)}, u32[]{:S(2)}, u32[]{:S(2)}) %collective-permute-start.2) | collective-permute-done | bytes 2080 | tf_op jit(solution)/shard_map/ppermute | solution.py:47
  10.0 1.6 %collective-permute-start.3 = (bf16[32,1,8,128]{3,0,2,1:T(8,128)(2,1)S(1)}, bf16[32,1,8,128]{3,0,2,1:T(8,128)(2,1)S(1)}, u32[]{:S(2)}, u32[]{:S(2)}) collective-permute-start(bf16[32,1,8,128]{3,0,2,1:T(8,128)(2,1)S(1)} %get-tuple-element.50), channel_id=1, source_target_pairs={{0,4},{4,8},{8,12},{12,16},{16,20},{20,24},{24,28},{28,0},{1,5},{5... | collective-permute-start | bytes 196616 | tf_op jit(solution)/shard_map/ppermute | solution.py:15
  11.6 3.2 %collective-permute-start.4 = (bf16[32,1,8,128]{3,0,2,1:T(8,128)(2,1)S(1)}, bf16[32,1,8,128]{3,0,2,1:T(8,128)(2,1)S(1)}, u32[]{:S(2)}, u32[]{:S(2)}) collective-permute-start(bf16[32,1,8,128]{3,0,2,1:T(8,128)(2,1)S(1)} %get-tuple-element.51), channel_id=1, source_target_pairs={{4,0},{8,4},{12,8},{16,12},{20,16},{24,20},{28,24},{0,28},{5,1},{9... | collective-permute-start | bytes 196616 | tf_op jit(solution)/shard_map/ppermute | solution.py:18
  14.8 2.3 %collective-permute-done.3 = bf16[32,1,8,128]{3,0,2,1:T(8,128)(2,1)S(1)} collective-permute-done((bf16[32,1,8,128]{3,0,2,1:T(8,128)(2,1)S(1)}, bf16[32,1,8,128]{3,0,2,1:T(8,128)(2,1)S(1)}, u32[]{:S(2)}, u32[]{:S(2)}) %collective-permute-start.3) | collective-permute-done | bytes 65568 | tf_op jit(solution)/shard_map/ppermute | solution.py:15
  17.2 1.7 %collective-permute-start.5 = (bf16[32,4,1,128]{3,0,2,1:T(8,128)(2,1)S(1)}, bf16[32,4,1,128]{3,0,2,1:T(8,128)(2,1)S(1)}, u32[]{:S(2)}, u32[]{:S(2)}) collective-permute-start(bf16[32,4,1,128]{3,0,2,1:T(8,128)(2,1)S(1)} %get-tuple-element.35), channel_id=1, source_target_pairs={{1,0},{2,1},{3,2},{0,3},{5,4},{6,5},{7,6},{4,7},{9,8},{10,9},{11,1... | collective-permute-start | bytes 98312 | tf_op jit(solution)/shard_map/ppermute | solution.py:18
  19.0 1.6 %collective-permute-done.6 = bf16[32,4,1,128]{3,0,2,1:T(8,128)(2,1)S(1)} collective-permute-done((bf16[32,4,1,128]{3,0,2,1:T(8,128)(2,1)S(1)}, bf16[32,4,1,128]{3,0,2,1:T(8,128)(2,1)S(1)}, u32[]{:S(2)}, u32[]{:S(2)}) %collective-permute-start.6) | collective-permute-done | bytes 32800 | tf_op jit(solution)/shard_map/ppermute | solution.py:15
  22.7 1.2 %collective-permute-start.7 = (bf16[32,1,8,128]{3,0,2,1:T(8,128)(2,1)S(1)}, bf16[32,1,8,128]{3,0,2,1:T(8,128)(2,1)S(1)}, u32[]{:S(2)}, u32[]{:S(2)}) collective-permute-start(bf16[32,1,8,128]{3,0,2,1:T(8,128)(2,1)S(1)} %get-tuple-element.48), channel_id=1, source_target_pairs={{0,4},{4,8},{8,12},{12,16},{16,20},{20,24},{24,28},{28,0},{1,5},{5... | collective-permute-start | bytes 196616 | tf_op jit(solution)/shard_map/ppermute | solution.py:15
  23.9 3.6 %collective-permute-start.8 = (bf16[32,1,8,128]{3,0,2,1:T(8,128)(2,1)S(1)}, bf16[32,1,8,128]{3,0,2,1:T(8,128)(2,1)S(1)}, u32[]{:S(2)}, u32[]{:S(2)}) collective-permute-start(bf16[32,1,8,128]{3,0,2,1:T(8,128)(2,1)S(1)} %get-tuple-element.49), channel_id=1, source_target_pairs={{4,0},{8,4},{12,8},{16,12},{20,16},{24,20},{28,24},{0,28},{5,1},{9... | collective-permute-start | bytes 196616 | tf_op jit(solution)/shard_map/ppermute | solution.py:18
  27.7 2.4 %collective-permute-done.7 = bf16[32,1,8,128]{3,0,2,1:T(8,128)(2,1)S(1)} collective-permute-done((bf16[32,1,8,128]{3,0,2,1:T(8,128)(2,1)S(1)}, bf16[32,1,8,128]{3,0,2,1:T(8,128)(2,1)S(1)}, u32[]{:S(2)}, u32[]{:S(2)}) %collective-permute-start.7) | collective-permute-done | bytes 65568 | tf_op jit(solution)/shard_map/ppermute | solution.py:15
  30.3 1.6 %collective-permute-start.9 = (bf16[32,4,1,128]{3,0,2,1:T(8,128)(2,1)S(1)}, bf16[32,4,1,128]{3,0,2,1:T(8,128)(2,1)S(1)}, u32[]{:S(2)}, u32[]{:S(2)}) collective-permute-start(bf16[32,4,1,128]{3,0,2,1:T(8,128)(2,1)S(1)} %get-tuple-element.31), channel_id=1, source_target_pairs={{1,0},{2,1},{3,2},{0,3},{5,4},{6,5},{7,6},{4,7},{9,8},{10,9},{11,1... | collective-permute-start | bytes 98312 | tf_op jit(solution)/shard_map/ppermute | solution.py:18
  31.9 1.1 %fusion.3 = f32[9,3,32,32]{2,3,0,1:T(8,128)S(1)} fusion(bf16[9,32,2,8,128]{4,1,3,2,0:T(8,128)(2,1)S(1)} %fusion.50, bf16[1,32,2,8,128]{4,1,3,2,0:T(8,128)(2,1)S(1)} %maximum_bitcast_fusion.5, bf16[1,32,2,8,128]{4,1,3,2,0:T(8,128)(2,1)S(1)} %bitcast.252, bf16[1,32,2,8,128]{4,1,3,2,0:T(8,128)(2,1)S(1)} %maximum_bitcast_fusion.4), kind=kOutput, calls=%fused_computation.7 | convolution fusion | flops 114453504 | bytes 1683456 | tf_op jit(solution)/shard_map/toxzy,sixzy->tsoi/dot_general | solution.py:146
  33.8 1.1 %fusion.1 = f32[9,3,32,32]{2,3,0,1:T(8,128)S(1)} fusion(bf16[1,32,2,8,128]{4,1,3,2,0:T(8,128)(2,1)S(1)} %get-tuple-element.60, bf16[1,32,2,8,128]{4,1,3,2,0:T(8,128)(2,1)S(1)} %bitcast.258, bf16[1,32,2,8,128]{4,1,3,2,0:T(8,128)(2,1)S(1)} %get-tuple-element.59, bf16[9,32,2,8,128]{4,1,3,2,0:T(8,128)(2,1)S(1)} %fusion.40), kind=kOutput, calls=%fused_computation.4 | convolution fusion | flops 114453504 | bytes 1683456 | tf_op jit(solution)/shard_map/toxzy,sixzy->tsoi/dot_general | solution.py:146
  35.3 1.4 %collective-permute-start.11 = (f32[224,128]{1,0:T(8,128)S(1)}, f32[224,128]{1,0:T(8,128)S(1)}, u32[]{:S(2)}, u32[]{:S(2)}) collective-permute-start(f32[224,128]{1,0:T(8,128)S(1)} %fusion.61), channel_id=1, source_target_pairs={{0,1},{1,0},{2,3},{3,2},{4,5},{5,4},{6,7},{7,6},{8,9},{9,8},{10,11... | collective-permute-start | bytes 344072 | tf_op jit(solution)/shard_map/ppermute | solution.py:66
  36.7 1.0 %collective-permute-done.11 = f32[224,128]{1,0:T(8,128)S(1)} collective-permute-done((f32[224,128]{1,0:T(8,128)S(1)}, f32[224,128]{1,0:T(8,128)S(1)}, u32[]{:S(2)}, u32[]{:S(2)}) %collective-permute-start.11) | collective-permute-done | bytes 114720 | tf_op jit(solution)/shard_map/ppermute | solution.py:66
  38.7 4.0 %collective-permute-done.12 = f32[224,128]{1,0:T(8,128)S(1)} collective-permute-done((f32[224,128]{1,0:T(8,128)S(1)}, f32[224,128]{1,0:T(8,128)S(1)}, u32[]{:S(2)}, u32[]{:S(2)}) %collective-permute-start.12) | collective-permute-done | bytes 114720 | tf_op jit(solution)/shard_map/ppermute | solution.py:71
  42.8 4.7 %collective-permute-done.13 = f32[224,128]{1,0:T(8,128)S(1)} collective-permute-done((f32[224,128]{1,0:T(8,128)S(1)}, f32[224,128]{1,0:T(8,128)S(1)}, u32[]{:S(2)}, u32[]{:S(2)}) %collective-permute-start.13) | collective-permute-done | bytes 114720 | tf_op jit(solution)/shard_map/ppermute | solution.py:71
  48.3 4.0 %collective-permute-done.14 = f32[224,128]{1,0:T(8,128)S(1)} collective-permute-done((f32[224,128]{1,0:T(8,128)S(1)}, f32[224,128]{1,0:T(8,128)S(1)}, u32[]{:S(2)}, u32[]{:S(2)}) %collective-permute-start.14) | collective-permute-done | bytes 114720 | tf_op jit(solution)/shard_map/ppermute | solution.py:71
  52.4 2.1 %collective-permute-start.15 = (f32[224,128]{1,0:T(8,128)S(1)}, f32[224,128]{1,0:T(8,128)S(1)}, u32[]{:S(2)}, u32[]{:S(2)}) collective-permute-start(f32[224,128]{1,0:T(8,128)S(1)} %add.111), channel_id=1, source_target_pairs={{0,16},{1,5},{2,18},{3,7},{4,20},{5,1},{6,22},{7,3},{8,24},{9,13},... | collective-permute-start | bytes 344072 | tf_op jit(solution)/shard_map/ppermute | solution.py:71
  54.8 4.6 %collective-permute-done.15 = f32[224,128]{1,0:T(8,128)S(1)} collective-permute-done((f32[224,128]{1,0:T(8,128)S(1)}, f32[224,128]{1,0:T(8,128)S(1)}, u32[]{:S(2)}, u32[]{:S(2)}) %collective-permute-start.15) | collective-permute-done | bytes 114720 | tf_op jit(solution)/shard_map/ppermute | solution.py:71
  62.0 0.9 %reshape.79 = f32[3,3,3,32,32]{4,3,2,1,0:T(8,128)} reshape(f32[216,128]{1,0:T(8,128)S(1)} %get-tuple-element.36) | data formatting | bytes 221184 | tf_op jit(solution)/shard_map/reshape | solution.py:105
  63.0 0.9 %reshape.78 = f32[3,3,3,32,32]{4,3,2,1,0:T(8,128)} reshape(f32[216,128]{1,0:T(8,128)S(1)} %get-tuple-element.37) | data formatting | bytes 221184 | tf_op jit(solution)/shard_map/reshape | solution.py:105
  (110 shorter events, 11.5 us)
Async XLA Ops:
  0.6 20.2 %copy-start = (bf16[3,3,3,32,32]{4,3,2,1,0:T(8,128)(2,1)S(1)}, bf16[3,3,3,32,32]{4,3,2,1,0:T(8,128)(2,1)}, u32[]{:S(2)}) copy-start(bf16[3,3,3,32,32]{4,3,2,1,0:T(8,128)(2,1)} %param.13) | copy-start | bytes 165892
  0.6 7.0 %copy-start.1 = (bf16[32,2,8,128]{3,2,1,0:T(8,128)(2,1)S(1)}, bf16[32,2,8,128]{3,2,1,0:T(8,128)(2,1)}, u32[]{:S(2)}) copy-start(bf16[32,2,8,128]{3,2,1,0:T(8,128)(2,1)} %param.9) | copy-start | bytes 393220
  3.3 4.9 %collective-permute-start.1 = (f32[2,2,128]{2,1,0:T(2,128)S(1)}, f32[2,2,128]{2,1,0:T(2,128)S(1)}, u32[]{:S(2)}, u32[]{:S(2)}) collective-permute-start(f32[2,2,128]{2,1,0:T(2,128)S(1)} %pad_maximum_fusion.16), channel_id=1, source_target_pairs={{0,2},{1,3},{2,0},{3,1},{4,6},{5,7},{6,4},{7,5},{8,10},{9,11},{10,... | collective-permute-start | bytes 6152 | tf_op jit(solution)/shard_map/ppermute | solution.py:47
  6.3 3.0 %collective-permute-start.2 = (f32[2,2,128]{2,1,0:T(2,128)S(1)}, f32[2,2,128]{2,1,0:T(2,128)S(1)}, u32[]{:S(2)}, u32[]{:S(2)}) collective-permute-start(f32[2,2,128]{2,1,0:T(2,128)S(1)} %pad_maximum_fusion.16), channel_id=1, source_target_pairs={{0,3},{1,2},{2,1},{3,0},{4,7},{5,6},{6,5},{7,4},{8,11},{9,10},{10,... | collective-permute-start | bytes 6152 | tf_op jit(solution)/shard_map/ppermute | solution.py:47
  6.3 3.0 %collective-permute-start = (f32[2,2,128]{2,1,0:T(2,128)S(1)}, f32[2,2,128]{2,1,0:T(2,128)S(1)}, u32[]{:S(2)}, u32[]{:S(2)}) collective-permute-start(f32[2,2,128]{2,1,0:T(2,128)S(1)} %pad_maximum_fusion.16), channel_id=1, source_target_pairs={{0,1},{1,0},{2,3},{3,2},{4,5},{5,4},{6,7},{7,6},{8,9},{9,8},{10,11... | collective-permute-start | bytes 6152 | tf_op jit(solution)/shard_map/ppermute | solution.py:47
  7.7 1.6 %copy-start.6 = (f32[2,128]{1,0:T(2,128)S(1)}, f32[2,128]{1,0:T(2,128)}, u32[]{:S(2)}) copy-start(f32[2,128]{1,0:T(2,128)} %param.16) | copy-start | bytes 3076
  7.7 1.6 %copy-start.7 = (f32[2,128]{1,0:T(2,128)S(1)}, f32[2,128]{1,0:T(2,128)}, u32[]{:S(2)}) copy-start(f32[2,128]{1,0:T(2,128)} %param.17) | copy-start | bytes 3076
  7.7 1.9 %copy-start.3 = (bf16[32,2,8,128]{3,2,1,0:T(8,128)(2,1)S(1)}, bf16[32,2,8,128]{3,2,1,0:T(8,128)(2,1)}, u32[]{:S(2)}) copy-start(bf16[32,2,8,128]{3,2,1,0:T(8,128)(2,1)} %param.11) | copy-start | bytes 393220
  7.8 1.9 %copy-start.5 = (bf16[3,32]{1,0:T(4,128)(2,1)S(1)}, bf16[3,32]{1,0:T(4,128)(2,1)}, u32[]{:S(2)}) copy-start(bf16[3,32]{1,0:T(4,128)(2,1)} %param.14) | copy-start | bytes 580
  10.0 7.1 %collective-permute-start.3 = (bf16[32,1,8,128]{3,0,2,1:T(8,128)(2,1)S(1)}, bf16[32,1,8,128]{3,0,2,1:T(8,128)(2,1)S(1)}, u32[]{:S(2)}, u32[]{:S(2)}) collective-permute-start(bf16[32,1,8,128]{3,0,2,1:T(8,128)(2,1)S(1)} %get-tuple-element.50), channel_id=1, source_target_pairs={{0,4},{4,8},{8,12},{12,16},{16,20},{20,24},{24,28},{28,0},{1,5},{5... | collective-permute-start | bytes 196616 | tf_op jit(solution)/shard_map/ppermute | solution.py:15
  11.6 5.6 %collective-permute-start.4 = (bf16[32,1,8,128]{3,0,2,1:T(8,128)(2,1)S(1)}, bf16[32,1,8,128]{3,0,2,1:T(8,128)(2,1)S(1)}, u32[]{:S(2)}, u32[]{:S(2)}) collective-permute-start(bf16[32,1,8,128]{3,0,2,1:T(8,128)(2,1)S(1)} %get-tuple-element.51), channel_id=1, source_target_pairs={{4,0},{8,4},{12,8},{16,12},{20,16},{24,20},{28,24},{0,28},{5,1},{9... | collective-permute-start | bytes 196616 | tf_op jit(solution)/shard_map/ppermute | solution.py:18
  17.1 3.4 %collective-permute-start.6 = (bf16[32,4,1,128]{3,0,2,1:T(8,128)(2,1)S(1)}, bf16[32,4,1,128]{3,0,2,1:T(8,128)(2,1)S(1)}, u32[]{:S(2)}, u32[]{:S(2)}) collective-permute-start(bf16[32,4,1,128]{3,0,2,1:T(8,128)(2,1)S(1)} %get-tuple-element.34), channel_id=1, source_target_pairs={{0,1},{1,2},{2,3},{3,0},{4,5},{5,6},{6,7},{7,4},{8,9},{9,10},{10,1... | collective-permute-start | bytes 98312 | tf_op jit(solution)/shard_map/ppermute | solution.py:15
  17.2 3.3 %collective-permute-start.5 = (bf16[32,4,1,128]{3,0,2,1:T(8,128)(2,1)S(1)}, bf16[32,4,1,128]{3,0,2,1:T(8,128)(2,1)S(1)}, u32[]{:S(2)}, u32[]{:S(2)}) collective-permute-start(bf16[32,4,1,128]{3,0,2,1:T(8,128)(2,1)S(1)} %get-tuple-element.35), channel_id=1, source_target_pairs={{1,0},{2,1},{3,2},{0,3},{5,4},{6,5},{7,6},{4,7},{9,8},{10,9},{11,1... | collective-permute-start | bytes 98312 | tf_op jit(solution)/shard_map/ppermute | solution.py:18
  22.7 7.4 %collective-permute-start.7 = (bf16[32,1,8,128]{3,0,2,1:T(8,128)(2,1)S(1)}, bf16[32,1,8,128]{3,0,2,1:T(8,128)(2,1)S(1)}, u32[]{:S(2)}, u32[]{:S(2)}) collective-permute-start(bf16[32,1,8,128]{3,0,2,1:T(8,128)(2,1)S(1)} %get-tuple-element.48), channel_id=1, source_target_pairs={{0,4},{4,8},{8,12},{12,16},{16,20},{20,24},{24,28},{28,0},{1,5},{5... | collective-permute-start | bytes 196616 | tf_op jit(solution)/shard_map/ppermute | solution.py:15
  23.9 6.2 %collective-permute-start.8 = (bf16[32,1,8,128]{3,0,2,1:T(8,128)(2,1)S(1)}, bf16[32,1,8,128]{3,0,2,1:T(8,128)(2,1)S(1)}, u32[]{:S(2)}, u32[]{:S(2)}) collective-permute-start(bf16[32,1,8,128]{3,0,2,1:T(8,128)(2,1)S(1)} %get-tuple-element.49), channel_id=1, source_target_pairs={{4,0},{8,4},{12,8},{16,12},{20,16},{24,20},{28,24},{0,28},{5,1},{9... | collective-permute-start | bytes 196616 | tf_op jit(solution)/shard_map/ppermute | solution.py:18
  30.1 3.4 %collective-permute-start.10 = (bf16[32,4,1,128]{3,0,2,1:T(8,128)(2,1)S(1)}, bf16[32,4,1,128]{3,0,2,1:T(8,128)(2,1)S(1)}, u32[]{:S(2)}, u32[]{:S(2)}) collective-permute-start(bf16[32,4,1,128]{3,0,2,1:T(8,128)(2,1)S(1)} %get-tuple-element.30), channel_id=1, source_target_pairs={{0,1},{1,2},{2,3},{3,0},{4,5},{5,6},{6,7},{7,4},{8,9},{9,10},{10,1... | collective-permute-start | bytes 98312 | tf_op jit(solution)/shard_map/ppermute | solution.py:15
  30.3 3.2 %collective-permute-start.9 = (bf16[32,4,1,128]{3,0,2,1:T(8,128)(2,1)S(1)}, bf16[32,4,1,128]{3,0,2,1:T(8,128)(2,1)S(1)}, u32[]{:S(2)}, u32[]{:S(2)}) collective-permute-start(bf16[32,4,1,128]{3,0,2,1:T(8,128)(2,1)S(1)} %get-tuple-element.31), channel_id=1, source_target_pairs={{1,0},{2,1},{3,2},{0,3},{5,4},{6,5},{7,6},{4,7},{9,8},{10,9},{11,1... | collective-permute-start | bytes 98312 | tf_op jit(solution)/shard_map/ppermute | solution.py:18
  35.1 12.8 %copy-start.2 = (bf16[3,3,3,32,32]{4,3,2,1,0:T(8,128)(2,1)S(1)}, bf16[3,3,3,32,32]{4,3,2,1,0:T(8,128)(2,1)}, u32[]{:S(2)}) copy-start(bf16[3,3,3,32,32]{4,3,2,1,0:T(8,128)(2,1)} %param.12) | copy-start | bytes 165892
  35.3 2.3 %collective-permute-start.11 = (f32[224,128]{1,0:T(8,128)S(1)}, f32[224,128]{1,0:T(8,128)S(1)}, u32[]{:S(2)}, u32[]{:S(2)}) collective-permute-start(f32[224,128]{1,0:T(8,128)S(1)} %fusion.61), channel_id=1, source_target_pairs={{0,1},{1,0},{2,3},{3,2},{4,5},{5,4},{6,7},{7,6},{8,9},{9,8},{10,11... | collective-permute-start | bytes 344072 | tf_op jit(solution)/shard_map/ppermute | solution.py:66
  37.8 4.9 %collective-permute-start.12 = (f32[224,128]{1,0:T(8,128)S(1)}, f32[224,128]{1,0:T(8,128)S(1)}, u32[]{:S(2)}, u32[]{:S(2)}) collective-permute-start(f32[224,128]{1,0:T(8,128)S(1)} %select_add_fusion), channel_id=1, source_target_pairs={{0,2},{1,9},{2,0},{3,11},{4,6},{5,13},{6,4},{7,15},{8,10},{9,1},{1... | collective-permute-start | bytes 344072 | tf_op jit(solution)/shard_map/ppermute | solution.py:71
  42.7 4.9 %collective-permute-start.13 = (f32[224,128]{1,0:T(8,128)S(1)}, f32[224,128]{1,0:T(8,128)S(1)}, u32[]{:S(2)}, u32[]{:S(2)}) collective-permute-start(f32[224,128]{1,0:T(8,128)S(1)} %add.109), channel_id=1, source_target_pairs={{0,4},{1,17},{2,6},{3,19},{4,0},{5,21},{6,2},{7,23},{8,12},{9,25},... | collective-permute-start | bytes 344072 | tf_op jit(solution)/shard_map/ppermute | solution.py:71
  47.5 4.9 %collective-permute-start.14 = (f32[224,128]{1,0:T(8,128)S(1)}, f32[224,128]{1,0:T(8,128)S(1)}, u32[]{:S(2)}, u32[]{:S(2)}) collective-permute-start(f32[224,128]{1,0:T(8,128)S(1)} %add.110), channel_id=1, source_target_pairs={{0,8},{1,3},{2,10},{3,1},{4,12},{5,7},{6,14},{7,5},{8,0},{9,11},{1... | collective-permute-start | bytes 344072 | tf_op jit(solution)/shard_map/ppermute | solution.py:71
  52.4 7.0 %collective-permute-start.15 = (f32[224,128]{1,0:T(8,128)S(1)}, f32[224,128]{1,0:T(8,128)S(1)}, u32[]{:S(2)}, u32[]{:S(2)}) collective-permute-start(f32[224,128]{1,0:T(8,128)S(1)} %add.111), channel_id=1, source_target_pairs={{0,16},{1,5},{2,18},{3,7},{4,20},{5,1},{6,22},{7,3},{8,24},{9,13},... | collective-permute-start | bytes 344072 | tf_op jit(solution)/shard_map/ppermute | solution.py:71
  59.4 1.4 %collective-permute-start.16 = (f32[224,128]{1,0:T(8,128)S(1)}, f32[224,128]{1,0:T(8,128)S(1)}, u32[]{:S(2)}, u32[]{:S(2)}) collective-permute-start(f32[224,128]{1,0:T(8,128)S(1)} %add.112), channel_id=1, source_target_pairs={{0,1},{1,0},{2,3},{3,2},{4,5},{5,4},{6,7},{7,6},{8,9},{9,8},{10,11... | collective-permute-start | bytes 344072 | tf_op jit(solution)/shard_map/ppermute | solution.py:72
  (1 other events, 0.9 us)

commit v13 on v12

--- a/solution.py
+++ b/solution.py
@@ -188,10 +188,10 @@
     grad_bias = jnp.sum(head_grad.astype(jnp.float32), axis=(1, 2, 3)) * norm_factor
     back_second = jnp.einsum("oi,oxzy->ixzy", w_out, head_grad, preferred_element_type=jnp.float32)
     grad_second_pre = (back_second * silu_slope(second_wide)).astype(jnp.bfloat16)
-    second_padded = extended(grad_second_pre, (("sky", 1), ("los", 2)), 1)
+    second_padded = extended(grad_second_pre, (("los", 2), ("sky", 1)), 1)
     back_first = spread_local(w_second, second_padded, shape)
     grad_first_pre = (back_first * silu_slope(first_wide)).astype(jnp.bfloat16)
-    first_padded = extended(grad_first_pre, (("sky", 1), ("los", 2)), 1)
+    first_padded = extended(grad_first_pre, (("los", 2), ("sky", 1)), 1)
     grad_features = spread_local(w_first, first_padded, shape).astype(jnp.bfloat16)
     hidden_first = jax.nn.silu(first_wide).astype(jnp.bfloat16)
     grad_second = taps_from_halo(second_padded, hidden_first)

time: 64.1 us -> 64.7 us (level)
  starting transfers between devices: 21.2 us -> 22.1 us
    ppermute x4, starting transfers between devices: 3.44 us -> 5.54 us  [split_sum(): keep = keep + lax.ppermute(keep, index_axes, pairs)]
    ppermute x4, waiting for transfers between devices: 17.3 us -> 15.2 us  [split_sum(): keep = keep + lax.ppermute(keep, index_axes, pairs)]
    ppermute x1, starting transfers between devices: 1.38 us -> 0.19 us  [split_sum(): keep = keep + lax.ppermute(send, index_axes, partner)]
    ppermute x4, waiting for transfers between devices: 6.5 us -> 7.48 us  [extended(): lax.ppermute(lax.slice_in_dim(block, block.shape[dim] - width, None, axis...]
  transfers between devices with their start and end apart: 17 -> 17, of which waited for: 11 -> 12; matrix products, arithmetic and copies ran while one was open for 8% -> 8% of each run, Pallas kernels for 0% -> 0%
where the time goes in v13:
time: 64.7 us; the launch traced here: 64.5 us
  waiting for transfers between devices  26 us (40%)
  starting transfers between devices  22.1 us (34%)
  local copies, waits for them, and re-layouts  7.68 us (12%)
  matrix products  4.25 us (7%)
  other arithmetic  3.26 us (5%)
  between operations  1.23 us (2%)
    ppermute x4, waiting for transfers between devices, split_sum(): keep = keep + lax.ppermute(keep, index_axes, pairs)  15.2 us
    ppermute x4, starting transfers between devices, extended(): lax.ppermute(lax.slice_in_dim(block, 0, width, axis=dim), axis, backward)  10.7 us
    ppermute x4, waiting for transfers between devices, extended(): lax.ppermute(lax.slice_in_dim(block, block.shape[dim] - width, None, axis...  7.48 us
    ppermute x4, starting transfers between devices, split_sum(): keep = keep + lax.ppermute(keep, index_axes, pairs)  5.54 us
    ppermute x3, starting transfers between devices, quad_sum(): lax.ppermute(value, axis, [(i, i ^ mask) for i in range(count)])  3.2 us
    reshape x3, local copies, waits for them, and re-layouts, unpack_rows(): parts.append(block.reshape(shape))  2.5 us
    ppermute x4, starting transfers between devices, extended(): lax.ppermute(lax.slice_in_dim(block, block.shape[dim] - width, None, axis...  2.39 us
    dot_general x2, matrix products, taps_from_halo(): jnp.einsum('toxzy,sixzy->tsoi', windows, rolled, preferred_element_type=j...  2.12 us
  transfers between devices with their start and end apart: 17, of which 12 were waited for; matrix products, arithmetic and copies ran while one was open for 8% of the time, Pallas kernels for 0%

profile of v13, /device:TPU:0, one launch (start us, length us, event | category | flops | bytes accessed | tf_op | source)
XLA Modules:
  0.0 64.5 jit_solution(17220859297005091949)
XLA Ops:
  0.7 1.0 %fusion.22 = bf16[32,2,8,128]{3,0,2,1:T(8,128)(2,1)S(1)} fusion(bf16[32,2,8,128]{3,2,1,0:T(8,128)(2,1)} %param.11), kind=kLoop, calls=%fused_computation.36 | loop fusion | flops 393216 | bytes 262144 | tf_op jit(solution)/shard_map/convert_element_type | solution.py:162
  3.3 3.0 %collective-permute-start.1 = (f32[2,2,128]{2,1,0:T(2,128)S(1)}, f32[2,2,128]{2,1,0:T(2,128)S(1)}, u32[]{:S(2)}, u32[]{:S(2)}) collective-permute-start(f32[2,2,128]{2,1,0:T(2,128)S(1)} %pad_maximum_fusion.12), channel_id=1, source_target_pairs={{0,2},{1,3},{2,0},{3,1},{4,6},{5,7},{6,4},{7,5},{8,10},{9,11},{10,... | collective-permute-start | bytes 6152 | tf_op jit(solution)/shard_map/ppermute | solution.py:47
  6.5 1.1 %fusion.91 = (bf16[32,2,8,127]{3,2,1,0:T(8,128)(2,1)S(1)}, bf16[32,2,8,127]{3,2,1,0:T(8,128)(2,1)S(1)}) fusion(bf16[32,2,8,128]{3,2,1,0:T(8,128)(2,1)} %param.9), kind=kLoop, calls=%fused_computation.169 | loop fusion | bytes 520192 | tf_op jit(solution)/shard_map/jit(_roll_static)/slice | solution.py:145
  8.2 1.1 %collective-permute-done.2 = f32[2,2,128]{2,1,0:T(2,128)S(1)} collective-permute-done((f32[2,2,128]{2,1,0:T(2,128)S(1)}, f32[2,2,128]{2,1,0:T(2,128)S(1)}, u32[]{:S(2)}, u32[]{:S(2)}) %collective-permute-start.2) | collective-permute-done | bytes 2080 | tf_op jit(solution)/shard_map/ppermute | solution.py:47
  10.1 1.7 %collective-permute-start.4 = (bf16[32,2,1,128]{3,0,2,1:T(8,128)(2,1)S(1)}, bf16[32,2,1,128]{3,0,2,1:T(8,128)(2,1)S(1)}, u32[]{:S(2)}, u32[]{:S(2)}) collective-permute-start(bf16[32,2,1,128]{3,0,2,1:T(8,128)(2,1)S(1)} %get-tuple-element.51), channel_id=1, source_target_pairs={{1,0},{2,1},{3,2},{0,3},{5,4},{6,5},{7,6},{4,7},{9,8},{10,9},{11,1... | collective-permute-start | bytes 49160 | tf_op jit(solution)/shard_map/ppermute | solution.py:18
  11.8 1.4 %collective-permute-done.3 = bf16[32,2,1,128]{3,0,2,1:T(8,128)(2,1)S(1)} collective-permute-done((bf16[32,2,1,128]{3,0,2,1:T(8,128)(2,1)S(1)}, bf16[32,2,1,128]{3,0,2,1:T(8,128)(2,1)S(1)}, u32[]{:S(2)}, u32[]{:S(2)}) %collective-permute-start.3) | collective-permute-done | bytes 16416 | tf_op jit(solution)/shard_map/ppermute | solution.py:15
  13.3 1.6 %collective-permute-start.6 = (bf16[32,1,10,128]{3,0,2,1:T(8,128)(2,1)S(1)}, bf16[32,1,10,128]{3,0,2,1:T(8,128)(2,1)S(1)}, u32[]{:S(2)}, u32[]{:S(2)}) collective-permute-start(bf16[32,1,10,128]{3,0,2,1:T(8,128)(2,1)S(1)} %get-tuple-element.36), channel_id=1, source_target_pairs={{0,4},{4,8},{8,12},{12,16},{16,20},{20,24},{24,28},{28,0},{1,5},{5... | collective-permute-start | bytes 245768 | tf_op jit(solution)/shard_map/ppermute | solution.py:15
  14.9 3.2 %collective-permute-start.5 = (bf16[32,1,10,128]{3,0,2,1:T(8,128)(2,1)S(1)}, bf16[32,1,10,128]{3,0,2,1:T(8,128)(2,1)S(1)}, u32[]{:S(2)}, u32[]{:S(2)}) collective-permute-start(bf16[32,1,10,128]{3,0,2,1:T(8,128)(2,1)S(1)} %get-tuple-element.37), channel_id=1, source_target_pairs={{4,0},{8,4},{12,8},{16,12},{20,16},{24,20},{28,24},{0,28},{5,1},{9... | collective-permute-start | bytes 245768 | tf_op jit(solution)/shard_map/ppermute | solution.py:18
  18.1 3.1 %collective-permute-done.6 = bf16[32,1,10,128]{3,0,2,1:T(8,128)(2,1)S(1)} collective-permute-done((bf16[32,1,10,128]{3,0,2,1:T(8,128)(2,1)S(1)}, bf16[32,1,10,128]{3,0,2,1:T(8,128)(2,1)S(1)}, u32[]{:S(2)}, u32[]{:S(2)}) %collective-permute-start.6) | collective-permute-done | bytes 81952 | tf_op jit(solution)/shard_map/ppermute | solution.py:15
  24.0 1.7 %collective-permute-start.8 = (bf16[32,2,1,128]{3,0,2,1:T(8,128)(2,1)S(1)}, bf16[32,2,1,128]{3,0,2,1:T(8,128)(2,1)S(1)}, u32[]{:S(2)}, u32[]{:S(2)}) collective-permute-start(bf16[32,2,1,128]{3,0,2,1:T(8,128)(2,1)S(1)} %get-tuple-element.49), channel_id=1, source_target_pairs={{1,0},{2,1},{3,2},{0,3},{5,4},{6,5},{7,6},{4,7},{9,8},{10,9},{11,1... | collective-permute-start | bytes 49160 | tf_op jit(solution)/shard_map/ppermute | solution.py:18
  25.9 1.2 %collective-permute-done.7 = bf16[32,2,1,128]{3,0,2,1:T(8,128)(2,1)S(1)} collective-permute-done((bf16[32,2,1,128]{3,0,2,1:T(8,128)(2,1)S(1)}, bf16[32,2,1,128]{3,0,2,1:T(8,128)(2,1)S(1)}, u32[]{:S(2)}, u32[]{:S(2)}) %collective-permute-start.7) | collective-permute-done | bytes 16416 | tf_op jit(solution)/shard_map/ppermute | solution.py:15
  27.9 4.1 %collective-permute-start.9 = (bf16[32,1,10,128]{3,0,2,1:T(8,128)(2,1)S(1)}, bf16[32,1,10,128]{3,0,2,1:T(8,128)(2,1)S(1)}, u32[]{:S(2)}, u32[]{:S(2)}) collective-permute-start(bf16[32,1,10,128]{3,0,2,1:T(8,128)(2,1)S(1)} %get-tuple-element.33), channel_id=1, source_target_pairs={{4,0},{8,4},{12,8},{16,12},{20,16},{24,20},{28,24},{0,28},{5,1},{9... | collective-permute-start | bytes 245768 | tf_op jit(solution)/shard_map/ppermute | solution.py:18
  32.0 1.1 %fusion.3 = f32[9,3,32,32]{2,3,0,1:T(8,128)S(1)} fusion(bf16[9,32,2,8,128]{4,1,3,2,0:T(8,128)(2,1)S(1)} %fusion.50, bf16[1,32,2,8,128]{4,1,3,2,0:T(8,128)(2,1)S(1)} %maximum_bitcast_fusion.5, bf16[1,32,2,8,128]{4,1,3,2,0:T(8,128)(2,1)S(1)} %bitcast.252, bf16[1,32,2,8,128]{4,1,3,2,0:T(8,128)(2,1)S(1)} %maximum_bitcast_fusion.4), kind=kOutput, calls=%fused_computation.7 | convolution fusion | flops 114453504 | bytes 1683456 | tf_op jit(solution)/shard_map/toxzy,sixzy->tsoi/dot_general | solution.py:146
  33.4 1.7 %collective-permute-done.10 = bf16[32,1,10,128]{3,0,2,1:T(8,128)(2,1)S(1)} collective-permute-done((bf16[32,1,10,128]{3,0,2,1:T(8,128)(2,1)S(1)}, bf16[32,1,10,128]{3,0,2,1:T(8,128)(2,1)S(1)}, u32[]{:S(2)}, u32[]{:S(2)}) %collective-permute-start.10) | collective-permute-done | bytes 81952 | tf_op jit(solution)/shard_map/ppermute | solution.py:15
  35.4 1.1 %fusion.1 = f32[9,3,32,32]{2,3,0,1:T(8,128)S(1)} fusion(bf16[1,32,2,8,128]{4,1,3,2,0:T(8,128)(2,1)S(1)} %get-tuple-element.60, bf16[1,32,2,8,128]{4,1,3,2,0:T(8,128)(2,1)S(1)} %bitcast.258, bf16[1,32,2,8,128]{4,1,3,2,0:T(8,128)(2,1)S(1)} %get-tuple-element.59, bf16[9,32,2,8,128]{4,1,3,2,0:T(8,128)(2,1)S(1)} %fusion.40), kind=kOutput, calls=%fused_computation.4 | convolution fusion | flops 114453504 | bytes 1683456 | tf_op jit(solution)/shard_map/toxzy,sixzy->tsoi/dot_general | solution.py:146
  37.1 1.2 %collective-permute-done.11 = f32[224,128]{1,0:T(8,128)S(1)} collective-permute-done((f32[224,128]{1,0:T(8,128)S(1)}, f32[224,128]{1,0:T(8,128)S(1)}, u32[]{:S(2)}, u32[]{:S(2)}) %collective-permute-start.11) | collective-permute-done | bytes 114720 | tf_op jit(solution)/shard_map/ppermute | solution.py:66
  38.4 1.1 %collective-permute-start.12 = (f32[224,128]{1,0:T(8,128)S(1)}, f32[224,128]{1,0:T(8,128)S(1)}, u32[]{:S(2)}, u32[]{:S(2)}) collective-permute-start(f32[224,128]{1,0:T(8,128)S(1)} %select_add_fusion), channel_id=1, source_target_pairs={{0,2},{1,9},{2,0},{3,11},{4,6},{5,13},{6,4},{7,15},{8,10},{9,1},{1... | collective-permute-start | bytes 344072 | tf_op jit(solution)/shard_map/ppermute | solution.py:71
  39.6 3.7 %collective-permute-done.12 = f32[224,128]{1,0:T(8,128)S(1)} collective-permute-done((f32[224,128]{1,0:T(8,128)S(1)}, f32[224,128]{1,0:T(8,128)S(1)}, u32[]{:S(2)}, u32[]{:S(2)}) %collective-permute-start.12) | collective-permute-done | bytes 114720 | tf_op jit(solution)/shard_map/ppermute | solution.py:71
  44.1 4.0 %collective-permute-done.13 = f32[224,128]{1,0:T(8,128)S(1)} collective-permute-done((f32[224,128]{1,0:T(8,128)S(1)}, f32[224,128]{1,0:T(8,128)S(1)}, u32[]{:S(2)}, u32[]{:S(2)}) %collective-permute-start.13) | collective-permute-done | bytes 114720 | tf_op jit(solution)/shard_map/ppermute | solution.py:71
  48.2 1.3 %collective-permute-start.14 = (f32[224,128]{1,0:T(8,128)S(1)}, f32[224,128]{1,0:T(8,128)S(1)}, u32[]{:S(2)}, u32[]{:S(2)}) collective-permute-start(f32[224,128]{1,0:T(8,128)S(1)} %add.110), channel_id=1, source_target_pairs={{0,8},{1,3},{2,10},{3,1},{4,12},{5,7},{6,14},{7,5},{8,0},{9,11},{1... | collective-permute-start | bytes 344072 | tf_op jit(solution)/shard_map/ppermute | solution.py:71
  49.9 3.1 %collective-permute-done.14 = f32[224,128]{1,0:T(8,128)S(1)} collective-permute-done((f32[224,128]{1,0:T(8,128)S(1)}, f32[224,128]{1,0:T(8,128)S(1)}, u32[]{:S(2)}, u32[]{:S(2)}) %collective-permute-start.14) | collective-permute-done | bytes 114720 | tf_op jit(solution)/shard_map/ppermute | solution.py:71
  53.1 2.3 %collective-permute-start.15 = (f32[224,128]{1,0:T(8,128)S(1)}, f32[224,128]{1,0:T(8,128)S(1)}, u32[]{:S(2)}, u32[]{:S(2)}) collective-permute-start(f32[224,128]{1,0:T(8,128)S(1)} %add.111), channel_id=1, source_target_pairs={{0,16},{1,5},{2,18},{3,7},{4,20},{5,1},{6,22},{7,3},{8,24},{9,13},... | collective-permute-start | bytes 344072 | tf_op jit(solution)/shard_map/ppermute | solution.py:71
  55.7 4.4 %collective-permute-done.15 = f32[224,128]{1,0:T(8,128)S(1)} collective-permute-done((f32[224,128]{1,0:T(8,128)S(1)}, f32[224,128]{1,0:T(8,128)S(1)}, u32[]{:S(2)}, u32[]{:S(2)}) %collective-permute-start.15) | collective-permute-done | bytes 114720 | tf_op jit(solution)/shard_map/ppermute | solution.py:71
  62.7 0.9 %reshape.79 = f32[3,3,3,32,32]{4,3,2,1,0:T(8,128)} reshape(f32[216,128]{1,0:T(8,128)S(1)} %get-tuple-element.28) | data formatting | bytes 221184 | tf_op jit(solution)/shard_map/reshape | solution.py:105
  (112 shorter events, 13.1 us)
Async XLA Ops:
  0.6 21.4 %copy-start = (bf16[3,3,3,32,32]{4,3,2,1,0:T(8,128)(2,1)S(1)}, bf16[3,3,3,32,32]{4,3,2,1,0:T(8,128)(2,1)}, u32[]{:S(2)}) copy-start(bf16[3,3,3,32,32]{4,3,2,1,0:T(8,128)(2,1)} %param.13) | copy-start | bytes 165892
  0.6 7.0 %copy-start.1 = (bf16[32,2,8,128]{3,2,1,0:T(8,128)(2,1)S(1)}, bf16[32,2,8,128]{3,2,1,0:T(8,128)(2,1)}, u32[]{:S(2)}) copy-start(bf16[32,2,8,128]{3,2,1,0:T(8,128)(2,1)} %param.9) | copy-start | bytes 393220
  3.3 4.9 %collective-permute-start.1 = (f32[2,2,128]{2,1,0:T(2,128)S(1)}, f32[2,2,128]{2,1,0:T(2,128)S(1)}, u32[]{:S(2)}, u32[]{:S(2)}) collective-permute-start(f32[2,2,128]{2,1,0:T(2,128)S(1)} %pad_maximum_fusion.12), channel_id=1, source_target_pairs={{0,2},{1,3},{2,0},{3,1},{4,6},{5,7},{6,4},{7,5},{8,10},{9,11},{10,... | collective-permute-start | bytes 6152 | tf_op jit(solution)/shard_map/ppermute | solution.py:47
  6.3 3.0 %collective-permute-start.2 = (f32[2,2,128]{2,1,0:T(2,128)S(1)}, f32[2,2,128]{2,1,0:T(2,128)S(1)}, u32[]{:S(2)}, u32[]{:S(2)}) collective-permute-start(f32[2,2,128]{2,1,0:T(2,128)S(1)} %pad_maximum_fusion.12), channel_id=1, source_target_pairs={{0,3},{1,2},{2,1},{3,0},{4,7},{5,6},{6,5},{7,4},{8,11},{9,10},{10,... | collective-permute-start | bytes 6152 | tf_op jit(solution)/shard_map/ppermute | solution.py:47
  6.3 3.0 %collective-permute-start = (f32[2,2,128]{2,1,0:T(2,128)S(1)}, f32[2,2,128]{2,1,0:T(2,128)S(1)}, u32[]{:S(2)}, u32[]{:S(2)}) collective-permute-start(f32[2,2,128]{2,1,0:T(2,128)S(1)} %pad_maximum_fusion.12), channel_id=1, source_target_pairs={{0,1},{1,0},{2,3},{3,2},{4,5},{5,4},{6,7},{7,6},{8,9},{9,8},{10,11... | collective-permute-start | bytes 6152 | tf_op jit(solution)/shard_map/ppermute | solution.py:47
  7.7 1.6 %copy-start.6 = (f32[2,128]{1,0:T(2,128)S(1)}, f32[2,128]{1,0:T(2,128)}, u32[]{:S(2)}) copy-start(f32[2,128]{1,0:T(2,128)} %param.16) | copy-start | bytes 3076
  7.7 1.6 %copy-start.7 = (f32[2,128]{1,0:T(2,128)S(1)}, f32[2,128]{1,0:T(2,128)}, u32[]{:S(2)}) copy-start(f32[2,128]{1,0:T(2,128)} %param.17) | copy-start | bytes 3076
  7.7 1.9 %copy-start.3 = (bf16[32,2,8,128]{3,2,1,0:T(8,128)(2,1)S(1)}, bf16[32,2,8,128]{3,2,1,0:T(8,128)(2,1)}, u32[]{:S(2)}) copy-start(bf16[32,2,8,128]{3,2,1,0:T(8,128)(2,1)} %param.11) | copy-start | bytes 393220
  7.8 1.9 %copy-start.5 = (bf16[3,32]{1,0:T(4,128)(2,1)S(1)}, bf16[3,32]{1,0:T(4,128)(2,1)}, u32[]{:S(2)}) copy-start(bf16[3,32]{1,0:T(4,128)(2,1)} %param.14) | copy-start | bytes 580
  10.0 3.2 %collective-permute-start.3 = (bf16[32,2,1,128]{3,0,2,1:T(8,128)(2,1)S(1)}, bf16[32,2,1,128]{3,0,2,1:T(8,128)(2,1)S(1)}, u32[]{:S(2)}, u32[]{:S(2)}) collective-permute-start(bf16[32,2,1,128]{3,0,2,1:T(8,128)(2,1)S(1)} %get-tuple-element.50), channel_id=1, source_target_pairs={{0,1},{1,2},{2,3},{3,0},{4,5},{5,6},{6,7},{7,4},{8,9},{9,10},{10,1... | collective-permute-start | bytes 49160 | tf_op jit(solution)/shard_map/ppermute | solution.py:15
  10.1 3.2 %collective-permute-start.4 = (bf16[32,2,1,128]{3,0,2,1:T(8,128)(2,1)S(1)}, bf16[32,2,1,128]{3,0,2,1:T(8,128)(2,1)S(1)}, u32[]{:S(2)}, u32[]{:S(2)}) collective-permute-start(bf16[32,2,1,128]{3,0,2,1:T(8,128)(2,1)S(1)} %get-tuple-element.51), channel_id=1, source_target_pairs={{1,0},{2,1},{3,2},{0,3},{5,4},{6,5},{7,6},{4,7},{9,8},{10,9},{11,1... | collective-permute-start | bytes 49160 | tf_op jit(solution)/shard_map/ppermute | solution.py:18
  13.3 7.9 %collective-permute-start.6 = (bf16[32,1,10,128]{3,0,2,1:T(8,128)(2,1)S(1)}, bf16[32,1,10,128]{3,0,2,1:T(8,128)(2,1)S(1)}, u32[]{:S(2)}, u32[]{:S(2)}) collective-permute-start(bf16[32,1,10,128]{3,0,2,1:T(8,128)(2,1)S(1)} %get-tuple-element.36), channel_id=1, source_target_pairs={{0,4},{4,8},{8,12},{12,16},{16,20},{20,24},{24,28},{28,0},{1,5},{5... | collective-permute-start | bytes 245768 | tf_op jit(solution)/shard_map/ppermute | solution.py:15
  14.9 6.9 %collective-permute-start.5 = (bf16[32,1,10,128]{3,0,2,1:T(8,128)(2,1)S(1)}, bf16[32,1,10,128]{3,0,2,1:T(8,128)(2,1)S(1)}, u32[]{:S(2)}, u32[]{:S(2)}) collective-permute-start(bf16[32,1,10,128]{3,0,2,1:T(8,128)(2,1)S(1)} %get-tuple-element.37), channel_id=1, source_target_pairs={{4,0},{8,4},{12,8},{16,12},{20,16},{24,20},{28,24},{0,28},{5,1},{9... | collective-permute-start | bytes 245768 | tf_op jit(solution)/shard_map/ppermute | solution.py:18
  23.9 3.2 %collective-permute-start.7 = (bf16[32,2,1,128]{3,0,2,1:T(8,128)(2,1)S(1)}, bf16[32,2,1,128]{3,0,2,1:T(8,128)(2,1)S(1)}, u32[]{:S(2)}, u32[]{:S(2)}) collective-permute-start(bf16[32,2,1,128]{3,0,2,1:T(8,128)(2,1)S(1)} %get-tuple-element.48), channel_id=1, source_target_pairs={{0,1},{1,2},{2,3},{3,0},{4,5},{5,6},{6,7},{7,4},{8,9},{9,10},{10,1... | collective-permute-start | bytes 49160 | tf_op jit(solution)/shard_map/ppermute | solution.py:15
  24.0 3.2 %collective-permute-start.8 = (bf16[32,2,1,128]{3,0,2,1:T(8,128)(2,1)S(1)}, bf16[32,2,1,128]{3,0,2,1:T(8,128)(2,1)S(1)}, u32[]{:S(2)}, u32[]{:S(2)}) collective-permute-start(bf16[32,2,1,128]{3,0,2,1:T(8,128)(2,1)S(1)} %get-tuple-element.49), channel_id=1, source_target_pairs={{1,0},{2,1},{3,2},{0,3},{5,4},{6,5},{7,6},{4,7},{9,8},{10,9},{11,1... | collective-permute-start | bytes 49160 | tf_op jit(solution)/shard_map/ppermute | solution.py:18
  27.2 7.9 %collective-permute-start.10 = (bf16[32,1,10,128]{3,0,2,1:T(8,128)(2,1)S(1)}, bf16[32,1,10,128]{3,0,2,1:T(8,128)(2,1)S(1)}, u32[]{:S(2)}, u32[]{:S(2)}) collective-permute-start(bf16[32,1,10,128]{3,0,2,1:T(8,128)(2,1)S(1)} %get-tuple-element.32), channel_id=1, source_target_pairs={{0,4},{4,8},{8,12},{12,16},{16,20},{20,24},{24,28},{28,0},{1,5},{5... | collective-permute-start | bytes 245768 | tf_op jit(solution)/shard_map/ppermute | solution.py:15
  27.9 7.2 %collective-permute-start.9 = (bf16[32,1,10,128]{3,0,2,1:T(8,128)(2,1)S(1)}, bf16[32,1,10,128]{3,0,2,1:T(8,128)(2,1)S(1)}, u32[]{:S(2)}, u32[]{:S(2)}) collective-permute-start(bf16[32,1,10,128]{3,0,2,1:T(8,128)(2,1)S(1)} %get-tuple-element.33), channel_id=1, source_target_pairs={{4,0},{8,4},{12,8},{16,12},{20,16},{24,20},{28,24},{0,28},{5,1},{9... | collective-permute-start | bytes 245768 | tf_op jit(solution)/shard_map/ppermute | solution.py:18
  36.7 12.8 %copy-start.2 = (bf16[3,3,3,32,32]{4,3,2,1,0:T(8,128)(2,1)S(1)}, bf16[3,3,3,32,32]{4,3,2,1,0:T(8,128)(2,1)}, u32[]{:S(2)}) copy-start(bf16[3,3,3,32,32]{4,3,2,1,0:T(8,128)(2,1)} %param.12) | copy-start | bytes 165892
  36.9 1.4 %collective-permute-start.11 = (f32[224,128]{1,0:T(8,128)S(1)}, f32[224,128]{1,0:T(8,128)S(1)}, u32[]{:S(2)}, u32[]{:S(2)}) collective-permute-start(f32[224,128]{1,0:T(8,128)S(1)} %fusion.61), channel_id=1, source_target_pairs={{0,1},{1,0},{2,3},{3,2},{4,5},{5,4},{6,7},{7,6},{8,9},{9,8},{10,11... | collective-permute-start | bytes 344072 | tf_op jit(solution)/shard_map/ppermute | solution.py:66
  38.4 4.9 %collective-permute-start.12 = (f32[224,128]{1,0:T(8,128)S(1)}, f32[224,128]{1,0:T(8,128)S(1)}, u32[]{:S(2)}, u32[]{:S(2)}) collective-permute-start(f32[224,128]{1,0:T(8,128)S(1)} %select_add_fusion), channel_id=1, source_target_pairs={{0,2},{1,9},{2,0},{3,11},{4,6},{5,13},{6,4},{7,15},{8,10},{9,1},{1... | collective-permute-start | bytes 344072 | tf_op jit(solution)/shard_map/ppermute | solution.py:71
  43.3 4.9 %collective-permute-start.13 = (f32[224,128]{1,0:T(8,128)S(1)}, f32[224,128]{1,0:T(8,128)S(1)}, u32[]{:S(2)}, u32[]{:S(2)}) collective-permute-start(f32[224,128]{1,0:T(8,128)S(1)} %add.109), channel_id=1, source_target_pairs={{0,4},{1,17},{2,6},{3,19},{4,0},{5,21},{6,2},{7,23},{8,12},{9,25},... | collective-permute-start | bytes 344072 | tf_op jit(solution)/shard_map/ppermute | solution.py:71
  48.2 4.9 %collective-permute-start.14 = (f32[224,128]{1,0:T(8,128)S(1)}, f32[224,128]{1,0:T(8,128)S(1)}, u32[]{:S(2)}, u32[]{:S(2)}) collective-permute-start(f32[224,128]{1,0:T(8,128)S(1)} %add.110), channel_id=1, source_target_pairs={{0,8},{1,3},{2,10},{3,1},{4,12},{5,7},{6,14},{7,5},{8,0},{9,11},{1... | collective-permute-start | bytes 344072 | tf_op jit(solution)/shard_map/ppermute | solution.py:71
  53.1 7.0 %collective-permute-start.15 = (f32[224,128]{1,0:T(8,128)S(1)}, f32[224,128]{1,0:T(8,128)S(1)}, u32[]{:S(2)}, u32[]{:S(2)}) collective-permute-start(f32[224,128]{1,0:T(8,128)S(1)} %add.111), channel_id=1, source_target_pairs={{0,16},{1,5},{2,18},{3,7},{4,20},{5,1},{6,22},{7,3},{8,24},{9,13},... | collective-permute-start | bytes 344072 | tf_op jit(solution)/shard_map/ppermute | solution.py:71
  60.1 1.4 %collective-permute-start.16 = (f32[224,128]{1,0:T(8,128)S(1)}, f32[224,128]{1,0:T(8,128)S(1)}, u32[]{:S(2)}, u32[]{:S(2)}) collective-permute-start(f32[224,128]{1,0:T(8,128)S(1)} %add.112), channel_id=1, source_target_pairs={{0,1},{1,0},{2,3},{3,2},{4,5},{5,4},{6,7},{7,6},{8,9},{9,8},{10,11... | collective-permute-start | bytes 344072 | tf_op jit(solution)/shard_map/ppermute | solution.py:72
  (1 other events, 0.9 us)

commit v14 on v12

--- a/solution.py
+++ b/solution.py
@@ -65,10 +65,15 @@
     partner = [(i, i ^ 1) for i in range(total)]
     keep = keep + lax.ppermute(send, index_axes, partner)
     bits = [1 << b for b in range(1, total.bit_length() - 1)]
-    turned = bits[len(bits) // 2 :] + bits[: len(bits) // 2]
-    for lower_bit, upper_bit in zip(bits, turned):
-        pairs = [(i, i ^ (upper_bit if i & 1 else lower_bit)) for i in range(total)]
-        keep = keep + lax.ppermute(keep, index_axes, pairs)
+    if len(bits) >= 2:
+        near, far, both = (
+            lax.ppermute(keep, index_axes, [(i, i ^ mask) for i in range(total)])
+            for mask in (bits[0], bits[1], bits[0] | bits[1])
+        )
+        keep = (keep + near) + (far + both)
+        bits = bits[2:]
+    for bit in bits:
+        keep = keep + lax.ppermute(keep, index_axes, [(i, i ^ bit) for i in range(total)])
     other = lax.ppermute(keep, index_axes, partner)
     return jnp.where(
         upper, jnp.concatenate((other, keep)), jnp.concatenate((keep, other))

time: 64.1 us -> 63.7 us (level)
  waiting for transfers between devices: 26.3 us -> 21.4 us
  starting transfers between devices: 21.2 us -> 25.7 us
    ppermute x4 -> x5, waiting for transfers between devices: 17.3 us -> 12.5 us  [the longest x2 7.83 us: split_sum(): lax.ppermute(keep, index_axes, [(i, i ^ bit) for i in range(total)])]
    ppermute x4 -> x5, starting transfers between devices: 3.44 us -> 7.93 us  [the longest x2 4.36 us: split_sum(): lax.ppermute(keep, index_axes, [(i, i ^ bit) for i in range(total)])]
  transfers between devices with their start and end apart: 17 -> 18, of which waited for: 11 -> 11; matrix products, arithmetic and copies ran while one was open for 8% -> 8% of each run, Pallas kernels for 0% -> 0%
where the time goes in v14:
time: 63.7 us; the launch traced here: 63.5 us
  starting transfers between devices  25.7 us (40%)
  waiting for transfers between devices  21.4 us (34%)
  local copies, waits for them, and re-layouts  7.66 us (12%)
  matrix products  4.25 us (7%)
  other arithmetic  3.26 us (5%)
  between operations  1.2 us (2%)
    ppermute x4, starting transfers between devices, extended(): lax.ppermute(lax.slice_in_dim(block, 0, width, axis=dim), axis, backward)  10.1 us
    ppermute x2, waiting for transfers between devices, split_sum(): lax.ppermute(keep, index_axes, [(i, i ^ bit) for i in range(total)])  7.83 us
    ppermute x4, waiting for transfers between devices, extended(): lax.ppermute(lax.slice_in_dim(block, block.shape[dim] - width, None, axis...  6.5 us
    ppermute x3, waiting for transfers between devices, split_sum(): lax.ppermute(keep, index_axes, [(i, i ^ mask) for i in range(total)])  4.64 us
    ppermute x2, starting transfers between devices, split_sum(): lax.ppermute(keep, index_axes, [(i, i ^ bit) for i in range(total)])  4.36 us
    ppermute x3, starting transfers between devices, split_sum(): lax.ppermute(keep, index_axes, [(i, i ^ mask) for i in range(total)])  3.57 us
    ppermute x3, starting transfers between devices, quad_sum(): lax.ppermute(value, axis, [(i, i ^ mask) for i in range(count)])  3.2 us
    ppermute x4, starting transfers between devices, extended(): lax.ppermute(lax.slice_in_dim(block, block.shape[dim] - width, None, axis...  3.01 us
  transfers between devices with their start and end apart: 18, of which 11 were waited for; matrix products, arithmetic and copies ran while one was open for 8% of the time, Pallas kernels for 0%

profile of v14, /device:TPU:0, one launch (start us, length us, event | category | flops | bytes accessed | tf_op | source)
XLA Modules:
  0.0 63.5 jit_solution(10345693872947037646)
XLA Ops:
  0.7 1.0 %fusion.22 = bf16[32,2,8,128]{3,0,2,1:T(8,128)(2,1)S(1)} fusion(bf16[32,2,8,128]{3,2,1,0:T(8,128)(2,1)} %param.11), kind=kLoop, calls=%fused_computation.40 | loop fusion | flops 393216 | bytes 262144 | tf_op jit(solution)/shard_map/convert_element_type | solution.py:167
  3.3 3.0 %collective-permute-start.1 = (f32[2,2,128]{2,1,0:T(2,128)S(1)}, f32[2,2,128]{2,1,0:T(2,128)S(1)}, u32[]{:S(2)}, u32[]{:S(2)}) collective-permute-start(f32[2,2,128]{2,1,0:T(2,128)S(1)} %pad_maximum_fusion.16), channel_id=1, source_target_pairs={{0,2},{1,3},{2,0},{3,1},{4,6},{5,7},{6,4},{7,5},{8,10},{9,11},{10,... | collective-permute-start | bytes 6152 | tf_op jit(solution)/shard_map/ppermute | solution.py:47
  6.5 1.1 %fusion.89 = (bf16[32,2,8,127]{3,2,1,0:T(8,128)(2,1)S(1)}, bf16[32,2,8,127]{3,2,1,0:T(8,128)(2,1)S(1)}) fusion(bf16[32,2,8,128]{3,2,1,0:T(8,128)(2,1)} %param.9), kind=kLoop, calls=%fused_computation.172 | loop fusion | bytes 520192 | tf_op jit(solution)/shard_map/jit(_roll_static)/slice | solution.py:150
  8.2 1.1 %collective-permute-done.2 = f32[2,2,128]{2,1,0:T(2,128)S(1)} collective-permute-done((f32[2,2,128]{2,1,0:T(2,128)S(1)}, f32[2,2,128]{2,1,0:T(2,128)S(1)}, u32[]{:S(2)}, u32[]{:S(2)}) %collective-permute-start.2) | collective-permute-done | bytes 2080 | tf_op jit(solution)/shard_map/ppermute | solution.py:47
  10.0 1.6 %collective-permute-start.3 = (bf16[32,1,8,128]{3,0,2,1:T(8,128)(2,1)S(1)}, bf16[32,1,8,128]{3,0,2,1:T(8,128)(2,1)S(1)}, u32[]{:S(2)}, u32[]{:S(2)}) collective-permute-start(bf16[32,1,8,128]{3,0,2,1:T(8,128)(2,1)S(1)} %get-tuple-element.50), channel_id=1, source_target_pairs={{0,4},{4,8},{8,12},{12,16},{16,20},{20,24},{24,28},{28,0},{1,5},{5... | collective-permute-start | bytes 196616 | tf_op jit(solution)/shard_map/ppermute | solution.py:15
  11.6 3.2 %collective-permute-start.4 = (bf16[32,1,8,128]{3,0,2,1:T(8,128)(2,1)S(1)}, bf16[32,1,8,128]{3,0,2,1:T(8,128)(2,1)S(1)}, u32[]{:S(2)}, u32[]{:S(2)}) collective-permute-start(bf16[32,1,8,128]{3,0,2,1:T(8,128)(2,1)S(1)} %get-tuple-element.51), channel_id=1, source_target_pairs={{4,0},{8,4},{12,8},{16,12},{20,16},{24,20},{28,24},{0,28},{5,1},{9... | collective-permute-start | bytes 196616 | tf_op jit(solution)/shard_map/ppermute | solution.py:18
  14.8 2.3 %collective-permute-done.3 = bf16[32,1,8,128]{3,0,2,1:T(8,128)(2,1)S(1)} collective-permute-done((bf16[32,1,8,128]{3,0,2,1:T(8,128)(2,1)S(1)}, bf16[32,1,8,128]{3,0,2,1:T(8,128)(2,1)S(1)}, u32[]{:S(2)}, u32[]{:S(2)}) %collective-permute-start.3) | collective-permute-done | bytes 65568 | tf_op jit(solution)/shard_map/ppermute | solution.py:15
  17.2 1.7 %collective-permute-start.5 = (bf16[32,4,1,128]{3,0,2,1:T(8,128)(2,1)S(1)}, bf16[32,4,1,128]{3,0,2,1:T(8,128)(2,1)S(1)}, u32[]{:S(2)}, u32[]{:S(2)}) collective-permute-start(bf16[32,4,1,128]{3,0,2,1:T(8,128)(2,1)S(1)} %get-tuple-element.35), channel_id=1, source_target_pairs={{1,0},{2,1},{3,2},{0,3},{5,4},{6,5},{7,6},{4,7},{9,8},{10,9},{11,1... | collective-permute-start | bytes 98312 | tf_op jit(solution)/shard_map/ppermute | solution.py:18
  19.0 1.6 %collective-permute-done.6 = bf16[32,4,1,128]{3,0,2,1:T(8,128)(2,1)S(1)} collective-permute-done((bf16[32,4,1,128]{3,0,2,1:T(8,128)(2,1)S(1)}, bf16[32,4,1,128]{3,0,2,1:T(8,128)(2,1)S(1)}, u32[]{:S(2)}, u32[]{:S(2)}) %collective-permute-start.6) | collective-permute-done | bytes 32800 | tf_op jit(solution)/shard_map/ppermute | solution.py:15
  22.7 1.2 %collective-permute-start.7 = (bf16[32,1,8,128]{3,0,2,1:T(8,128)(2,1)S(1)}, bf16[32,1,8,128]{3,0,2,1:T(8,128)(2,1)S(1)}, u32[]{:S(2)}, u32[]{:S(2)}) collective-permute-start(bf16[32,1,8,128]{3,0,2,1:T(8,128)(2,1)S(1)} %get-tuple-element.48), channel_id=1, source_target_pairs={{0,4},{4,8},{8,12},{12,16},{16,20},{20,24},{24,28},{28,0},{1,5},{5... | collective-permute-start | bytes 196616 | tf_op jit(solution)/shard_map/ppermute | solution.py:15
  23.9 3.6 %collective-permute-start.8 = (bf16[32,1,8,128]{3,0,2,1:T(8,128)(2,1)S(1)}, bf16[32,1,8,128]{3,0,2,1:T(8,128)(2,1)S(1)}, u32[]{:S(2)}, u32[]{:S(2)}) collective-permute-start(bf16[32,1,8,128]{3,0,2,1:T(8,128)(2,1)S(1)} %get-tuple-element.49), channel_id=1, source_target_pairs={{4,0},{8,4},{12,8},{16,12},{20,16},{24,20},{28,24},{0,28},{5,1},{9... | collective-permute-start | bytes 196616 | tf_op jit(solution)/shard_map/ppermute | solution.py:18
  27.7 2.4 %collective-permute-done.7 = bf16[32,1,8,128]{3,0,2,1:T(8,128)(2,1)S(1)} collective-permute-done((bf16[32,1,8,128]{3,0,2,1:T(8,128)(2,1)S(1)}, bf16[32,1,8,128]{3,0,2,1:T(8,128)(2,1)S(1)}, u32[]{:S(2)}, u32[]{:S(2)}) %collective-permute-start.7) | collective-permute-done | bytes 65568 | tf_op jit(solution)/shard_map/ppermute | solution.py:15
  30.3 1.6 %collective-permute-start.9 = (bf16[32,4,1,128]{3,0,2,1:T(8,128)(2,1)S(1)}, bf16[32,4,1,128]{3,0,2,1:T(8,128)(2,1)S(1)}, u32[]{:S(2)}, u32[]{:S(2)}) collective-permute-start(bf16[32,4,1,128]{3,0,2,1:T(8,128)(2,1)S(1)} %get-tuple-element.31), channel_id=1, source_target_pairs={{1,0},{2,1},{3,2},{0,3},{5,4},{6,5},{7,6},{4,7},{9,8},{10,9},{11,1... | collective-permute-start | bytes 98312 | tf_op jit(solution)/shard_map/ppermute | solution.py:18
  31.9 1.1 %fusion.3 = f32[9,3,32,32]{2,3,0,1:T(8,128)S(1)} fusion(bf16[9,32,2,8,128]{4,1,3,2,0:T(8,128)(2,1)S(1)} %fusion.50, bf16[1,32,2,8,128]{4,1,3,2,0:T(8,128)(2,1)S(1)} %maximum_bitcast_fusion.5, bf16[1,32,2,8,128]{4,1,3,2,0:T(8,128)(2,1)S(1)} %bitcast.252, bf16[1,32,2,8,128]{4,1,3,2,0:T(8,128)(2,1)S(1)} %maximum_bitcast_fusion.4), kind=kOutput, calls=%fused_computation.7 | convolution fusion | flops 114453504 | bytes 1683456 | tf_op jit(solution)/shard_map/toxzy,sixzy->tsoi/dot_general | solution.py:151
  33.8 1.1 %fusion.1 = f32[9,3,32,32]{2,3,0,1:T(8,128)S(1)} fusion(bf16[1,32,2,8,128]{4,1,3,2,0:T(8,128)(2,1)S(1)} %get-tuple-element.60, bf16[1,32,2,8,128]{4,1,3,2,0:T(8,128)(2,1)S(1)} %bitcast.258, bf16[1,32,2,8,128]{4,1,3,2,0:T(8,128)(2,1)S(1)} %get-tuple-element.59, bf16[9,32,2,8,128]{4,1,3,2,0:T(8,128)(2,1)S(1)} %fusion.40), kind=kOutput, calls=%fused_computation.4 | convolution fusion | flops 114453504 | bytes 1683456 | tf_op jit(solution)/shard_map/toxzy,sixzy->tsoi/dot_general | solution.py:151
  35.3 1.4 %collective-permute-start.11 = (f32[224,128]{1,0:T(8,128)S(1)}, f32[224,128]{1,0:T(8,128)S(1)}, u32[]{:S(2)}, u32[]{:S(2)}) collective-permute-start(f32[224,128]{1,0:T(8,128)S(1)} %fusion.61), channel_id=1, source_target_pairs={{0,1},{1,0},{2,3},{3,2},{4,5},{5,4},{6,7},{7,6},{8,9},{9,8},{10,11... | collective-permute-start | bytes 344072 | tf_op jit(solution)/shard_map/ppermute | solution.py:66
  36.7 1.0 %collective-permute-done.11 = f32[224,128]{1,0:T(8,128)S(1)} collective-permute-done((f32[224,128]{1,0:T(8,128)S(1)}, f32[224,128]{1,0:T(8,128)S(1)}, u32[]{:S(2)}, u32[]{:S(2)}) %collective-permute-start.11) | collective-permute-done | bytes 114720 | tf_op jit(solution)/shard_map/ppermute | solution.py:66
  38.2 2.0 %collective-permute-start.13 = (f32[224,128]{1,0:T(8,128)S(1)}, f32[224,128]{1,0:T(8,128)S(1)}, u32[]{:S(2)}, u32[]{:S(2)}) collective-permute-start(f32[224,128]{1,0:T(8,128)S(1)} %select_add_fusion), channel_id=1, source_target_pairs={{0,4},{1,5},{2,6},{3,7},{4,0},{5,1},{6,2},{7,3},{8,12},{9,13},{10,... | collective-permute-start | bytes 344072 | tf_op jit(solution)/shard_map/ppermute | solution.py:70
  40.2 1.2 %collective-permute-start.12 = (f32[224,128]{1,0:T(8,128)S(1)}, f32[224,128]{1,0:T(8,128)S(1)}, u32[]{:S(2)}, u32[]{:S(2)}) collective-permute-start(f32[224,128]{1,0:T(8,128)S(1)} %select_add_fusion), channel_id=1, source_target_pairs={{0,2},{1,3},{2,0},{3,1},{4,6},{5,7},{6,4},{7,5},{8,10},{9,11},{10,... | collective-permute-start | bytes 344072 | tf_op jit(solution)/shard_map/ppermute | solution.py:70
  41.4 3.4 %collective-permute-done.14 = f32[224,128]{1,0:T(8,128)S(1)} collective-permute-done((f32[224,128]{1,0:T(8,128)S(1)}, f32[224,128]{1,0:T(8,128)S(1)}, u32[]{:S(2)}, u32[]{:S(2)}) %collective-permute-start.14) | collective-permute-done | bytes 114720 | tf_op jit(solution)/shard_map/ppermute | solution.py:70
  44.8 1.2 %collective-permute-done.13 = f32[224,128]{1,0:T(8,128)S(1)} collective-permute-done((f32[224,128]{1,0:T(8,128)S(1)}, f32[224,128]{1,0:T(8,128)S(1)}, u32[]{:S(2)}, u32[]{:S(2)}) %collective-permute-start.13) | collective-permute-done | bytes 114720 | tf_op jit(solution)/shard_map/ppermute | solution.py:70
  47.5 3.4 %collective-permute-done.15 = f32[224,128]{1,0:T(8,128)S(1)} collective-permute-done((f32[224,128]{1,0:T(8,128)S(1)}, f32[224,128]{1,0:T(8,128)S(1)}, u32[]{:S(2)}, u32[]{:S(2)}) %collective-permute-start.15) | collective-permute-done | bytes 114720 | tf_op jit(solution)/shard_map/ppermute | solution.py:76
  50.9 3.4 %collective-permute-start.16 = (f32[224,128]{1,0:T(8,128)S(1)}, f32[224,128]{1,0:T(8,128)S(1)}, u32[]{:S(2)}, u32[]{:S(2)}) collective-permute-start(f32[224,128]{1,0:T(8,128)S(1)} %add.115), channel_id=1, source_target_pairs={{0,16},{1,17},{2,18},{3,19},{4,20},{5,21},{6,22},{7,23},{8,24},{9,... | collective-permute-start | bytes 344072 | tf_op jit(solution)/shard_map/ppermute | solution.py:76
  54.6 4.4 %collective-permute-done.16 = f32[224,128]{1,0:T(8,128)S(1)} collective-permute-done((f32[224,128]{1,0:T(8,128)S(1)}, f32[224,128]{1,0:T(8,128)S(1)}, u32[]{:S(2)}, u32[]{:S(2)}) %collective-permute-start.16) | collective-permute-done | bytes 114720 | tf_op jit(solution)/shard_map/ppermute | solution.py:76
  (111 shorter events, 13.4 us)
Async XLA Ops:
  0.6 20.2 %copy-start = (bf16[3,3,3,32,32]{4,3,2,1,0:T(8,128)(2,1)S(1)}, bf16[3,3,3,32,32]{4,3,2,1,0:T(8,128)(2,1)}, u32[]{:S(2)}) copy-start(bf16[3,3,3,32,32]{4,3,2,1,0:T(8,128)(2,1)} %param.13) | copy-start | bytes 165892
  0.6 7.0 %copy-start.1 = (bf16[32,2,8,128]{3,2,1,0:T(8,128)(2,1)S(1)}, bf16[32,2,8,128]{3,2,1,0:T(8,128)(2,1)}, u32[]{:S(2)}) copy-start(bf16[32,2,8,128]{3,2,1,0:T(8,128)(2,1)} %param.9) | copy-start | bytes 393220
  3.3 4.9 %collective-permute-start.1 = (f32[2,2,128]{2,1,0:T(2,128)S(1)}, f32[2,2,128]{2,1,0:T(2,128)S(1)}, u32[]{:S(2)}, u32[]{:S(2)}) collective-permute-start(f32[2,2,128]{2,1,0:T(2,128)S(1)} %pad_maximum_fusion.16), channel_id=1, source_target_pairs={{0,2},{1,3},{2,0},{3,1},{4,6},{5,7},{6,4},{7,5},{8,10},{9,11},{10,... | collective-permute-start | bytes 6152 | tf_op jit(solution)/shard_map/ppermute | solution.py:47
  6.3 3.0 %collective-permute-start.2 = (f32[2,2,128]{2,1,0:T(2,128)S(1)}, f32[2,2,128]{2,1,0:T(2,128)S(1)}, u32[]{:S(2)}, u32[]{:S(2)}) collective-permute-start(f32[2,2,128]{2,1,0:T(2,128)S(1)} %pad_maximum_fusion.16), channel_id=1, source_target_pairs={{0,3},{1,2},{2,1},{3,0},{4,7},{5,6},{6,5},{7,4},{8,11},{9,10},{10,... | collective-permute-start | bytes 6152 | tf_op jit(solution)/shard_map/ppermute | solution.py:47
  6.3 3.0 %collective-permute-start = (f32[2,2,128]{2,1,0:T(2,128)S(1)}, f32[2,2,128]{2,1,0:T(2,128)S(1)}, u32[]{:S(2)}, u32[]{:S(2)}) collective-permute-start(f32[2,2,128]{2,1,0:T(2,128)S(1)} %pad_maximum_fusion.16), channel_id=1, source_target_pairs={{0,1},{1,0},{2,3},{3,2},{4,5},{5,4},{6,7},{7,6},{8,9},{9,8},{10,11... | collective-permute-start | bytes 6152 | tf_op jit(solution)/shard_map/ppermute | solution.py:47
  7.7 1.6 %copy-start.6 = (f32[2,128]{1,0:T(2,128)S(1)}, f32[2,128]{1,0:T(2,128)}, u32[]{:S(2)}) copy-start(f32[2,128]{1,0:T(2,128)} %param.16) | copy-start | bytes 3076
  7.7 1.9 %copy-start.3 = (bf16[32,2,8,128]{3,2,1,0:T(8,128)(2,1)S(1)}, bf16[32,2,8,128]{3,2,1,0:T(8,128)(2,1)}, u32[]{:S(2)}) copy-start(bf16[32,2,8,128]{3,2,1,0:T(8,128)(2,1)} %param.11) | copy-start | bytes 393220
  7.8 1.9 %copy-start.5 = (bf16[3,32]{1,0:T(4,128)(2,1)S(1)}, bf16[3,32]{1,0:T(4,128)(2,1)}, u32[]{:S(2)}) copy-start(bf16[3,32]{1,0:T(4,128)(2,1)} %param.14) | copy-start | bytes 580
  10.0 7.1 %collective-permute-start.3 = (bf16[32,1,8,128]{3,0,2,1:T(8,128)(2,1)S(1)}, bf16[32,1,8,128]{3,0,2,1:T(8,128)(2,1)S(1)}, u32[]{:S(2)}, u32[]{:S(2)}) collective-permute-start(bf16[32,1,8,128]{3,0,2,1:T(8,128)(2,1)S(1)} %get-tuple-element.50), channel_id=1, source_target_pairs={{0,4},{4,8},{8,12},{12,16},{16,20},{20,24},{24,28},{28,0},{1,5},{5... | collective-permute-start | bytes 196616 | tf_op jit(solution)/shard_map/ppermute | solution.py:15
  11.6 5.6 %collective-permute-start.4 = (bf16[32,1,8,128]{3,0,2,1:T(8,128)(2,1)S(1)}, bf16[32,1,8,128]{3,0,2,1:T(8,128)(2,1)S(1)}, u32[]{:S(2)}, u32[]{:S(2)}) collective-permute-start(bf16[32,1,8,128]{3,0,2,1:T(8,128)(2,1)S(1)} %get-tuple-element.51), channel_id=1, source_target_pairs={{4,0},{8,4},{12,8},{16,12},{20,16},{24,20},{28,24},{0,28},{5,1},{9... | collective-permute-start | bytes 196616 | tf_op jit(solution)/shard_map/ppermute | solution.py:18
  17.1 3.4 %collective-permute-start.6 = (bf16[32,4,1,128]{3,0,2,1:T(8,128)(2,1)S(1)}, bf16[32,4,1,128]{3,0,2,1:T(8,128)(2,1)S(1)}, u32[]{:S(2)}, u32[]{:S(2)}) collective-permute-start(bf16[32,4,1,128]{3,0,2,1:T(8,128)(2,1)S(1)} %get-tuple-element.34), channel_id=1, source_target_pairs={{0,1},{1,2},{2,3},{3,0},{4,5},{5,6},{6,7},{7,4},{8,9},{9,10},{10,1... | collective-permute-start | bytes 98312 | tf_op jit(solution)/shard_map/ppermute | solution.py:15
  17.2 3.3 %collective-permute-start.5 = (bf16[32,4,1,128]{3,0,2,1:T(8,128)(2,1)S(1)}, bf16[32,4,1,128]{3,0,2,1:T(8,128)(2,1)S(1)}, u32[]{:S(2)}, u32[]{:S(2)}) collective-permute-start(bf16[32,4,1,128]{3,0,2,1:T(8,128)(2,1)S(1)} %get-tuple-element.35), channel_id=1, source_target_pairs={{1,0},{2,1},{3,2},{0,3},{5,4},{6,5},{7,6},{4,7},{9,8},{10,9},{11,1... | collective-permute-start | bytes 98312 | tf_op jit(solution)/shard_map/ppermute | solution.py:18
  22.7 7.4 %collective-permute-start.7 = (bf16[32,1,8,128]{3,0,2,1:T(8,128)(2,1)S(1)}, bf16[32,1,8,128]{3,0,2,1:T(8,128)(2,1)S(1)}, u32[]{:S(2)}, u32[]{:S(2)}) collective-permute-start(bf16[32,1,8,128]{3,0,2,1:T(8,128)(2,1)S(1)} %get-tuple-element.48), channel_id=1, source_target_pairs={{0,4},{4,8},{8,12},{12,16},{16,20},{20,24},{24,28},{28,0},{1,5},{5... | collective-permute-start | bytes 196616 | tf_op jit(solution)/shard_map/ppermute | solution.py:15
  23.9 6.2 %collective-permute-start.8 = (bf16[32,1,8,128]{3,0,2,1:T(8,128)(2,1)S(1)}, bf16[32,1,8,128]{3,0,2,1:T(8,128)(2,1)S(1)}, u32[]{:S(2)}, u32[]{:S(2)}) collective-permute-start(bf16[32,1,8,128]{3,0,2,1:T(8,128)(2,1)S(1)} %get-tuple-element.49), channel_id=1, source_target_pairs={{4,0},{8,4},{12,8},{16,12},{20,16},{24,20},{28,24},{0,28},{5,1},{9... | collective-permute-start | bytes 196616 | tf_op jit(solution)/shard_map/ppermute | solution.py:18
  30.1 3.4 %collective-permute-start.10 = (bf16[32,4,1,128]{3,0,2,1:T(8,128)(2,1)S(1)}, bf16[32,4,1,128]{3,0,2,1:T(8,128)(2,1)S(1)}, u32[]{:S(2)}, u32[]{:S(2)}) collective-permute-start(bf16[32,4,1,128]{3,0,2,1:T(8,128)(2,1)S(1)} %get-tuple-element.30), channel_id=1, source_target_pairs={{0,1},{1,2},{2,3},{3,0},{4,5},{5,6},{6,7},{7,4},{8,9},{9,10},{10,1... | collective-permute-start | bytes 98312 | tf_op jit(solution)/shard_map/ppermute | solution.py:15
  30.3 3.2 %collective-permute-start.9 = (bf16[32,4,1,128]{3,0,2,1:T(8,128)(2,1)S(1)}, bf16[32,4,1,128]{3,0,2,1:T(8,128)(2,1)S(1)}, u32[]{:S(2)}, u32[]{:S(2)}) collective-permute-start(bf16[32,4,1,128]{3,0,2,1:T(8,128)(2,1)S(1)} %get-tuple-element.31), channel_id=1, source_target_pairs={{1,0},{2,1},{3,2},{0,3},{5,4},{6,5},{7,6},{4,7},{9,8},{10,9},{11,1... | collective-permute-start | bytes 98312 | tf_op jit(solution)/shard_map/ppermute | solution.py:18
  35.1 11.9 %copy-start.2 = (bf16[3,3,3,32,32]{4,3,2,1,0:T(8,128)(2,1)S(1)}, bf16[3,3,3,32,32]{4,3,2,1,0:T(8,128)(2,1)}, u32[]{:S(2)}) copy-start(bf16[3,3,3,32,32]{4,3,2,1,0:T(8,128)(2,1)} %param.12) | copy-start | bytes 165892
  35.3 2.3 %collective-permute-start.11 = (f32[224,128]{1,0:T(8,128)S(1)}, f32[224,128]{1,0:T(8,128)S(1)}, u32[]{:S(2)}, u32[]{:S(2)}) collective-permute-start(f32[224,128]{1,0:T(8,128)S(1)} %fusion.61), channel_id=1, source_target_pairs={{0,1},{1,0},{2,3},{3,2},{4,5},{5,4},{6,7},{7,6},{8,9},{9,8},{10,11... | collective-permute-start | bytes 344072 | tf_op jit(solution)/shard_map/ppermute | solution.py:66
  37.8 7.0 %collective-permute-start.14 = (f32[224,128]{1,0:T(8,128)S(1)}, f32[224,128]{1,0:T(8,128)S(1)}, u32[]{:S(2)}, u32[]{:S(2)}) collective-permute-start(f32[224,128]{1,0:T(8,128)S(1)} %select_add_fusion), channel_id=1, source_target_pairs={{0,6},{1,7},{2,4},{3,5},{4,2},{5,3},{6,0},{7,1},{8,14},{9,15},{10,... | collective-permute-start | bytes 344072 | tf_op jit(solution)/shard_map/ppermute | solution.py:70
  38.2 7.8 %collective-permute-start.13 = (f32[224,128]{1,0:T(8,128)S(1)}, f32[224,128]{1,0:T(8,128)S(1)}, u32[]{:S(2)}, u32[]{:S(2)}) collective-permute-start(f32[224,128]{1,0:T(8,128)S(1)} %select_add_fusion), channel_id=1, source_target_pairs={{0,4},{1,5},{2,6},{3,7},{4,0},{5,1},{6,2},{7,3},{8,12},{9,13},{10,... | collective-permute-start | bytes 344072 | tf_op jit(solution)/shard_map/ppermute | solution.py:70
  40.2 5.8 %collective-permute-start.12 = (f32[224,128]{1,0:T(8,128)S(1)}, f32[224,128]{1,0:T(8,128)S(1)}, u32[]{:S(2)}, u32[]{:S(2)}) collective-permute-start(f32[224,128]{1,0:T(8,128)S(1)} %select_add_fusion), channel_id=1, source_target_pairs={{0,2},{1,3},{2,0},{3,1},{4,6},{5,7},{6,4},{7,5},{8,10},{9,11},{10,... | collective-permute-start | bytes 344072 | tf_op jit(solution)/shard_map/ppermute | solution.py:70
  46.0 4.9 %collective-permute-start.15 = (f32[224,128]{1,0:T(8,128)S(1)}, f32[224,128]{1,0:T(8,128)S(1)}, u32[]{:S(2)}, u32[]{:S(2)}) collective-permute-start(f32[224,128]{1,0:T(8,128)S(1)} %add_add_fusion), channel_id=1, source_target_pairs={{0,8},{1,9},{2,10},{3,11},{4,12},{5,13},{6,14},{7,15},{8,0},{9,1},... | collective-permute-start | bytes 344072 | tf_op jit(solution)/shard_map/ppermute | solution.py:76
  50.9 8.1 %collective-permute-start.16 = (f32[224,128]{1,0:T(8,128)S(1)}, f32[224,128]{1,0:T(8,128)S(1)}, u32[]{:S(2)}, u32[]{:S(2)}) collective-permute-start(f32[224,128]{1,0:T(8,128)S(1)} %add.115), channel_id=1, source_target_pairs={{0,16},{1,17},{2,18},{3,19},{4,20},{5,21},{6,22},{7,23},{8,24},{9,... | collective-permute-start | bytes 344072 | tf_op jit(solution)/shard_map/ppermute | solution.py:76
  59.0 1.4 %collective-permute-start.17 = (f32[224,128]{1,0:T(8,128)S(1)}, f32[224,128]{1,0:T(8,128)S(1)}, u32[]{:S(2)}, u32[]{:S(2)}) collective-permute-start(f32[224,128]{1,0:T(8,128)S(1)} %add.116), channel_id=1, source_target_pairs={{0,1},{1,0},{2,3},{3,2},{4,5},{5,4},{6,7},{7,6},{8,9},{9,8},{10,11... | collective-permute-start | bytes 344072 | tf_op jit(solution)/shard_map/ppermute | solution.py:77
  (2 other events, 2.5 us)

commit v15 on v14

--- a/solution.py
+++ b/solution.py
@@ -65,7 +65,7 @@
     partner = [(i, i ^ 1) for i in range(total)]
     keep = keep + lax.ppermute(send, index_axes, partner)
     bits = [1 << b for b in range(1, total.bit_length() - 1)]
-    if len(bits) >= 2:
+    while len(bits) >= 2:
         near, far, both = (
             lax.ppermute(keep, index_axes, [(i, i ^ mask) for i in range(total)])
             for mask in (bits[0], bits[1], bits[0] | bits[1])

time: 63.7 us -> 63.6 us (level)
  waiting for transfers between devices: 21.4 us -> 20.2 us
  starting transfers between devices: 25.7 us -> 26.8 us
    ppermute x2 -> x0, waiting for transfers between devices: 7.83 us -> none  [split_sum(): lax.ppermute(keep, index_axes, [(i, i ^ bit) for i in range(total)])]
    ppermute x3 -> x6, waiting for transfers between devices: 4.64 us -> 11.3 us  [split_sum(): lax.ppermute(keep, index_axes, [(i, i ^ mask) for i in range(total)])]
    ppermute x3 -> x6, starting transfers between devices: 3.57 us -> 8.99 us  [split_sum(): lax.ppermute(keep, index_axes, [(i, i ^ mask) for i in range(total)])]
    ppermute x2 -> x0, starting transfers between devices: 4.36 us -> none  [split_sum(): lax.ppermute(keep, index_axes, [(i, i ^ bit) for i in range(total)])]
  transfers between devices with their start and end apart: 18 -> 19, of which waited for: 11 -> 11; matrix products, arithmetic and copies ran while one was open for 8% -> 8% of each run, Pallas kernels for 0% -> 0%
where the time goes in v15:
time: 63.6 us; the launch traced here: 63.4 us
  starting transfers between devices  26.8 us (42%)
  waiting for transfers between devices  20.2 us (32%)
  local copies, waits for them, and re-layouts  7.66 us (12%)
  matrix products  4.26 us (7%)
  other arithmetic  3.26 us (5%)
  between operations  1.2 us (2%)
    ppermute x6, waiting for transfers between devices, split_sum(): lax.ppermute(keep, index_axes, [(i, i ^ mask) for i in range(total)])  11.3 us
    ppermute x4, starting transfers between devices, extended(): lax.ppermute(lax.slice_in_dim(block, 0, width, axis=dim), axis, backward)  10.1 us
    ppermute x6, starting transfers between devices, split_sum(): lax.ppermute(keep, index_axes, [(i, i ^ mask) for i in range(total)])  8.99 us
    ppermute x4, waiting for transfers between devices, extended(): lax.ppermute(lax.slice_in_dim(block, block.shape[dim] - width, None, axis...  6.5 us
    ppermute x3, starting transfers between devices, quad_sum(): lax.ppermute(value, axis, [(i, i ^ mask) for i in range(count)])  3.2 us
    ppermute x4, starting transfers between devices, extended(): lax.ppermute(lax.slice_in_dim(block, block.shape[dim] - width, None, axis...  3.01 us
    reshape x3, local copies, waits for them, and re-layouts, unpack_rows(): parts.append(block.reshape(shape))  2.5 us
    dot_general x2, matrix products, taps_from_halo(): jnp.einsum('toxzy,sixzy->tsoi', windows, rolled, preferred_element_type=j...  2.13 us
  transfers between devices with their start and end apart: 19, of which 11 were waited for; matrix products, arithmetic and copies ran while one was open for 8% of the time, Pallas kernels for 0%

profile of v15, /device:TPU:0, one launch (start us, length us, event | category | flops | bytes accessed | tf_op | source)
XLA Modules:
  0.0 63.4 jit_solution(6728874729825662178)
XLA Ops:
  0.7 1.0 %fusion.22 = bf16[32,2,8,128]{3,0,2,1:T(8,128)(2,1)S(1)} fusion(bf16[32,2,8,128]{3,2,1,0:T(8,128)(2,1)} %param.11), kind=kLoop, calls=%fused_computation.40 | loop fusion | flops 393216 | bytes 262144 | tf_op jit(solution)/shard_map/convert_element_type | solution.py:167
  3.3 3.0 %collective-permute-start.1 = (f32[2,2,128]{2,1,0:T(2,128)S(1)}, f32[2,2,128]{2,1,0:T(2,128)S(1)}, u32[]{:S(2)}, u32[]{:S(2)}) collective-permute-start(f32[2,2,128]{2,1,0:T(2,128)S(1)} %pad_maximum_fusion.16), channel_id=1, source_target_pairs={{0,2},{1,3},{2,0},{3,1},{4,6},{5,7},{6,4},{7,5},{8,10},{9,11},{10,... | collective-permute-start | bytes 6152 | tf_op jit(solution)/shard_map/ppermute | solution.py:47
  6.5 1.1 %fusion.89 = (bf16[32,2,8,127]{3,2,1,0:T(8,128)(2,1)S(1)}, bf16[32,2,8,127]{3,2,1,0:T(8,128)(2,1)S(1)}) fusion(bf16[32,2,8,128]{3,2,1,0:T(8,128)(2,1)} %param.9), kind=kLoop, calls=%fused_computation.173 | loop fusion | bytes 520192 | tf_op jit(solution)/shard_map/jit(_roll_static)/slice | solution.py:150
  8.2 1.1 %collective-permute-done.2 = f32[2,2,128]{2,1,0:T(2,128)S(1)} collective-permute-done((f32[2,2,128]{2,1,0:T(2,128)S(1)}, f32[2,2,128]{2,1,0:T(2,128)S(1)}, u32[]{:S(2)}, u32[]{:S(2)}) %collective-permute-start.2) | collective-permute-done | bytes 2080 | tf_op jit(solution)/shard_map/ppermute | solution.py:47
  10.0 1.6 %collective-permute-start.3 = (bf16[32,1,8,128]{3,0,2,1:T(8,128)(2,1)S(1)}, bf16[32,1,8,128]{3,0,2,1:T(8,128)(2,1)S(1)}, u32[]{:S(2)}, u32[]{:S(2)}) collective-permute-start(bf16[32,1,8,128]{3,0,2,1:T(8,128)(2,1)S(1)} %get-tuple-element.50), channel_id=1, source_target_pairs={{0,4},{4,8},{8,12},{12,16},{16,20},{20,24},{24,28},{28,0},{1,5},{5... | collective-permute-start | bytes 196616 | tf_op jit(solution)/shard_map/ppermute | solution.py:15
  11.6 3.2 %collective-permute-start.4 = (bf16[32,1,8,128]{3,0,2,1:T(8,128)(2,1)S(1)}, bf16[32,1,8,128]{3,0,2,1:T(8,128)(2,1)S(1)}, u32[]{:S(2)}, u32[]{:S(2)}) collective-permute-start(bf16[32,1,8,128]{3,0,2,1:T(8,128)(2,1)S(1)} %get-tuple-element.51), channel_id=1, source_target_pairs={{4,0},{8,4},{12,8},{16,12},{20,16},{24,20},{28,24},{0,28},{5,1},{9... | collective-permute-start | bytes 196616 | tf_op jit(solution)/shard_map/ppermute | solution.py:18
  14.8 2.3 %collective-permute-done.3 = bf16[32,1,8,128]{3,0,2,1:T(8,128)(2,1)S(1)} collective-permute-done((bf16[32,1,8,128]{3,0,2,1:T(8,128)(2,1)S(1)}, bf16[32,1,8,128]{3,0,2,1:T(8,128)(2,1)S(1)}, u32[]{:S(2)}, u32[]{:S(2)}) %collective-permute-start.3) | collective-permute-done | bytes 65568 | tf_op jit(solution)/shard_map/ppermute | solution.py:15
  17.2 1.7 %collective-permute-start.5 = (bf16[32,4,1,128]{3,0,2,1:T(8,128)(2,1)S(1)}, bf16[32,4,1,128]{3,0,2,1:T(8,128)(2,1)S(1)}, u32[]{:S(2)}, u32[]{:S(2)}) collective-permute-start(bf16[32,4,1,128]{3,0,2,1:T(8,128)(2,1)S(1)} %get-tuple-element.35), channel_id=1, source_target_pairs={{1,0},{2,1},{3,2},{0,3},{5,4},{6,5},{7,6},{4,7},{9,8},{10,9},{11,1... | collective-permute-start | bytes 98312 | tf_op jit(solution)/shard_map/ppermute | solution.py:18
  19.0 1.6 %collective-permute-done.6 = bf16[32,4,1,128]{3,0,2,1:T(8,128)(2,1)S(1)} collective-permute-done((bf16[32,4,1,128]{3,0,2,1:T(8,128)(2,1)S(1)}, bf16[32,4,1,128]{3,0,2,1:T(8,128)(2,1)S(1)}, u32[]{:S(2)}, u32[]{:S(2)}) %collective-permute-start.6) | collective-permute-done | bytes 32800 | tf_op jit(solution)/shard_map/ppermute | solution.py:15
  22.7 1.2 %collective-permute-start.7 = (bf16[32,1,8,128]{3,0,2,1:T(8,128)(2,1)S(1)}, bf16[32,1,8,128]{3,0,2,1:T(8,128)(2,1)S(1)}, u32[]{:S(2)}, u32[]{:S(2)}) collective-permute-start(bf16[32,1,8,128]{3,0,2,1:T(8,128)(2,1)S(1)} %get-tuple-element.48), channel_id=1, source_target_pairs={{0,4},{4,8},{8,12},{12,16},{16,20},{20,24},{24,28},{28,0},{1,5},{5... | collective-permute-start | bytes 196616 | tf_op jit(solution)/shard_map/ppermute | solution.py:15
  23.9 3.6 %collective-permute-start.8 = (bf16[32,1,8,128]{3,0,2,1:T(8,128)(2,1)S(1)}, bf16[32,1,8,128]{3,0,2,1:T(8,128)(2,1)S(1)}, u32[]{:S(2)}, u32[]{:S(2)}) collective-permute-start(bf16[32,1,8,128]{3,0,2,1:T(8,128)(2,1)S(1)} %get-tuple-element.49), channel_id=1, source_target_pairs={{4,0},{8,4},{12,8},{16,12},{20,16},{24,20},{28,24},{0,28},{5,1},{9... | collective-permute-start | bytes 196616 | tf_op jit(solution)/shard_map/ppermute | solution.py:18
  27.7 2.4 %collective-permute-done.7 = bf16[32,1,8,128]{3,0,2,1:T(8,128)(2,1)S(1)} collective-permute-done((bf16[32,1,8,128]{3,0,2,1:T(8,128)(2,1)S(1)}, bf16[32,1,8,128]{3,0,2,1:T(8,128)(2,1)S(1)}, u32[]{:S(2)}, u32[]{:S(2)}) %collective-permute-start.7) | collective-permute-done | bytes 65568 | tf_op jit(solution)/shard_map/ppermute | solution.py:15
  30.3 1.6 %collective-permute-start.9 = (bf16[32,4,1,128]{3,0,2,1:T(8,128)(2,1)S(1)}, bf16[32,4,1,128]{3,0,2,1:T(8,128)(2,1)S(1)}, u32[]{:S(2)}, u32[]{:S(2)}) collective-permute-start(bf16[32,4,1,128]{3,0,2,1:T(8,128)(2,1)S(1)} %get-tuple-element.31), channel_id=1, source_target_pairs={{1,0},{2,1},{3,2},{0,3},{5,4},{6,5},{7,6},{4,7},{9,8},{10,9},{11,1... | collective-permute-start | bytes 98312 | tf_op jit(solution)/shard_map/ppermute | solution.py:18
  31.9 1.1 %fusion.3 = f32[9,3,32,32]{2,3,0,1:T(8,128)S(1)} fusion(bf16[9,32,2,8,128]{4,1,3,2,0:T(8,128)(2,1)S(1)} %fusion.50, bf16[1,32,2,8,128]{4,1,3,2,0:T(8,128)(2,1)S(1)} %maximum_bitcast_fusion.5, bf16[1,32,2,8,128]{4,1,3,2,0:T(8,128)(2,1)S(1)} %bitcast.252, bf16[1,32,2,8,128]{4,1,3,2,0:T(8,128)(2,1)S(1)} %maximum_bitcast_fusion.4), kind=kOutput, calls=%fused_computation.7 | convolution fusion | flops 114453504 | bytes 1683456 | tf_op jit(solution)/shard_map/toxzy,sixzy->tsoi/dot_general | solution.py:151
  33.8 1.1 %fusion.1 = f32[9,3,32,32]{2,3,0,1:T(8,128)S(1)} fusion(bf16[1,32,2,8,128]{4,1,3,2,0:T(8,128)(2,1)S(1)} %get-tuple-element.60, bf16[1,32,2,8,128]{4,1,3,2,0:T(8,128)(2,1)S(1)} %bitcast.258, bf16[1,32,2,8,128]{4,1,3,2,0:T(8,128)(2,1)S(1)} %get-tuple-element.59, bf16[9,32,2,8,128]{4,1,3,2,0:T(8,128)(2,1)S(1)} %fusion.40), kind=kOutput, calls=%fused_computation.4 | convolution fusion | flops 114453504 | bytes 1683456 | tf_op jit(solution)/shard_map/toxzy,sixzy->tsoi/dot_general | solution.py:151
  35.3 1.4 %collective-permute-start.11 = (f32[224,128]{1,0:T(8,128)S(1)}, f32[224,128]{1,0:T(8,128)S(1)}, u32[]{:S(2)}, u32[]{:S(2)}) collective-permute-start(f32[224,128]{1,0:T(8,128)S(1)} %fusion.61), channel_id=1, source_target_pairs={{0,1},{1,0},{2,3},{3,2},{4,5},{5,4},{6,7},{7,6},{8,9},{9,8},{10,11... | collective-permute-start | bytes 344072 | tf_op jit(solution)/shard_map/ppermute | solution.py:66
  36.7 1.0 %collective-permute-done.11 = f32[224,128]{1,0:T(8,128)S(1)} collective-permute-done((f32[224,128]{1,0:T(8,128)S(1)}, f32[224,128]{1,0:T(8,128)S(1)}, u32[]{:S(2)}, u32[]{:S(2)}) %collective-permute-start.11) | collective-permute-done | bytes 114720 | tf_op jit(solution)/shard_map/ppermute | solution.py:66
  38.2 2.0 %collective-permute-start.13 = (f32[224,128]{1,0:T(8,128)S(1)}, f32[224,128]{1,0:T(8,128)S(1)}, u32[]{:S(2)}, u32[]{:S(2)}) collective-permute-start(f32[224,128]{1,0:T(8,128)S(1)} %select_add_fusion), channel_id=1, source_target_pairs={{0,4},{1,5},{2,6},{3,7},{4,0},{5,1},{6,2},{7,3},{8,12},{9,13},{10,... | collective-permute-start | bytes 344072 | tf_op jit(solution)/shard_map/ppermute | solution.py:70
  40.2 1.2 %collective-permute-start.12 = (f32[224,128]{1,0:T(8,128)S(1)}, f32[224,128]{1,0:T(8,128)S(1)}, u32[]{:S(2)}, u32[]{:S(2)}) collective-permute-start(f32[224,128]{1,0:T(8,128)S(1)} %select_add_fusion), channel_id=1, source_target_pairs={{0,2},{1,3},{2,0},{3,1},{4,6},{5,7},{6,4},{7,5},{8,10},{9,11},{10,... | collective-permute-start | bytes 344072 | tf_op jit(solution)/shard_map/ppermute | solution.py:70
  41.8 2.9 %collective-permute-done.14 = f32[224,128]{1,0:T(8,128)S(1)} collective-permute-done((f32[224,128]{1,0:T(8,128)S(1)}, f32[224,128]{1,0:T(8,128)S(1)}, u32[]{:S(2)}, u32[]{:S(2)}) %collective-permute-start.14) | collective-permute-done | bytes 114720 | tf_op jit(solution)/shard_map/ppermute | solution.py:70
  44.8 1.2 %collective-permute-done.13 = f32[224,128]{1,0:T(8,128)S(1)} collective-permute-done((f32[224,128]{1,0:T(8,128)S(1)}, f32[224,128]{1,0:T(8,128)S(1)}, u32[]{:S(2)}, u32[]{:S(2)}) %collective-permute-start.13) | collective-permute-done | bytes 114720 | tf_op jit(solution)/shard_map/ppermute | solution.py:70
  46.0 4.8 %collective-permute-start.17 = (f32[224,128]{1,0:T(8,128)S(1)}, f32[224,128]{1,0:T(8,128)S(1)}, u32[]{:S(2)}, u32[]{:S(2)}) collective-permute-start(f32[224,128]{1,0:T(8,128)S(1)} %add_add_fusion.1), channel_id=1, source_target_pairs={{0,24},{1,25},{2,26},{3,27},{4,28},{5,29},{6,30},{7,31},{8,16},{9,... | collective-permute-start | bytes 344072 | tf_op jit(solution)/shard_map/ppermute | solution.py:70
  51.7 3.1 %collective-permute-done.17 = f32[224,128]{1,0:T(8,128)S(1)} collective-permute-done((f32[224,128]{1,0:T(8,128)S(1)}, f32[224,128]{1,0:T(8,128)S(1)}, u32[]{:S(2)}, u32[]{:S(2)}) %collective-permute-start.17) | collective-permute-done | bytes 114720 | tf_op jit(solution)/shard_map/ppermute | solution.py:70
  54.9 4.0 %collective-permute-done.16 = f32[224,128]{1,0:T(8,128)S(1)} collective-permute-done((f32[224,128]{1,0:T(8,128)S(1)}, f32[224,128]{1,0:T(8,128)S(1)}, u32[]{:S(2)}, u32[]{:S(2)}) %collective-permute-start.16) | collective-permute-done | bytes 114720 | tf_op jit(solution)/shard_map/ppermute | solution.py:70
  (112 shorter events, 13.1 us)
Async XLA Ops:
  0.6 20.2 %copy-start = (bf16[3,3,3,32,32]{4,3,2,1,0:T(8,128)(2,1)S(1)}, bf16[3,3,3,32,32]{4,3,2,1,0:T(8,128)(2,1)}, u32[]{:S(2)}) copy-start(bf16[3,3,3,32,32]{4,3,2,1,0:T(8,128)(2,1)} %param.13) | copy-start | bytes 165892
  0.6 7.0 %copy-start.1 = (bf16[32,2,8,128]{3,2,1,0:T(8,128)(2,1)S(1)}, bf16[32,2,8,128]{3,2,1,0:T(8,128)(2,1)}, u32[]{:S(2)}) copy-start(bf16[32,2,8,128]{3,2,1,0:T(8,128)(2,1)} %param.9) | copy-start | bytes 393220
  3.3 4.9 %collective-permute-start.1 = (f32[2,2,128]{2,1,0:T(2,128)S(1)}, f32[2,2,128]{2,1,0:T(2,128)S(1)}, u32[]{:S(2)}, u32[]{:S(2)}) collective-permute-start(f32[2,2,128]{2,1,0:T(2,128)S(1)} %pad_maximum_fusion.16), channel_id=1, source_target_pairs={{0,2},{1,3},{2,0},{3,1},{4,6},{5,7},{6,4},{7,5},{8,10},{9,11},{10,... | collective-permute-start | bytes 6152 | tf_op jit(solution)/shard_map/ppermute | solution.py:47
  6.3 3.0 %collective-permute-start.2 = (f32[2,2,128]{2,1,0:T(2,128)S(1)}, f32[2,2,128]{2,1,0:T(2,128)S(1)}, u32[]{:S(2)}, u32[]{:S(2)}) collective-permute-start(f32[2,2,128]{2,1,0:T(2,128)S(1)} %pad_maximum_fusion.16), channel_id=1, source_target_pairs={{0,3},{1,2},{2,1},{3,0},{4,7},{5,6},{6,5},{7,4},{8,11},{9,10},{10,... | collective-permute-start | bytes 6152 | tf_op jit(solution)/shard_map/ppermute | solution.py:47
  6.3 3.0 %collective-permute-start = (f32[2,2,128]{2,1,0:T(2,128)S(1)}, f32[2,2,128]{2,1,0:T(2,128)S(1)}, u32[]{:S(2)}, u32[]{:S(2)}) collective-permute-start(f32[2,2,128]{2,1,0:T(2,128)S(1)} %pad_maximum_fusion.16), channel_id=1, source_target_pairs={{0,1},{1,0},{2,3},{3,2},{4,5},{5,4},{6,7},{7,6},{8,9},{9,8},{10,11... | collective-permute-start | bytes 6152 | tf_op jit(solution)/shard_map/ppermute | solution.py:47
  7.7 1.9 %copy-start.3 = (bf16[32,2,8,128]{3,2,1,0:T(8,128)(2,1)S(1)}, bf16[32,2,8,128]{3,2,1,0:T(8,128)(2,1)}, u32[]{:S(2)}) copy-start(bf16[32,2,8,128]{3,2,1,0:T(8,128)(2,1)} %param.11) | copy-start | bytes 393220
  7.8 1.9 %copy-start.5 = (bf16[3,32]{1,0:T(4,128)(2,1)S(1)}, bf16[3,32]{1,0:T(4,128)(2,1)}, u32[]{:S(2)}) copy-start(bf16[3,32]{1,0:T(4,128)(2,1)} %param.14) | copy-start | bytes 580
  10.0 7.1 %collective-permute-start.3 = (bf16[32,1,8,128]{3,0,2,1:T(8,128)(2,1)S(1)}, bf16[32,1,8,128]{3,0,2,1:T(8,128)(2,1)S(1)}, u32[]{:S(2)}, u32[]{:S(2)}) collective-permute-start(bf16[32,1,8,128]{3,0,2,1:T(8,128)(2,1)S(1)} %get-tuple-element.50), channel_id=1, source_target_pairs={{0,4},{4,8},{8,12},{12,16},{16,20},{20,24},{24,28},{28,0},{1,5},{5... | collective-permute-start | bytes 196616 | tf_op jit(solution)/shard_map/ppermute | solution.py:15
  11.6 5.6 %collective-permute-start.4 = (bf16[32,1,8,128]{3,0,2,1:T(8,128)(2,1)S(1)}, bf16[32,1,8,128]{3,0,2,1:T(8,128)(2,1)S(1)}, u32[]{:S(2)}, u32[]{:S(2)}) collective-permute-start(bf16[32,1,8,128]{3,0,2,1:T(8,128)(2,1)S(1)} %get-tuple-element.51), channel_id=1, source_target_pairs={{4,0},{8,4},{12,8},{16,12},{20,16},{24,20},{28,24},{0,28},{5,1},{9... | collective-permute-start | bytes 196616 | tf_op jit(solution)/shard_map/ppermute | solution.py:18
  17.1 3.4 %collective-permute-start.6 = (bf16[32,4,1,128]{3,0,2,1:T(8,128)(2,1)S(1)}, bf16[32,4,1,128]{3,0,2,1:T(8,128)(2,1)S(1)}, u32[]{:S(2)}, u32[]{:S(2)}) collective-permute-start(bf16[32,4,1,128]{3,0,2,1:T(8,128)(2,1)S(1)} %get-tuple-element.34), channel_id=1, source_target_pairs={{0,1},{1,2},{2,3},{3,0},{4,5},{5,6},{6,7},{7,4},{8,9},{9,10},{10,1... | collective-permute-start | bytes 98312 | tf_op jit(solution)/shard_map/ppermute | solution.py:15
  17.2 3.3 %collective-permute-start.5 = (bf16[32,4,1,128]{3,0,2,1:T(8,128)(2,1)S(1)}, bf16[32,4,1,128]{3,0,2,1:T(8,128)(2,1)S(1)}, u32[]{:S(2)}, u32[]{:S(2)}) collective-permute-start(bf16[32,4,1,128]{3,0,2,1:T(8,128)(2,1)S(1)} %get-tuple-element.35), channel_id=1, source_target_pairs={{1,0},{2,1},{3,2},{0,3},{5,4},{6,5},{7,6},{4,7},{9,8},{10,9},{11,1... | collective-permute-start | bytes 98312 | tf_op jit(solution)/shard_map/ppermute | solution.py:18
  22.7 7.4 %collective-permute-start.7 = (bf16[32,1,8,128]{3,0,2,1:T(8,128)(2,1)S(1)}, bf16[32,1,8,128]{3,0,2,1:T(8,128)(2,1)S(1)}, u32[]{:S(2)}, u32[]{:S(2)}) collective-permute-start(bf16[32,1,8,128]{3,0,2,1:T(8,128)(2,1)S(1)} %get-tuple-element.48), channel_id=1, source_target_pairs={{0,4},{4,8},{8,12},{12,16},{16,20},{20,24},{24,28},{28,0},{1,5},{5... | collective-permute-start | bytes 196616 | tf_op jit(solution)/shard_map/ppermute | solution.py:15
  23.9 6.2 %collective-permute-start.8 = (bf16[32,1,8,128]{3,0,2,1:T(8,128)(2,1)S(1)}, bf16[32,1,8,128]{3,0,2,1:T(8,128)(2,1)S(1)}, u32[]{:S(2)}, u32[]{:S(2)}) collective-permute-start(bf16[32,1,8,128]{3,0,2,1:T(8,128)(2,1)S(1)} %get-tuple-element.49), channel_id=1, source_target_pairs={{4,0},{8,4},{12,8},{16,12},{20,16},{24,20},{28,24},{0,28},{5,1},{9... | collective-permute-start | bytes 196616 | tf_op jit(solution)/shard_map/ppermute | solution.py:18
  30.1 3.4 %collective-permute-start.10 = (bf16[32,4,1,128]{3,0,2,1:T(8,128)(2,1)S(1)}, bf16[32,4,1,128]{3,0,2,1:T(8,128)(2,1)S(1)}, u32[]{:S(2)}, u32[]{:S(2)}) collective-permute-start(bf16[32,4,1,128]{3,0,2,1:T(8,128)(2,1)S(1)} %get-tuple-element.30), channel_id=1, source_target_pairs={{0,1},{1,2},{2,3},{3,0},{4,5},{5,6},{6,7},{7,4},{8,9},{9,10},{10,1... | collective-permute-start | bytes 98312 | tf_op jit(solution)/shard_map/ppermute | solution.py:15
  30.3 3.2 %collective-permute-start.9 = (bf16[32,4,1,128]{3,0,2,1:T(8,128)(2,1)S(1)}, bf16[32,4,1,128]{3,0,2,1:T(8,128)(2,1)S(1)}, u32[]{:S(2)}, u32[]{:S(2)}) collective-permute-start(bf16[32,4,1,128]{3,0,2,1:T(8,128)(2,1)S(1)} %get-tuple-element.31), channel_id=1, source_target_pairs={{1,0},{2,1},{3,2},{0,3},{5,4},{6,5},{7,6},{4,7},{9,8},{10,9},{11,1... | collective-permute-start | bytes 98312 | tf_op jit(solution)/shard_map/ppermute | solution.py:18
  34.9 6.5 %copy-start.2 = (bf16[3,3,3,32,32]{4,3,2,1,0:T(8,128)(2,1)S(1)}, bf16[3,3,3,32,32]{4,3,2,1,0:T(8,128)(2,1)}, u32[]{:S(2)}) copy-start(bf16[3,3,3,32,32]{4,3,2,1,0:T(8,128)(2,1)} %param.12) | copy-start | bytes 165892
  35.3 2.3 %collective-permute-start.11 = (f32[224,128]{1,0:T(8,128)S(1)}, f32[224,128]{1,0:T(8,128)S(1)}, u32[]{:S(2)}, u32[]{:S(2)}) collective-permute-start(f32[224,128]{1,0:T(8,128)S(1)} %fusion.61), channel_id=1, source_target_pairs={{0,1},{1,0},{2,3},{3,2},{4,5},{5,4},{6,7},{7,6},{8,9},{9,8},{10,11... | collective-permute-start | bytes 344072 | tf_op jit(solution)/shard_map/ppermute | solution.py:66
  37.8 7.0 %collective-permute-start.14 = (f32[224,128]{1,0:T(8,128)S(1)}, f32[224,128]{1,0:T(8,128)S(1)}, u32[]{:S(2)}, u32[]{:S(2)}) collective-permute-start(f32[224,128]{1,0:T(8,128)S(1)} %select_add_fusion), channel_id=1, source_target_pairs={{0,6},{1,7},{2,4},{3,5},{4,2},{5,3},{6,0},{7,1},{8,14},{9,15},{10,... | collective-permute-start | bytes 344072 | tf_op jit(solution)/shard_map/ppermute | solution.py:70
  38.2 7.8 %collective-permute-start.13 = (f32[224,128]{1,0:T(8,128)S(1)}, f32[224,128]{1,0:T(8,128)S(1)}, u32[]{:S(2)}, u32[]{:S(2)}) collective-permute-start(f32[224,128]{1,0:T(8,128)S(1)} %select_add_fusion), channel_id=1, source_target_pairs={{0,4},{1,5},{2,6},{3,7},{4,0},{5,1},{6,2},{7,3},{8,12},{9,13},{10,... | collective-permute-start | bytes 344072 | tf_op jit(solution)/shard_map/ppermute | solution.py:70
  40.2 5.8 %collective-permute-start.12 = (f32[224,128]{1,0:T(8,128)S(1)}, f32[224,128]{1,0:T(8,128)S(1)}, u32[]{:S(2)}, u32[]{:S(2)}) collective-permute-start(f32[224,128]{1,0:T(8,128)S(1)} %select_add_fusion), channel_id=1, source_target_pairs={{0,2},{1,3},{2,0},{3,1},{4,6},{5,7},{6,4},{7,5},{8,10},{9,11},{10,... | collective-permute-start | bytes 344072 | tf_op jit(solution)/shard_map/ppermute | solution.py:70
  46.0 8.8 %collective-permute-start.17 = (f32[224,128]{1,0:T(8,128)S(1)}, f32[224,128]{1,0:T(8,128)S(1)}, u32[]{:S(2)}, u32[]{:S(2)}) collective-permute-start(f32[224,128]{1,0:T(8,128)S(1)} %add_add_fusion.1), channel_id=1, source_target_pairs={{0,24},{1,25},{2,26},{3,27},{4,28},{5,29},{6,30},{7,31},{8,16},{9,... | collective-permute-start | bytes 344072 | tf_op jit(solution)/shard_map/ppermute | solution.py:70
  50.8 8.1 %collective-permute-start.16 = (f32[224,128]{1,0:T(8,128)S(1)}, f32[224,128]{1,0:T(8,128)S(1)}, u32[]{:S(2)}, u32[]{:S(2)}) collective-permute-start(f32[224,128]{1,0:T(8,128)S(1)} %add_add_fusion.1), channel_id=1, source_target_pairs={{0,16},{1,17},{2,18},{3,19},{4,20},{5,21},{6,22},{7,23},{8,24},{9,... | collective-permute-start | bytes 344072 | tf_op jit(solution)/shard_map/ppermute | solution.py:70
  50.8 8.1 %collective-permute-start.15 = (f32[224,128]{1,0:T(8,128)S(1)}, f32[224,128]{1,0:T(8,128)S(1)}, u32[]{:S(2)}, u32[]{:S(2)}) collective-permute-start(f32[224,128]{1,0:T(8,128)S(1)} %add_add_fusion.1), channel_id=1, source_target_pairs={{0,8},{1,9},{2,10},{3,11},{4,12},{5,13},{6,14},{7,15},{8,0},{9,1},... | collective-permute-start | bytes 344072 | tf_op jit(solution)/shard_map/ppermute | solution.py:70
  58.9 1.4 %collective-permute-start.18 = (f32[224,128]{1,0:T(8,128)S(1)}, f32[224,128]{1,0:T(8,128)S(1)}, u32[]{:S(2)}, u32[]{:S(2)}) collective-permute-start(f32[224,128]{1,0:T(8,128)S(1)} %add_add_fusion), channel_id=1, source_target_pairs={{0,1},{1,0},{2,3},{3,2},{4,5},{5,4},{6,7},{7,6},{8,9},{9,8},{10,11... | collective-permute-start | bytes 344072 | tf_op jit(solution)/shard_map/ppermute | solution.py:77
  (3 other events, 4.1 us)

commit v16 on v14

--- a/solution.py
+++ b/solution.py
@@ -58,9 +58,9 @@
     if total & (total - 1) or sizes[0] % 2:
         return lax.psum(value, axes)
     half = value.shape[0] // 2
-    upper = lax.axis_index(axes[0]) % 2 == 1
-    keep = jnp.where(upper, value[half:], value[:half])
-    send = jnp.where(upper, value[:half], value[half:])
+    side = lax.axis_index(axes[0]) % 2
+    keep = lax.dynamic_slice_in_dim(value, side * half, half)
+    send = lax.dynamic_slice_in_dim(value, (1 - side) * half, half)
     index_axes = tuple(reversed(axes))
     partner = [(i, i ^ 1) for i in range(total)]
     keep = keep + lax.ppermute(send, index_axes, partner)
@@ -75,8 +75,8 @@
     for bit in bits:
         keep = keep + lax.ppermute(keep, index_axes, [(i, i ^ bit) for i in range(total)])
     other = lax.ppermute(keep, index_axes, partner)
-    return jnp.where(
-        upper, jnp.concatenate((other, keep)), jnp.concatenate((keep, other))
+    return lax.dynamic_update_slice_in_dim(
+        jnp.concatenate((other, other)), keep, side * half, axis=0
     )
 
 

time: 63.7 us -> 62.6 us (0.983)
  starting transfers between devices: 25.7 us -> 23.6 us
  waiting for transfers between devices: 21.4 us -> 22.6 us
    ppermute x4, starting transfers between devices: 10.1 us -> 8.71 us  [extended(): lax.ppermute(lax.slice_in_dim(block, 0, width, axis=dim), axis, backward)]
    ppermute x4, waiting for transfers between devices: 0.02 us -> 1.2 us  [extended(): lax.ppermute(lax.slice_in_dim(block, 0, width, axis=dim), axis, backward)]
  transfers between devices with their start and end apart: 18 -> 18, of which waited for: 11 -> 13; matrix products, arithmetic and copies ran while one was open for 8% -> 8% of each run, Pallas kernels for 0% -> 0%
where the time goes in v16:
time: 62.6 us; the launch traced here: 62.4 us
  starting transfers between devices  23.6 us (38%)
  waiting for transfers between devices  22.6 us (36%)
  local copies, waits for them, and re-layouts  7.78 us (12%)
  matrix products  4.25 us (7%)
  other arithmetic  3.07 us (5%)
  between operations  1.24 us (2%)
    ppermute x4, starting transfers between devices, extended(): lax.ppermute(lax.slice_in_dim(block, 0, width, axis=dim), axis, backward)  8.71 us
    ppermute x2, waiting for transfers between devices, split_sum(): lax.ppermute(keep, index_axes, [(i, i ^ bit) for i in range(total)])  7.22 us
    ppermute x4, waiting for transfers between devices, extended(): lax.ppermute(lax.slice_in_dim(block, block.shape[dim] - width, None, axis...  6.27 us
    ppermute x3, waiting for transfers between devices, split_sum(): lax.ppermute(keep, index_axes, [(i, i ^ mask) for i in range(total)])  5.24 us
    ppermute x2, starting transfers between devices, split_sum(): lax.ppermute(keep, index_axes, [(i, i ^ bit) for i in range(total)])  3.83 us
    ppermute x3, starting transfers between devices, split_sum(): lax.ppermute(keep, index_axes, [(i, i ^ mask) for i in range(total)])  3.57 us
    ppermute x4, starting transfers between devices, extended(): lax.ppermute(lax.slice_in_dim(block, block.shape[dim] - width, None, axis...  3.19 us
    ppermute x3, starting transfers between devices, quad_sum(): lax.ppermute(value, axis, [(i, i ^ mask) for i in range(count)])  3.15 us
  transfers between devices with their start and end apart: 18, of which 13 were waited for; matrix products, arithmetic and copies ran while one was open for 8% of the time, Pallas kernels for 0%

profile of v16, /device:TPU:0, one launch (start us, length us, event | category | flops | bytes accessed | tf_op | source)
XLA Modules:
  0.0 62.4 jit_solution(4978390891678338639)
XLA Ops:
  0.7 1.0 %fusion.22 = bf16[32,2,8,128]{3,0,2,1:T(8,128)(2,1)S(1)} fusion(bf16[32,2,8,128]{3,2,1,0:T(8,128)(2,1)} %param.11), kind=kLoop, calls=%fused_computation.40 | loop fusion | flops 393216 | bytes 262144 | tf_op jit(solution)/shard_map/convert_element_type | solution.py:167
  3.8 2.6 %collective-permute-start.1 = (f32[2,2,128]{2,1,0:T(2,128)S(1)}, f32[2,2,128]{2,1,0:T(2,128)S(1)}, u32[]{:S(2)}, u32[]{:S(2)}) collective-permute-start(f32[2,2,128]{2,1,0:T(2,128)S(1)} %pad_maximum_fusion.14), channel_id=1, source_target_pairs={{0,2},{1,3},{2,0},{3,1},{4,6},{5,7},{6,4},{7,5},{8,10},{9,11},{10,... | collective-permute-start | bytes 6152 | tf_op jit(solution)/shard_map/ppermute | solution.py:47
  6.5 1.1 %fusion.88 = (bf16[32,2,8,1]{3,2,1,0:T(8,128)(2,1)S(1)}, bf16[32,2,8,1]{3,2,1,0:T(8,128)(2,1)S(1)}) fusion(bf16[32,2,8,128]{3,2,1,0:T(8,128)(2,1)} %param.9), kind=kLoop, calls=%fused_computation.169 | loop fusion | bytes 4096 | tf_op jit(solution)/shard_map/jit(_roll_static)/slice | solution.py:150
  8.1 1.3 %collective-permute-done.2 = f32[2,2,128]{2,1,0:T(2,128)S(1)} collective-permute-done((f32[2,2,128]{2,1,0:T(2,128)S(1)}, f32[2,2,128]{2,1,0:T(2,128)S(1)}, u32[]{:S(2)}, u32[]{:S(2)}) %collective-permute-start.2) | collective-permute-done | bytes 2080 | tf_op jit(solution)/shard_map/ppermute | solution.py:47
  10.0 1.6 %collective-permute-start.3 = (bf16[32,1,8,128]{3,0,2,1:T(8,128)(2,1)S(1)}, bf16[32,1,8,128]{3,0,2,1:T(8,128)(2,1)S(1)}, u32[]{:S(2)}, u32[]{:S(2)}) collective-permute-start(bf16[32,1,8,128]{3,0,2,1:T(8,128)(2,1)S(1)} %get-tuple-element.50), channel_id=1, source_target_pairs={{0,4},{4,8},{8,12},{12,16},{16,20},{20,24},{24,28},{28,0},{1,5},{5... | collective-permute-start | bytes 196616 | tf_op jit(solution)/shard_map/ppermute | solution.py:15
  11.6 3.2 %collective-permute-start.4 = (bf16[32,1,8,128]{3,0,2,1:T(8,128)(2,1)S(1)}, bf16[32,1,8,128]{3,0,2,1:T(8,128)(2,1)S(1)}, u32[]{:S(2)}, u32[]{:S(2)}) collective-permute-start(bf16[32,1,8,128]{3,0,2,1:T(8,128)(2,1)S(1)} %get-tuple-element.51), channel_id=1, source_target_pairs={{4,0},{8,4},{12,8},{16,12},{20,16},{24,20},{28,24},{0,28},{5,1},{9... | collective-permute-start | bytes 196616 | tf_op jit(solution)/shard_map/ppermute | solution.py:18
  14.9 2.3 %collective-permute-done.3 = bf16[32,1,8,128]{3,0,2,1:T(8,128)(2,1)S(1)} collective-permute-done((bf16[32,1,8,128]{3,0,2,1:T(8,128)(2,1)S(1)}, bf16[32,1,8,128]{3,0,2,1:T(8,128)(2,1)S(1)}, u32[]{:S(2)}, u32[]{:S(2)}) %collective-permute-start.3) | collective-permute-done | bytes 65568 | tf_op jit(solution)/shard_map/ppermute | solution.py:15
  17.8 1.1 %collective-permute-done.5 = bf16[32,4,1,128]{3,0,2,1:T(8,128)(2,1)S(1)} collective-permute-done((bf16[32,4,1,128]{3,0,2,1:T(8,128)(2,1)S(1)}, bf16[32,4,1,128]{3,0,2,1:T(8,128)(2,1)S(1)}, u32[]{:S(2)}, u32[]{:S(2)}) %collective-permute-start.5) | collective-permute-done | bytes 32800 | tf_op jit(solution)/shard_map/ppermute | solution.py:18
  18.9 1.8 %collective-permute-done.6 = bf16[32,4,1,128]{3,0,2,1:T(8,128)(2,1)S(1)} collective-permute-done((bf16[32,4,1,128]{3,0,2,1:T(8,128)(2,1)S(1)}, bf16[32,4,1,128]{3,0,2,1:T(8,128)(2,1)S(1)}, u32[]{:S(2)}, u32[]{:S(2)}) %collective-permute-start.6) | collective-permute-done | bytes 32800 | tf_op jit(solution)/shard_map/ppermute | solution.py:15
  22.9 1.1 %collective-permute-start.7 = (bf16[32,1,8,128]{3,0,2,1:T(8,128)(2,1)S(1)}, bf16[32,1,8,128]{3,0,2,1:T(8,128)(2,1)S(1)}, u32[]{:S(2)}, u32[]{:S(2)}) collective-permute-start(bf16[32,1,8,128]{3,0,2,1:T(8,128)(2,1)S(1)} %get-tuple-element.48), channel_id=1, source_target_pairs={{0,4},{4,8},{8,12},{12,16},{16,20},{20,24},{24,28},{28,0},{1,5},{5... | collective-permute-start | bytes 196616 | tf_op jit(solution)/shard_map/ppermute | solution.py:15
  23.9 3.7 %collective-permute-start.8 = (bf16[32,1,8,128]{3,0,2,1:T(8,128)(2,1)S(1)}, bf16[32,1,8,128]{3,0,2,1:T(8,128)(2,1)S(1)}, u32[]{:S(2)}, u32[]{:S(2)}) collective-permute-start(bf16[32,1,8,128]{3,0,2,1:T(8,128)(2,1)S(1)} %get-tuple-element.49), channel_id=1, source_target_pairs={{4,0},{8,4},{12,8},{16,12},{20,16},{24,20},{28,24},{0,28},{5,1},{9... | collective-permute-start | bytes 196616 | tf_op jit(solution)/shard_map/ppermute | solution.py:18
  27.9 2.0 %collective-permute-done.7 = bf16[32,1,8,128]{3,0,2,1:T(8,128)(2,1)S(1)} collective-permute-done((bf16[32,1,8,128]{3,0,2,1:T(8,128)(2,1)S(1)}, bf16[32,1,8,128]{3,0,2,1:T(8,128)(2,1)S(1)}, u32[]{:S(2)}, u32[]{:S(2)}) %collective-permute-start.7) | collective-permute-done | bytes 65568 | tf_op jit(solution)/shard_map/ppermute | solution.py:15
  30.0 1.7 %collective-permute-start.9 = (bf16[32,4,1,128]{3,0,2,1:T(8,128)(2,1)S(1)}, bf16[32,4,1,128]{3,0,2,1:T(8,128)(2,1)S(1)}, u32[]{:S(2)}, u32[]{:S(2)}) collective-permute-start(bf16[32,4,1,128]{3,0,2,1:T(8,128)(2,1)S(1)} %get-tuple-element.31), channel_id=1, source_target_pairs={{1,0},{2,1},{3,2},{0,3},{5,4},{6,5},{7,6},{4,7},{9,8},{10,9},{11,1... | collective-permute-start | bytes 98312 | tf_op jit(solution)/shard_map/ppermute | solution.py:18
  31.7 1.1 %fusion.1 = f32[9,3,32,32]{2,3,0,1:T(8,128)S(1)} fusion(bf16[9,32,2,8,128]{4,1,3,2,0:T(8,128)(2,1)S(1)} %fusion.50, bf16[1,32,2,8,128]{4,1,3,2,0:T(8,128)(2,1)S(1)} %maximum_bitcast_fusion.7, bf16[1,32,2,8,128]{4,1,3,2,0:T(8,128)(2,1)S(1)} %bitcast.252, bf16[1,32,2,8,128]{4,1,3,2,0:T(8,128)(2,1)S(1)} %maximum_bitcast_fusion.6), kind=kOutput, calls=%fused_computation.4 | convolution fusion | flops 114453504 | bytes 1683456 | tf_op jit(solution)/shard_map/toxzy,sixzy->tsoi/dot_general | solution.py:151
  33.6 1.1 %fusion.3 = f32[9,3,32,32]{2,3,0,1:T(8,128)S(1)} fusion(bf16[1,32,2,8,128]{4,1,3,2,0:T(8,128)(2,1)S(1)} %get-tuple-element.60, bf16[1,32,2,8,128]{4,1,3,2,0:T(8,128)(2,1)S(1)} %bitcast.258, bf16[1,32,2,8,128]{4,1,3,2,0:T(8,128)(2,1)S(1)} %get-tuple-element.59, bf16[9,32,2,8,128]{4,1,3,2,0:T(8,128)(2,1)S(1)} %fusion.40), kind=kOutput, calls=%fused_computation.7 | convolution fusion | flops 114453504 | bytes 1683456 | tf_op jit(solution)/shard_map/toxzy,sixzy->tsoi/dot_general | solution.py:151
  35.2 1.0 %collective-permute-start.11 = (f32[224,128]{1,0:T(8,128)S(1)}, f32[224,128]{1,0:T(8,128)S(1)}, u32[]{:S(2)}, u32[]{:S(2)}) collective-permute-start(f32[224,128]{1,0:T(8,128)S(1)} %constant_dynamic-slice_fusion), channel_id=1, source_target_pairs={{0,1},{1,0},{2,3},{3,2},{4,5},{5,4},{6,7},{7,6},{8,9},{9,8},{10,11... | collective-permute-start | bytes 344072 | tf_op jit(solution)/shard_map/ppermute | solution.py:66
  37.2 1.2 %collective-permute-start.12 = (f32[224,128]{1,0:T(8,128)S(1)}, f32[224,128]{1,0:T(8,128)S(1)}, u32[]{:S(2)}, u32[]{:S(2)}) collective-permute-start(f32[224,128]{1,0:T(8,128)S(1)} %dynamic-slice_add_fusion), channel_id=1, source_target_pairs={{0,2},{1,3},{2,0},{3,1},{4,6},{5,7},{6,4},{7,5},{8,10},{9,11},{10,... | collective-permute-start | bytes 344072 | tf_op jit(solution)/shard_map/ppermute | solution.py:70
  39.5 1.3 %collective-permute-start.14 = (f32[224,128]{1,0:T(8,128)S(1)}, f32[224,128]{1,0:T(8,128)S(1)}, u32[]{:S(2)}, u32[]{:S(2)}) collective-permute-start(f32[224,128]{1,0:T(8,128)S(1)} %dynamic-slice_add_fusion), channel_id=1, source_target_pairs={{0,6},{1,7},{2,4},{3,5},{4,2},{5,3},{6,0},{7,1},{8,14},{9,15},{10,... | collective-permute-start | bytes 344072 | tf_op jit(solution)/shard_map/ppermute | solution.py:70
  40.8 2.2 %collective-permute-done.12 = f32[224,128]{1,0:T(8,128)S(1)} collective-permute-done((f32[224,128]{1,0:T(8,128)S(1)}, f32[224,128]{1,0:T(8,128)S(1)}, u32[]{:S(2)}, u32[]{:S(2)}) %collective-permute-start.12) | collective-permute-done | bytes 114720 | tf_op jit(solution)/shard_map/ppermute | solution.py:70
  43.0 3.0 %collective-permute-done.13 = f32[224,128]{1,0:T(8,128)S(1)} collective-permute-done((f32[224,128]{1,0:T(8,128)S(1)}, f32[224,128]{1,0:T(8,128)S(1)}, u32[]{:S(2)}, u32[]{:S(2)}) %collective-permute-start.13) | collective-permute-done | bytes 114720 | tf_op jit(solution)/shard_map/ppermute | solution.py:70
  46.1 1.4 %collective-permute-start.15 = (f32[224,128]{1,0:T(8,128)S(1)}, f32[224,128]{1,0:T(8,128)S(1)}, u32[]{:S(2)}, u32[]{:S(2)}) collective-permute-start(f32[224,128]{1,0:T(8,128)S(1)} %add_add_fusion), channel_id=1, source_target_pairs={{0,8},{1,9},{2,10},{3,11},{4,12},{5,13},{6,14},{7,15},{8,0},{9,1},... | collective-permute-start | bytes 344072 | tf_op jit(solution)/shard_map/ppermute | solution.py:76
  47.9 3.0 %collective-permute-done.15 = f32[224,128]{1,0:T(8,128)S(1)} collective-permute-done((f32[224,128]{1,0:T(8,128)S(1)}, f32[224,128]{1,0:T(8,128)S(1)}, u32[]{:S(2)}, u32[]{:S(2)}) %collective-permute-start.15) | collective-permute-done | bytes 114720 | tf_op jit(solution)/shard_map/ppermute | solution.py:76
  50.9 2.5 %collective-permute-start.16 = (f32[224,128]{1,0:T(8,128)S(1)}, f32[224,128]{1,0:T(8,128)S(1)}, u32[]{:S(2)}, u32[]{:S(2)}) collective-permute-start(f32[224,128]{1,0:T(8,128)S(1)} %add.124), channel_id=1, source_target_pairs={{0,16},{1,17},{2,18},{3,19},{4,20},{5,21},{6,22},{7,23},{8,24},{9,... | collective-permute-start | bytes 344072 | tf_op jit(solution)/shard_map/ppermute | solution.py:76
  53.7 4.2 %collective-permute-done.16 = f32[224,128]{1,0:T(8,128)S(1)} collective-permute-done((f32[224,128]{1,0:T(8,128)S(1)}, f32[224,128]{1,0:T(8,128)S(1)}, u32[]{:S(2)}, u32[]{:S(2)}) %collective-permute-start.16) | collective-permute-done | bytes 114720 | tf_op jit(solution)/shard_map/ppermute | solution.py:76
  (112 shorter events, 14.8 us)
Async XLA Ops:
  0.6 20.4 %copy-start = (bf16[3,3,3,32,32]{4,3,2,1,0:T(8,128)(2,1)S(1)}, bf16[3,3,3,32,32]{4,3,2,1,0:T(8,128)(2,1)}, u32[]{:S(2)}) copy-start(bf16[3,3,3,32,32]{4,3,2,1,0:T(8,128)(2,1)} %param.13) | copy-start | bytes 165892
  0.6 6.9 %copy-start.1 = (bf16[32,2,8,128]{3,2,1,0:T(8,128)(2,1)S(1)}, bf16[32,2,8,128]{3,2,1,0:T(8,128)(2,1)}, u32[]{:S(2)}) copy-start(bf16[32,2,8,128]{3,2,1,0:T(8,128)(2,1)} %param.9) | copy-start | bytes 393220
  3.3 4.8 %collective-permute-start = (f32[2,2,128]{2,1,0:T(2,128)S(1)}, f32[2,2,128]{2,1,0:T(2,128)S(1)}, u32[]{:S(2)}, u32[]{:S(2)}) collective-permute-start(f32[2,2,128]{2,1,0:T(2,128)S(1)} %pad_maximum_fusion.14), channel_id=1, source_target_pairs={{0,1},{1,0},{2,3},{3,2},{4,5},{5,4},{6,7},{7,6},{8,9},{9,8},{10,11... | collective-permute-start | bytes 6152 | tf_op jit(solution)/shard_map/ppermute | solution.py:47
  3.8 4.3 %collective-permute-start.1 = (f32[2,2,128]{2,1,0:T(2,128)S(1)}, f32[2,2,128]{2,1,0:T(2,128)S(1)}, u32[]{:S(2)}, u32[]{:S(2)}) collective-permute-start(f32[2,2,128]{2,1,0:T(2,128)S(1)} %pad_maximum_fusion.14), channel_id=1, source_target_pairs={{0,2},{1,3},{2,0},{3,1},{4,6},{5,7},{6,4},{7,5},{8,10},{9,11},{10,... | collective-permute-start | bytes 6152 | tf_op jit(solution)/shard_map/ppermute | solution.py:47
  6.4 3.0 %collective-permute-start.2 = (f32[2,2,128]{2,1,0:T(2,128)S(1)}, f32[2,2,128]{2,1,0:T(2,128)S(1)}, u32[]{:S(2)}, u32[]{:S(2)}) collective-permute-start(f32[2,2,128]{2,1,0:T(2,128)S(1)} %pad_maximum_fusion.14), channel_id=1, source_target_pairs={{0,3},{1,2},{2,1},{3,0},{4,7},{5,6},{6,5},{7,4},{8,11},{9,10},{10,... | collective-permute-start | bytes 6152 | tf_op jit(solution)/shard_map/ppermute | solution.py:47
  7.7 1.7 %copy-start.6 = (f32[2,128]{1,0:T(2,128)S(1)}, f32[2,128]{1,0:T(2,128)}, u32[]{:S(2)}) copy-start(f32[2,128]{1,0:T(2,128)} %param.16) | copy-start | bytes 3076
  7.7 1.9 %copy-start.3 = (bf16[32,2,8,128]{3,2,1,0:T(8,128)(2,1)S(1)}, bf16[32,2,8,128]{3,2,1,0:T(8,128)(2,1)}, u32[]{:S(2)}) copy-start(bf16[32,2,8,128]{3,2,1,0:T(8,128)(2,1)} %param.11) | copy-start | bytes 393220
  7.7 1.9 %copy-start.5 = (bf16[3,32]{1,0:T(4,128)(2,1)S(1)}, bf16[3,32]{1,0:T(4,128)(2,1)}, u32[]{:S(2)}) copy-start(bf16[3,32]{1,0:T(4,128)(2,1)} %param.14) | copy-start | bytes 580
  10.0 7.1 %collective-permute-start.3 = (bf16[32,1,8,128]{3,0,2,1:T(8,128)(2,1)S(1)}, bf16[32,1,8,128]{3,0,2,1:T(8,128)(2,1)S(1)}, u32[]{:S(2)}, u32[]{:S(2)}) collective-permute-start(bf16[32,1,8,128]{3,0,2,1:T(8,128)(2,1)S(1)} %get-tuple-element.50), channel_id=1, source_target_pairs={{0,4},{4,8},{8,12},{12,16},{16,20},{20,24},{24,28},{28,0},{1,5},{5... | collective-permute-start | bytes 196616 | tf_op jit(solution)/shard_map/ppermute | solution.py:15
  11.6 5.7 %collective-permute-start.4 = (bf16[32,1,8,128]{3,0,2,1:T(8,128)(2,1)S(1)}, bf16[32,1,8,128]{3,0,2,1:T(8,128)(2,1)S(1)}, u32[]{:S(2)}, u32[]{:S(2)}) collective-permute-start(bf16[32,1,8,128]{3,0,2,1:T(8,128)(2,1)S(1)} %get-tuple-element.51), channel_id=1, source_target_pairs={{4,0},{8,4},{12,8},{16,12},{20,16},{24,20},{28,24},{0,28},{5,1},{9... | collective-permute-start | bytes 196616 | tf_op jit(solution)/shard_map/ppermute | solution.py:18
  17.2 1.7 %collective-permute-start.5 = (bf16[32,4,1,128]{3,0,2,1:T(8,128)(2,1)S(1)}, bf16[32,4,1,128]{3,0,2,1:T(8,128)(2,1)S(1)}, u32[]{:S(2)}, u32[]{:S(2)}) collective-permute-start(bf16[32,4,1,128]{3,0,2,1:T(8,128)(2,1)S(1)} %get-tuple-element.35), channel_id=1, source_target_pairs={{1,0},{2,1},{3,2},{0,3},{5,4},{6,5},{7,6},{4,7},{9,8},{10,9},{11,1... | collective-permute-start | bytes 98312 | tf_op jit(solution)/shard_map/ppermute | solution.py:18
  17.3 3.4 %collective-permute-start.6 = (bf16[32,4,1,128]{3,0,2,1:T(8,128)(2,1)S(1)}, bf16[32,4,1,128]{3,0,2,1:T(8,128)(2,1)S(1)}, u32[]{:S(2)}, u32[]{:S(2)}) collective-permute-start(bf16[32,4,1,128]{3,0,2,1:T(8,128)(2,1)S(1)} %get-tuple-element.34), channel_id=1, source_target_pairs={{0,1},{1,2},{2,3},{3,0},{4,5},{5,6},{6,7},{7,4},{8,9},{9,10},{10,1... | collective-permute-start | bytes 98312 | tf_op jit(solution)/shard_map/ppermute | solution.py:15
  22.9 7.0 %collective-permute-start.7 = (bf16[32,1,8,128]{3,0,2,1:T(8,128)(2,1)S(1)}, bf16[32,1,8,128]{3,0,2,1:T(8,128)(2,1)S(1)}, u32[]{:S(2)}, u32[]{:S(2)}) collective-permute-start(bf16[32,1,8,128]{3,0,2,1:T(8,128)(2,1)S(1)} %get-tuple-element.48), channel_id=1, source_target_pairs={{0,4},{4,8},{8,12},{12,16},{16,20},{20,24},{24,28},{28,0},{1,5},{5... | collective-permute-start | bytes 196616 | tf_op jit(solution)/shard_map/ppermute | solution.py:15
  23.9 6.0 %collective-permute-start.8 = (bf16[32,1,8,128]{3,0,2,1:T(8,128)(2,1)S(1)}, bf16[32,1,8,128]{3,0,2,1:T(8,128)(2,1)S(1)}, u32[]{:S(2)}, u32[]{:S(2)}) collective-permute-start(bf16[32,1,8,128]{3,0,2,1:T(8,128)(2,1)S(1)} %get-tuple-element.49), channel_id=1, source_target_pairs={{4,0},{8,4},{12,8},{16,12},{20,16},{24,20},{28,24},{0,28},{5,1},{9... | collective-permute-start | bytes 196616 | tf_op jit(solution)/shard_map/ppermute | solution.py:18
  29.9 3.4 %collective-permute-start.10 = (bf16[32,4,1,128]{3,0,2,1:T(8,128)(2,1)S(1)}, bf16[32,4,1,128]{3,0,2,1:T(8,128)(2,1)S(1)}, u32[]{:S(2)}, u32[]{:S(2)}) collective-permute-start(bf16[32,4,1,128]{3,0,2,1:T(8,128)(2,1)S(1)} %get-tuple-element.30), channel_id=1, source_target_pairs={{0,1},{1,2},{2,3},{3,0},{4,5},{5,6},{6,7},{7,4},{8,9},{9,10},{10,1... | collective-permute-start | bytes 98312 | tf_op jit(solution)/shard_map/ppermute | solution.py:15
  30.0 3.3 %collective-permute-start.9 = (bf16[32,4,1,128]{3,0,2,1:T(8,128)(2,1)S(1)}, bf16[32,4,1,128]{3,0,2,1:T(8,128)(2,1)S(1)}, u32[]{:S(2)}, u32[]{:S(2)}) collective-permute-start(bf16[32,4,1,128]{3,0,2,1:T(8,128)(2,1)S(1)} %get-tuple-element.31), channel_id=1, source_target_pairs={{1,0},{2,1},{3,2},{0,3},{5,4},{6,5},{7,6},{4,7},{9,8},{10,9},{11,1... | collective-permute-start | bytes 98312 | tf_op jit(solution)/shard_map/ppermute | solution.py:18
  34.8 12.6 %copy-start.2 = (bf16[3,3,3,32,32]{4,3,2,1,0:T(8,128)(2,1)S(1)}, bf16[3,3,3,32,32]{4,3,2,1,0:T(8,128)(2,1)}, u32[]{:S(2)}) copy-start(bf16[3,3,3,32,32]{4,3,2,1,0:T(8,128)(2,1)} %param.12) | copy-start | bytes 165892
  35.2 2.0 %collective-permute-start.11 = (f32[224,128]{1,0:T(8,128)S(1)}, f32[224,128]{1,0:T(8,128)S(1)}, u32[]{:S(2)}, u32[]{:S(2)}) collective-permute-start(f32[224,128]{1,0:T(8,128)S(1)} %constant_dynamic-slice_fusion), channel_id=1, source_target_pairs={{0,1},{1,0},{2,3},{3,2},{4,5},{5,4},{6,7},{7,6},{8,9},{9,8},{10,11... | collective-permute-start | bytes 344072 | tf_op jit(solution)/shard_map/ppermute | solution.py:66
  37.2 5.8 %collective-permute-start.12 = (f32[224,128]{1,0:T(8,128)S(1)}, f32[224,128]{1,0:T(8,128)S(1)}, u32[]{:S(2)}, u32[]{:S(2)}) collective-permute-start(f32[224,128]{1,0:T(8,128)S(1)} %dynamic-slice_add_fusion), channel_id=1, source_target_pairs={{0,2},{1,3},{2,0},{3,1},{4,6},{5,7},{6,4},{7,5},{8,10},{9,11},{10,... | collective-permute-start | bytes 344072 | tf_op jit(solution)/shard_map/ppermute | solution.py:70
  38.5 7.6 %collective-permute-start.13 = (f32[224,128]{1,0:T(8,128)S(1)}, f32[224,128]{1,0:T(8,128)S(1)}, u32[]{:S(2)}, u32[]{:S(2)}) collective-permute-start(f32[224,128]{1,0:T(8,128)S(1)} %dynamic-slice_add_fusion), channel_id=1, source_target_pairs={{0,4},{1,5},{2,6},{3,7},{4,0},{5,1},{6,2},{7,3},{8,12},{9,13},{10,... | collective-permute-start | bytes 344072 | tf_op jit(solution)/shard_map/ppermute | solution.py:70
  39.5 6.6 %collective-permute-start.14 = (f32[224,128]{1,0:T(8,128)S(1)}, f32[224,128]{1,0:T(8,128)S(1)}, u32[]{:S(2)}, u32[]{:S(2)}) collective-permute-start(f32[224,128]{1,0:T(8,128)S(1)} %dynamic-slice_add_fusion), channel_id=1, source_target_pairs={{0,6},{1,7},{2,4},{3,5},{4,2},{5,3},{6,0},{7,1},{8,14},{9,15},{10,... | collective-permute-start | bytes 344072 | tf_op jit(solution)/shard_map/ppermute | solution.py:70
  46.1 4.9 %collective-permute-start.15 = (f32[224,128]{1,0:T(8,128)S(1)}, f32[224,128]{1,0:T(8,128)S(1)}, u32[]{:S(2)}, u32[]{:S(2)}) collective-permute-start(f32[224,128]{1,0:T(8,128)S(1)} %add_add_fusion), channel_id=1, source_target_pairs={{0,8},{1,9},{2,10},{3,11},{4,12},{5,13},{6,14},{7,15},{8,0},{9,1},... | collective-permute-start | bytes 344072 | tf_op jit(solution)/shard_map/ppermute | solution.py:76
  50.9 7.0 %collective-permute-start.16 = (f32[224,128]{1,0:T(8,128)S(1)}, f32[224,128]{1,0:T(8,128)S(1)}, u32[]{:S(2)}, u32[]{:S(2)}) collective-permute-start(f32[224,128]{1,0:T(8,128)S(1)} %add.124), channel_id=1, source_target_pairs={{0,16},{1,17},{2,18},{3,19},{4,20},{5,21},{6,22},{7,23},{8,24},{9,... | collective-permute-start | bytes 344072 | tf_op jit(solution)/shard_map/ppermute | solution.py:76
  57.9 1.4 %collective-permute-start.17 = (f32[224,128]{1,0:T(8,128)S(1)}, f32[224,128]{1,0:T(8,128)S(1)}, u32[]{:S(2)}, u32[]{:S(2)}) collective-permute-start(f32[224,128]{1,0:T(8,128)S(1)} %add.125), channel_id=1, source_target_pairs={{0,1},{1,0},{2,3},{3,2},{4,5},{5,4},{6,7},{7,6},{8,9},{9,8},{10,11... | collective-permute-start | bytes 344072 | tf_op jit(solution)/shard_map/ppermute | solution.py:77
  (2 other events, 2.6 us)

commit v17 on v16

--- a/solution.py
+++ b/solution.py
@@ -55,9 +55,10 @@
 def split_sum(value, axes):
     sizes = [lax.axis_size(axis) for axis in axes]
     total = math.prod(sizes)
+    half = value.shape[0] // 2
     if total & (total - 1) or sizes[0] % 2:
-        return lax.psum(value, axes)
-    half = value.shape[0] // 2
+        value = lax.psum(value, axes)
+        return value[:half], value[half:], 0
     side = lax.axis_index(axes[0]) % 2
     keep = lax.dynamic_slice_in_dim(value, side * half, half)
     send = lax.dynamic_slice_in_dim(value, (1 - side) * half, half)
@@ -74,10 +75,7 @@
         bits = bits[2:]
     for bit in bits:
         keep = keep + lax.ppermute(keep, index_axes, [(i, i ^ bit) for i in range(total)])
-    other = lax.ppermute(keep, index_axes, partner)
-    return lax.dynamic_update_slice_in_dim(
-        jnp.concatenate((other, other)), keep, side * half, axis=0
-    )
+    return keep, lax.ppermute(keep, index_axes, partner), side
 
 
 def row_count(shape):
@@ -201,11 +199,21 @@
     hidden_first = jax.nn.silu(first_wide).astype(jnp.bfloat16)
     grad_second = taps_from_halo(second_padded, hidden_first)
     grad_first = taps_from_halo(first_padded, features)
-    reduced = (grad_first * norm_factor, grad_second * norm_factor, grad_out, grad_bias)
-    reduced_shapes = [part.shape for part in reduced]
-    grad_first, grad_second, grad_out, grad_bias = unpack_rows(
-        split_sum(pack_rows(reduced), ("los", "sky")), reduced_shapes
-    )
+    first_half = pack_rows((grad_first * norm_factor, grad_out, grad_bias))
+    second_half = pack_rows((grad_second * norm_factor,))
+    rows = max(first_half.shape[0], second_half.shape[0])
+    first_half, second_half = (
+        jnp.pad(part, ((0, rows - part.shape[0]), (0, 0))) for part in (first_half, second_half)
+    )
+    keep, other, side = split_sum(jnp.concatenate((first_half, second_half)), ("los", "sky"))
+    main_rows = row_count(grad_first.shape)
+    keep_grad = keep[:main_rows].reshape(grad_first.shape)
+    other_grad = other[:main_rows].reshape(grad_first.shape)
+    keep_first = side == 0
+    grad_first = jnp.where(keep_first, keep_grad, other_grad)
+    grad_second = jnp.where(keep_first, other_grad, keep_grad)
+    small = jnp.where(keep_first, keep[main_rows:], other[main_rows:])
+    grad_out, grad_bias = unpack_rows(small, [grad_out.shape, grad_bias.shape])
     return (grad_features, grad_first, grad_second, grad_out, grad_bias)
 
 

time: 62.6 us -> 62.5 us (level)
    reshape x3 -> x1, local copies, waits for them, and re-layouts: 2.5 us -> 0.66 us  [unpack_rows(): parts.append(block.reshape(shape))]
    select_n x0 -> x2, local copies, waits for them, and re-layouts: none -> 1.84 us  [the longest x1 0.92 us: per_device(): grad_first = jnp.where(keep_first, keep_grad, other_grad)]
where the time goes in v17:
time: 62.5 us; the launch traced here: 62.3 us
  starting transfers between devices  23.6 us (38%)
  waiting for transfers between devices  22.6 us (36%)
  local copies, waits for them, and re-layouts  7.63 us (12%)
  matrix products  4.25 us (7%)
  other arithmetic  3.08 us (5%)
  between operations  1.22 us (2%)
    ppermute x4, starting transfers between devices, extended(): lax.ppermute(lax.slice_in_dim(block, 0, width, axis=dim), axis, backward)  8.71 us
    ppermute x2, waiting for transfers between devices, split_sum(): lax.ppermute(keep, index_axes, [(i, i ^ bit) for i in range(total)])  7.22 us
    ppermute x4, waiting for transfers between devices, extended(): lax.ppermute(lax.slice_in_dim(block, block.shape[dim] - width, None, axis...  6.27 us
    ppermute x3, waiting for transfers between devices, split_sum(): lax.ppermute(keep, index_axes, [(i, i ^ mask) for i in range(total)])  5.24 us
    ppermute x2, starting transfers between devices, split_sum(): lax.ppermute(keep, index_axes, [(i, i ^ bit) for i in range(total)])  3.83 us
    ppermute x3, starting transfers between devices, split_sum(): lax.ppermute(keep, index_axes, [(i, i ^ mask) for i in range(total)])  3.57 us
    ppermute x4, starting transfers between devices, extended(): lax.ppermute(lax.slice_in_dim(block, block.shape[dim] - width, None, axis...  3.19 us
    ppermute x3, starting transfers between devices, quad_sum(): lax.ppermute(value, axis, [(i, i ^ mask) for i in range(count)])  3.15 us
  transfers between devices with their start and end apart: 18, of which 13 were waited for; matrix products, arithmetic and copies ran while one was open for 8% of the time, Pallas kernels for 0%

profile of v17, /device:TPU:0, one launch (start us, length us, event | category | flops | bytes accessed | tf_op | source)
XLA Modules:
  0.0 62.3 jit_solution(475932048370026975)
XLA Ops:
  0.7 1.0 %fusion.22 = bf16[32,2,8,128]{3,0,2,1:T(8,128)(2,1)S(1)} fusion(bf16[32,2,8,128]{3,2,1,0:T(8,128)(2,1)} %param.11), kind=kLoop, calls=%fused_computation.40 | loop fusion | flops 393216 | bytes 262144 | tf_op jit(solution)/shard_map/convert_element_type | solution.py:165
  3.8 2.6 %collective-permute-start.1 = (f32[2,2,128]{2,1,0:T(2,128)S(1)}, f32[2,2,128]{2,1,0:T(2,128)S(1)}, u32[]{:S(2)}, u32[]{:S(2)}) collective-permute-start(f32[2,2,128]{2,1,0:T(2,128)S(1)} %pad_maximum_fusion.13), channel_id=1, source_target_pairs={{0,2},{1,3},{2,0},{3,1},{4,6},{5,7},{6,4},{7,5},{8,10},{9,11},{10,... | collective-permute-start | bytes 6152 | tf_op jit(solution)/shard_map/ppermute | solution.py:47
  6.5 1.1 %fusion.87 = (bf16[32,2,8,1]{3,2,1,0:T(8,128)(2,1)S(1)}, bf16[32,2,8,1]{3,2,1,0:T(8,128)(2,1)S(1)}) fusion(bf16[32,2,8,128]{3,2,1,0:T(8,128)(2,1)} %param.9), kind=kLoop, calls=%fused_computation.169 | loop fusion | bytes 4096 | tf_op jit(solution)/shard_map/jit(_roll_static)/slice | solution.py:148
  8.1 1.3 %collective-permute-done.2 = f32[2,2,128]{2,1,0:T(2,128)S(1)} collective-permute-done((f32[2,2,128]{2,1,0:T(2,128)S(1)}, f32[2,2,128]{2,1,0:T(2,128)S(1)}, u32[]{:S(2)}, u32[]{:S(2)}) %collective-permute-start.2) | collective-permute-done | bytes 2080 | tf_op jit(solution)/shard_map/ppermute | solution.py:47
  10.0 1.6 %collective-permute-start.3 = (bf16[32,1,8,128]{3,0,2,1:T(8,128)(2,1)S(1)}, bf16[32,1,8,128]{3,0,2,1:T(8,128)(2,1)S(1)}, u32[]{:S(2)}, u32[]{:S(2)}) collective-permute-start(bf16[32,1,8,128]{3,0,2,1:T(8,128)(2,1)S(1)} %get-tuple-element.50), channel_id=1, source_target_pairs={{0,4},{4,8},{8,12},{12,16},{16,20},{20,24},{24,28},{28,0},{1,5},{5... | collective-permute-start | bytes 196616 | tf_op jit(solution)/shard_map/ppermute | solution.py:15
  11.6 3.2 %collective-permute-start.4 = (bf16[32,1,8,128]{3,0,2,1:T(8,128)(2,1)S(1)}, bf16[32,1,8,128]{3,0,2,1:T(8,128)(2,1)S(1)}, u32[]{:S(2)}, u32[]{:S(2)}) collective-permute-start(bf16[32,1,8,128]{3,0,2,1:T(8,128)(2,1)S(1)} %get-tuple-element.51), channel_id=1, source_target_pairs={{4,0},{8,4},{12,8},{16,12},{20,16},{24,20},{28,24},{0,28},{5,1},{9... | collective-permute-start | bytes 196616 | tf_op jit(solution)/shard_map/ppermute | solution.py:18
  14.9 2.3 %collective-permute-done.3 = bf16[32,1,8,128]{3,0,2,1:T(8,128)(2,1)S(1)} collective-permute-done((bf16[32,1,8,128]{3,0,2,1:T(8,128)(2,1)S(1)}, bf16[32,1,8,128]{3,0,2,1:T(8,128)(2,1)S(1)}, u32[]{:S(2)}, u32[]{:S(2)}) %collective-permute-start.3) | collective-permute-done | bytes 65568 | tf_op jit(solution)/shard_map/ppermute | solution.py:15
  17.8 1.1 %collective-permute-done.5 = bf16[32,4,1,128]{3,0,2,1:T(8,128)(2,1)S(1)} collective-permute-done((bf16[32,4,1,128]{3,0,2,1:T(8,128)(2,1)S(1)}, bf16[32,4,1,128]{3,0,2,1:T(8,128)(2,1)S(1)}, u32[]{:S(2)}, u32[]{:S(2)}) %collective-permute-start.5) | collective-permute-done | bytes 32800 | tf_op jit(solution)/shard_map/ppermute | solution.py:18
  18.9 1.8 %collective-permute-done.6 = bf16[32,4,1,128]{3,0,2,1:T(8,128)(2,1)S(1)} collective-permute-done((bf16[32,4,1,128]{3,0,2,1:T(8,128)(2,1)S(1)}, bf16[32,4,1,128]{3,0,2,1:T(8,128)(2,1)S(1)}, u32[]{:S(2)}, u32[]{:S(2)}) %collective-permute-start.6) | collective-permute-done | bytes 32800 | tf_op jit(solution)/shard_map/ppermute | solution.py:15
  22.9 1.1 %collective-permute-start.7 = (bf16[32,1,8,128]{3,0,2,1:T(8,128)(2,1)S(1)}, bf16[32,1,8,128]{3,0,2,1:T(8,128)(2,1)S(1)}, u32[]{:S(2)}, u32[]{:S(2)}) collective-permute-start(bf16[32,1,8,128]{3,0,2,1:T(8,128)(2,1)S(1)} %get-tuple-element.48), channel_id=1, source_target_pairs={{0,4},{4,8},{8,12},{12,16},{16,20},{20,24},{24,28},{28,0},{1,5},{5... | collective-permute-start | bytes 196616 | tf_op jit(solution)/shard_map/ppermute | solution.py:15
  23.9 3.7 %collective-permute-start.8 = (bf16[32,1,8,128]{3,0,2,1:T(8,128)(2,1)S(1)}, bf16[32,1,8,128]{3,0,2,1:T(8,128)(2,1)S(1)}, u32[]{:S(2)}, u32[]{:S(2)}) collective-permute-start(bf16[32,1,8,128]{3,0,2,1:T(8,128)(2,1)S(1)} %get-tuple-element.49), channel_id=1, source_target_pairs={{4,0},{8,4},{12,8},{16,12},{20,16},{24,20},{28,24},{0,28},{5,1},{9... | collective-permute-start | bytes 196616 | tf_op jit(solution)/shard_map/ppermute | solution.py:18
  27.9 2.0 %collective-permute-done.7 = bf16[32,1,8,128]{3,0,2,1:T(8,128)(2,1)S(1)} collective-permute-done((bf16[32,1,8,128]{3,0,2,1:T(8,128)(2,1)S(1)}, bf16[32,1,8,128]{3,0,2,1:T(8,128)(2,1)S(1)}, u32[]{:S(2)}, u32[]{:S(2)}) %collective-permute-start.7) | collective-permute-done | bytes 65568 | tf_op jit(solution)/shard_map/ppermute | solution.py:15
  30.0 1.7 %collective-permute-start.9 = (bf16[32,4,1,128]{3,0,2,1:T(8,128)(2,1)S(1)}, bf16[32,4,1,128]{3,0,2,1:T(8,128)(2,1)S(1)}, u32[]{:S(2)}, u32[]{:S(2)}) collective-permute-start(bf16[32,4,1,128]{3,0,2,1:T(8,128)(2,1)S(1)} %get-tuple-element.31), channel_id=1, source_target_pairs={{1,0},{2,1},{3,2},{0,3},{5,4},{6,5},{7,6},{4,7},{9,8},{10,9},{11,1... | collective-permute-start | bytes 98312 | tf_op jit(solution)/shard_map/ppermute | solution.py:18
  31.7 1.1 %fusion.1 = f32[9,3,32,32]{2,3,0,1:T(8,128)S(1)} fusion(bf16[9,32,2,8,128]{4,1,3,2,0:T(8,128)(2,1)S(1)} %fusion.50, bf16[1,32,2,8,128]{4,1,3,2,0:T(8,128)(2,1)S(1)} %maximum_bitcast_fusion.7, bf16[1,32,2,8,128]{4,1,3,2,0:T(8,128)(2,1)S(1)} %bitcast.252, bf16[1,32,2,8,128]{4,1,3,2,0:T(8,128)(2,1)S(1)} %maximum_bitcast_fusion.6), kind=kOutput, calls=%fused_computation.4 | convolution fusion | flops 114453504 | bytes 1683456 | tf_op jit(solution)/shard_map/toxzy,sixzy->tsoi/dot_general | solution.py:149
  33.6 1.1 %fusion.3 = f32[9,3,32,32]{2,3,0,1:T(8,128)S(1)} fusion(bf16[1,32,2,8,128]{4,1,3,2,0:T(8,128)(2,1)S(1)} %get-tuple-element.60, bf16[1,32,2,8,128]{4,1,3,2,0:T(8,128)(2,1)S(1)} %bitcast.258, bf16[1,32,2,8,128]{4,1,3,2,0:T(8,128)(2,1)S(1)} %get-tuple-element.59, bf16[9,32,2,8,128]{4,1,3,2,0:T(8,128)(2,1)S(1)} %fusion.40), kind=kOutput, calls=%fused_computation.7 | convolution fusion | flops 114453504 | bytes 1683456 | tf_op jit(solution)/shard_map/toxzy,sixzy->tsoi/dot_general | solution.py:149
  35.1 1.0 %collective-permute-start.11 = (f32[224,128]{1,0:T(8,128)S(1)}, f32[224,128]{1,0:T(8,128)S(1)}, u32[]{:S(2)}, u32[]{:S(2)}) collective-permute-start(f32[224,128]{1,0:T(8,128)S(1)} %constant_dynamic-slice_fusion), channel_id=1, source_target_pairs={{0,1},{1,0},{2,3},{3,2},{4,5},{5,4},{6,7},{7,6},{8,9},{9,8},{10,11... | collective-permute-start | bytes 344072 | tf_op jit(solution)/shard_map/ppermute | solution.py:67
  37.1 1.2 %collective-permute-start.12 = (f32[224,128]{1,0:T(8,128)S(1)}, f32[224,128]{1,0:T(8,128)S(1)}, u32[]{:S(2)}, u32[]{:S(2)}) collective-permute-start(f32[224,128]{1,0:T(8,128)S(1)} %dynamic-slice_add_fusion), channel_id=1, source_target_pairs={{0,2},{1,3},{2,0},{3,1},{4,6},{5,7},{6,4},{7,5},{8,10},{9,11},{10,... | collective-permute-start | bytes 344072 | tf_op jit(solution)/shard_map/ppermute | solution.py:71
  39.4 1.3 %collective-permute-start.14 = (f32[224,128]{1,0:T(8,128)S(1)}, f32[224,128]{1,0:T(8,128)S(1)}, u32[]{:S(2)}, u32[]{:S(2)}) collective-permute-start(f32[224,128]{1,0:T(8,128)S(1)} %dynamic-slice_add_fusion), channel_id=1, source_target_pairs={{0,6},{1,7},{2,4},{3,5},{4,2},{5,3},{6,0},{7,1},{8,14},{9,15},{10,... | collective-permute-start | bytes 344072 | tf_op jit(solution)/shard_map/ppermute | solution.py:71
  40.7 2.2 %collective-permute-done.12 = f32[224,128]{1,0:T(8,128)S(1)} collective-permute-done((f32[224,128]{1,0:T(8,128)S(1)}, f32[224,128]{1,0:T(8,128)S(1)}, u32[]{:S(2)}, u32[]{:S(2)}) %collective-permute-start.12) | collective-permute-done | bytes 114720 | tf_op jit(solution)/shard_map/ppermute | solution.py:71
  42.9 3.0 %collective-permute-done.13 = f32[224,128]{1,0:T(8,128)S(1)} collective-permute-done((f32[224,128]{1,0:T(8,128)S(1)}, f32[224,128]{1,0:T(8,128)S(1)}, u32[]{:S(2)}, u32[]{:S(2)}) %collective-permute-start.13) | collective-permute-done | bytes 114720 | tf_op jit(solution)/shard_map/ppermute | solution.py:71
  46.0 1.4 %collective-permute-start.15 = (f32[224,128]{1,0:T(8,128)S(1)}, f32[224,128]{1,0:T(8,128)S(1)}, u32[]{:S(2)}, u32[]{:S(2)}) collective-permute-start(f32[224,128]{1,0:T(8,128)S(1)} %add_add_fusion), channel_id=1, source_target_pairs={{0,8},{1,9},{2,10},{3,11},{4,12},{5,13},{6,14},{7,15},{8,0},{9,1},... | collective-permute-start | bytes 344072 | tf_op jit(solution)/shard_map/ppermute | solution.py:77
  47.8 3.0 %collective-permute-done.15 = f32[224,128]{1,0:T(8,128)S(1)} collective-permute-done((f32[224,128]{1,0:T(8,128)S(1)}, f32[224,128]{1,0:T(8,128)S(1)}, u32[]{:S(2)}, u32[]{:S(2)}) %collective-permute-start.15) | collective-permute-done | bytes 114720 | tf_op jit(solution)/shard_map/ppermute | solution.py:77
  50.8 2.5 %collective-permute-start.16 = (f32[224,128]{1,0:T(8,128)S(1)}, f32[224,128]{1,0:T(8,128)S(1)}, u32[]{:S(2)}, u32[]{:S(2)}) collective-permute-start(f32[224,128]{1,0:T(8,128)S(1)} %add.123), channel_id=1, source_target_pairs={{0,16},{1,17},{2,18},{3,19},{4,20},{5,21},{6,22},{7,23},{8,24},{9,... | collective-permute-start | bytes 344072 | tf_op jit(solution)/shard_map/ppermute | solution.py:77
  53.6 4.2 %collective-permute-done.16 = f32[224,128]{1,0:T(8,128)S(1)} collective-permute-done((f32[224,128]{1,0:T(8,128)S(1)}, f32[224,128]{1,0:T(8,128)S(1)}, u32[]{:S(2)}, u32[]{:S(2)}) %collective-permute-start.16) | collective-permute-done | bytes 114720 | tf_op jit(solution)/shard_map/ppermute | solution.py:77
  (112 shorter events, 14.6 us)
Async XLA Ops:
  0.6 20.4 %copy-start = (bf16[3,3,3,32,32]{4,3,2,1,0:T(8,128)(2,1)S(1)}, bf16[3,3,3,32,32]{4,3,2,1,0:T(8,128)(2,1)}, u32[]{:S(2)}) copy-start(bf16[3,3,3,32,32]{4,3,2,1,0:T(8,128)(2,1)} %param.13) | copy-start | bytes 165892
  0.6 6.9 %copy-start.1 = (bf16[32,2,8,128]{3,2,1,0:T(8,128)(2,1)S(1)}, bf16[32,2,8,128]{3,2,1,0:T(8,128)(2,1)}, u32[]{:S(2)}) copy-start(bf16[32,2,8,128]{3,2,1,0:T(8,128)(2,1)} %param.9) | copy-start | bytes 393220
  3.3 4.8 %collective-permute-start = (f32[2,2,128]{2,1,0:T(2,128)S(1)}, f32[2,2,128]{2,1,0:T(2,128)S(1)}, u32[]{:S(2)}, u32[]{:S(2)}) collective-permute-start(f32[2,2,128]{2,1,0:T(2,128)S(1)} %pad_maximum_fusion.13), channel_id=1, source_target_pairs={{0,1},{1,0},{2,3},{3,2},{4,5},{5,4},{6,7},{7,6},{8,9},{9,8},{10,11... | collective-permute-start | bytes 6152 | tf_op jit(solution)/shard_map/ppermute | solution.py:47
  3.8 4.3 %collective-permute-start.1 = (f32[2,2,128]{2,1,0:T(2,128)S(1)}, f32[2,2,128]{2,1,0:T(2,128)S(1)}, u32[]{:S(2)}, u32[]{:S(2)}) collective-permute-start(f32[2,2,128]{2,1,0:T(2,128)S(1)} %pad_maximum_fusion.13), channel_id=1, source_target_pairs={{0,2},{1,3},{2,0},{3,1},{4,6},{5,7},{6,4},{7,5},{8,10},{9,11},{10,... | collective-permute-start | bytes 6152 | tf_op jit(solution)/shard_map/ppermute | solution.py:47
  6.4 3.0 %collective-permute-start.2 = (f32[2,2,128]{2,1,0:T(2,128)S(1)}, f32[2,2,128]{2,1,0:T(2,128)S(1)}, u32[]{:S(2)}, u32[]{:S(2)}) collective-permute-start(f32[2,2,128]{2,1,0:T(2,128)S(1)} %pad_maximum_fusion.13), channel_id=1, source_target_pairs={{0,3},{1,2},{2,1},{3,0},{4,7},{5,6},{6,5},{7,4},{8,11},{9,10},{10,... | collective-permute-start | bytes 6152 | tf_op jit(solution)/shard_map/ppermute | solution.py:47
  7.7 1.7 %copy-start.6 = (f32[2,128]{1,0:T(2,128)S(1)}, f32[2,128]{1,0:T(2,128)}, u32[]{:S(2)}) copy-start(f32[2,128]{1,0:T(2,128)} %param.16) | copy-start | bytes 3076
  7.7 1.9 %copy-start.3 = (bf16[32,2,8,128]{3,2,1,0:T(8,128)(2,1)S(1)}, bf16[32,2,8,128]{3,2,1,0:T(8,128)(2,1)}, u32[]{:S(2)}) copy-start(bf16[32,2,8,128]{3,2,1,0:T(8,128)(2,1)} %param.11) | copy-start | bytes 393220
  7.7 1.9 %copy-start.5 = (bf16[3,32]{1,0:T(4,128)(2,1)S(1)}, bf16[3,32]{1,0:T(4,128)(2,1)}, u32[]{:S(2)}) copy-start(bf16[3,32]{1,0:T(4,128)(2,1)} %param.14) | copy-start | bytes 580
  10.0 7.1 %collective-permute-start.3 = (bf16[32,1,8,128]{3,0,2,1:T(8,128)(2,1)S(1)}, bf16[32,1,8,128]{3,0,2,1:T(8,128)(2,1)S(1)}, u32[]{:S(2)}, u32[]{:S(2)}) collective-permute-start(bf16[32,1,8,128]{3,0,2,1:T(8,128)(2,1)S(1)} %get-tuple-element.50), channel_id=1, source_target_pairs={{0,4},{4,8},{8,12},{12,16},{16,20},{20,24},{24,28},{28,0},{1,5},{5... | collective-permute-start | bytes 196616 | tf_op jit(solution)/shard_map/ppermute | solution.py:15
  11.6 5.7 %collective-permute-start.4 = (bf16[32,1,8,128]{3,0,2,1:T(8,128)(2,1)S(1)}, bf16[32,1,8,128]{3,0,2,1:T(8,128)(2,1)S(1)}, u32[]{:S(2)}, u32[]{:S(2)}) collective-permute-start(bf16[32,1,8,128]{3,0,2,1:T(8,128)(2,1)S(1)} %get-tuple-element.51), channel_id=1, source_target_pairs={{4,0},{8,4},{12,8},{16,12},{20,16},{24,20},{28,24},{0,28},{5,1},{9... | collective-permute-start | bytes 196616 | tf_op jit(solution)/shard_map/ppermute | solution.py:18
  17.2 1.7 %collective-permute-start.5 = (bf16[32,4,1,128]{3,0,2,1:T(8,128)(2,1)S(1)}, bf16[32,4,1,128]{3,0,2,1:T(8,128)(2,1)S(1)}, u32[]{:S(2)}, u32[]{:S(2)}) collective-permute-start(bf16[32,4,1,128]{3,0,2,1:T(8,128)(2,1)S(1)} %get-tuple-element.35), channel_id=1, source_target_pairs={{1,0},{2,1},{3,2},{0,3},{5,4},{6,5},{7,6},{4,7},{9,8},{10,9},{11,1... | collective-permute-start | bytes 98312 | tf_op jit(solution)/shard_map/ppermute | solution.py:18
  17.3 3.4 %collective-permute-start.6 = (bf16[32,4,1,128]{3,0,2,1:T(8,128)(2,1)S(1)}, bf16[32,4,1,128]{3,0,2,1:T(8,128)(2,1)S(1)}, u32[]{:S(2)}, u32[]{:S(2)}) collective-permute-start(bf16[32,4,1,128]{3,0,2,1:T(8,128)(2,1)S(1)} %get-tuple-element.34), channel_id=1, source_target_pairs={{0,1},{1,2},{2,3},{3,0},{4,5},{5,6},{6,7},{7,4},{8,9},{9,10},{10,1... | collective-permute-start | bytes 98312 | tf_op jit(solution)/shard_map/ppermute | solution.py:15
  22.9 7.0 %collective-permute-start.7 = (bf16[32,1,8,128]{3,0,2,1:T(8,128)(2,1)S(1)}, bf16[32,1,8,128]{3,0,2,1:T(8,128)(2,1)S(1)}, u32[]{:S(2)}, u32[]{:S(2)}) collective-permute-start(bf16[32,1,8,128]{3,0,2,1:T(8,128)(2,1)S(1)} %get-tuple-element.48), channel_id=1, source_target_pairs={{0,4},{4,8},{8,12},{12,16},{16,20},{20,24},{24,28},{28,0},{1,5},{5... | collective-permute-start | bytes 196616 | tf_op jit(solution)/shard_map/ppermute | solution.py:15
  23.9 6.0 %collective-permute-start.8 = (bf16[32,1,8,128]{3,0,2,1:T(8,128)(2,1)S(1)}, bf16[32,1,8,128]{3,0,2,1:T(8,128)(2,1)S(1)}, u32[]{:S(2)}, u32[]{:S(2)}) collective-permute-start(bf16[32,1,8,128]{3,0,2,1:T(8,128)(2,1)S(1)} %get-tuple-element.49), channel_id=1, source_target_pairs={{4,0},{8,4},{12,8},{16,12},{20,16},{24,20},{28,24},{0,28},{5,1},{9... | collective-permute-start | bytes 196616 | tf_op jit(solution)/shard_map/ppermute | solution.py:18
  29.9 3.4 %collective-permute-start.10 = (bf16[32,4,1,128]{3,0,2,1:T(8,128)(2,1)S(1)}, bf16[32,4,1,128]{3,0,2,1:T(8,128)(2,1)S(1)}, u32[]{:S(2)}, u32[]{:S(2)}) collective-permute-start(bf16[32,4,1,128]{3,0,2,1:T(8,128)(2,1)S(1)} %get-tuple-element.30), channel_id=1, source_target_pairs={{0,1},{1,2},{2,3},{3,0},{4,5},{5,6},{6,7},{7,4},{8,9},{9,10},{10,1... | collective-permute-start | bytes 98312 | tf_op jit(solution)/shard_map/ppermute | solution.py:15
  30.0 3.3 %collective-permute-start.9 = (bf16[32,4,1,128]{3,0,2,1:T(8,128)(2,1)S(1)}, bf16[32,4,1,128]{3,0,2,1:T(8,128)(2,1)S(1)}, u32[]{:S(2)}, u32[]{:S(2)}) collective-permute-start(bf16[32,4,1,128]{3,0,2,1:T(8,128)(2,1)S(1)} %get-tuple-element.31), channel_id=1, source_target_pairs={{1,0},{2,1},{3,2},{0,3},{5,4},{6,5},{7,6},{4,7},{9,8},{10,9},{11,1... | collective-permute-start | bytes 98312 | tf_op jit(solution)/shard_map/ppermute | solution.py:18
  34.8 12.5 %copy-start.2 = (bf16[3,3,3,32,32]{4,3,2,1,0:T(8,128)(2,1)S(1)}, bf16[3,3,3,32,32]{4,3,2,1,0:T(8,128)(2,1)}, u32[]{:S(2)}) copy-start(bf16[3,3,3,32,32]{4,3,2,1,0:T(8,128)(2,1)} %param.12) | copy-start | bytes 165892
  35.1 2.0 %collective-permute-start.11 = (f32[224,128]{1,0:T(8,128)S(1)}, f32[224,128]{1,0:T(8,128)S(1)}, u32[]{:S(2)}, u32[]{:S(2)}) collective-permute-start(f32[224,128]{1,0:T(8,128)S(1)} %constant_dynamic-slice_fusion), channel_id=1, source_target_pairs={{0,1},{1,0},{2,3},{3,2},{4,5},{5,4},{6,7},{7,6},{8,9},{9,8},{10,11... | collective-permute-start | bytes 344072 | tf_op jit(solution)/shard_map/ppermute | solution.py:67
  37.1 5.8 %collective-permute-start.12 = (f32[224,128]{1,0:T(8,128)S(1)}, f32[224,128]{1,0:T(8,128)S(1)}, u32[]{:S(2)}, u32[]{:S(2)}) collective-permute-start(f32[224,128]{1,0:T(8,128)S(1)} %dynamic-slice_add_fusion), channel_id=1, source_target_pairs={{0,2},{1,3},{2,0},{3,1},{4,6},{5,7},{6,4},{7,5},{8,10},{9,11},{10,... | collective-permute-start | bytes 344072 | tf_op jit(solution)/shard_map/ppermute | solution.py:71
  38.3 7.6 %collective-permute-start.13 = (f32[224,128]{1,0:T(8,128)S(1)}, f32[224,128]{1,0:T(8,128)S(1)}, u32[]{:S(2)}, u32[]{:S(2)}) collective-permute-start(f32[224,128]{1,0:T(8,128)S(1)} %dynamic-slice_add_fusion), channel_id=1, source_target_pairs={{0,4},{1,5},{2,6},{3,7},{4,0},{5,1},{6,2},{7,3},{8,12},{9,13},{10,... | collective-permute-start | bytes 344072 | tf_op jit(solution)/shard_map/ppermute | solution.py:71
  39.4 6.6 %collective-permute-start.14 = (f32[224,128]{1,0:T(8,128)S(1)}, f32[224,128]{1,0:T(8,128)S(1)}, u32[]{:S(2)}, u32[]{:S(2)}) collective-permute-start(f32[224,128]{1,0:T(8,128)S(1)} %dynamic-slice_add_fusion), channel_id=1, source_target_pairs={{0,6},{1,7},{2,4},{3,5},{4,2},{5,3},{6,0},{7,1},{8,14},{9,15},{10,... | collective-permute-start | bytes 344072 | tf_op jit(solution)/shard_map/ppermute | solution.py:71
  46.0 4.9 %collective-permute-start.15 = (f32[224,128]{1,0:T(8,128)S(1)}, f32[224,128]{1,0:T(8,128)S(1)}, u32[]{:S(2)}, u32[]{:S(2)}) collective-permute-start(f32[224,128]{1,0:T(8,128)S(1)} %add_add_fusion), channel_id=1, source_target_pairs={{0,8},{1,9},{2,10},{3,11},{4,12},{5,13},{6,14},{7,15},{8,0},{9,1},... | collective-permute-start | bytes 344072 | tf_op jit(solution)/shard_map/ppermute | solution.py:77
  50.8 7.0 %collective-permute-start.16 = (f32[224,128]{1,0:T(8,128)S(1)}, f32[224,128]{1,0:T(8,128)S(1)}, u32[]{:S(2)}, u32[]{:S(2)}) collective-permute-start(f32[224,128]{1,0:T(8,128)S(1)} %add.123), channel_id=1, source_target_pairs={{0,16},{1,17},{2,18},{3,19},{4,20},{5,21},{6,22},{7,23},{8,24},{9,... | collective-permute-start | bytes 344072 | tf_op jit(solution)/shard_map/ppermute | solution.py:77
  57.8 1.4 %collective-permute-start.17 = (f32[224,128]{1,0:T(8,128)S(1)}, f32[224,128]{1,0:T(8,128)S(1)}, u32[]{:S(2)}, u32[]{:S(2)}) collective-permute-start(f32[224,128]{1,0:T(8,128)S(1)} %add.124), channel_id=1, source_target_pairs={{0,1},{1,0},{2,3},{3,2},{4,5},{5,4},{6,7},{7,6},{8,9},{9,8},{10,11... | collective-permute-start | bytes 344072 | tf_op jit(solution)/shard_map/ppermute | solution.py:78
  (2 other events, 2.6 us)

commit v18 on v16

--- a/solution.py
+++ b/solution.py
@@ -72,7 +72,7 @@
         )
         keep = (keep + near) + (far + both)
         bits = bits[2:]
-    for bit in bits:
+    for bit in reversed(bits):
         keep = keep + lax.ppermute(keep, index_axes, [(i, i ^ bit) for i in range(total)])
     other = lax.ppermute(keep, index_axes, partner)
     return lax.dynamic_update_slice_in_dim(

time: 62.6 us -> 63.4 us (1.013)
  waiting for transfers between devices: 22.6 us -> 24.1 us
  starting transfers between devices: 23.6 us -> 22.8 us
    ppermute x2, waiting for transfers between devices: 7.22 us -> 8.79 us  [split_sum(): lax.ppermute(keep, index_axes, [(i, i ^ bit) for i in range(total)])]
    ppermute x2, starting transfers between devices: 3.83 us -> 3.03 us  [split_sum(): lax.ppermute(keep, index_axes, [(i, i ^ bit) for i in range(total)])]
where the time goes in v18:
time: 63.4 us; the launch traced here: 63.2 us
  waiting for transfers between devices  24.1 us (38%)
  starting transfers between devices  22.8 us (36%)
  local copies, waits for them, and re-layouts  7.78 us (12%)
  matrix products  4.24 us (7%)
  other arithmetic  3.07 us (5%)
  between operations  1.24 us (2%)
    ppermute x2, waiting for transfers between devices, split_sum(): lax.ppermute(keep, index_axes, [(i, i ^ bit) for i in range(total)])  8.79 us
    ppermute x4, starting transfers between devices, extended(): lax.ppermute(lax.slice_in_dim(block, 0, width, axis=dim), axis, backward)  8.71 us
    ppermute x4, waiting for transfers between devices, extended(): lax.ppermute(lax.slice_in_dim(block, block.shape[dim] - width, None, axis...  6.27 us
    ppermute x3, waiting for transfers between devices, split_sum(): lax.ppermute(keep, index_axes, [(i, i ^ mask) for i in range(total)])  5.24 us
    ppermute x3, starting transfers between devices, split_sum(): lax.ppermute(keep, index_axes, [(i, i ^ mask) for i in range(total)])  3.57 us
    ppermute x4, starting transfers between devices, extended(): lax.ppermute(lax.slice_in_dim(block, block.shape[dim] - width, None, axis...  3.19 us
    ppermute x3, starting transfers between devices, quad_sum(): lax.ppermute(value, axis, [(i, i ^ mask) for i in range(count)])  3.15 us
    ppermute x2, starting transfers between devices, split_sum(): lax.ppermute(keep, index_axes, [(i, i ^ bit) for i in range(total)])  3.03 us
  transfers between devices with their start and end apart: 18, of which 13 were waited for; matrix products, arithmetic and copies ran while one was open for 8% of the time, Pallas kernels for 0%

profile of v18, /device:TPU:0, one launch (start us, length us, event | category | flops | bytes accessed | tf_op | source)
XLA Modules:
  0.0 63.2 jit_solution(307133597515110644)
XLA Ops:
  0.7 1.0 %fusion.22 = bf16[32,2,8,128]{3,0,2,1:T(8,128)(2,1)S(1)} fusion(bf16[32,2,8,128]{3,2,1,0:T(8,128)(2,1)} %param.11), kind=kLoop, calls=%fused_computation.40 | loop fusion | flops 393216 | bytes 262144 | tf_op jit(solution)/shard_map/convert_element_type | solution.py:167
  3.8 2.6 %collective-permute-start.1 = (f32[2,2,128]{2,1,0:T(2,128)S(1)}, f32[2,2,128]{2,1,0:T(2,128)S(1)}, u32[]{:S(2)}, u32[]{:S(2)}) collective-permute-start(f32[2,2,128]{2,1,0:T(2,128)S(1)} %pad_maximum_fusion.14), channel_id=1, source_target_pairs={{0,2},{1,3},{2,0},{3,1},{4,6},{5,7},{6,4},{7,5},{8,10},{9,11},{10,... | collective-permute-start | bytes 6152 | tf_op jit(solution)/shard_map/ppermute | solution.py:47
  6.5 1.1 %fusion.88 = (bf16[32,2,8,1]{3,2,1,0:T(8,128)(2,1)S(1)}, bf16[32,2,8,1]{3,2,1,0:T(8,128)(2,1)S(1)}) fusion(bf16[32,2,8,128]{3,2,1,0:T(8,128)(2,1)} %param.9), kind=kLoop, calls=%fused_computation.169 | loop fusion | bytes 4096 | tf_op jit(solution)/shard_map/jit(_roll_static)/slice | solution.py:150
  8.1 1.3 %collective-permute-done.2 = f32[2,2,128]{2,1,0:T(2,128)S(1)} collective-permute-done((f32[2,2,128]{2,1,0:T(2,128)S(1)}, f32[2,2,128]{2,1,0:T(2,128)S(1)}, u32[]{:S(2)}, u32[]{:S(2)}) %collective-permute-start.2) | collective-permute-done | bytes 2080 | tf_op jit(solution)/shard_map/ppermute | solution.py:47
  10.0 1.6 %collective-permute-start.3 = (bf16[32,1,8,128]{3,0,2,1:T(8,128)(2,1)S(1)}, bf16[32,1,8,128]{3,0,2,1:T(8,128)(2,1)S(1)}, u32[]{:S(2)}, u32[]{:S(2)}) collective-permute-start(bf16[32,1,8,128]{3,0,2,1:T(8,128)(2,1)S(1)} %get-tuple-element.50), channel_id=1, source_target_pairs={{0,4},{4,8},{8,12},{12,16},{16,20},{20,24},{24,28},{28,0},{1,5},{5... | collective-permute-start | bytes 196616 | tf_op jit(solution)/shard_map/ppermute | solution.py:15
  11.6 3.2 %collective-permute-start.4 = (bf16[32,1,8,128]{3,0,2,1:T(8,128)(2,1)S(1)}, bf16[32,1,8,128]{3,0,2,1:T(8,128)(2,1)S(1)}, u32[]{:S(2)}, u32[]{:S(2)}) collective-permute-start(bf16[32,1,8,128]{3,0,2,1:T(8,128)(2,1)S(1)} %get-tuple-element.51), channel_id=1, source_target_pairs={{4,0},{8,4},{12,8},{16,12},{20,16},{24,20},{28,24},{0,28},{5,1},{9... | collective-permute-start | bytes 196616 | tf_op jit(solution)/shard_map/ppermute | solution.py:18
  14.9 2.3 %collective-permute-done.3 = bf16[32,1,8,128]{3,0,2,1:T(8,128)(2,1)S(1)} collective-permute-done((bf16[32,1,8,128]{3,0,2,1:T(8,128)(2,1)S(1)}, bf16[32,1,8,128]{3,0,2,1:T(8,128)(2,1)S(1)}, u32[]{:S(2)}, u32[]{:S(2)}) %collective-permute-start.3) | collective-permute-done | bytes 65568 | tf_op jit(solution)/shard_map/ppermute | solution.py:15
  17.8 1.1 %collective-permute-done.5 = bf16[32,4,1,128]{3,0,2,1:T(8,128)(2,1)S(1)} collective-permute-done((bf16[32,4,1,128]{3,0,2,1:T(8,128)(2,1)S(1)}, bf16[32,4,1,128]{3,0,2,1:T(8,128)(2,1)S(1)}, u32[]{:S(2)}, u32[]{:S(2)}) %collective-permute-start.5) | collective-permute-done | bytes 32800 | tf_op jit(solution)/shard_map/ppermute | solution.py:18
  18.9 1.8 %collective-permute-done.6 = bf16[32,4,1,128]{3,0,2,1:T(8,128)(2,1)S(1)} collective-permute-done((bf16[32,4,1,128]{3,0,2,1:T(8,128)(2,1)S(1)}, bf16[32,4,1,128]{3,0,2,1:T(8,128)(2,1)S(1)}, u32[]{:S(2)}, u32[]{:S(2)}) %collective-permute-start.6) | collective-permute-done | bytes 32800 | tf_op jit(solution)/shard_map/ppermute | solution.py:15
  22.9 1.1 %collective-permute-start.7 = (bf16[32,1,8,128]{3,0,2,1:T(8,128)(2,1)S(1)}, bf16[32,1,8,128]{3,0,2,1:T(8,128)(2,1)S(1)}, u32[]{:S(2)}, u32[]{:S(2)}) collective-permute-start(bf16[32,1,8,128]{3,0,2,1:T(8,128)(2,1)S(1)} %get-tuple-element.48), channel_id=1, source_target_pairs={{0,4},{4,8},{8,12},{12,16},{16,20},{20,24},{24,28},{28,0},{1,5},{5... | collective-permute-start | bytes 196616 | tf_op jit(solution)/shard_map/ppermute | solution.py:15
  23.9 3.7 %collective-permute-start.8 = (bf16[32,1,8,128]{3,0,2,1:T(8,128)(2,1)S(1)}, bf16[32,1,8,128]{3,0,2,1:T(8,128)(2,1)S(1)}, u32[]{:S(2)}, u32[]{:S(2)}) collective-permute-start(bf16[32,1,8,128]{3,0,2,1:T(8,128)(2,1)S(1)} %get-tuple-element.49), channel_id=1, source_target_pairs={{4,0},{8,4},{12,8},{16,12},{20,16},{24,20},{28,24},{0,28},{5,1},{9... | collective-permute-start | bytes 196616 | tf_op jit(solution)/shard_map/ppermute | solution.py:18
  27.9 2.0 %collective-permute-done.7 = bf16[32,1,8,128]{3,0,2,1:T(8,128)(2,1)S(1)} collective-permute-done((bf16[32,1,8,128]{3,0,2,1:T(8,128)(2,1)S(1)}, bf16[32,1,8,128]{3,0,2,1:T(8,128)(2,1)S(1)}, u32[]{:S(2)}, u32[]{:S(2)}) %collective-permute-start.7) | collective-permute-done | bytes 65568 | tf_op jit(solution)/shard_map/ppermute | solution.py:15
  30.0 1.7 %collective-permute-start.9 = (bf16[32,4,1,128]{3,0,2,1:T(8,128)(2,1)S(1)}, bf16[32,4,1,128]{3,0,2,1:T(8,128)(2,1)S(1)}, u32[]{:S(2)}, u32[]{:S(2)}) collective-permute-start(bf16[32,4,1,128]{3,0,2,1:T(8,128)(2,1)S(1)} %get-tuple-element.31), channel_id=1, source_target_pairs={{1,0},{2,1},{3,2},{0,3},{5,4},{6,5},{7,6},{4,7},{9,8},{10,9},{11,1... | collective-permute-start | bytes 98312 | tf_op jit(solution)/shard_map/ppermute | solution.py:18
  31.7 1.1 %fusion.1 = f32[9,3,32,32]{2,3,0,1:T(8,128)S(1)} fusion(bf16[9,32,2,8,128]{4,1,3,2,0:T(8,128)(2,1)S(1)} %fusion.50, bf16[1,32,2,8,128]{4,1,3,2,0:T(8,128)(2,1)S(1)} %maximum_bitcast_fusion.7, bf16[1,32,2,8,128]{4,1,3,2,0:T(8,128)(2,1)S(1)} %bitcast.252, bf16[1,32,2,8,128]{4,1,3,2,0:T(8,128)(2,1)S(1)} %maximum_bitcast_fusion.6), kind=kOutput, calls=%fused_computation.4 | convolution fusion | flops 114453504 | bytes 1683456 | tf_op jit(solution)/shard_map/toxzy,sixzy->tsoi/dot_general | solution.py:151
  33.6 1.1 %fusion.3 = f32[9,3,32,32]{2,3,0,1:T(8,128)S(1)} fusion(bf16[1,32,2,8,128]{4,1,3,2,0:T(8,128)(2,1)S(1)} %get-tuple-element.60, bf16[1,32,2,8,128]{4,1,3,2,0:T(8,128)(2,1)S(1)} %bitcast.258, bf16[1,32,2,8,128]{4,1,3,2,0:T(8,128)(2,1)S(1)} %get-tuple-element.59, bf16[9,32,2,8,128]{4,1,3,2,0:T(8,128)(2,1)S(1)} %fusion.40), kind=kOutput, calls=%fused_computation.7 | convolution fusion | flops 114453504 | bytes 1683456 | tf_op jit(solution)/shard_map/toxzy,sixzy->tsoi/dot_general | solution.py:151
  35.2 1.0 %collective-permute-start.11 = (f32[224,128]{1,0:T(8,128)S(1)}, f32[224,128]{1,0:T(8,128)S(1)}, u32[]{:S(2)}, u32[]{:S(2)}) collective-permute-start(f32[224,128]{1,0:T(8,128)S(1)} %constant_dynamic-slice_fusion), channel_id=1, source_target_pairs={{0,1},{1,0},{2,3},{3,2},{4,5},{5,4},{6,7},{7,6},{8,9},{9,8},{10,11... | collective-permute-start | bytes 344072 | tf_op jit(solution)/shard_map/ppermute | solution.py:66
  37.2 1.2 %collective-permute-start.12 = (f32[224,128]{1,0:T(8,128)S(1)}, f32[224,128]{1,0:T(8,128)S(1)}, u32[]{:S(2)}, u32[]{:S(2)}) collective-permute-start(f32[224,128]{1,0:T(8,128)S(1)} %dynamic-slice_add_fusion), channel_id=1, source_target_pairs={{0,2},{1,3},{2,0},{3,1},{4,6},{5,7},{6,4},{7,5},{8,10},{9,11},{10,... | collective-permute-start | bytes 344072 | tf_op jit(solution)/shard_map/ppermute | solution.py:70
  38.5 1.0 %collective-permute-start.13 = (f32[224,128]{1,0:T(8,128)S(1)}, f32[224,128]{1,0:T(8,128)S(1)}, u32[]{:S(2)}, u32[]{:S(2)}) collective-permute-start(f32[224,128]{1,0:T(8,128)S(1)} %dynamic-slice_add_fusion), channel_id=1, source_target_pairs={{0,4},{1,5},{2,6},{3,7},{4,0},{5,1},{6,2},{7,3},{8,12},{9,13},{10,... | collective-permute-start | bytes 344072 | tf_op jit(solution)/shard_map/ppermute | solution.py:70
  39.5 1.3 %collective-permute-start.14 = (f32[224,128]{1,0:T(8,128)S(1)}, f32[224,128]{1,0:T(8,128)S(1)}, u32[]{:S(2)}, u32[]{:S(2)}) collective-permute-start(f32[224,128]{1,0:T(8,128)S(1)} %dynamic-slice_add_fusion), channel_id=1, source_target_pairs={{0,6},{1,7},{2,4},{3,5},{4,2},{5,3},{6,0},{7,1},{8,14},{9,15},{10,... | collective-permute-start | bytes 344072 | tf_op jit(solution)/shard_map/ppermute | solution.py:70
  40.8 2.2 %collective-permute-done.12 = f32[224,128]{1,0:T(8,128)S(1)} collective-permute-done((f32[224,128]{1,0:T(8,128)S(1)}, f32[224,128]{1,0:T(8,128)S(1)}, u32[]{:S(2)}, u32[]{:S(2)}) %collective-permute-start.12) | collective-permute-done | bytes 114720 | tf_op jit(solution)/shard_map/ppermute | solution.py:70
  43.0 3.0 %collective-permute-done.13 = f32[224,128]{1,0:T(8,128)S(1)} collective-permute-done((f32[224,128]{1,0:T(8,128)S(1)}, f32[224,128]{1,0:T(8,128)S(1)}, u32[]{:S(2)}, u32[]{:S(2)}) %collective-permute-start.13) | collective-permute-done | bytes 114720 | tf_op jit(solution)/shard_map/ppermute | solution.py:70
  46.1 2.4 %collective-permute-start.15 = (f32[224,128]{1,0:T(8,128)S(1)}, f32[224,128]{1,0:T(8,128)S(1)}, u32[]{:S(2)}, u32[]{:S(2)}) collective-permute-start(f32[224,128]{1,0:T(8,128)S(1)} %add_add_fusion), channel_id=1, source_target_pairs={{0,16},{1,17},{2,18},{3,19},{4,20},{5,21},{6,22},{7,23},{8,24},{9,... | collective-permute-start | bytes 344072 | tf_op jit(solution)/shard_map/ppermute | solution.py:76
  48.9 4.9 %collective-permute-done.15 = f32[224,128]{1,0:T(8,128)S(1)} collective-permute-done((f32[224,128]{1,0:T(8,128)S(1)}, f32[224,128]{1,0:T(8,128)S(1)}, u32[]{:S(2)}, u32[]{:S(2)}) %collective-permute-start.15) | collective-permute-done | bytes 114720 | tf_op jit(solution)/shard_map/ppermute | solution.py:76
  54.8 3.9 %collective-permute-done.16 = f32[224,128]{1,0:T(8,128)S(1)} collective-permute-done((f32[224,128]{1,0:T(8,128)S(1)}, f32[224,128]{1,0:T(8,128)S(1)}, u32[]{:S(2)}, u32[]{:S(2)}) %collective-permute-start.16) | collective-permute-done | bytes 114720 | tf_op jit(solution)/shard_map/ppermute | solution.py:76
  (112 shorter events, 14.4 us)
Async XLA Ops:
  0.6 20.4 %copy-start = (bf16[3,3,3,32,32]{4,3,2,1,0:T(8,128)(2,1)S(1)}, bf16[3,3,3,32,32]{4,3,2,1,0:T(8,128)(2,1)}, u32[]{:S(2)}) copy-start(bf16[3,3,3,32,32]{4,3,2,1,0:T(8,128)(2,1)} %param.13) | copy-start | bytes 165892
  0.6 6.9 %copy-start.1 = (bf16[32,2,8,128]{3,2,1,0:T(8,128)(2,1)S(1)}, bf16[32,2,8,128]{3,2,1,0:T(8,128)(2,1)}, u32[]{:S(2)}) copy-start(bf16[32,2,8,128]{3,2,1,0:T(8,128)(2,1)} %param.9) | copy-start | bytes 393220
  3.3 4.8 %collective-permute-start = (f32[2,2,128]{2,1,0:T(2,128)S(1)}, f32[2,2,128]{2,1,0:T(2,128)S(1)}, u32[]{:S(2)}, u32[]{:S(2)}) collective-permute-start(f32[2,2,128]{2,1,0:T(2,128)S(1)} %pad_maximum_fusion.14), channel_id=1, source_target_pairs={{0,1},{1,0},{2,3},{3,2},{4,5},{5,4},{6,7},{7,6},{8,9},{9,8},{10,11... | collective-permute-start | bytes 6152 | tf_op jit(solution)/shard_map/ppermute | solution.py:47
  3.8 4.3 %collective-permute-start.1 = (f32[2,2,128]{2,1,0:T(2,128)S(1)}, f32[2,2,128]{2,1,0:T(2,128)S(1)}, u32[]{:S(2)}, u32[]{:S(2)}) collective-permute-start(f32[2,2,128]{2,1,0:T(2,128)S(1)} %pad_maximum_fusion.14), channel_id=1, source_target_pairs={{0,2},{1,3},{2,0},{3,1},{4,6},{5,7},{6,4},{7,5},{8,10},{9,11},{10,... | collective-permute-start | bytes 6152 | tf_op jit(solution)/shard_map/ppermute | solution.py:47
  6.4 3.0 %collective-permute-start.2 = (f32[2,2,128]{2,1,0:T(2,128)S(1)}, f32[2,2,128]{2,1,0:T(2,128)S(1)}, u32[]{:S(2)}, u32[]{:S(2)}) collective-permute-start(f32[2,2,128]{2,1,0:T(2,128)S(1)} %pad_maximum_fusion.14), channel_id=1, source_target_pairs={{0,3},{1,2},{2,1},{3,0},{4,7},{5,6},{6,5},{7,4},{8,11},{9,10},{10,... | collective-permute-start | bytes 6152 | tf_op jit(solution)/shard_map/ppermute | solution.py:47
  7.7 1.7 %copy-start.6 = (f32[2,128]{1,0:T(2,128)S(1)}, f32[2,128]{1,0:T(2,128)}, u32[]{:S(2)}) copy-start(f32[2,128]{1,0:T(2,128)} %param.16) | copy-start | bytes 3076
  7.7 1.9 %copy-start.3 = (bf16[32,2,8,128]{3,2,1,0:T(8,128)(2,1)S(1)}, bf16[32,2,8,128]{3,2,1,0:T(8,128)(2,1)}, u32[]{:S(2)}) copy-start(bf16[32,2,8,128]{3,2,1,0:T(8,128)(2,1)} %param.11) | copy-start | bytes 393220
  7.7 1.9 %copy-start.5 = (bf16[3,32]{1,0:T(4,128)(2,1)S(1)}, bf16[3,32]{1,0:T(4,128)(2,1)}, u32[]{:S(2)}) copy-start(bf16[3,32]{1,0:T(4,128)(2,1)} %param.14) | copy-start | bytes 580
  10.0 7.1 %collective-permute-start.3 = (bf16[32,1,8,128]{3,0,2,1:T(8,128)(2,1)S(1)}, bf16[32,1,8,128]{3,0,2,1:T(8,128)(2,1)S(1)}, u32[]{:S(2)}, u32[]{:S(2)}) collective-permute-start(bf16[32,1,8,128]{3,0,2,1:T(8,128)(2,1)S(1)} %get-tuple-element.50), channel_id=1, source_target_pairs={{0,4},{4,8},{8,12},{12,16},{16,20},{20,24},{24,28},{28,0},{1,5},{5... | collective-permute-start | bytes 196616 | tf_op jit(solution)/shard_map/ppermute | solution.py:15
  11.6 5.7 %collective-permute-start.4 = (bf16[32,1,8,128]{3,0,2,1:T(8,128)(2,1)S(1)}, bf16[32,1,8,128]{3,0,2,1:T(8,128)(2,1)S(1)}, u32[]{:S(2)}, u32[]{:S(2)}) collective-permute-start(bf16[32,1,8,128]{3,0,2,1:T(8,128)(2,1)S(1)} %get-tuple-element.51), channel_id=1, source_target_pairs={{4,0},{8,4},{12,8},{16,12},{20,16},{24,20},{28,24},{0,28},{5,1},{9... | collective-permute-start | bytes 196616 | tf_op jit(solution)/shard_map/ppermute | solution.py:18
  17.2 1.7 %collective-permute-start.5 = (bf16[32,4,1,128]{3,0,2,1:T(8,128)(2,1)S(1)}, bf16[32,4,1,128]{3,0,2,1:T(8,128)(2,1)S(1)}, u32[]{:S(2)}, u32[]{:S(2)}) collective-permute-start(bf16[32,4,1,128]{3,0,2,1:T(8,128)(2,1)S(1)} %get-tuple-element.35), channel_id=1, source_target_pairs={{1,0},{2,1},{3,2},{0,3},{5,4},{6,5},{7,6},{4,7},{9,8},{10,9},{11,1... | collective-permute-start | bytes 98312 | tf_op jit(solution)/shard_map/ppermute | solution.py:18
  17.3 3.4 %collective-permute-start.6 = (bf16[32,4,1,128]{3,0,2,1:T(8,128)(2,1)S(1)}, bf16[32,4,1,128]{3,0,2,1:T(8,128)(2,1)S(1)}, u32[]{:S(2)}, u32[]{:S(2)}) collective-permute-start(bf16[32,4,1,128]{3,0,2,1:T(8,128)(2,1)S(1)} %get-tuple-element.34), channel_id=1, source_target_pairs={{0,1},{1,2},{2,3},{3,0},{4,5},{5,6},{6,7},{7,4},{8,9},{9,10},{10,1... | collective-permute-start | bytes 98312 | tf_op jit(solution)/shard_map/ppermute | solution.py:15
  22.9 7.0 %collective-permute-start.7 = (bf16[32,1,8,128]{3,0,2,1:T(8,128)(2,1)S(1)}, bf16[32,1,8,128]{3,0,2,1:T(8,128)(2,1)S(1)}, u32[]{:S(2)}, u32[]{:S(2)}) collective-permute-start(bf16[32,1,8,128]{3,0,2,1:T(8,128)(2,1)S(1)} %get-tuple-element.48), channel_id=1, source_target_pairs={{0,4},{4,8},{8,12},{12,16},{16,20},{20,24},{24,28},{28,0},{1,5},{5... | collective-permute-start | bytes 196616 | tf_op jit(solution)/shard_map/ppermute | solution.py:15
  23.9 6.0 %collective-permute-start.8 = (bf16[32,1,8,128]{3,0,2,1:T(8,128)(2,1)S(1)}, bf16[32,1,8,128]{3,0,2,1:T(8,128)(2,1)S(1)}, u32[]{:S(2)}, u32[]{:S(2)}) collective-permute-start(bf16[32,1,8,128]{3,0,2,1:T(8,128)(2,1)S(1)} %get-tuple-element.49), channel_id=1, source_target_pairs={{4,0},{8,4},{12,8},{16,12},{20,16},{24,20},{28,24},{0,28},{5,1},{9... | collective-permute-start | bytes 196616 | tf_op jit(solution)/shard_map/ppermute | solution.py:18
  29.9 3.4 %collective-permute-start.10 = (bf16[32,4,1,128]{3,0,2,1:T(8,128)(2,1)S(1)}, bf16[32,4,1,128]{3,0,2,1:T(8,128)(2,1)S(1)}, u32[]{:S(2)}, u32[]{:S(2)}) collective-permute-start(bf16[32,4,1,128]{3,0,2,1:T(8,128)(2,1)S(1)} %get-tuple-element.30), channel_id=1, source_target_pairs={{0,1},{1,2},{2,3},{3,0},{4,5},{5,6},{6,7},{7,4},{8,9},{9,10},{10,1... | collective-permute-start | bytes 98312 | tf_op jit(solution)/shard_map/ppermute | solution.py:15
  30.0 3.3 %collective-permute-start.9 = (bf16[32,4,1,128]{3,0,2,1:T(8,128)(2,1)S(1)}, bf16[32,4,1,128]{3,0,2,1:T(8,128)(2,1)S(1)}, u32[]{:S(2)}, u32[]{:S(2)}) collective-permute-start(bf16[32,4,1,128]{3,0,2,1:T(8,128)(2,1)S(1)} %get-tuple-element.31), channel_id=1, source_target_pairs={{1,0},{2,1},{3,2},{0,3},{5,4},{6,5},{7,6},{4,7},{9,8},{10,9},{11,1... | collective-permute-start | bytes 98312 | tf_op jit(solution)/shard_map/ppermute | solution.py:18
  34.8 13.6 %copy-start.2 = (bf16[3,3,3,32,32]{4,3,2,1,0:T(8,128)(2,1)S(1)}, bf16[3,3,3,32,32]{4,3,2,1,0:T(8,128)(2,1)}, u32[]{:S(2)}) copy-start(bf16[3,3,3,32,32]{4,3,2,1,0:T(8,128)(2,1)} %param.12) | copy-start | bytes 165892
  35.2 2.0 %collective-permute-start.11 = (f32[224,128]{1,0:T(8,128)S(1)}, f32[224,128]{1,0:T(8,128)S(1)}, u32[]{:S(2)}, u32[]{:S(2)}) collective-permute-start(f32[224,128]{1,0:T(8,128)S(1)} %constant_dynamic-slice_fusion), channel_id=1, source_target_pairs={{0,1},{1,0},{2,3},{3,2},{4,5},{5,4},{6,7},{7,6},{8,9},{9,8},{10,11... | collective-permute-start | bytes 344072 | tf_op jit(solution)/shard_map/ppermute | solution.py:66
  37.2 5.8 %collective-permute-start.12 = (f32[224,128]{1,0:T(8,128)S(1)}, f32[224,128]{1,0:T(8,128)S(1)}, u32[]{:S(2)}, u32[]{:S(2)}) collective-permute-start(f32[224,128]{1,0:T(8,128)S(1)} %dynamic-slice_add_fusion), channel_id=1, source_target_pairs={{0,2},{1,3},{2,0},{3,1},{4,6},{5,7},{6,4},{7,5},{8,10},{9,11},{10,... | collective-permute-start | bytes 344072 | tf_op jit(solution)/shard_map/ppermute | solution.py:70
  38.5 7.6 %collective-permute-start.13 = (f32[224,128]{1,0:T(8,128)S(1)}, f32[224,128]{1,0:T(8,128)S(1)}, u32[]{:S(2)}, u32[]{:S(2)}) collective-permute-start(f32[224,128]{1,0:T(8,128)S(1)} %dynamic-slice_add_fusion), channel_id=1, source_target_pairs={{0,4},{1,5},{2,6},{3,7},{4,0},{5,1},{6,2},{7,3},{8,12},{9,13},{10,... | collective-permute-start | bytes 344072 | tf_op jit(solution)/shard_map/ppermute | solution.py:70
  39.5 6.6 %collective-permute-start.14 = (f32[224,128]{1,0:T(8,128)S(1)}, f32[224,128]{1,0:T(8,128)S(1)}, u32[]{:S(2)}, u32[]{:S(2)}) collective-permute-start(f32[224,128]{1,0:T(8,128)S(1)} %dynamic-slice_add_fusion), channel_id=1, source_target_pairs={{0,6},{1,7},{2,4},{3,5},{4,2},{5,3},{6,0},{7,1},{8,14},{9,15},{10,... | collective-permute-start | bytes 344072 | tf_op jit(solution)/shard_map/ppermute | solution.py:70
  46.1 7.8 %collective-permute-start.15 = (f32[224,128]{1,0:T(8,128)S(1)}, f32[224,128]{1,0:T(8,128)S(1)}, u32[]{:S(2)}, u32[]{:S(2)}) collective-permute-start(f32[224,128]{1,0:T(8,128)S(1)} %add_add_fusion), channel_id=1, source_target_pairs={{0,16},{1,17},{2,18},{3,19},{4,20},{5,21},{6,22},{7,23},{8,24},{9,... | collective-permute-start | bytes 344072 | tf_op jit(solution)/shard_map/ppermute | solution.py:76
  53.8 4.9 %collective-permute-start.16 = (f32[224,128]{1,0:T(8,128)S(1)}, f32[224,128]{1,0:T(8,128)S(1)}, u32[]{:S(2)}, u32[]{:S(2)}) collective-permute-start(f32[224,128]{1,0:T(8,128)S(1)} %add.124), channel_id=1, source_target_pairs={{0,8},{1,9},{2,10},{3,11},{4,12},{5,13},{6,14},{7,15},{8,0},{9,1},... | collective-permute-start | bytes 344072 | tf_op jit(solution)/shard_map/ppermute | solution.py:76
  58.7 1.4 %collective-permute-start.17 = (f32[224,128]{1,0:T(8,128)S(1)}, f32[224,128]{1,0:T(8,128)S(1)}, u32[]{:S(2)}, u32[]{:S(2)}) collective-permute-start(f32[224,128]{1,0:T(8,128)S(1)} %add.125), channel_id=1, source_target_pairs={{0,1},{1,0},{2,3},{3,2},{4,5},{5,4},{6,7},{7,6},{8,9},{9,8},{10,11... | collective-permute-start | bytes 344072 | tf_op jit(solution)/shard_map/ppermute | solution.py:77
  (2 other events, 2.6 us)

commit v19 on v16

--- a/solution.py
+++ b/solution.py
@@ -65,7 +65,7 @@
     partner = [(i, i ^ 1) for i in range(total)]
     keep = keep + lax.ppermute(send, index_axes, partner)
     bits = [1 << b for b in range(1, total.bit_length() - 1)]
-    if len(bits) >= 2:
+    while len(bits) >= 2:
         near, far, both = (
             lax.ppermute(keep, index_axes, [(i, i ^ mask) for i in range(total)])
             for mask in (bits[0], bits[1], bits[0] | bits[1])

time: 62.6 us -> 63.8 us (1.019)
    ppermute x3 -> x6, waiting for transfers between devices: 5.24 us -> 12.9 us  [split_sum(): lax.ppermute(keep, index_axes, [(i, i ^ mask) for i in range(total)])]
    ppermute x2 -> x0, waiting for transfers between devices: 7.22 us -> none  [split_sum(): lax.ppermute(keep, index_axes, [(i, i ^ bit) for i in range(total)])]
    ppermute x3 -> x6, starting transfers between devices: 3.57 us -> 8.04 us  [split_sum(): lax.ppermute(keep, index_axes, [(i, i ^ mask) for i in range(total)])]
    ppermute x2 -> x0, starting transfers between devices: 3.83 us -> none  [split_sum(): lax.ppermute(keep, index_axes, [(i, i ^ bit) for i in range(total)])]
  transfers between devices with their start and end apart: 18 -> 19, of which waited for: 13 -> 13; matrix products, arithmetic and copies ran while one was open for 8% -> 8% of each run, Pallas kernels for 0% -> 0%
where the time goes in v19:
time: 63.8 us; the launch traced here: 63.6 us
  starting transfers between devices  24.2 us (38%)
  waiting for transfers between devices  23 us (36%)
  local copies, waits for them, and re-layouts  7.78 us (12%)
  matrix products  4.25 us (7%)
  other arithmetic  3.06 us (5%)
  between operations  1.24 us (2%)
    ppermute x6, waiting for transfers between devices, split_sum(): lax.ppermute(keep, index_axes, [(i, i ^ mask) for i in range(total)])  12.9 us
    ppermute x4, starting transfers between devices, extended(): lax.ppermute(lax.slice_in_dim(block, 0, width, axis=dim), axis, backward)  8.71 us
    ppermute x6, starting transfers between devices, split_sum(): lax.ppermute(keep, index_axes, [(i, i ^ mask) for i in range(total)])  8.04 us
    ppermute x4, waiting for transfers between devices, extended(): lax.ppermute(lax.slice_in_dim(block, block.shape[dim] - width, None, axis...  6.27 us
    ppermute x4, starting transfers between devices, extended(): lax.ppermute(lax.slice_in_dim(block, block.shape[dim] - width, None, axis...  3.19 us
    ppermute x3, starting transfers between devices, quad_sum(): lax.ppermute(value, axis, [(i, i ^ mask) for i in range(count)])  3.15 us
    reshape x3, local copies, waits for them, and re-layouts, unpack_rows(): parts.append(block.reshape(shape))  2.5 us
    dot_general x2, matrix products, taps_from_halo(): jnp.einsum('toxzy,sixzy->tsoi', windows, rolled, preferred_element_type=j...  2.12 us
  transfers between devices with their start and end apart: 19, of which 13 were waited for; matrix products, arithmetic and copies ran while one was open for 8% of the time, Pallas kernels for 0%

profile of v19, /device:TPU:0, one launch (start us, length us, event | category | flops | bytes accessed | tf_op | source)
XLA Modules:
  0.0 63.6 jit_solution(5611426470973770069)
XLA Ops:
  0.7 1.0 %fusion.22 = bf16[32,2,8,128]{3,0,2,1:T(8,128)(2,1)S(1)} fusion(bf16[32,2,8,128]{3,2,1,0:T(8,128)(2,1)} %param.11), kind=kLoop, calls=%fused_computation.40 | loop fusion | flops 393216 | bytes 262144 | tf_op jit(solution)/shard_map/convert_element_type | solution.py:167
  3.8 2.6 %collective-permute-start.1 = (f32[2,2,128]{2,1,0:T(2,128)S(1)}, f32[2,2,128]{2,1,0:T(2,128)S(1)}, u32[]{:S(2)}, u32[]{:S(2)}) collective-permute-start(f32[2,2,128]{2,1,0:T(2,128)S(1)} %pad_maximum_fusion.14), channel_id=1, source_target_pairs={{0,2},{1,3},{2,0},{3,1},{4,6},{5,7},{6,4},{7,5},{8,10},{9,11},{10,... | collective-permute-start | bytes 6152 | tf_op jit(solution)/shard_map/ppermute | solution.py:47
  6.5 1.1 %fusion.88 = (bf16[32,2,8,1]{3,2,1,0:T(8,128)(2,1)S(1)}, bf16[32,2,8,1]{3,2,1,0:T(8,128)(2,1)S(1)}) fusion(bf16[32,2,8,128]{3,2,1,0:T(8,128)(2,1)} %param.9), kind=kLoop, calls=%fused_computation.170 | loop fusion | bytes 4096 | tf_op jit(solution)/shard_map/jit(_roll_static)/slice | solution.py:150
  8.1 1.3 %collective-permute-done.2 = f32[2,2,128]{2,1,0:T(2,128)S(1)} collective-permute-done((f32[2,2,128]{2,1,0:T(2,128)S(1)}, f32[2,2,128]{2,1,0:T(2,128)S(1)}, u32[]{:S(2)}, u32[]{:S(2)}) %collective-permute-start.2) | collective-permute-done | bytes 2080 | tf_op jit(solution)/shard_map/ppermute | solution.py:47
  10.0 1.6 %collective-permute-start.3 = (bf16[32,1,8,128]{3,0,2,1:T(8,128)(2,1)S(1)}, bf16[32,1,8,128]{3,0,2,1:T(8,128)(2,1)S(1)}, u32[]{:S(2)}, u32[]{:S(2)}) collective-permute-start(bf16[32,1,8,128]{3,0,2,1:T(8,128)(2,1)S(1)} %get-tuple-element.50), channel_id=1, source_target_pairs={{0,4},{4,8},{8,12},{12,16},{16,20},{20,24},{24,28},{28,0},{1,5},{5... | collective-permute-start | bytes 196616 | tf_op jit(solution)/shard_map/ppermute | solution.py:15
  11.6 3.2 %collective-permute-start.4 = (bf16[32,1,8,128]{3,0,2,1:T(8,128)(2,1)S(1)}, bf16[32,1,8,128]{3,0,2,1:T(8,128)(2,1)S(1)}, u32[]{:S(2)}, u32[]{:S(2)}) collective-permute-start(bf16[32,1,8,128]{3,0,2,1:T(8,128)(2,1)S(1)} %get-tuple-element.51), channel_id=1, source_target_pairs={{4,0},{8,4},{12,8},{16,12},{20,16},{24,20},{28,24},{0,28},{5,1},{9... | collective-permute-start | bytes 196616 | tf_op jit(solution)/shard_map/ppermute | solution.py:18
  14.9 2.3 %collective-permute-done.3 = bf16[32,1,8,128]{3,0,2,1:T(8,128)(2,1)S(1)} collective-permute-done((bf16[32,1,8,128]{3,0,2,1:T(8,128)(2,1)S(1)}, bf16[32,1,8,128]{3,0,2,1:T(8,128)(2,1)S(1)}, u32[]{:S(2)}, u32[]{:S(2)}) %collective-permute-start.3) | collective-permute-done | bytes 65568 | tf_op jit(solution)/shard_map/ppermute | solution.py:15
  17.8 1.1 %collective-permute-done.5 = bf16[32,4,1,128]{3,0,2,1:T(8,128)(2,1)S(1)} collective-permute-done((bf16[32,4,1,128]{3,0,2,1:T(8,128)(2,1)S(1)}, bf16[32,4,1,128]{3,0,2,1:T(8,128)(2,1)S(1)}, u32[]{:S(2)}, u32[]{:S(2)}) %collective-permute-start.5) | collective-permute-done | bytes 32800 | tf_op jit(solution)/shard_map/ppermute | solution.py:18
  18.9 1.8 %collective-permute-done.6 = bf16[32,4,1,128]{3,0,2,1:T(8,128)(2,1)S(1)} collective-permute-done((bf16[32,4,1,128]{3,0,2,1:T(8,128)(2,1)S(1)}, bf16[32,4,1,128]{3,0,2,1:T(8,128)(2,1)S(1)}, u32[]{:S(2)}, u32[]{:S(2)}) %collective-permute-start.6) | collective-permute-done | bytes 32800 | tf_op jit(solution)/shard_map/ppermute | solution.py:15
  22.9 1.1 %collective-permute-start.7 = (bf16[32,1,8,128]{3,0,2,1:T(8,128)(2,1)S(1)}, bf16[32,1,8,128]{3,0,2,1:T(8,128)(2,1)S(1)}, u32[]{:S(2)}, u32[]{:S(2)}) collective-permute-start(bf16[32,1,8,128]{3,0,2,1:T(8,128)(2,1)S(1)} %get-tuple-element.48), channel_id=1, source_target_pairs={{0,4},{4,8},{8,12},{12,16},{16,20},{20,24},{24,28},{28,0},{1,5},{5... | collective-permute-start | bytes 196616 | tf_op jit(solution)/shard_map/ppermute | solution.py:15
  23.9 3.7 %collective-permute-start.8 = (bf16[32,1,8,128]{3,0,2,1:T(8,128)(2,1)S(1)}, bf16[32,1,8,128]{3,0,2,1:T(8,128)(2,1)S(1)}, u32[]{:S(2)}, u32[]{:S(2)}) collective-permute-start(bf16[32,1,8,128]{3,0,2,1:T(8,128)(2,1)S(1)} %get-tuple-element.49), channel_id=1, source_target_pairs={{4,0},{8,4},{12,8},{16,12},{20,16},{24,20},{28,24},{0,28},{5,1},{9... | collective-permute-start | bytes 196616 | tf_op jit(solution)/shard_map/ppermute | solution.py:18
  27.9 2.0 %collective-permute-done.7 = bf16[32,1,8,128]{3,0,2,1:T(8,128)(2,1)S(1)} collective-permute-done((bf16[32,1,8,128]{3,0,2,1:T(8,128)(2,1)S(1)}, bf16[32,1,8,128]{3,0,2,1:T(8,128)(2,1)S(1)}, u32[]{:S(2)}, u32[]{:S(2)}) %collective-permute-start.7) | collective-permute-done | bytes 65568 | tf_op jit(solution)/shard_map/ppermute | solution.py:15
  30.0 1.7 %collective-permute-start.9 = (bf16[32,4,1,128]{3,0,2,1:T(8,128)(2,1)S(1)}, bf16[32,4,1,128]{3,0,2,1:T(8,128)(2,1)S(1)}, u32[]{:S(2)}, u32[]{:S(2)}) collective-permute-start(bf16[32,4,1,128]{3,0,2,1:T(8,128)(2,1)S(1)} %get-tuple-element.31), channel_id=1, source_target_pairs={{1,0},{2,1},{3,2},{0,3},{5,4},{6,5},{7,6},{4,7},{9,8},{10,9},{11,1... | collective-permute-start | bytes 98312 | tf_op jit(solution)/shard_map/ppermute | solution.py:18
  31.7 1.1 %fusion.1 = f32[9,3,32,32]{2,3,0,1:T(8,128)S(1)} fusion(bf16[9,32,2,8,128]{4,1,3,2,0:T(8,128)(2,1)S(1)} %fusion.50, bf16[1,32,2,8,128]{4,1,3,2,0:T(8,128)(2,1)S(1)} %maximum_bitcast_fusion.7, bf16[1,32,2,8,128]{4,1,3,2,0:T(8,128)(2,1)S(1)} %bitcast.252, bf16[1,32,2,8,128]{4,1,3,2,0:T(8,128)(2,1)S(1)} %maximum_bitcast_fusion.6), kind=kOutput, calls=%fused_computation.4 | convolution fusion | flops 114453504 | bytes 1683456 | tf_op jit(solution)/shard_map/toxzy,sixzy->tsoi/dot_general | solution.py:151
  33.6 1.1 %fusion.3 = f32[9,3,32,32]{2,3,0,1:T(8,128)S(1)} fusion(bf16[1,32,2,8,128]{4,1,3,2,0:T(8,128)(2,1)S(1)} %get-tuple-element.60, bf16[1,32,2,8,128]{4,1,3,2,0:T(8,128)(2,1)S(1)} %bitcast.258, bf16[1,32,2,8,128]{4,1,3,2,0:T(8,128)(2,1)S(1)} %get-tuple-element.59, bf16[9,32,2,8,128]{4,1,3,2,0:T(8,128)(2,1)S(1)} %fusion.40), kind=kOutput, calls=%fused_computation.7 | convolution fusion | flops 114453504 | bytes 1683456 | tf_op jit(solution)/shard_map/toxzy,sixzy->tsoi/dot_general | solution.py:151
  35.2 1.0 %collective-permute-start.11 = (f32[224,128]{1,0:T(8,128)S(1)}, f32[224,128]{1,0:T(8,128)S(1)}, u32[]{:S(2)}, u32[]{:S(2)}) collective-permute-start(f32[224,128]{1,0:T(8,128)S(1)} %constant_dynamic-slice_fusion), channel_id=1, source_target_pairs={{0,1},{1,0},{2,3},{3,2},{4,5},{5,4},{6,7},{7,6},{8,9},{9,8},{10,11... | collective-permute-start | bytes 344072 | tf_op jit(solution)/shard_map/ppermute | solution.py:66
  37.2 1.2 %collective-permute-start.12 = (f32[224,128]{1,0:T(8,128)S(1)}, f32[224,128]{1,0:T(8,128)S(1)}, u32[]{:S(2)}, u32[]{:S(2)}) collective-permute-start(f32[224,128]{1,0:T(8,128)S(1)} %dynamic-slice_add_fusion), channel_id=1, source_target_pairs={{0,2},{1,3},{2,0},{3,1},{4,6},{5,7},{6,4},{7,5},{8,10},{9,11},{10,... | collective-permute-start | bytes 344072 | tf_op jit(solution)/shard_map/ppermute | solution.py:70
  39.5 1.3 %collective-permute-start.14 = (f32[224,128]{1,0:T(8,128)S(1)}, f32[224,128]{1,0:T(8,128)S(1)}, u32[]{:S(2)}, u32[]{:S(2)}) collective-permute-start(f32[224,128]{1,0:T(8,128)S(1)} %dynamic-slice_add_fusion), channel_id=1, source_target_pairs={{0,6},{1,7},{2,4},{3,5},{4,2},{5,3},{6,0},{7,1},{8,14},{9,15},{10,... | collective-permute-start | bytes 344072 | tf_op jit(solution)/shard_map/ppermute | solution.py:70
  41.3 1.8 %collective-permute-done.12 = f32[224,128]{1,0:T(8,128)S(1)} collective-permute-done((f32[224,128]{1,0:T(8,128)S(1)}, f32[224,128]{1,0:T(8,128)S(1)}, u32[]{:S(2)}, u32[]{:S(2)}) %collective-permute-start.12) | collective-permute-done | bytes 114720 | tf_op jit(solution)/shard_map/ppermute | solution.py:70
  43.0 3.0 %collective-permute-done.13 = f32[224,128]{1,0:T(8,128)S(1)} collective-permute-done((f32[224,128]{1,0:T(8,128)S(1)}, f32[224,128]{1,0:T(8,128)S(1)}, u32[]{:S(2)}, u32[]{:S(2)}) %collective-permute-start.13) | collective-permute-done | bytes 114720 | tf_op jit(solution)/shard_map/ppermute | solution.py:70
  46.1 1.4 %collective-permute-start.15 = (f32[224,128]{1,0:T(8,128)S(1)}, f32[224,128]{1,0:T(8,128)S(1)}, u32[]{:S(2)}, u32[]{:S(2)}) collective-permute-start(f32[224,128]{1,0:T(8,128)S(1)} %add_add_fusion.1), channel_id=1, source_target_pairs={{0,8},{1,9},{2,10},{3,11},{4,12},{5,13},{6,14},{7,15},{8,0},{9,1},... | collective-permute-start | bytes 344072 | tf_op jit(solution)/shard_map/ppermute | solution.py:70
  47.4 3.1 %collective-permute-start.16 = (f32[224,128]{1,0:T(8,128)S(1)}, f32[224,128]{1,0:T(8,128)S(1)}, u32[]{:S(2)}, u32[]{:S(2)}) collective-permute-start(f32[224,128]{1,0:T(8,128)S(1)} %add_add_fusion.1), channel_id=1, source_target_pairs={{0,16},{1,17},{2,18},{3,19},{4,20},{5,21},{6,22},{7,23},{8,24},{9,... | collective-permute-start | bytes 344072 | tf_op jit(solution)/shard_map/ppermute | solution.py:70
  50.9 1.3 %collective-permute-done.15 = f32[224,128]{1,0:T(8,128)S(1)} collective-permute-done((f32[224,128]{1,0:T(8,128)S(1)}, f32[224,128]{1,0:T(8,128)S(1)}, u32[]{:S(2)}, u32[]{:S(2)}) %collective-permute-start.15) | collective-permute-done | bytes 114720 | tf_op jit(solution)/shard_map/ppermute | solution.py:70
  52.2 6.9 %collective-permute-done.16 = f32[224,128]{1,0:T(8,128)S(1)} collective-permute-done((f32[224,128]{1,0:T(8,128)S(1)}, f32[224,128]{1,0:T(8,128)S(1)}, u32[]{:S(2)}, u32[]{:S(2)}) %collective-permute-start.16) | collective-permute-done | bytes 114720 | tf_op jit(solution)/shard_map/ppermute | solution.py:70
  (113 shorter events, 14.8 us)
Async XLA Ops:
  0.6 20.4 %copy-start = (bf16[3,3,3,32,32]{4,3,2,1,0:T(8,128)(2,1)S(1)}, bf16[3,3,3,32,32]{4,3,2,1,0:T(8,128)(2,1)}, u32[]{:S(2)}) copy-start(bf16[3,3,3,32,32]{4,3,2,1,0:T(8,128)(2,1)} %param.13) | copy-start | bytes 165892
  0.6 6.9 %copy-start.1 = (bf16[32,2,8,128]{3,2,1,0:T(8,128)(2,1)S(1)}, bf16[32,2,8,128]{3,2,1,0:T(8,128)(2,1)}, u32[]{:S(2)}) copy-start(bf16[32,2,8,128]{3,2,1,0:T(8,128)(2,1)} %param.9) | copy-start | bytes 393220
  3.3 4.8 %collective-permute-start = (f32[2,2,128]{2,1,0:T(2,128)S(1)}, f32[2,2,128]{2,1,0:T(2,128)S(1)}, u32[]{:S(2)}, u32[]{:S(2)}) collective-permute-start(f32[2,2,128]{2,1,0:T(2,128)S(1)} %pad_maximum_fusion.14), channel_id=1, source_target_pairs={{0,1},{1,0},{2,3},{3,2},{4,5},{5,4},{6,7},{7,6},{8,9},{9,8},{10,11... | collective-permute-start | bytes 6152 | tf_op jit(solution)/shard_map/ppermute | solution.py:47
  3.8 4.3 %collective-permute-start.1 = (f32[2,2,128]{2,1,0:T(2,128)S(1)}, f32[2,2,128]{2,1,0:T(2,128)S(1)}, u32[]{:S(2)}, u32[]{:S(2)}) collective-permute-start(f32[2,2,128]{2,1,0:T(2,128)S(1)} %pad_maximum_fusion.14), channel_id=1, source_target_pairs={{0,2},{1,3},{2,0},{3,1},{4,6},{5,7},{6,4},{7,5},{8,10},{9,11},{10,... | collective-permute-start | bytes 6152 | tf_op jit(solution)/shard_map/ppermute | solution.py:47
  6.4 3.0 %collective-permute-start.2 = (f32[2,2,128]{2,1,0:T(2,128)S(1)}, f32[2,2,128]{2,1,0:T(2,128)S(1)}, u32[]{:S(2)}, u32[]{:S(2)}) collective-permute-start(f32[2,2,128]{2,1,0:T(2,128)S(1)} %pad_maximum_fusion.14), channel_id=1, source_target_pairs={{0,3},{1,2},{2,1},{3,0},{4,7},{5,6},{6,5},{7,4},{8,11},{9,10},{10,... | collective-permute-start | bytes 6152 | tf_op jit(solution)/shard_map/ppermute | solution.py:47
  7.7 1.9 %copy-start.3 = (bf16[32,2,8,128]{3,2,1,0:T(8,128)(2,1)S(1)}, bf16[32,2,8,128]{3,2,1,0:T(8,128)(2,1)}, u32[]{:S(2)}) copy-start(bf16[32,2,8,128]{3,2,1,0:T(8,128)(2,1)} %param.11) | copy-start | bytes 393220
  7.7 1.9 %copy-start.5 = (bf16[3,32]{1,0:T(4,128)(2,1)S(1)}, bf16[3,32]{1,0:T(4,128)(2,1)}, u32[]{:S(2)}) copy-start(bf16[3,32]{1,0:T(4,128)(2,1)} %param.14) | copy-start | bytes 580
  10.0 7.1 %collective-permute-start.3 = (bf16[32,1,8,128]{3,0,2,1:T(8,128)(2,1)S(1)}, bf16[32,1,8,128]{3,0,2,1:T(8,128)(2,1)S(1)}, u32[]{:S(2)}, u32[]{:S(2)}) collective-permute-start(bf16[32,1,8,128]{3,0,2,1:T(8,128)(2,1)S(1)} %get-tuple-element.50), channel_id=1, source_target_pairs={{0,4},{4,8},{8,12},{12,16},{16,20},{20,24},{24,28},{28,0},{1,5},{5... | collective-permute-start | bytes 196616 | tf_op jit(solution)/shard_map/ppermute | solution.py:15
  11.6 5.7 %collective-permute-start.4 = (bf16[32,1,8,128]{3,0,2,1:T(8,128)(2,1)S(1)}, bf16[32,1,8,128]{3,0,2,1:T(8,128)(2,1)S(1)}, u32[]{:S(2)}, u32[]{:S(2)}) collective-permute-start(bf16[32,1,8,128]{3,0,2,1:T(8,128)(2,1)S(1)} %get-tuple-element.51), channel_id=1, source_target_pairs={{4,0},{8,4},{12,8},{16,12},{20,16},{24,20},{28,24},{0,28},{5,1},{9... | collective-permute-start | bytes 196616 | tf_op jit(solution)/shard_map/ppermute | solution.py:18
  17.2 1.7 %collective-permute-start.5 = (bf16[32,4,1,128]{3,0,2,1:T(8,128)(2,1)S(1)}, bf16[32,4,1,128]{3,0,2,1:T(8,128)(2,1)S(1)}, u32[]{:S(2)}, u32[]{:S(2)}) collective-permute-start(bf16[32,4,1,128]{3,0,2,1:T(8,128)(2,1)S(1)} %get-tuple-element.35), channel_id=1, source_target_pairs={{1,0},{2,1},{3,2},{0,3},{5,4},{6,5},{7,6},{4,7},{9,8},{10,9},{11,1... | collective-permute-start | bytes 98312 | tf_op jit(solution)/shard_map/ppermute | solution.py:18
  17.3 3.4 %collective-permute-start.6 = (bf16[32,4,1,128]{3,0,2,1:T(8,128)(2,1)S(1)}, bf16[32,4,1,128]{3,0,2,1:T(8,128)(2,1)S(1)}, u32[]{:S(2)}, u32[]{:S(2)}) collective-permute-start(bf16[32,4,1,128]{3,0,2,1:T(8,128)(2,1)S(1)} %get-tuple-element.34), channel_id=1, source_target_pairs={{0,1},{1,2},{2,3},{3,0},{4,5},{5,6},{6,7},{7,4},{8,9},{9,10},{10,1... | collective-permute-start | bytes 98312 | tf_op jit(solution)/shard_map/ppermute | solution.py:15
  22.9 7.0 %collective-permute-start.7 = (bf16[32,1,8,128]{3,0,2,1:T(8,128)(2,1)S(1)}, bf16[32,1,8,128]{3,0,2,1:T(8,128)(2,1)S(1)}, u32[]{:S(2)}, u32[]{:S(2)}) collective-permute-start(bf16[32,1,8,128]{3,0,2,1:T(8,128)(2,1)S(1)} %get-tuple-element.48), channel_id=1, source_target_pairs={{0,4},{4,8},{8,12},{12,16},{16,20},{20,24},{24,28},{28,0},{1,5},{5... | collective-permute-start | bytes 196616 | tf_op jit(solution)/shard_map/ppermute | solution.py:15
  23.9 6.0 %collective-permute-start.8 = (bf16[32,1,8,128]{3,0,2,1:T(8,128)(2,1)S(1)}, bf16[32,1,8,128]{3,0,2,1:T(8,128)(2,1)S(1)}, u32[]{:S(2)}, u32[]{:S(2)}) collective-permute-start(bf16[32,1,8,128]{3,0,2,1:T(8,128)(2,1)S(1)} %get-tuple-element.49), channel_id=1, source_target_pairs={{4,0},{8,4},{12,8},{16,12},{20,16},{24,20},{28,24},{0,28},{5,1},{9... | collective-permute-start | bytes 196616 | tf_op jit(solution)/shard_map/ppermute | solution.py:18
  29.9 3.4 %collective-permute-start.10 = (bf16[32,4,1,128]{3,0,2,1:T(8,128)(2,1)S(1)}, bf16[32,4,1,128]{3,0,2,1:T(8,128)(2,1)S(1)}, u32[]{:S(2)}, u32[]{:S(2)}) collective-permute-start(bf16[32,4,1,128]{3,0,2,1:T(8,128)(2,1)S(1)} %get-tuple-element.30), channel_id=1, source_target_pairs={{0,1},{1,2},{2,3},{3,0},{4,5},{5,6},{6,7},{7,4},{8,9},{9,10},{10,1... | collective-permute-start | bytes 98312 | tf_op jit(solution)/shard_map/ppermute | solution.py:15
  30.0 3.3 %collective-permute-start.9 = (bf16[32,4,1,128]{3,0,2,1:T(8,128)(2,1)S(1)}, bf16[32,4,1,128]{3,0,2,1:T(8,128)(2,1)S(1)}, u32[]{:S(2)}, u32[]{:S(2)}) collective-permute-start(bf16[32,4,1,128]{3,0,2,1:T(8,128)(2,1)S(1)} %get-tuple-element.31), channel_id=1, source_target_pairs={{1,0},{2,1},{3,2},{0,3},{5,4},{6,5},{7,6},{4,7},{9,8},{10,9},{11,1... | collective-permute-start | bytes 98312 | tf_op jit(solution)/shard_map/ppermute | solution.py:18
  34.7 6.1 %copy-start.2 = (bf16[3,3,3,32,32]{4,3,2,1,0:T(8,128)(2,1)S(1)}, bf16[3,3,3,32,32]{4,3,2,1,0:T(8,128)(2,1)}, u32[]{:S(2)}) copy-start(bf16[3,3,3,32,32]{4,3,2,1,0:T(8,128)(2,1)} %param.12) | copy-start | bytes 165892
  35.2 2.0 %collective-permute-start.11 = (f32[224,128]{1,0:T(8,128)S(1)}, f32[224,128]{1,0:T(8,128)S(1)}, u32[]{:S(2)}, u32[]{:S(2)}) collective-permute-start(f32[224,128]{1,0:T(8,128)S(1)} %constant_dynamic-slice_fusion), channel_id=1, source_target_pairs={{0,1},{1,0},{2,3},{3,2},{4,5},{5,4},{6,7},{7,6},{8,9},{9,8},{10,11... | collective-permute-start | bytes 344072 | tf_op jit(solution)/shard_map/ppermute | solution.py:66
  37.2 5.8 %collective-permute-start.12 = (f32[224,128]{1,0:T(8,128)S(1)}, f32[224,128]{1,0:T(8,128)S(1)}, u32[]{:S(2)}, u32[]{:S(2)}) collective-permute-start(f32[224,128]{1,0:T(8,128)S(1)} %dynamic-slice_add_fusion), channel_id=1, source_target_pairs={{0,2},{1,3},{2,0},{3,1},{4,6},{5,7},{6,4},{7,5},{8,10},{9,11},{10,... | collective-permute-start | bytes 344072 | tf_op jit(solution)/shard_map/ppermute | solution.py:70
  38.5 7.6 %collective-permute-start.13 = (f32[224,128]{1,0:T(8,128)S(1)}, f32[224,128]{1,0:T(8,128)S(1)}, u32[]{:S(2)}, u32[]{:S(2)}) collective-permute-start(f32[224,128]{1,0:T(8,128)S(1)} %dynamic-slice_add_fusion), channel_id=1, source_target_pairs={{0,4},{1,5},{2,6},{3,7},{4,0},{5,1},{6,2},{7,3},{8,12},{9,13},{10,... | collective-permute-start | bytes 344072 | tf_op jit(solution)/shard_map/ppermute | solution.py:70
  39.5 6.6 %collective-permute-start.14 = (f32[224,128]{1,0:T(8,128)S(1)}, f32[224,128]{1,0:T(8,128)S(1)}, u32[]{:S(2)}, u32[]{:S(2)}) collective-permute-start(f32[224,128]{1,0:T(8,128)S(1)} %dynamic-slice_add_fusion), channel_id=1, source_target_pairs={{0,6},{1,7},{2,4},{3,5},{4,2},{5,3},{6,0},{7,1},{8,14},{9,15},{10,... | collective-permute-start | bytes 344072 | tf_op jit(solution)/shard_map/ppermute | solution.py:70
  46.1 6.1 %collective-permute-start.15 = (f32[224,128]{1,0:T(8,128)S(1)}, f32[224,128]{1,0:T(8,128)S(1)}, u32[]{:S(2)}, u32[]{:S(2)}) collective-permute-start(f32[224,128]{1,0:T(8,128)S(1)} %add_add_fusion.1), channel_id=1, source_target_pairs={{0,8},{1,9},{2,10},{3,11},{4,12},{5,13},{6,14},{7,15},{8,0},{9,1},... | collective-permute-start | bytes 344072 | tf_op jit(solution)/shard_map/ppermute | solution.py:70
  47.4 11.6 %collective-permute-start.16 = (f32[224,128]{1,0:T(8,128)S(1)}, f32[224,128]{1,0:T(8,128)S(1)}, u32[]{:S(2)}, u32[]{:S(2)}) collective-permute-start(f32[224,128]{1,0:T(8,128)S(1)} %add_add_fusion.1), channel_id=1, source_target_pairs={{0,16},{1,17},{2,18},{3,19},{4,20},{5,21},{6,22},{7,23},{8,24},{9,... | collective-permute-start | bytes 344072 | tf_op jit(solution)/shard_map/ppermute | solution.py:70
  50.5 8.5 %collective-permute-start.17 = (f32[224,128]{1,0:T(8,128)S(1)}, f32[224,128]{1,0:T(8,128)S(1)}, u32[]{:S(2)}, u32[]{:S(2)}) collective-permute-start(f32[224,128]{1,0:T(8,128)S(1)} %add_add_fusion.1), channel_id=1, source_target_pairs={{0,24},{1,25},{2,26},{3,27},{4,28},{5,29},{6,30},{7,31},{8,16},{9,... | collective-permute-start | bytes 344072 | tf_op jit(solution)/shard_map/ppermute | solution.py:70
  59.1 1.4 %collective-permute-start.18 = (f32[224,128]{1,0:T(8,128)S(1)}, f32[224,128]{1,0:T(8,128)S(1)}, u32[]{:S(2)}, u32[]{:S(2)}) collective-permute-start(f32[224,128]{1,0:T(8,128)S(1)} %add_add_fusion), channel_id=1, source_target_pairs={{0,1},{1,0},{2,3},{3,2},{4,5},{5,4},{6,7},{7,6},{8,9},{9,8},{10,11... | collective-permute-start | bytes 344072 | tf_op jit(solution)/shard_map/ppermute | solution.py:77
  (3 other events, 4.4 us)

commit v20 on v19

--- a/solution.py
+++ b/solution.py
@@ -65,7 +65,7 @@
     partner = [(i, i ^ 1) for i in range(total)]
     keep = keep + lax.ppermute(send, index_axes, partner)
     bits = [1 << b for b in range(1, total.bit_length() - 1)]
-    while len(bits) >= 2:
+    if len(bits) >= 8:
         near, far, both = (
             lax.ppermute(keep, index_axes, [(i, i ^ mask) for i in range(total)])
             for mask in (bits[0], bits[1], bits[0] | bits[1])

time: 63.8 us -> 64.2 us (level)
  waiting for transfers between devices: 23 us -> 26.2 us
  starting transfers between devices: 24.2 us -> 21.5 us
    ppermute x6 -> x4, waiting for transfers between devices: 12.9 us -> 16.1 us  [split_sum(): lax.ppermute(keep, index_axes, [(i, i ^ bit) for i in range(total)])]
    ppermute x6 -> x4, starting transfers between devices: 8.04 us -> 5.31 us  [split_sum(): lax.ppermute(keep, index_axes, [(i, i ^ bit) for i in range(total)])]
  transfers between devices with their start and end apart: 19 -> 17, of which waited for: 13 -> 13; matrix products, arithmetic and copies ran while one was open for 8% -> 8% of each run, Pallas kernels for 0% -> 0%
where the time goes in v20:
time: 64.2 us; the launch traced here: 64 us
  waiting for transfers between devices  26.2 us (41%)
  starting transfers between devices  21.5 us (33%)
  local copies, waits for them, and re-layouts  7.78 us (12%)
  matrix products  4.25 us (7%)
  other arithmetic  3.07 us (5%)
  between operations  1.24 us (2%)
    ppermute x4, waiting for transfers between devices, split_sum(): lax.ppermute(keep, index_axes, [(i, i ^ bit) for i in range(total)])  16.1 us
    ppermute x4, starting transfers between devices, extended(): lax.ppermute(lax.slice_in_dim(block, 0, width, axis=dim), axis, backward)  8.71 us
    ppermute x4, waiting for transfers between devices, extended(): lax.ppermute(lax.slice_in_dim(block, block.shape[dim] - width, None, axis...  6.27 us
    ppermute x4, starting transfers between devices, split_sum(): lax.ppermute(keep, index_axes, [(i, i ^ bit) for i in range(total)])  5.31 us
    ppermute x4, starting transfers between devices, extended(): lax.ppermute(lax.slice_in_dim(block, block.shape[dim] - width, None, axis...  3.19 us
    ppermute x3, starting transfers between devices, quad_sum(): lax.ppermute(value, axis, [(i, i ^ mask) for i in range(count)])  3.15 us
    reshape x3, local copies, waits for them, and re-layouts, unpack_rows(): parts.append(block.reshape(shape))  2.5 us
    dot_general x2, matrix products, taps_from_halo(): jnp.einsum('toxzy,sixzy->tsoi', windows, rolled, preferred_element_type=j...  2.12 us
  transfers between devices with their start and end apart: 17, of which 13 were waited for; matrix products, arithmetic and copies ran while one was open for 8% of the time, Pallas kernels for 0%

profile of v20, /device:TPU:0, one launch (start us, length us, event | category | flops | bytes accessed | tf_op | source)
XLA Modules:
  0.0 64.0 jit_solution(4385778571315451247)
XLA Ops:
  0.7 1.0 %fusion.22 = bf16[32,2,8,128]{3,0,2,1:T(8,128)(2,1)S(1)} fusion(bf16[32,2,8,128]{3,2,1,0:T(8,128)(2,1)} %param.11), kind=kLoop, calls=%fused_computation.40 | loop fusion | flops 393216 | bytes 262144 | tf_op jit(solution)/shard_map/convert_element_type | solution.py:167
  3.8 2.6 %collective-permute-start.1 = (f32[2,2,128]{2,1,0:T(2,128)S(1)}, f32[2,2,128]{2,1,0:T(2,128)S(1)}, u32[]{:S(2)}, u32[]{:S(2)}) collective-permute-start(f32[2,2,128]{2,1,0:T(2,128)S(1)} %pad_maximum_fusion.14), channel_id=1, source_target_pairs={{0,2},{1,3},{2,0},{3,1},{4,6},{5,7},{6,4},{7,5},{8,10},{9,11},{10,... | collective-permute-start | bytes 6152 | tf_op jit(solution)/shard_map/ppermute | solution.py:47
  6.5 1.1 %fusion.88 = (bf16[32,2,8,1]{3,2,1,0:T(8,128)(2,1)S(1)}, bf16[32,2,8,1]{3,2,1,0:T(8,128)(2,1)S(1)}) fusion(bf16[32,2,8,128]{3,2,1,0:T(8,128)(2,1)} %param.9), kind=kLoop, calls=%fused_computation.168 | loop fusion | bytes 4096 | tf_op jit(solution)/shard_map/jit(_roll_static)/slice | solution.py:150
  8.1 1.3 %collective-permute-done.2 = f32[2,2,128]{2,1,0:T(2,128)S(1)} collective-permute-done((f32[2,2,128]{2,1,0:T(2,128)S(1)}, f32[2,2,128]{2,1,0:T(2,128)S(1)}, u32[]{:S(2)}, u32[]{:S(2)}) %collective-permute-start.2) | collective-permute-done | bytes 2080 | tf_op jit(solution)/shard_map/ppermute | solution.py:47
  10.0 1.6 %collective-permute-start.3 = (bf16[32,1,8,128]{3,0,2,1:T(8,128)(2,1)S(1)}, bf16[32,1,8,128]{3,0,2,1:T(8,128)(2,1)S(1)}, u32[]{:S(2)}, u32[]{:S(2)}) collective-permute-start(bf16[32,1,8,128]{3,0,2,1:T(8,128)(2,1)S(1)} %get-tuple-element.50), channel_id=1, source_target_pairs={{0,4},{4,8},{8,12},{12,16},{16,20},{20,24},{24,28},{28,0},{1,5},{5... | collective-permute-start | bytes 196616 | tf_op jit(solution)/shard_map/ppermute | solution.py:15
  11.6 3.2 %collective-permute-start.4 = (bf16[32,1,8,128]{3,0,2,1:T(8,128)(2,1)S(1)}, bf16[32,1,8,128]{3,0,2,1:T(8,128)(2,1)S(1)}, u32[]{:S(2)}, u32[]{:S(2)}) collective-permute-start(bf16[32,1,8,128]{3,0,2,1:T(8,128)(2,1)S(1)} %get-tuple-element.51), channel_id=1, source_target_pairs={{4,0},{8,4},{12,8},{16,12},{20,16},{24,20},{28,24},{0,28},{5,1},{9... | collective-permute-start | bytes 196616 | tf_op jit(solution)/shard_map/ppermute | solution.py:18
  14.9 2.3 %collective-permute-done.3 = bf16[32,1,8,128]{3,0,2,1:T(8,128)(2,1)S(1)} collective-permute-done((bf16[32,1,8,128]{3,0,2,1:T(8,128)(2,1)S(1)}, bf16[32,1,8,128]{3,0,2,1:T(8,128)(2,1)S(1)}, u32[]{:S(2)}, u32[]{:S(2)}) %collective-permute-start.3) | collective-permute-done | bytes 65568 | tf_op jit(solution)/shard_map/ppermute | solution.py:15
  17.8 1.1 %collective-permute-done.5 = bf16[32,4,1,128]{3,0,2,1:T(8,128)(2,1)S(1)} collective-permute-done((bf16[32,4,1,128]{3,0,2,1:T(8,128)(2,1)S(1)}, bf16[32,4,1,128]{3,0,2,1:T(8,128)(2,1)S(1)}, u32[]{:S(2)}, u32[]{:S(2)}) %collective-permute-start.5) | collective-permute-done | bytes 32800 | tf_op jit(solution)/shard_map/ppermute | solution.py:18
  18.9 1.8 %collective-permute-done.6 = bf16[32,4,1,128]{3,0,2,1:T(8,128)(2,1)S(1)} collective-permute-done((bf16[32,4,1,128]{3,0,2,1:T(8,128)(2,1)S(1)}, bf16[32,4,1,128]{3,0,2,1:T(8,128)(2,1)S(1)}, u32[]{:S(2)}, u32[]{:S(2)}) %collective-permute-start.6) | collective-permute-done | bytes 32800 | tf_op jit(solution)/shard_map/ppermute | solution.py:15
  22.9 1.1 %collective-permute-start.7 = (bf16[32,1,8,128]{3,0,2,1:T(8,128)(2,1)S(1)}, bf16[32,1,8,128]{3,0,2,1:T(8,128)(2,1)S(1)}, u32[]{:S(2)}, u32[]{:S(2)}) collective-permute-start(bf16[32,1,8,128]{3,0,2,1:T(8,128)(2,1)S(1)} %get-tuple-element.48), channel_id=1, source_target_pairs={{0,4},{4,8},{8,12},{12,16},{16,20},{20,24},{24,28},{28,0},{1,5},{5... | collective-permute-start | bytes 196616 | tf_op jit(solution)/shard_map/ppermute | solution.py:15
  23.9 3.7 %collective-permute-start.8 = (bf16[32,1,8,128]{3,0,2,1:T(8,128)(2,1)S(1)}, bf16[32,1,8,128]{3,0,2,1:T(8,128)(2,1)S(1)}, u32[]{:S(2)}, u32[]{:S(2)}) collective-permute-start(bf16[32,1,8,128]{3,0,2,1:T(8,128)(2,1)S(1)} %get-tuple-element.49), channel_id=1, source_target_pairs={{4,0},{8,4},{12,8},{16,12},{20,16},{24,20},{28,24},{0,28},{5,1},{9... | collective-permute-start | bytes 196616 | tf_op jit(solution)/shard_map/ppermute | solution.py:18
  27.9 2.0 %collective-permute-done.7 = bf16[32,1,8,128]{3,0,2,1:T(8,128)(2,1)S(1)} collective-permute-done((bf16[32,1,8,128]{3,0,2,1:T(8,128)(2,1)S(1)}, bf16[32,1,8,128]{3,0,2,1:T(8,128)(2,1)S(1)}, u32[]{:S(2)}, u32[]{:S(2)}) %collective-permute-start.7) | collective-permute-done | bytes 65568 | tf_op jit(solution)/shard_map/ppermute | solution.py:15
  30.0 1.7 %collective-permute-start.9 = (bf16[32,4,1,128]{3,0,2,1:T(8,128)(2,1)S(1)}, bf16[32,4,1,128]{3,0,2,1:T(8,128)(2,1)S(1)}, u32[]{:S(2)}, u32[]{:S(2)}) collective-permute-start(bf16[32,4,1,128]{3,0,2,1:T(8,128)(2,1)S(1)} %get-tuple-element.31), channel_id=1, source_target_pairs={{1,0},{2,1},{3,2},{0,3},{5,4},{6,5},{7,6},{4,7},{9,8},{10,9},{11,1... | collective-permute-start | bytes 98312 | tf_op jit(solution)/shard_map/ppermute | solution.py:18
  31.7 1.1 %fusion.1 = f32[9,3,32,32]{2,3,0,1:T(8,128)S(1)} fusion(bf16[9,32,2,8,128]{4,1,3,2,0:T(8,128)(2,1)S(1)} %fusion.50, bf16[1,32,2,8,128]{4,1,3,2,0:T(8,128)(2,1)S(1)} %maximum_bitcast_fusion.7, bf16[1,32,2,8,128]{4,1,3,2,0:T(8,128)(2,1)S(1)} %bitcast.252, bf16[1,32,2,8,128]{4,1,3,2,0:T(8,128)(2,1)S(1)} %maximum_bitcast_fusion.6), kind=kOutput, calls=%fused_computation.4 | convolution fusion | flops 114453504 | bytes 1683456 | tf_op jit(solution)/shard_map/toxzy,sixzy->tsoi/dot_general | solution.py:151
  33.6 1.1 %fusion.3 = f32[9,3,32,32]{2,3,0,1:T(8,128)S(1)} fusion(bf16[1,32,2,8,128]{4,1,3,2,0:T(8,128)(2,1)S(1)} %get-tuple-element.60, bf16[1,32,2,8,128]{4,1,3,2,0:T(8,128)(2,1)S(1)} %bitcast.258, bf16[1,32,2,8,128]{4,1,3,2,0:T(8,128)(2,1)S(1)} %get-tuple-element.59, bf16[9,32,2,8,128]{4,1,3,2,0:T(8,128)(2,1)S(1)} %fusion.40), kind=kOutput, calls=%fused_computation.7 | convolution fusion | flops 114453504 | bytes 1683456 | tf_op jit(solution)/shard_map/toxzy,sixzy->tsoi/dot_general | solution.py:151
  35.2 1.0 %collective-permute-start.11 = (f32[224,128]{1,0:T(8,128)S(1)}, f32[224,128]{1,0:T(8,128)S(1)}, u32[]{:S(2)}, u32[]{:S(2)}) collective-permute-start(f32[224,128]{1,0:T(8,128)S(1)} %constant_dynamic-slice_fusion), channel_id=1, source_target_pairs={{0,1},{1,0},{2,3},{3,2},{4,5},{5,4},{6,7},{7,6},{8,9},{9,8},{10,11... | collective-permute-start | bytes 344072 | tf_op jit(solution)/shard_map/ppermute | solution.py:66
  36.2 1.0 %collective-permute-done.11 = f32[224,128]{1,0:T(8,128)S(1)} collective-permute-done((f32[224,128]{1,0:T(8,128)S(1)}, f32[224,128]{1,0:T(8,128)S(1)}, u32[]{:S(2)}, u32[]{:S(2)}) %collective-permute-start.11) | collective-permute-done | bytes 114720 | tf_op jit(solution)/shard_map/ppermute | solution.py:66
  37.2 1.2 %collective-permute-start.12 = (f32[224,128]{1,0:T(8,128)S(1)}, f32[224,128]{1,0:T(8,128)S(1)}, u32[]{:S(2)}, u32[]{:S(2)}) collective-permute-start(f32[224,128]{1,0:T(8,128)S(1)} %dynamic-slice_add_fusion), channel_id=1, source_target_pairs={{0,2},{1,3},{2,0},{3,1},{4,6},{5,7},{6,4},{7,5},{8,10},{9,11},{10,... | collective-permute-start | bytes 344072 | tf_op jit(solution)/shard_map/ppermute | solution.py:76
  38.5 4.2 %collective-permute-done.12 = f32[224,128]{1,0:T(8,128)S(1)} collective-permute-done((f32[224,128]{1,0:T(8,128)S(1)}, f32[224,128]{1,0:T(8,128)S(1)}, u32[]{:S(2)}, u32[]{:S(2)}) %collective-permute-start.12) | collective-permute-done | bytes 114720 | tf_op jit(solution)/shard_map/ppermute | solution.py:76
  42.7 1.2 %collective-permute-start.13 = (f32[224,128]{1,0:T(8,128)S(1)}, f32[224,128]{1,0:T(8,128)S(1)}, u32[]{:S(2)}, u32[]{:S(2)}) collective-permute-start(f32[224,128]{1,0:T(8,128)S(1)} %add.118), channel_id=1, source_target_pairs={{0,4},{1,5},{2,6},{3,7},{4,0},{5,1},{6,2},{7,3},{8,12},{9,13},{10,... | collective-permute-start | bytes 344072 | tf_op jit(solution)/shard_map/ppermute | solution.py:76
  44.0 3.6 %collective-permute-done.13 = f32[224,128]{1,0:T(8,128)S(1)} collective-permute-done((f32[224,128]{1,0:T(8,128)S(1)}, f32[224,128]{1,0:T(8,128)S(1)}, u32[]{:S(2)}, u32[]{:S(2)}) %collective-permute-start.13) | collective-permute-done | bytes 114720 | tf_op jit(solution)/shard_map/ppermute | solution.py:76
  49.0 3.5 %collective-permute-done.14 = f32[224,128]{1,0:T(8,128)S(1)} collective-permute-done((f32[224,128]{1,0:T(8,128)S(1)}, f32[224,128]{1,0:T(8,128)S(1)}, u32[]{:S(2)}, u32[]{:S(2)}) %collective-permute-start.14) | collective-permute-done | bytes 114720 | tf_op jit(solution)/shard_map/ppermute | solution.py:76
  52.5 2.0 %collective-permute-start.15 = (f32[224,128]{1,0:T(8,128)S(1)}, f32[224,128]{1,0:T(8,128)S(1)}, u32[]{:S(2)}, u32[]{:S(2)}) collective-permute-start(f32[224,128]{1,0:T(8,128)S(1)} %add.120), channel_id=1, source_target_pairs={{0,16},{1,17},{2,18},{3,19},{4,20},{5,21},{6,22},{7,23},{8,24},{9,... | collective-permute-start | bytes 344072 | tf_op jit(solution)/shard_map/ppermute | solution.py:76
  54.7 4.7 %collective-permute-done.15 = f32[224,128]{1,0:T(8,128)S(1)} collective-permute-done((f32[224,128]{1,0:T(8,128)S(1)}, f32[224,128]{1,0:T(8,128)S(1)}, u32[]{:S(2)}, u32[]{:S(2)}) %collective-permute-start.15) | collective-permute-done | bytes 114720 | tf_op jit(solution)/shard_map/ppermute | solution.py:76
  (111 shorter events, 13.7 us)
Async XLA Ops:
  0.6 20.4 %copy-start = (bf16[3,3,3,32,32]{4,3,2,1,0:T(8,128)(2,1)S(1)}, bf16[3,3,3,32,32]{4,3,2,1,0:T(8,128)(2,1)}, u32[]{:S(2)}) copy-start(bf16[3,3,3,32,32]{4,3,2,1,0:T(8,128)(2,1)} %param.13) | copy-start | bytes 165892
  0.6 6.9 %copy-start.1 = (bf16[32,2,8,128]{3,2,1,0:T(8,128)(2,1)S(1)}, bf16[32,2,8,128]{3,2,1,0:T(8,128)(2,1)}, u32[]{:S(2)}) copy-start(bf16[32,2,8,128]{3,2,1,0:T(8,128)(2,1)} %param.9) | copy-start | bytes 393220
  3.3 4.8 %collective-permute-start = (f32[2,2,128]{2,1,0:T(2,128)S(1)}, f32[2,2,128]{2,1,0:T(2,128)S(1)}, u32[]{:S(2)}, u32[]{:S(2)}) collective-permute-start(f32[2,2,128]{2,1,0:T(2,128)S(1)} %pad_maximum_fusion.14), channel_id=1, source_target_pairs={{0,1},{1,0},{2,3},{3,2},{4,5},{5,4},{6,7},{7,6},{8,9},{9,8},{10,11... | collective-permute-start | bytes 6152 | tf_op jit(solution)/shard_map/ppermute | solution.py:47
  3.8 4.3 %collective-permute-start.1 = (f32[2,2,128]{2,1,0:T(2,128)S(1)}, f32[2,2,128]{2,1,0:T(2,128)S(1)}, u32[]{:S(2)}, u32[]{:S(2)}) collective-permute-start(f32[2,2,128]{2,1,0:T(2,128)S(1)} %pad_maximum_fusion.14), channel_id=1, source_target_pairs={{0,2},{1,3},{2,0},{3,1},{4,6},{5,7},{6,4},{7,5},{8,10},{9,11},{10,... | collective-permute-start | bytes 6152 | tf_op jit(solution)/shard_map/ppermute | solution.py:47
  6.4 3.0 %collective-permute-start.2 = (f32[2,2,128]{2,1,0:T(2,128)S(1)}, f32[2,2,128]{2,1,0:T(2,128)S(1)}, u32[]{:S(2)}, u32[]{:S(2)}) collective-permute-start(f32[2,2,128]{2,1,0:T(2,128)S(1)} %pad_maximum_fusion.14), channel_id=1, source_target_pairs={{0,3},{1,2},{2,1},{3,0},{4,7},{5,6},{6,5},{7,4},{8,11},{9,10},{10,... | collective-permute-start | bytes 6152 | tf_op jit(solution)/shard_map/ppermute | solution.py:47
  7.7 1.7 %copy-start.6 = (f32[2,128]{1,0:T(2,128)S(1)}, f32[2,128]{1,0:T(2,128)}, u32[]{:S(2)}) copy-start(f32[2,128]{1,0:T(2,128)} %param.16) | copy-start | bytes 3076
  7.7 1.7 %copy-start.7 = (f32[2,128]{1,0:T(2,128)S(1)}, f32[2,128]{1,0:T(2,128)}, u32[]{:S(2)}) copy-start(f32[2,128]{1,0:T(2,128)} %param.17) | copy-start | bytes 3076
  7.7 1.9 %copy-start.3 = (bf16[32,2,8,128]{3,2,1,0:T(8,128)(2,1)S(1)}, bf16[32,2,8,128]{3,2,1,0:T(8,128)(2,1)}, u32[]{:S(2)}) copy-start(bf16[32,2,8,128]{3,2,1,0:T(8,128)(2,1)} %param.11) | copy-start | bytes 393220
  7.7 1.9 %copy-start.5 = (bf16[3,32]{1,0:T(4,128)(2,1)S(1)}, bf16[3,32]{1,0:T(4,128)(2,1)}, u32[]{:S(2)}) copy-start(bf16[3,32]{1,0:T(4,128)(2,1)} %param.14) | copy-start | bytes 580
  10.0 7.1 %collective-permute-start.3 = (bf16[32,1,8,128]{3,0,2,1:T(8,128)(2,1)S(1)}, bf16[32,1,8,128]{3,0,2,1:T(8,128)(2,1)S(1)}, u32[]{:S(2)}, u32[]{:S(2)}) collective-permute-start(bf16[32,1,8,128]{3,0,2,1:T(8,128)(2,1)S(1)} %get-tuple-element.50), channel_id=1, source_target_pairs={{0,4},{4,8},{8,12},{12,16},{16,20},{20,24},{24,28},{28,0},{1,5},{5... | collective-permute-start | bytes 196616 | tf_op jit(solution)/shard_map/ppermute | solution.py:15
  11.6 5.7 %collective-permute-start.4 = (bf16[32,1,8,128]{3,0,2,1:T(8,128)(2,1)S(1)}, bf16[32,1,8,128]{3,0,2,1:T(8,128)(2,1)S(1)}, u32[]{:S(2)}, u32[]{:S(2)}) collective-permute-start(bf16[32,1,8,128]{3,0,2,1:T(8,128)(2,1)S(1)} %get-tuple-element.51), channel_id=1, source_target_pairs={{4,0},{8,4},{12,8},{16,12},{20,16},{24,20},{28,24},{0,28},{5,1},{9... | collective-permute-start | bytes 196616 | tf_op jit(solution)/shard_map/ppermute | solution.py:18
  17.2 1.7 %collective-permute-start.5 = (bf16[32,4,1,128]{3,0,2,1:T(8,128)(2,1)S(1)}, bf16[32,4,1,128]{3,0,2,1:T(8,128)(2,1)S(1)}, u32[]{:S(2)}, u32[]{:S(2)}) collective-permute-start(bf16[32,4,1,128]{3,0,2,1:T(8,128)(2,1)S(1)} %get-tuple-element.35), channel_id=1, source_target_pairs={{1,0},{2,1},{3,2},{0,3},{5,4},{6,5},{7,6},{4,7},{9,8},{10,9},{11,1... | collective-permute-start | bytes 98312 | tf_op jit(solution)/shard_map/ppermute | solution.py:18
  17.3 3.4 %collective-permute-start.6 = (bf16[32,4,1,128]{3,0,2,1:T(8,128)(2,1)S(1)}, bf16[32,4,1,128]{3,0,2,1:T(8,128)(2,1)S(1)}, u32[]{:S(2)}, u32[]{:S(2)}) collective-permute-start(bf16[32,4,1,128]{3,0,2,1:T(8,128)(2,1)S(1)} %get-tuple-element.34), channel_id=1, source_target_pairs={{0,1},{1,2},{2,3},{3,0},{4,5},{5,6},{6,7},{7,4},{8,9},{9,10},{10,1... | collective-permute-start | bytes 98312 | tf_op jit(solution)/shard_map/ppermute | solution.py:15
  22.9 7.0 %collective-permute-start.7 = (bf16[32,1,8,128]{3,0,2,1:T(8,128)(2,1)S(1)}, bf16[32,1,8,128]{3,0,2,1:T(8,128)(2,1)S(1)}, u32[]{:S(2)}, u32[]{:S(2)}) collective-permute-start(bf16[32,1,8,128]{3,0,2,1:T(8,128)(2,1)S(1)} %get-tuple-element.48), channel_id=1, source_target_pairs={{0,4},{4,8},{8,12},{12,16},{16,20},{20,24},{24,28},{28,0},{1,5},{5... | collective-permute-start | bytes 196616 | tf_op jit(solution)/shard_map/ppermute | solution.py:15
  23.9 6.0 %collective-permute-start.8 = (bf16[32,1,8,128]{3,0,2,1:T(8,128)(2,1)S(1)}, bf16[32,1,8,128]{3,0,2,1:T(8,128)(2,1)S(1)}, u32[]{:S(2)}, u32[]{:S(2)}) collective-permute-start(bf16[32,1,8,128]{3,0,2,1:T(8,128)(2,1)S(1)} %get-tuple-element.49), channel_id=1, source_target_pairs={{4,0},{8,4},{12,8},{16,12},{20,16},{24,20},{28,24},{0,28},{5,1},{9... | collective-permute-start | bytes 196616 | tf_op jit(solution)/shard_map/ppermute | solution.py:18
  29.9 3.4 %collective-permute-start.10 = (bf16[32,4,1,128]{3,0,2,1:T(8,128)(2,1)S(1)}, bf16[32,4,1,128]{3,0,2,1:T(8,128)(2,1)S(1)}, u32[]{:S(2)}, u32[]{:S(2)}) collective-permute-start(bf16[32,4,1,128]{3,0,2,1:T(8,128)(2,1)S(1)} %get-tuple-element.30), channel_id=1, source_target_pairs={{0,1},{1,2},{2,3},{3,0},{4,5},{5,6},{6,7},{7,4},{8,9},{9,10},{10,1... | collective-permute-start | bytes 98312 | tf_op jit(solution)/shard_map/ppermute | solution.py:15
  30.0 3.3 %collective-permute-start.9 = (bf16[32,4,1,128]{3,0,2,1:T(8,128)(2,1)S(1)}, bf16[32,4,1,128]{3,0,2,1:T(8,128)(2,1)S(1)}, u32[]{:S(2)}, u32[]{:S(2)}) collective-permute-start(bf16[32,4,1,128]{3,0,2,1:T(8,128)(2,1)S(1)} %get-tuple-element.31), channel_id=1, source_target_pairs={{1,0},{2,1},{3,2},{0,3},{5,4},{6,5},{7,6},{4,7},{9,8},{10,9},{11,1... | collective-permute-start | bytes 98312 | tf_op jit(solution)/shard_map/ppermute | solution.py:18
  34.8 13.6 %copy-start.2 = (bf16[3,3,3,32,32]{4,3,2,1,0:T(8,128)(2,1)S(1)}, bf16[3,3,3,32,32]{4,3,2,1,0:T(8,128)(2,1)}, u32[]{:S(2)}) copy-start(bf16[3,3,3,32,32]{4,3,2,1,0:T(8,128)(2,1)} %param.12) | copy-start | bytes 165892
  35.2 2.0 %collective-permute-start.11 = (f32[224,128]{1,0:T(8,128)S(1)}, f32[224,128]{1,0:T(8,128)S(1)}, u32[]{:S(2)}, u32[]{:S(2)}) collective-permute-start(f32[224,128]{1,0:T(8,128)S(1)} %constant_dynamic-slice_fusion), channel_id=1, source_target_pairs={{0,1},{1,0},{2,3},{3,2},{4,5},{5,4},{6,7},{7,6},{8,9},{9,8},{10,11... | collective-permute-start | bytes 344072 | tf_op jit(solution)/shard_map/ppermute | solution.py:66
  37.2 5.5 %collective-permute-start.12 = (f32[224,128]{1,0:T(8,128)S(1)}, f32[224,128]{1,0:T(8,128)S(1)}, u32[]{:S(2)}, u32[]{:S(2)}) collective-permute-start(f32[224,128]{1,0:T(8,128)S(1)} %dynamic-slice_add_fusion), channel_id=1, source_target_pairs={{0,2},{1,3},{2,0},{3,1},{4,6},{5,7},{6,4},{7,5},{8,10},{9,11},{10,... | collective-permute-start | bytes 344072 | tf_op jit(solution)/shard_map/ppermute | solution.py:76
  42.7 4.9 %collective-permute-start.13 = (f32[224,128]{1,0:T(8,128)S(1)}, f32[224,128]{1,0:T(8,128)S(1)}, u32[]{:S(2)}, u32[]{:S(2)}) collective-permute-start(f32[224,128]{1,0:T(8,128)S(1)} %add.118), channel_id=1, source_target_pairs={{0,4},{1,5},{2,6},{3,7},{4,0},{5,1},{6,2},{7,3},{8,12},{9,13},{10,... | collective-permute-start | bytes 344072 | tf_op jit(solution)/shard_map/ppermute | solution.py:76
  47.6 4.9 %collective-permute-start.14 = (f32[224,128]{1,0:T(8,128)S(1)}, f32[224,128]{1,0:T(8,128)S(1)}, u32[]{:S(2)}, u32[]{:S(2)}) collective-permute-start(f32[224,128]{1,0:T(8,128)S(1)} %add.119), channel_id=1, source_target_pairs={{0,8},{1,9},{2,10},{3,11},{4,12},{5,13},{6,14},{7,15},{8,0},{9,1},... | collective-permute-start | bytes 344072 | tf_op jit(solution)/shard_map/ppermute | solution.py:76
  52.5 7.0 %collective-permute-start.15 = (f32[224,128]{1,0:T(8,128)S(1)}, f32[224,128]{1,0:T(8,128)S(1)}, u32[]{:S(2)}, u32[]{:S(2)}) collective-permute-start(f32[224,128]{1,0:T(8,128)S(1)} %add.120), channel_id=1, source_target_pairs={{0,16},{1,17},{2,18},{3,19},{4,20},{5,21},{6,22},{7,23},{8,24},{9,... | collective-permute-start | bytes 344072 | tf_op jit(solution)/shard_map/ppermute | solution.py:76
  59.5 1.4 %collective-permute-start.16 = (f32[224,128]{1,0:T(8,128)S(1)}, f32[224,128]{1,0:T(8,128)S(1)}, u32[]{:S(2)}, u32[]{:S(2)}) collective-permute-start(f32[224,128]{1,0:T(8,128)S(1)} %add.121), channel_id=1, source_target_pairs={{0,1},{1,0},{2,3},{3,2},{4,5},{5,4},{6,7},{7,6},{8,9},{9,8},{10,11... | collective-permute-start | bytes 344072 | tf_op jit(solution)/shard_map/ppermute | solution.py:77
  (1 other events, 0.9 us)

commit v21 on v16

--- a/solution.py
+++ b/solution.py
@@ -193,7 +193,7 @@
     grad_bias = jnp.sum(head_grad.astype(jnp.float32), axis=(1, 2, 3)) * norm_factor
     back_second = jnp.einsum("oi,oxzy->ixzy", w_out, head_grad, preferred_element_type=jnp.float32)
     grad_second_pre = (back_second * silu_slope(second_wide)).astype(jnp.bfloat16)
-    second_padded = extended(grad_second_pre, (("sky", 1), ("los", 2)), 1)
+    second_padded = extended(grad_second_pre, (("los", 2), ("sky", 1)), 1)
     back_first = spread_local(w_second, second_padded, shape)
     grad_first_pre = (back_first * silu_slope(first_wide)).astype(jnp.bfloat16)
     first_padded = extended(grad_first_pre, (("sky", 1), ("los", 2)), 1)

time: 62.6 us -> 67.4 us (1.077)
  waiting for transfers between devices: 22.6 us -> 27.2 us
    ppermute x4, starting transfers between devices: 8.71 us -> 12.6 us  [extended(): lax.ppermute(lax.slice_in_dim(block, 0, width, axis=dim), axis, backward)]
    ppermute x4, starting transfers between devices: 3.19 us -> 0.29 us  [extended(): lax.ppermute(lax.slice_in_dim(block, block.shape[dim] - width, None, axis...]
    ppermute x4, waiting for transfers between devices: 6.27 us -> 8.41 us  [extended(): lax.ppermute(lax.slice_in_dim(block, block.shape[dim] - width, None, axis...]
    ppermute x4, waiting for transfers between devices: 1.2 us -> 2.74 us  [extended(): lax.ppermute(lax.slice_in_dim(block, 0, width, axis=dim), axis, backward)]
    ppermute x2, starting transfers between devices: 3.83 us -> 2.69 us  [split_sum(): lax.ppermute(keep, index_axes, [(i, i ^ bit) for i in range(total)])]
    ppermute x2, waiting for transfers between devices: 7.22 us -> 8.34 us  [split_sum(): lax.ppermute(keep, index_axes, [(i, i ^ bit) for i in range(total)])]
  transfers between devices with their start and end apart: 18 -> 18, of which waited for: 13 -> 12; matrix products, arithmetic and copies ran while one was open for 8% -> 7% of each run, Pallas kernels for 0% -> 0%
where the time goes in v21:
time: 67.4 us; the launch traced here: 67.2 us
  waiting for transfers between devices  27.2 us (40%)
  starting transfers between devices  23.6 us (35%)
  local copies, waits for them, and re-layouts  7.78 us (12%)
  matrix products  4.26 us (6%)
  other arithmetic  3.07 us (5%)
  between operations  1.26 us (2%)
    ppermute x4, starting transfers between devices, extended(): lax.ppermute(lax.slice_in_dim(block, 0, width, axis=dim), axis, backward)  12.6 us
    ppermute x4, waiting for transfers between devices, extended(): lax.ppermute(lax.slice_in_dim(block, block.shape[dim] - width, None, axis...  8.41 us
    ppermute x2, waiting for transfers between devices, split_sum(): lax.ppermute(keep, index_axes, [(i, i ^ bit) for i in range(total)])  8.34 us
    ppermute x3, waiting for transfers between devices, split_sum(): lax.ppermute(keep, index_axes, [(i, i ^ mask) for i in range(total)])  5.08 us
    ppermute x3, starting transfers between devices, split_sum(): lax.ppermute(keep, index_axes, [(i, i ^ mask) for i in range(total)])  3.57 us
    ppermute x3, starting transfers between devices, quad_sum(): lax.ppermute(value, axis, [(i, i ^ mask) for i in range(count)])  3.15 us
    ppermute x4, waiting for transfers between devices, extended(): lax.ppermute(lax.slice_in_dim(block, 0, width, axis=dim), axis, backward)  2.74 us
    ppermute x2, starting transfers between devices, split_sum(): lax.ppermute(keep, index_axes, [(i, i ^ bit) for i in range(total)])  2.69 us
  transfers between devices with their start and end apart: 18, of which 12 were waited for; matrix products, arithmetic and copies ran while one was open for 7% of the time, Pallas kernels for 0%

profile of v21, /device:TPU:0, one launch (start us, length us, event | category | flops | bytes accessed | tf_op | source)
XLA Modules:
  0.0 67.2 jit_solution(1470207220073448484)
XLA Ops:
  0.7 1.0 %fusion.22 = bf16[32,2,8,128]{3,0,2,1:T(8,128)(2,1)S(1)} fusion(bf16[32,2,8,128]{3,2,1,0:T(8,128)(2,1)} %param.11), kind=kLoop, calls=%fused_computation.38 | loop fusion | flops 393216 | bytes 262144 | tf_op jit(solution)/shard_map/convert_element_type | solution.py:167
  3.8 2.6 %collective-permute-start.1 = (f32[2,2,128]{2,1,0:T(2,128)S(1)}, f32[2,2,128]{2,1,0:T(2,128)S(1)}, u32[]{:S(2)}, u32[]{:S(2)}) collective-permute-start(f32[2,2,128]{2,1,0:T(2,128)S(1)} %pad_maximum_fusion.12), channel_id=1, source_target_pairs={{0,2},{1,3},{2,0},{3,1},{4,6},{5,7},{6,4},{7,5},{8,10},{9,11},{10,... | collective-permute-start | bytes 6152 | tf_op jit(solution)/shard_map/ppermute | solution.py:47
  6.5 1.1 %fusion.89 = (bf16[32,2,8,1]{3,2,1,0:T(8,128)(2,1)S(1)}, bf16[32,2,8,1]{3,2,1,0:T(8,128)(2,1)S(1)}) fusion(bf16[32,2,8,128]{3,2,1,0:T(8,128)(2,1)} %param.9), kind=kLoop, calls=%fused_computation.168 | loop fusion | bytes 4096 | tf_op jit(solution)/shard_map/jit(_roll_static)/slice | solution.py:150
  8.1 1.3 %collective-permute-done.2 = f32[2,2,128]{2,1,0:T(2,128)S(1)} collective-permute-done((f32[2,2,128]{2,1,0:T(2,128)S(1)}, f32[2,2,128]{2,1,0:T(2,128)S(1)}, u32[]{:S(2)}, u32[]{:S(2)}) %collective-permute-start.2) | collective-permute-done | bytes 2080 | tf_op jit(solution)/shard_map/ppermute | solution.py:47
  10.1 1.6 %collective-permute-start.4 = (bf16[32,2,1,128]{3,0,2,1:T(8,128)(2,1)S(1)}, bf16[32,2,1,128]{3,0,2,1:T(8,128)(2,1)S(1)}, u32[]{:S(2)}, u32[]{:S(2)}) collective-permute-start(bf16[32,2,1,128]{3,0,2,1:T(8,128)(2,1)S(1)} %get-tuple-element.51), channel_id=1, source_target_pairs={{1,0},{2,1},{3,2},{0,3},{5,4},{6,5},{7,6},{4,7},{9,8},{10,9},{11,1... | collective-permute-start | bytes 49160 | tf_op jit(solution)/shard_map/ppermute | solution.py:18
  11.8 1.3 %collective-permute-done.3 = bf16[32,2,1,128]{3,0,2,1:T(8,128)(2,1)S(1)} collective-permute-done((bf16[32,2,1,128]{3,0,2,1:T(8,128)(2,1)S(1)}, bf16[32,2,1,128]{3,0,2,1:T(8,128)(2,1)S(1)}, u32[]{:S(2)}, u32[]{:S(2)}) %collective-permute-start.3) | collective-permute-done | bytes 16416 | tf_op jit(solution)/shard_map/ppermute | solution.py:15
  13.2 4.6 %collective-permute-start.5 = (bf16[32,1,10,128]{3,0,2,1:T(8,128)(2,1)S(1)}, bf16[32,1,10,128]{3,0,2,1:T(8,128)(2,1)S(1)}, u32[]{:S(2)}, u32[]{:S(2)}) collective-permute-start(bf16[32,1,10,128]{3,0,2,1:T(8,128)(2,1)S(1)} %get-tuple-element.37), channel_id=1, source_target_pairs={{4,0},{8,4},{12,8},{16,12},{20,16},{24,20},{28,24},{0,28},{5,1},{9... | collective-permute-start | bytes 245768 | tf_op jit(solution)/shard_map/ppermute | solution.py:18
  17.8 2.7 %collective-permute-done.5 = bf16[32,1,10,128]{3,0,2,1:T(8,128)(2,1)S(1)} collective-permute-done((bf16[32,1,10,128]{3,0,2,1:T(8,128)(2,1)S(1)}, bf16[32,1,10,128]{3,0,2,1:T(8,128)(2,1)S(1)}, u32[]{:S(2)}, u32[]{:S(2)}) %collective-permute-start.5) | collective-permute-done | bytes 81952 | tf_op jit(solution)/shard_map/ppermute | solution.py:18
  20.5 4.9 %collective-permute-done.6 = bf16[32,1,10,128]{3,0,2,1:T(8,128)(2,1)S(1)} collective-permute-done((bf16[32,1,10,128]{3,0,2,1:T(8,128)(2,1)S(1)}, bf16[32,1,10,128]{3,0,2,1:T(8,128)(2,1)S(1)}, u32[]{:S(2)}, u32[]{:S(2)}) %collective-permute-start.6) | collective-permute-done | bytes 81952 | tf_op jit(solution)/shard_map/ppermute | solution.py:15
  27.7 4.7 %collective-permute-start.8 = (bf16[32,1,8,128]{3,0,2,1:T(8,128)(2,1)S(1)}, bf16[32,1,8,128]{3,0,2,1:T(8,128)(2,1)S(1)}, u32[]{:S(2)}, u32[]{:S(2)}) collective-permute-start(bf16[32,1,8,128]{3,0,2,1:T(8,128)(2,1)S(1)} %get-tuple-element.49), channel_id=1, source_target_pairs={{4,0},{8,4},{12,8},{16,12},{20,16},{24,20},{28,24},{0,28},{5,1},{9... | collective-permute-start | bytes 196616 | tf_op jit(solution)/shard_map/ppermute | solution.py:18
  32.6 2.0 %collective-permute-done.7 = bf16[32,1,8,128]{3,0,2,1:T(8,128)(2,1)S(1)} collective-permute-done((bf16[32,1,8,128]{3,0,2,1:T(8,128)(2,1)S(1)}, bf16[32,1,8,128]{3,0,2,1:T(8,128)(2,1)S(1)}, u32[]{:S(2)}, u32[]{:S(2)}) %collective-permute-start.7) | collective-permute-done | bytes 65568 | tf_op jit(solution)/shard_map/ppermute | solution.py:15
  34.7 1.7 %collective-permute-start.9 = (bf16[32,4,1,128]{3,0,2,1:T(8,128)(2,1)S(1)}, bf16[32,4,1,128]{3,0,2,1:T(8,128)(2,1)S(1)}, u32[]{:S(2)}, u32[]{:S(2)}) collective-permute-start(bf16[32,4,1,128]{3,0,2,1:T(8,128)(2,1)S(1)} %get-tuple-element.31), channel_id=1, source_target_pairs={{1,0},{2,1},{3,2},{0,3},{5,4},{6,5},{7,6},{4,7},{9,8},{10,9},{11,1... | collective-permute-start | bytes 98312 | tf_op jit(solution)/shard_map/ppermute | solution.py:18
  36.4 1.1 %fusion.1 = f32[9,3,32,32]{2,3,0,1:T(8,128)S(1)} fusion(bf16[9,32,2,8,128]{4,1,3,2,0:T(8,128)(2,1)S(1)} %fusion.50, bf16[1,32,2,8,128]{4,1,3,2,0:T(8,128)(2,1)S(1)} %maximum_bitcast_fusion.7, bf16[1,32,2,8,128]{4,1,3,2,0:T(8,128)(2,1)S(1)} %bitcast.252, bf16[1,32,2,8,128]{4,1,3,2,0:T(8,128)(2,1)S(1)} %maximum_bitcast_fusion.6), kind=kOutput, calls=%fused_computation.4 | convolution fusion | flops 114453504 | bytes 1683456 | tf_op jit(solution)/shard_map/toxzy,sixzy->tsoi/dot_general | solution.py:151
  38.3 1.1 %fusion.3 = f32[9,3,32,32]{2,3,0,1:T(8,128)S(1)} fusion(bf16[1,32,2,8,128]{4,1,3,2,0:T(8,128)(2,1)S(1)} %get-tuple-element.60, bf16[1,32,2,8,128]{4,1,3,2,0:T(8,128)(2,1)S(1)} %bitcast.258, bf16[1,32,2,8,128]{4,1,3,2,0:T(8,128)(2,1)S(1)} %get-tuple-element.59, bf16[9,32,2,8,128]{4,1,3,2,0:T(8,128)(2,1)S(1)} %fusion.40), kind=kOutput, calls=%fused_computation.7 | convolution fusion | flops 114453504 | bytes 1683456 | tf_op jit(solution)/shard_map/toxzy,sixzy->tsoi/dot_general | solution.py:151
  39.9 1.2 %collective-permute-start.11 = (f32[224,128]{1,0:T(8,128)S(1)}, f32[224,128]{1,0:T(8,128)S(1)}, u32[]{:S(2)}, u32[]{:S(2)}) collective-permute-start(f32[224,128]{1,0:T(8,128)S(1)} %constant_dynamic-slice_fusion), channel_id=1, source_target_pairs={{0,1},{1,0},{2,3},{3,2},{4,5},{5,4},{6,7},{7,6},{8,9},{9,8},{10,11... | collective-permute-start | bytes 344072 | tf_op jit(solution)/shard_map/ppermute | solution.py:66
  41.1 1.0 %collective-permute-done.11 = f32[224,128]{1,0:T(8,128)S(1)} collective-permute-done((f32[224,128]{1,0:T(8,128)S(1)}, f32[224,128]{1,0:T(8,128)S(1)}, u32[]{:S(2)}, u32[]{:S(2)}) %collective-permute-start.11) | collective-permute-done | bytes 114720 | tf_op jit(solution)/shard_map/ppermute | solution.py:66
  42.1 1.1 %collective-permute-start.12 = (f32[224,128]{1,0:T(8,128)S(1)}, f32[224,128]{1,0:T(8,128)S(1)}, u32[]{:S(2)}, u32[]{:S(2)}) collective-permute-start(f32[224,128]{1,0:T(8,128)S(1)} %dynamic-slice_add_fusion), channel_id=1, source_target_pairs={{0,2},{1,3},{2,0},{3,1},{4,6},{5,7},{6,4},{7,5},{8,10},{9,11},{10,... | collective-permute-start | bytes 344072 | tf_op jit(solution)/shard_map/ppermute | solution.py:70
  43.2 2.5 %collective-permute-start.14 = (f32[224,128]{1,0:T(8,128)S(1)}, f32[224,128]{1,0:T(8,128)S(1)}, u32[]{:S(2)}, u32[]{:S(2)}) collective-permute-start(f32[224,128]{1,0:T(8,128)S(1)} %dynamic-slice_add_fusion), channel_id=1, source_target_pairs={{0,6},{1,7},{2,4},{3,5},{4,2},{5,3},{6,0},{7,1},{8,14},{9,15},{10,... | collective-permute-start | bytes 344072 | tf_op jit(solution)/shard_map/ppermute | solution.py:70
  45.7 2.4 %collective-permute-done.12 = f32[224,128]{1,0:T(8,128)S(1)} collective-permute-done((f32[224,128]{1,0:T(8,128)S(1)}, f32[224,128]{1,0:T(8,128)S(1)}, u32[]{:S(2)}, u32[]{:S(2)}) %collective-permute-start.12) | collective-permute-done | bytes 114720 | tf_op jit(solution)/shard_map/ppermute | solution.py:70
  48.1 2.6 %collective-permute-done.13 = f32[224,128]{1,0:T(8,128)S(1)} collective-permute-done((f32[224,128]{1,0:T(8,128)S(1)}, f32[224,128]{1,0:T(8,128)S(1)}, u32[]{:S(2)}, u32[]{:S(2)}) %collective-permute-start.13) | collective-permute-done | bytes 114720 | tf_op jit(solution)/shard_map/ppermute | solution.py:70
  51.4 4.3 %collective-permute-done.15 = f32[224,128]{1,0:T(8,128)S(1)} collective-permute-done((f32[224,128]{1,0:T(8,128)S(1)}, f32[224,128]{1,0:T(8,128)S(1)}, u32[]{:S(2)}, u32[]{:S(2)}) %collective-permute-start.15) | collective-permute-done | bytes 114720 | tf_op jit(solution)/shard_map/ppermute | solution.py:76
  55.7 2.6 %collective-permute-start.16 = (f32[224,128]{1,0:T(8,128)S(1)}, f32[224,128]{1,0:T(8,128)S(1)}, u32[]{:S(2)}, u32[]{:S(2)}) collective-permute-start(f32[224,128]{1,0:T(8,128)S(1)} %add.124), channel_id=1, source_target_pairs={{0,16},{1,17},{2,18},{3,19},{4,20},{5,21},{6,22},{7,23},{8,24},{9,... | collective-permute-start | bytes 344072 | tf_op jit(solution)/shard_map/ppermute | solution.py:76
  58.6 4.1 %collective-permute-done.16 = f32[224,128]{1,0:T(8,128)S(1)} collective-permute-done((f32[224,128]{1,0:T(8,128)S(1)}, f32[224,128]{1,0:T(8,128)S(1)}, u32[]{:S(2)}, u32[]{:S(2)}) %collective-permute-start.16) | collective-permute-done | bytes 114720 | tf_op jit(solution)/shard_map/ppermute | solution.py:76
  64.7 0.9 %reshape.78 = f32[3,3,3,32,32]{4,3,2,1,0:T(8,128)} reshape(f32[216,128]{1,0:T(8,128)S(1)} %get-tuple-element.33) | data formatting | bytes 221184 | tf_op jit(solution)/shard_map/reshape | solution.py:110
  (113 shorter events, 11.6 us)
Async XLA Ops:
  0.6 25.1 %copy-start = (bf16[3,3,3,32,32]{4,3,2,1,0:T(8,128)(2,1)S(1)}, bf16[3,3,3,32,32]{4,3,2,1,0:T(8,128)(2,1)}, u32[]{:S(2)}) copy-start(bf16[3,3,3,32,32]{4,3,2,1,0:T(8,128)(2,1)} %param.13) | copy-start | bytes 165892
  0.6 6.9 %copy-start.1 = (bf16[32,2,8,128]{3,2,1,0:T(8,128)(2,1)S(1)}, bf16[32,2,8,128]{3,2,1,0:T(8,128)(2,1)}, u32[]{:S(2)}) copy-start(bf16[32,2,8,128]{3,2,1,0:T(8,128)(2,1)} %param.9) | copy-start | bytes 393220
  3.3 4.8 %collective-permute-start = (f32[2,2,128]{2,1,0:T(2,128)S(1)}, f32[2,2,128]{2,1,0:T(2,128)S(1)}, u32[]{:S(2)}, u32[]{:S(2)}) collective-permute-start(f32[2,2,128]{2,1,0:T(2,128)S(1)} %pad_maximum_fusion.12), channel_id=1, source_target_pairs={{0,1},{1,0},{2,3},{3,2},{4,5},{5,4},{6,7},{7,6},{8,9},{9,8},{10,11... | collective-permute-start | bytes 6152 | tf_op jit(solution)/shard_map/ppermute | solution.py:47
  3.8 4.3 %collective-permute-start.1 = (f32[2,2,128]{2,1,0:T(2,128)S(1)}, f32[2,2,128]{2,1,0:T(2,128)S(1)}, u32[]{:S(2)}, u32[]{:S(2)}) collective-permute-start(f32[2,2,128]{2,1,0:T(2,128)S(1)} %pad_maximum_fusion.12), channel_id=1, source_target_pairs={{0,2},{1,3},{2,0},{3,1},{4,6},{5,7},{6,4},{7,5},{8,10},{9,11},{10,... | collective-permute-start | bytes 6152 | tf_op jit(solution)/shard_map/ppermute | solution.py:47
  6.4 3.0 %collective-permute-start.2 = (f32[2,2,128]{2,1,0:T(2,128)S(1)}, f32[2,2,128]{2,1,0:T(2,128)S(1)}, u32[]{:S(2)}, u32[]{:S(2)}) collective-permute-start(f32[2,2,128]{2,1,0:T(2,128)S(1)} %pad_maximum_fusion.12), channel_id=1, source_target_pairs={{0,3},{1,2},{2,1},{3,0},{4,7},{5,6},{6,5},{7,4},{8,11},{9,10},{10,... | collective-permute-start | bytes 6152 | tf_op jit(solution)/shard_map/ppermute | solution.py:47
  7.7 1.7 %copy-start.6 = (f32[2,128]{1,0:T(2,128)S(1)}, f32[2,128]{1,0:T(2,128)}, u32[]{:S(2)}) copy-start(f32[2,128]{1,0:T(2,128)} %param.16) | copy-start | bytes 3076
  7.7 1.9 %copy-start.3 = (bf16[32,2,8,128]{3,2,1,0:T(8,128)(2,1)S(1)}, bf16[32,2,8,128]{3,2,1,0:T(8,128)(2,1)}, u32[]{:S(2)}) copy-start(bf16[32,2,8,128]{3,2,1,0:T(8,128)(2,1)} %param.11) | copy-start | bytes 393220
  7.7 1.9 %copy-start.5 = (bf16[3,32]{1,0:T(4,128)(2,1)S(1)}, bf16[3,32]{1,0:T(4,128)(2,1)}, u32[]{:S(2)}) copy-start(bf16[3,32]{1,0:T(4,128)(2,1)} %param.14) | copy-start | bytes 580
  10.0 3.2 %collective-permute-start.3 = (bf16[32,2,1,128]{3,0,2,1:T(8,128)(2,1)S(1)}, bf16[32,2,1,128]{3,0,2,1:T(8,128)(2,1)S(1)}, u32[]{:S(2)}, u32[]{:S(2)}) collective-permute-start(bf16[32,2,1,128]{3,0,2,1:T(8,128)(2,1)S(1)} %get-tuple-element.50), channel_id=1, source_target_pairs={{0,1},{1,2},{2,3},{3,0},{4,5},{5,6},{6,7},{7,4},{8,9},{9,10},{10,1... | collective-permute-start | bytes 49160 | tf_op jit(solution)/shard_map/ppermute | solution.py:15
  10.1 3.0 %collective-permute-start.4 = (bf16[32,2,1,128]{3,0,2,1:T(8,128)(2,1)S(1)}, bf16[32,2,1,128]{3,0,2,1:T(8,128)(2,1)S(1)}, u32[]{:S(2)}, u32[]{:S(2)}) collective-permute-start(bf16[32,2,1,128]{3,0,2,1:T(8,128)(2,1)S(1)} %get-tuple-element.51), channel_id=1, source_target_pairs={{1,0},{2,1},{3,2},{0,3},{5,4},{6,5},{7,6},{4,7},{9,8},{10,9},{11,1... | collective-permute-start | bytes 49160 | tf_op jit(solution)/shard_map/ppermute | solution.py:18
  13.2 7.3 %collective-permute-start.5 = (bf16[32,1,10,128]{3,0,2,1:T(8,128)(2,1)S(1)}, bf16[32,1,10,128]{3,0,2,1:T(8,128)(2,1)S(1)}, u32[]{:S(2)}, u32[]{:S(2)}) collective-permute-start(bf16[32,1,10,128]{3,0,2,1:T(8,128)(2,1)S(1)} %get-tuple-element.37), channel_id=1, source_target_pairs={{4,0},{8,4},{12,8},{16,12},{20,16},{24,20},{28,24},{0,28},{5,1},{9... | collective-permute-start | bytes 245768 | tf_op jit(solution)/shard_map/ppermute | solution.py:18
  17.8 7.6 %collective-permute-start.6 = (bf16[32,1,10,128]{3,0,2,1:T(8,128)(2,1)S(1)}, bf16[32,1,10,128]{3,0,2,1:T(8,128)(2,1)S(1)}, u32[]{:S(2)}, u32[]{:S(2)}) collective-permute-start(bf16[32,1,10,128]{3,0,2,1:T(8,128)(2,1)S(1)} %get-tuple-element.36), channel_id=1, source_target_pairs={{0,4},{4,8},{8,12},{12,16},{16,20},{20,24},{24,28},{28,0},{1,5},{5... | collective-permute-start | bytes 245768 | tf_op jit(solution)/shard_map/ppermute | solution.py:15
  27.6 7.0 %collective-permute-start.7 = (bf16[32,1,8,128]{3,0,2,1:T(8,128)(2,1)S(1)}, bf16[32,1,8,128]{3,0,2,1:T(8,128)(2,1)S(1)}, u32[]{:S(2)}, u32[]{:S(2)}) collective-permute-start(bf16[32,1,8,128]{3,0,2,1:T(8,128)(2,1)S(1)} %get-tuple-element.48), channel_id=1, source_target_pairs={{0,4},{4,8},{8,12},{12,16},{16,20},{20,24},{24,28},{28,0},{1,5},{5... | collective-permute-start | bytes 196616 | tf_op jit(solution)/shard_map/ppermute | solution.py:15
  27.7 7.0 %collective-permute-start.8 = (bf16[32,1,8,128]{3,0,2,1:T(8,128)(2,1)S(1)}, bf16[32,1,8,128]{3,0,2,1:T(8,128)(2,1)S(1)}, u32[]{:S(2)}, u32[]{:S(2)}) collective-permute-start(bf16[32,1,8,128]{3,0,2,1:T(8,128)(2,1)S(1)} %get-tuple-element.49), channel_id=1, source_target_pairs={{4,0},{8,4},{12,8},{16,12},{20,16},{24,20},{28,24},{0,28},{5,1},{9... | collective-permute-start | bytes 196616 | tf_op jit(solution)/shard_map/ppermute | solution.py:18
  34.6 3.4 %collective-permute-start.10 = (bf16[32,4,1,128]{3,0,2,1:T(8,128)(2,1)S(1)}, bf16[32,4,1,128]{3,0,2,1:T(8,128)(2,1)S(1)}, u32[]{:S(2)}, u32[]{:S(2)}) collective-permute-start(bf16[32,4,1,128]{3,0,2,1:T(8,128)(2,1)S(1)} %get-tuple-element.30), channel_id=1, source_target_pairs={{0,1},{1,2},{2,3},{3,0},{4,5},{5,6},{6,7},{7,4},{8,9},{9,10},{10,1... | collective-permute-start | bytes 98312 | tf_op jit(solution)/shard_map/ppermute | solution.py:15
  34.7 3.3 %collective-permute-start.9 = (bf16[32,4,1,128]{3,0,2,1:T(8,128)(2,1)S(1)}, bf16[32,4,1,128]{3,0,2,1:T(8,128)(2,1)S(1)}, u32[]{:S(2)}, u32[]{:S(2)}) collective-permute-start(bf16[32,4,1,128]{3,0,2,1:T(8,128)(2,1)S(1)} %get-tuple-element.31), channel_id=1, source_target_pairs={{1,0},{2,1},{3,2},{0,3},{5,4},{6,5},{7,6},{4,7},{9,8},{10,9},{11,1... | collective-permute-start | bytes 98312 | tf_op jit(solution)/shard_map/ppermute | solution.py:18
  39.6 11.3 %copy-start.2 = (bf16[3,3,3,32,32]{4,3,2,1,0:T(8,128)(2,1)S(1)}, bf16[3,3,3,32,32]{4,3,2,1,0:T(8,128)(2,1)}, u32[]{:S(2)}) copy-start(bf16[3,3,3,32,32]{4,3,2,1,0:T(8,128)(2,1)} %param.12) | copy-start | bytes 165892
  39.9 2.2 %collective-permute-start.11 = (f32[224,128]{1,0:T(8,128)S(1)}, f32[224,128]{1,0:T(8,128)S(1)}, u32[]{:S(2)}, u32[]{:S(2)}) collective-permute-start(f32[224,128]{1,0:T(8,128)S(1)} %constant_dynamic-slice_fusion), channel_id=1, source_target_pairs={{0,1},{1,0},{2,3},{3,2},{4,5},{5,4},{6,7},{7,6},{8,9},{9,8},{10,11... | collective-permute-start | bytes 344072 | tf_op jit(solution)/shard_map/ppermute | solution.py:66
  42.1 6.0 %collective-permute-start.12 = (f32[224,128]{1,0:T(8,128)S(1)}, f32[224,128]{1,0:T(8,128)S(1)}, u32[]{:S(2)}, u32[]{:S(2)}) collective-permute-start(f32[224,128]{1,0:T(8,128)S(1)} %dynamic-slice_add_fusion), channel_id=1, source_target_pairs={{0,2},{1,3},{2,0},{3,1},{4,6},{5,7},{6,4},{7,5},{8,10},{9,11},{10,... | collective-permute-start | bytes 344072 | tf_op jit(solution)/shard_map/ppermute | solution.py:70
  43.2 7.6 %collective-permute-start.13 = (f32[224,128]{1,0:T(8,128)S(1)}, f32[224,128]{1,0:T(8,128)S(1)}, u32[]{:S(2)}, u32[]{:S(2)}) collective-permute-start(f32[224,128]{1,0:T(8,128)S(1)} %dynamic-slice_add_fusion), channel_id=1, source_target_pairs={{0,4},{1,5},{2,6},{3,7},{4,0},{5,1},{6,2},{7,3},{8,12},{9,13},{10,... | collective-permute-start | bytes 344072 | tf_op jit(solution)/shard_map/ppermute | solution.py:70
  43.2 7.6 %collective-permute-start.14 = (f32[224,128]{1,0:T(8,128)S(1)}, f32[224,128]{1,0:T(8,128)S(1)}, u32[]{:S(2)}, u32[]{:S(2)}) collective-permute-start(f32[224,128]{1,0:T(8,128)S(1)} %dynamic-slice_add_fusion), channel_id=1, source_target_pairs={{0,6},{1,7},{2,4},{3,5},{4,2},{5,3},{6,0},{7,1},{8,14},{9,15},{10,... | collective-permute-start | bytes 344072 | tf_op jit(solution)/shard_map/ppermute | solution.py:70
  50.8 4.9 %collective-permute-start.15 = (f32[224,128]{1,0:T(8,128)S(1)}, f32[224,128]{1,0:T(8,128)S(1)}, u32[]{:S(2)}, u32[]{:S(2)}) collective-permute-start(f32[224,128]{1,0:T(8,128)S(1)} %add_add_fusion), channel_id=1, source_target_pairs={{0,8},{1,9},{2,10},{3,11},{4,12},{5,13},{6,14},{7,15},{8,0},{9,1},... | collective-permute-start | bytes 344072 | tf_op jit(solution)/shard_map/ppermute | solution.py:76
  55.7 7.0 %collective-permute-start.16 = (f32[224,128]{1,0:T(8,128)S(1)}, f32[224,128]{1,0:T(8,128)S(1)}, u32[]{:S(2)}, u32[]{:S(2)}) collective-permute-start(f32[224,128]{1,0:T(8,128)S(1)} %add.124), channel_id=1, source_target_pairs={{0,16},{1,17},{2,18},{3,19},{4,20},{5,21},{6,22},{7,23},{8,24},{9,... | collective-permute-start | bytes 344072 | tf_op jit(solution)/shard_map/ppermute | solution.py:76
  62.7 1.4 %collective-permute-start.17 = (f32[224,128]{1,0:T(8,128)S(1)}, f32[224,128]{1,0:T(8,128)S(1)}, u32[]{:S(2)}, u32[]{:S(2)}) collective-permute-start(f32[224,128]{1,0:T(8,128)S(1)} %add.125), channel_id=1, source_target_pairs={{0,1},{1,0},{2,3},{3,2},{4,5},{5,4},{6,7},{7,6},{8,9},{9,8},{10,11... | collective-permute-start | bytes 344072 | tf_op jit(solution)/shard_map/ppermute | solution.py:77
  (2 other events, 2.6 us)
